TPU v7x, 32 devices: a whole 2x2x4 slice. The times are simulated.
32 devices in a mesh: outer: 4 (over y, x), inner: 8 (over z, core).
Axes of the slice: x: 2, y: 2, z: 4, core: 2. Of those that a mesh axis runs over, the one named last changes fastest.
Arguments:
- tokens: bfloat16 [12288, 1024], P(('outer', 'inner')), may hold values from -6 to 6
- log_decay: float32 [12288, 16], P(('outer', 'inner')), may hold values from -1 to 0, as said below
- query_weight: bfloat16 [1024, 1024], replicated, may hold values from -0.1875 to 0.1875
- key_weight: bfloat16 [1024, 1024], replicated, may hold values from -0.1875 to 0.1875
- value_weight: bfloat16 [1024, 1024], replicated, may hold values from -0.1875 to 0.1875
- norm_gain: float32 [1024], replicated, may hold values from 0.1 to 1.9
- output_weight: bfloat16 [1024, 1024], replicated, may hold values from -0.1875 to 0.1875
Outputs:
- mixed: bfloat16 [12288, 1024], P(('outer', 'inner'))
Inputs may be any that keep to these rules, and one draw needn't show every extreme that they name: log_decay is negative.
All inputs are finite; a program needn't handle non-finite values.
Results may differ from a plain program's by a relative error of at most 0.0063.
Values sent between devices are 32-bit elements; how exact they have to be, the bound alone decides.
No kernel may reach another device: no remote copies, remote signals or barrier semaphores. Data moves between devices by JAX's collectives and lax.ppermute only.
A program may use at most 320 MiB of HBM per device.

v0:
```python
import jax
import jax.numpy as jnp
from jax import lax
from jax.sharding import PartitionSpec as P


def prefix(value, axis, join, neutral):
    count, mine = (lax.axis_size(axis), lax.axis_index(axis))
    pieces = jax.tree.map(lambda part: lax.all_gather(part, axis), value)
    running = jax.tree.map(
        lambda part, zero: jnp.full_like(part, 0) + jnp.asarray(zero, part.dtype), value, neutral
    )

    def lap(position, running):
        longer = join(running, jax.tree.map(lambda part: part[position], pieces))
        return jax.tree.map(lambda new, old: jnp.where(position < mine, new, old), longer, running)

    return lax.fori_loop(0, count - 1, lap, running)


def broadcast(value, axis, source):
    kept = jnp.where(lax.axis_index(axis) == source, value, 0).astype(value.dtype)
    return lax.psum(kept, axis)


def local_head(q_head, k_head, v_head, g_head):
    cum = jnp.cumsum(g_head)
    count = cum.shape[0]
    rows = lax.broadcasted_iota(jnp.int32, (count, count), 0)
    cols = lax.broadcasted_iota(jnp.int32, (count, count), 1)
    lower = cols <= rows
    diff = jnp.where(lower, cum[:, None] - cum[None, :], 0.0)
    decay = jnp.where(lower, jnp.exp(diff), 0.0)
    scores = jnp.dot(q_head, k_head.T, preferred_element_type=jnp.float32)
    weights = (scores * decay).astype(jnp.bfloat16)
    intra = jnp.dot(weights, v_head, preferred_element_type=jnp.float32)
    last = cum[-1]
    scaled = (k_head.astype(jnp.float32) * jnp.exp(last - cum)[:, None]).astype(jnp.bfloat16)
    local = jnp.dot(scaled.T, v_head, preferred_element_type=jnp.float32)
    return (intra, local, jnp.exp(last))


def combine(earlier, later):
    return (earlier[0] * later[0], later[0][:, None, None] * earlier[1] + later[1])


def shards(tokens, log_decay, query_weight, key_weight, value_weight, norm_gain, output_weight):
    count = tokens.shape[0]
    heads = log_decay.shape[1]
    queries = jax.nn.silu(jnp.dot(tokens, query_weight, preferred_element_type=jnp.float32)).astype(
        jnp.bfloat16
    )
    keys = jax.nn.silu(jnp.dot(tokens, key_weight, preferred_element_type=jnp.float32)).astype(
        jnp.bfloat16
    )
    value_rows = jnp.dot(tokens, value_weight, preferred_element_type=jnp.float32).astype(
        jnp.bfloat16
    )
    split = lambda arr: arr.reshape(count, heads, -1).transpose(1, 0, 2)
    queries, keys, value_rows = (split(queries), split(keys), split(value_rows))
    intra, local, fall = lax.map(
        lambda token_parts: local_head(*token_parts), (queries, keys, value_rows, log_decay.T)
    )
    own = (fall, local)
    identity = (jnp.ones_like(fall), jnp.zeros_like(local))
    inner_before = prefix(own, "inner", combine, identity)
    inclusive = combine(inner_before, own)
    total = (
        broadcast(inclusive[0], "inner", lax.axis_size("inner") - 1),
        broadcast(inclusive[1], "inner", lax.axis_size("inner") - 1),
    )
    outer_before = prefix(total, "outer", combine, identity)
    incoming = combine(outer_before, inner_before)[1]
    cum = jnp.cumsum(log_decay, axis=0)
    qfloat = queries.astype(jnp.float32)
    inter = (
        jnp.einsum("htd,hde->the", qfloat, incoming, precision=lax.Precision.HIGHEST)
        * jnp.exp(cum)[:, :, None]
    )
    attended = intra.transpose(1, 0, 2) + inter
    scale = lax.rsqrt(jnp.mean(attended * attended, axis=-1, keepdims=True) + 1e-05)
    normalized_output = ((attended * scale).reshape(count, -1) * norm_gain).astype(jnp.bfloat16)
    return jnp.dot(normalized_output, output_weight, preferred_element_type=jnp.float32).astype(
        jnp.bfloat16
    )


def solution(mesh):
    in_specs = (P(("outer", "inner"), None), P(("outer", "inner"), None), P(), P(), P(), P(), P())
    out_specs = P(("outer", "inner"), None)
    return jax.shard_map(shards, mesh=mesh, in_specs=in_specs, out_specs=out_specs, check_vma=False)
```

profile of v0, /device:TPU:0, one launch (start us, length us, event | category | flops | bytes accessed | tf_op | source)
XLA Modules:
  0.0 309.8 jit_solution(17604811757617093735)
XLA Ops:
  8.1 3.2 %multiply_convert_fusion.2 = bf16[384,1024]{1,0:T(8,128)(2,1)} fusion(bf16[384,1024]{1,0:T(8,128)(2,1)} %param.13, bf16[1024,1024]{1,0:T(8,128)(2,1)S(1)} %copy-done), kind=kOutput, calls=%fused_computation.48 | convolution fusion | flops 807272448 | bytes 3670016 | tf_op jit(solution)/shard_map/dot_general | solution.py:50
  12.8 3.9 %multiply_convert_fusion.1 = bf16[384,1024]{1,0:T(8,128)(2,1)} fusion(bf16[384,1024]{1,0:T(8,128)(2,1)} %param.13, bf16[1024,1024]{1,0:T(8,128)(2,1)} %param.16), kind=kOutput, calls=%fused_computation.47 | convolution fusion | flops 807272448 | bytes 3670016 | tf_op jit(solution)/shard_map/dot_general | solution.py:53
  16.6 2.3 copy.24
  18.9 3.7 %convolution_convert_fusion.1 = bf16[384,1024]{1,0:T(8,128)(2,1)} fusion(bf16[384,1024]{1,0:T(8,128)(2,1)} %param.13, bf16[1024,1024]{1,0:T(8,128)(2,1)} %param.17), kind=kOutput, calls=%fused_computation.50 | convolution fusion | flops 805699584 | bytes 3670016 | tf_op jit(solution)/shard_map/dot_general | solution.py:56
  22.6 2.3 copy.25
  25.0 115.7 %while.47 = (s32[]{:T(128)}, f32[16,384,64]{1,2,0:T(8,128)}, f32[16,64,64]{2,1,0:T(8,128)}, f32[16]{0:T(128)S(1)}, bf16[16,384,64]{1,2,0:T(8,128)(2,1)S(1)}, /*i...) while((s32[]{:T(128)}, f32[16,384,64]{1,2,0:T(8,128)}, ...), condition=%wide.region_3.4_spmd.clone, body=%wide.region_0.3_spmd.sunk.clone | while | flops 41902472 | bytes 594653 | solution.py:61
  27.8 1.7 fusion.75
  29.5 1.9 fusion.74
  35.0 1.7 fusion.75
  36.7 1.9 fusion.74
  42.2 1.7 fusion.75
  43.9 1.9 fusion.74
  49.5 1.7 fusion.75
  51.2 1.9 fusion.74
  56.7 1.7 fusion.75
  58.4 1.9 fusion.74
  63.9 1.7 fusion.75
  65.6 1.9 fusion.74
  71.2 1.7 fusion.75
  72.9 1.9 fusion.74
  78.4 1.7 fusion.75
  80.1 1.9 fusion.74
  85.6 1.7 fusion.75
  87.3 1.9 fusion.74
  92.9 1.7 fusion.75
  94.5 1.9 fusion.74
  100.1 1.7 fusion.75
  101.8 1.9 fusion.74
  107.3 1.7 fusion.75
  109.0 1.9 fusion.74
  116.2 1.9 fusion.74
  121.7 1.7 fusion.75
  123.4 1.9 fusion.74
  129.0 1.7 fusion.75
  130.7 1.9 fusion.74
  136.2 1.7 fusion.75
  137.9 1.9 fusion.74
  142.3 18.8 %all-reduce = f32[128]{0:T(128)S(1)} all-reduce(f32[128]{0:T(128)S(1)} %dynamic-update-slice), channel_id=2, replica_groups=mesh['outer'=4,'inner'=8] {'inner'}, use_global_device_ids=true, to_apply=%add | all-reduce | flops 128 | bytes 1024
  161.2 29.3 %all-gather.8.cloned.1.call-done = f32[128,64,64]{2,1,0:T(8,128)} async-done(((f32[16,64,64]{2,1,0:T(8,128)}), f32[128,64,64]{2,1,0:T(8,128)}) %all-gather.8.cloned.1.call-update) | async-done | bytes 2097168 | tf_op jit(solution)/shard_map/all_gather | solution.py:9
  190.5 8.5 %while.48 = (s32[]{:T(128)}, f32[16]{0:T(128)S(1)}, f32[16,64,64]{2,1,0:T(8,128)S(1)}, s32[]{:T(128)}, f32[8,16]{1,0:T(8,128)S(1)}, /*index=5*/f32[8,16,64,64]{3,2,1,0:T(8,128)}) while((s32[]{:T(128)}, f32[16]{0:T(128)S(1)}, f32[16,64,64]{2,1,0:T(8,128)S(1)}, s32[]{:T(128)}, f32[8,16]{1,0:T(8,128)S(1)}, ...), condition=%wide.region_5.6_spmd.clone.clone, body=%wide.region_4.5_spmd.clone.sunk.clone | while | flops 262196 | bytes 786851 | solution.py:18
  199.0 2.0 select_bitcast_fusion
  201.1 55.4 %all-reduce.3.cloned.1.call-done = f32[1,16,64,64]{3,2,1,0:T(8,128)} async-done(((f32[1,16,64,64]{3,2,1,0:T(8,128)}), f32[1,16,64,64]{3,2,1,0:T(8,128)}) %all-reduce.3.cloned.1.call-update) | async-done | bytes 262160 | tf_op jit(solution)/shard_map/psum | solution.py:23
  257.7 13.7 %psum.14 = f32[1,16]{1,0:T(1,128)S(1)} all-reduce(f32[1,16]{1,0:T(1,128)S(1)} %fusion.37), channel_id=1, replica_groups=mesh['outer'=4,'inner'=8] {'inner'}, use_global_device_ids=true, to_apply=%region_6.7 | all-reduce | flops 16 | bytes 128 | tf_op jit(solution)/shard_map/psum | solution.py:23
  271.4 7.9 %all-gather.2 = f32[4,1,16]{2,1,0:T(1,128)S(1)} all-gather(f32[1,1,16]{2,1,0:T(1,128)S(1)} %bitcast.147), channel_id=1, replica_groups=mesh['outer'=4,'inner'=8] {'outer'}, dimensions={0}, use_global_device_ids=true | all-gather | bytes 320 | tf_op jit(solution)/shard_map/all_gather | solution.py:9
  279.3 13.3 %all-gather.6.cloned.1.call-done = f32[4,16,64,64]{3,2,1,0:T(8,128)} async-done(((f32[1,16,64,64]{3,2,1,0:T(8,128)}), f32[4,16,64,64]{3,2,1,0:T(8,128)}) %all-gather.6.cloned.1.call-update) | async-done | bytes 1048592 | tf_op jit(solution)/shard_map/all_gather | solution.py:9
  292.6 3.6 %while.49 = (s32[]{:T(128)}, f32[16,64,64]{2,1,0:T(8,128)S(1)}, s32[]{:T(128)}, f32[4,16]{1,0:T(4,128)S(1)}, f32[4,16,64,64]{3,2,1,0:T(8,128)}) while((s32[]{:T(128)}, f32[16,64,64]{2,1,0:T(8,128)S(1)}, s32[]{:T(128)}, f32[4,16]{1,0:T(4,128)S(1)}, f32[4,16,64,64]{3,2,1,0:T(8,128)}) %tuple.108), condition=%wide.region_9.10_spmd.clone.clone, body=%wide.region_8.9_spmd.clone.sunk.clone | while | flops 262148 | bytes 786713 | solution.py:18
  296.2 2.9 multiply_reduce_fusion
  301.4 1.9 convolution_convert_fusion
  (235 shorter events, 68.0 us)
Async XLA Ops:
  6.5 1.6 copy-start
  6.5 184.0 %all-gather.8.cloned.1.call-start = ((), (), s32[]{:S(2)}) async-start(), calls=%async_computation.2 | async-start | bytes 4718592 | tf_op jit(solution)/shard_map/all_gather | solution.py:9
  22.6 2.3 copy-start.3
  25.0 115.8 %copy-start.5 = (u32[32]{0:T(128)S(1)}, u32[32]{0:T(128)}, u32[]{:S(2)}) copy-start(u32[32]{0:T(128)} %constant.97) | copy-start | bytes 388
  140.6 49.9 %copy-start.1 = (bf16[16,384,64]{1,2,0:T(8,128)(2,1)}, bf16[16,384,64]{1,2,0:T(8,128)(2,1)S(1)}, u32[]{:S(2)}) copy-start(bf16[16,384,64]{1,2,0:T(8,128)(2,1)S(1)} %get-tuple-element.587) | copy-start | bytes 2359300
  140.7 115.8 %all-reduce.3.cloned.1.call-start = ((), (), s32[]{:S(2)}) async-start(), calls=%async_computation | async-start | bytes 1048576 | tf_op jit(solution)/shard_map/psum | solution.py:23
  201.0 91.6 %all-gather.6.cloned.1.call-start = ((), (), s32[]{:S(2)}) async-start(), calls=%async_computation.1 | async-start | bytes 2621440 | tf_op jit(solution)/shard_map/all_gather | solution.py:9
  299.1 0.7 copy-start.4
  299.8 1.6 copy-start.2
Sparse Core Ops, SparseCore 0:
  140.8 49.6 all-gather.7
  201.2 55.2 all-reduce.2
  258.3 34.2 all-gather.5
where the time goes:
time: 314 us; the launch traced here: 310 us
  waiting for transfers between devices  98.1 us (31%)
  matrix products  73.1 us (23%)
  local copies, waits for them, and re-layouts  40.4 us (13%)
  blocking collectives  40.4 us (13%)
  other arithmetic  32.3 us (10%)
  between operations  13.9 us (4%)
  loops' own time  11.5 us (4%)
    psum x1, waiting for transfers between devices, broadcast(): return lax.psum(kept, axis)  55.4 us
    all_gather x2, waiting for transfers between devices, prefix(): pieces = jax.tree.map(lambda part: lax.all_gather(part, axis), value)  42.6 us
    dot_general x16, matrix products, local_head(): intra = jnp.dot(weights, v_head, preferred_element_type=jnp.float32)  30.6 us
    dot_general x16, matrix products, local_head(): local = jnp.dot(scaled.T, v_head, preferred_element_type=jnp.float32)  27 us
    unnamed x1, blocking collectives  18.8 us
    dynamic_slice x48, local copies, waits for them, and re-layouts, shards(): lax.map(lambda token_parts: local_head(*token_parts), (queries, keys, val...  15.3 us
    psum x1, blocking collectives, broadcast(): return lax.psum(kept, axis)  13.7 us
    select_n x17, other arithmetic, lap(): jnp.where(position < mine, new, old)  11.9 us
  transfers between devices with their start and end apart: 3, of which 3 were waited for; matrix products, arithmetic and copies ran while one was open for 1% of the time, Pallas kernels for 0%

commit v1 on v0

v1 whole, which is shorter than its diff:
```python
import jax
import jax.numpy as jnp
from jax import lax
from jax.sharding import PartitionSpec as P

AXES = ("outer", "inner")


def combine(earlier, later):
    g_e, s_e = earlier
    g_l, s_l = later
    return (g_e + g_l, jnp.exp(g_l)[:, None, None] * s_e + s_l)


def exclusive_scan(own, count):
    before = (jnp.zeros_like(own[0]), jnp.zeros_like(own[1]))
    through = own
    shift = 1
    while shift < count:
        perm = [(i, i + shift) for i in range(count - shift)]
        got = jax.tree.map(lambda part: lax.ppermute(part, AXES, perm), through)
        before = combine(got, before)
        shift *= 2
        if shift < count:
            through = combine(before, own)
    return before[1]


def shards(count, tokens, log_decay, query_weight, key_weight, value_weight, norm_gain, output_weight):
    rows = tokens.shape[0]
    heads = log_decay.shape[1]
    f32 = jnp.float32
    keys = jax.nn.silu(jnp.dot(tokens, key_weight, preferred_element_type=f32)).astype(jnp.bfloat16)
    value_rows = jnp.dot(tokens, value_weight, preferred_element_type=f32).astype(jnp.bfloat16)
    keys = keys.reshape(rows, heads, -1)
    value_rows = value_rows.reshape(rows, heads, -1)
    cum = jnp.cumsum(log_decay, axis=0)
    last = cum[-1]
    scaled = (keys.astype(f32) * jnp.exp(last[None, :] - cum)[:, :, None]).astype(jnp.bfloat16)
    local = jnp.einsum("thd,the->hde", scaled, value_rows, preferred_element_type=f32)
    incoming = exclusive_scan((last, local), count)

    queries = jax.nn.silu(jnp.dot(tokens, query_weight, preferred_element_type=f32)).astype(jnp.bfloat16)
    queries = queries.reshape(rows, heads, -1)
    t_idx = lax.broadcasted_iota(jnp.int32, (rows, rows), 0)
    s_idx = lax.broadcasted_iota(jnp.int32, (rows, rows), 1)
    lower = (s_idx <= t_idx)[None]
    cum_h = cum.T
    diff = jnp.where(lower, cum_h[:, :, None] - cum_h[:, None, :], 0.0)
    decay = jnp.where(lower, jnp.exp(diff), 0.0)
    scores = jnp.einsum("thd,shd->hts", queries, keys, preferred_element_type=f32)
    weights = (scores * decay).astype(jnp.bfloat16)
    intra = jnp.einsum("hts,shd->thd", weights, value_rows, preferred_element_type=f32)

    qfloat = queries.astype(f32)
    inter = (
        jnp.einsum("thd,hde->the", qfloat, incoming, precision=lax.Precision.HIGHEST)
        * jnp.exp(cum)[:, :, None]
    )
    attended = intra + inter
    scale = lax.rsqrt(jnp.mean(attended * attended, axis=-1, keepdims=True) + 1e-05)
    normalized_output = ((attended * scale).reshape(rows, -1) * norm_gain).astype(jnp.bfloat16)
    return jnp.dot(normalized_output, output_weight, preferred_element_type=f32).astype(jnp.bfloat16)


def solution(mesh):
    count = mesh.shape["outer"] * mesh.shape["inner"]
    in_specs = (P(AXES, None), P(AXES, None), P(), P(), P(), P(), P())
    out_specs = P(AXES, None)
    body = lambda *args: shards(count, *args)
    return jax.shard_map(body, mesh=mesh, in_specs=in_specs, out_specs=out_specs, check_vma=False)
```

time: 314 us -> 123 us (0.39); the launches traced: 310 us -> 122 us
  waiting for transfers between devices: 98.1 us -> 26.7 us
  starting transfers between devices: 0.09 us -> 58.8 us
  matrix products: 73.1 us -> 22.7 us
  blocking collectives: 40.4 us -> 0 us
  local copies, waits for them, and re-layouts: 40.4 us -> 9.23 us
  other arithmetic: 32.3 us -> 4.76 us
  between operations: 13.9 us -> 0.24 us
  loops' own time: 11.5 us -> 0 us
    ppermute x0 -> x9, starting transfers between devices: none -> 58.8 us  [exclusive_scan(): got = jax.tree.map(lambda part: lax.ppermute(part, AXES, perm), through)]
    psum x1 -> x0, waiting for transfers between devices: 55.4 us -> none  [broadcast(): return lax.psum(kept, axis)]
    dot_general x37 -> x7, matrix products: 73.1 us -> 22.7 us  [the longest x1 7.06 us: shards(): jnp.einsum('hts,shd->thd', weights, value_rows, preferred_element_type=f32)]
    all_gather x2 -> x0, waiting for transfers between devices: 42.6 us -> none  [prefix(): pieces = jax.tree.map(lambda part: lax.all_gather(part, axis), value)]
    ppermute x0 -> x9, waiting for transfers between devices: none -> 26.7 us  [exclusive_scan(): got = jax.tree.map(lambda part: lax.ppermute(part, AXES, perm), through)]
    unnamed x1 -> x0, blocking collectives: 18.8 us -> none
    dynamic_slice x48 -> x0, local copies, waits for them, and re-layouts: 15.3 us -> none  [shards(): lax.map(lambda token_parts: local_head(*token_parts), (queries, keys, val...]
    psum x1 -> x0, blocking collectives: 13.7 us -> none  [broadcast(): return lax.psum(kept, axis)]
  transfers between devices with their start and end apart: 3 -> 9, of which waited for: 3 -> 5; matrix products, arithmetic and copies ran while one was open for 1% -> 20% of each run, Pallas kernels for 0% -> 0%
where the time goes in v1:
time: 123 us; the launch traced here: 122 us
  starting transfers between devices  58.8 us (48%)
  waiting for transfers between devices  26.7 us (22%)
  matrix products  22.7 us (18%)
  local copies, waits for them, and re-layouts  9.23 us (8%)
  other arithmetic  4.76 us (4%)
    ppermute x9, starting transfers between devices, exclusive_scan(): got = jax.tree.map(lambda part: lax.ppermute(part, AXES, perm), through)  58.8 us
    ppermute x9, waiting for transfers between devices, exclusive_scan(): got = jax.tree.map(lambda part: lax.ppermute(part, AXES, perm), through)  26.7 us
    dot_general x1, matrix products, shards(): jnp.einsum('hts,shd->thd', weights, value_rows, preferred_element_type=f32)  7.06 us
    dot_general x1, matrix products, shards(): jnp.dot(tokens, value_weight, preferred_element_type=f32)  3.97 us
    add x7, other arithmetic, combine(): return (g_e + g_l, jnp.exp(g_l)[:, None, None] * s_e + s_l)  3.31 us
    dot_general x1, matrix products, shards(): jnp.dot(tokens, key_weight, preferred_element_type=f32)  3.16 us
    dot_general x1, matrix products, shards(): jnp.einsum('thd,hde->the', qfloat, incoming, precision=lax.Precision.HIGH...  3.06 us
  transfers between devices with their start and end apart: 9, of which 5 were waited for; matrix products, arithmetic and copies ran while one was open for 20% of the time, Pallas kernels for 0%

profile of v1, /device:TPU:0, one launch (start us, length us, event | category | flops | bytes accessed | tf_op | source)
XLA Modules:
  0.0 122.5 jit_solution(17674526134094538060)
XLA Ops:
  0.0 0.0 copy-start
  0.0 0.9 copy_bitcast_fusion.1
  0.9 0.9 reduce-window.6
  1.7 0.2 slice_reduce_fusion
  1.9 0.1 fusion.12
  2.0 0.2 slice_reduce_fusion.1
  2.2 2.4 %collective-permute-start = (f32[16]{0:T(128)S(1)}, f32[16]{0:T(128)S(1)}, u32[]{:S(2)}, u32[]{:S(2)}) collective-permute-start(f32[16]{0:T(128)S(1)} %slice_reduce_fusion.1), channel_id=1, source_target_pairs={{0,1},{1,2},{2,3},{3,4},{4,5},{5,6},{6,7},{7,8},{8,9},{9,10},{10,1... | collective-permute-start | bytes 200 | tf_op jit(solution)/shard_map/ppermute | solution.py:21
  4.6 0.1 subtract_exponential_fusion
  4.7 0.0 copy-done
  4.7 3.2 %multiply_convert_fusion.3 = bf16[384,1024]{1,0:T(8,128)(2,1)} fusion(bf16[384,1024]{1,0:T(8,128)(2,1)} %param.7, bf16[1024,1024]{1,0:T(8,128)(2,1)S(1)} %copy-done), kind=kOutput, calls=%fused_computation.10 | convolution fusion | flops 807272448 | bytes 3670016 | tf_op jit(solution)/shard_map/dot_general | solution.py:33
  7.9 1.5 %copy.26 = bf16[384,1024]{0,1:T(8,128)(2,1)S(1)} copy(bf16[384,1024]{1,0:T(8,128)(2,1)} %multiply_convert_fusion.3) | data formatting | bytes 1572864 | tf_op jit(solution)/shard_map/convert_element_type | solution.py:33
  9.4 4.0 %convolution_convert_fusion.1 = bf16[384,1024]{1,0:T(8,128)(2,1)} fusion(bf16[384,1024]{1,0:T(8,128)(2,1)} %param.7, bf16[1024,1024]{1,0:T(8,128)(2,1)} %param.11), kind=kOutput, calls=%fused_computation.13 | convolution fusion | flops 805699584 | bytes 3670016 | tf_op jit(solution)/shard_map/dot_general | solution.py:34
  13.4 2.3 %copy.24 = bf16[384,1024]{0,1:T(8,128)(2,1)} copy(bf16[384,1024]{1,0:T(8,128)(2,1)} %convolution_convert_fusion.1) | data formatting | bytes 1572864 | tf_op jit(solution)/shard_map/convert_element_type | solution.py:34
  15.6 0.0 copy-done.1
  15.6 1.5 %fusion.6 = f32[16,64,64]{2,1,0:T(8,128)S(1)} fusion(bf16[384,16,64]{0,2,1:T(8,128)(2,1)} %bitcast.53, bf16[384,16,64]{0,2,1:T(8,128)(2,1)S(1)} %bitcast.51, f32[384,16]{0,1:T(8,128)S(1)} %get-tuple-element.11), kind=kOutput, calls=%fused_computation.14 | convolution fusion | flops 51511296 | bytes 1859584 | tf_op jit(solution)/shard_map/thd,the->hde/dot_general | solution.py:40
  17.2 0.0 collective-permute-done
  17.2 4.5 %collective-permute-start.1 = (f32[16]{0:T(128)S(1)}, f32[16]{0:T(128)S(1)}, u32[]{:S(2)}, u32[]{:S(2)}) collective-permute-start(f32[16]{0:T(128)S(1)} %add.65), channel_id=1, source_target_pairs={{0,2},{1,3},{2,4},{3,5},{4,6},{5,7},{6,8},{7,9},{8,10},{9,11},{10,... | collective-permute-start | bytes 200 | tf_op jit(solution)/shard_map/ppermute | solution.py:21
  21.7 3.3 %collective-permute-start.4 = (f32[16,64,64]{2,1,0:T(8,128)S(1)}, f32[16,64,64]{2,1,0:T(8,128)S(1)}, u32[]{:S(2)}, u32[]{:S(2)}) collective-permute-start(f32[16,64,64]{2,1,0:T(8,128)S(1)} %fusion.6), channel_id=1, source_target_pairs={{0,1},{1,2},{2,3},{3,4},{4,5},{5,6},{6,7},{7,8},{8,9},{9,10},{10,1... | collective-permute-start | bytes 786440 | tf_op jit(solution)/shard_map/ppermute | solution.py:21
  25.1 0.0 collective-permute-done.1
  25.1 4.0 %collective-permute-start.2 = (f32[16]{0:T(128)S(1)}, f32[16]{0:T(128)S(1)}, u32[]{:S(2)}, u32[]{:S(2)}) collective-permute-start(f32[16]{0:T(128)S(1)} %get-tuple-element.7), channel_id=1, source_target_pairs={{0,4},{1,5},{2,6},{3,7},{4,8},{5,9},{6,10},{7,11},{8,12},{9,13},{1... | collective-permute-start | bytes 200 | tf_op jit(solution)/shard_map/ppermute | solution.py:21
  29.1 1.3 %collective-permute-done.2 = f32[16]{0:T(128)S(1)} collective-permute-done((f32[16]{0:T(128)S(1)}, f32[16]{0:T(128)S(1)}, u32[]{:S(2)}, u32[]{:S(2)}) %collective-permute-start.2) | collective-permute-done | bytes 96 | tf_op jit(solution)/shard_map/ppermute | solution.py:21
  30.4 0.0 collective-permute-done.4
  30.4 0.0 copy-start.4
  30.4 0.0 copy-start.5
  30.4 0.1 multiply_add_fusion.6
  30.6 5.4 %collective-permute-start.5 = (f32[16,64,64]{2,1,0:T(8,128)S(1)}, f32[16,64,64]{2,1,0:T(8,128)S(1)}, u32[]{:S(2)}, u32[]{:S(2)}) collective-permute-start(f32[16,64,64]{2,1,0:T(8,128)S(1)} %multiply_add_fusion.6), channel_id=1, source_target_pairs={{0,2},{1,3},{2,4},{3,5},{4,6},{5,7},{6,8},{7,9},{8,10},{9,11},{10,... | collective-permute-start | bytes 786440 | tf_op jit(solution)/shard_map/ppermute | solution.py:21
  36.0 10.6 %collective-permute-done.5 = f32[16,64,64]{2,1,0:T(8,128)S(1)} collective-permute-done((f32[16,64,64]{2,1,0:T(8,128)S(1)}, f32[16,64,64]{2,1,0:T(8,128)S(1)}, u32[]{:S(2)}, u32[]{:S(2)}) %collective-permute-start.5) | collective-permute-done | bytes 262176 | tf_op jit(solution)/shard_map/ppermute | solution.py:21
  46.7 0.2 multiply_add_fusion.4
  46.8 5.8 %collective-permute-start.6 = (f32[16,64,64]{2,1,0:T(8,128)S(1)}, f32[16,64,64]{2,1,0:T(8,128)S(1)}, u32[]{:S(2)}, u32[]{:S(2)}) collective-permute-start(f32[16,64,64]{2,1,0:T(8,128)S(1)} %multiply_add_fusion.4), channel_id=1, source_target_pairs={{0,4},{1,5},{2,6},{3,7},{4,8},{5,9},{6,10},{7,11},{8,12},{9,13},{1... | collective-permute-start | bytes 786440 | tf_op jit(solution)/shard_map/ppermute | solution.py:21
  52.7 2.1 %multiply_convert_fusion.4 = bf16[384,1024]{1,0:T(8,128)(2,1)} fusion(bf16[384,1024]{1,0:T(8,128)(2,1)S(1)} %copy-done.5, bf16[1024,1024]{1,0:T(8,128)(2,1)S(1)} %copy-done.4), kind=kOutput, calls=%fused_computation.11 | convolution fusion | flops 807272448 | bytes 3670016 | tf_op jit(solution)/shard_map/dot_general | solution.py:43
  54.8 8.1 %collective-permute-done.6 = f32[16,64,64]{2,1,0:T(8,128)S(1)} collective-permute-done((f32[16,64,64]{2,1,0:T(8,128)S(1)}, f32[16,64,64]{2,1,0:T(8,128)S(1)}, u32[]{:S(2)}, u32[]{:S(2)}) %collective-permute-start.6) | collective-permute-done | bytes 262176 | tf_op jit(solution)/shard_map/ppermute | solution.py:21
  62.9 1.0 multiply_add_fusion.2
  63.9 19.9 %collective-permute-start.7 = (f32[16,64,64]{2,1,0:T(8,128)}, f32[16,64,64]{2,1,0:T(8,128)}, u32[]{:S(2)}, u32[]{:S(2)}) collective-permute-start(f32[16,64,64]{2,1,0:T(8,128)} %get-tuple-element.9), channel_id=1, source_target_pairs={{0,8},{1,9},{2,10},{3,11},{4,12},{5,13},{6,14},{7,15},{8,16},{9,17... | collective-permute-start | bytes 786440 | tf_op jit(solution)/shard_map/ppermute | solution.py:21
  83.9 5.0 %collective-permute-start.3 = (f32[16]{0:T(128)S(1)}, f32[16]{0:T(128)S(1)}, u32[]{:S(2)}, u32[]{:S(2)}) collective-permute-start(f32[16]{0:T(128)S(1)} %get-tuple-element.5), channel_id=1, source_target_pairs={{0,8},{1,9},{2,10},{3,11},{4,12},{5,13},{6,14},{7,15},{8,16},{9,17... | collective-permute-start | bytes 200 | tf_op jit(solution)/shard_map/ppermute | solution.py:21
  88.9 2.3 %copy.25 = bf16[384,1024]{0,1:T(8,128)(2,1)} copy(bf16[384,1024]{1,0:T(8,128)(2,1)} %multiply_convert_fusion.4) | data formatting | bytes 1572864 | tf_op jit(solution)/shard_map/convert_element_type | solution.py:43
  91.2 2.9 %collective-permute-done.3 = f32[16]{0:T(128)S(1)} collective-permute-done((f32[16]{0:T(128)S(1)}, f32[16]{0:T(128)S(1)}, u32[]{:S(2)}, u32[]{:S(2)}) %collective-permute-start.3) | collective-permute-done | bytes 96 | tf_op jit(solution)/shard_map/ppermute | solution.py:21
  94.1 0.0 collective-permute-done.7
  94.1 2.0 %multiply_add_fusion = f32[16,64,64]{2,1,0:T(8,128)} fusion(f32[16,64,64]{2,1,0:T(8,128)S(1)} %fusion.6, f32[16]{0:T(128)S(1)} %get-tuple-element.18, f32[16,64,64]{2,1,0:T(8,128)S(1)} %get-tuple-element.10, f32[16,64,64]{2,1,0:T(8,128)} %collective-permute-done.7, f32[16]{0:T(128)S(1)} %get-tuple-element.16), kind=kLoop, calls=%fused_computation.20 | loop fusion | flops 262144 | bytes 1048704 | tf_op jit(solution)/shard_map/add | solution.py:12
  96.1 8.4 %collective-permute-start.8 = (f32[16,64,64]{2,1,0:T(8,128)}, f32[16,64,64]{2,1,0:T(8,128)S(1)}, u32[]{:S(2)}, u32[]{:S(2)}) collective-permute-start(f32[16,64,64]{2,1,0:T(8,128)} %multiply_add_fusion), channel_id=1, source_target_pairs={{0,16},{1,17},{2,18},{3,19},{4,20},{5,21},{6,22},{7,23},{8,24},{9,... | collective-permute-start | bytes 786440 | tf_op jit(solution)/shard_map/ppermute | solution.py:21
  104.5 7.1 %fusion = f32[16,64,384]{2,1,0:T(8,128)} fusion(bf16[384,16,64]{0,2,1:T(8,128)(2,1)} %bitcast.54, f32[16,384]{1,0:T(8,128)S(1)} %get-tuple-element.14, pred[384,384]{1,0:T(8,128)(4,1)S(1)} %iota_compare_fusion, bf16[384,16,64]{0,2,1:T(8,128)(2,1)} %bitcast.49, bf16[384,16,64]{0,2,1:T(8,128)(2,1)} %bitcast.52), kind=kOutput, calls=%fused_computation.1 | convolution fusion | flops 615776256 | bytes 4104192 | tf_op jit(solution)/shard_map/hts,shd->thd/dot_general | solution.py:53
  111.5 3.7 %collective-permute-done.8 = f32[16,64,64]{2,1,0:T(8,128)S(1)} collective-permute-done((f32[16,64,64]{2,1,0:T(8,128)}, f32[16,64,64]{2,1,0:T(8,128)S(1)}, u32[]{:S(2)}, u32[]{:S(2)}) %collective-permute-start.8) | collective-permute-done | bytes 262176 | tf_op jit(solution)/shard_map/ppermute | solution.py:21
  115.3 3.1 %multiply_reduce_fusion = (f32[384,16]{0,1:T(8,128)S(1)}, f32[384,16,64]{0,2,1:T(8,128)S(1)}) fusion(f32[384,16]{0,1:T(8,128)S(1)} %get-tuple-element.12, bf16[384,16,64]{0,2,1:T(8,128)(2,1)} %bitcast.50, f32[16,64,64]{2,1,0:T(8,128)S(1)} %collective-permute-done.8, f32[16]{0:T(128)S(1)} %get-tuple-element.15, f32[16,64,64]{2,1,0:T(8,128)S(1)} %get-tuple-element.10, ...), kind=kOutput, calls=%fused_computation.8 | convolution fusion | flops 303818752 | bytes 4767872 | tf_op jit(solution)/shard_map/thd,hde->the/dot_general | solution.py:57
  118.3 0.0 copy-start.3
  118.3 0.1 broadcast_multiply_fusion
  118.5 0.5 copy-done.3
  119.0 0.2 fusion.4
  119.2 1.4 %copy-done.2 = bf16[1024,1024]{1,0:T(8,128)(2,1)S(1)} copy-done((bf16[1024,1024]{1,0:T(8,128)(2,1)S(1)}, bf16[1024,1024]{1,0:T(8,128)(2,1)}, u32[]{:S(2)}) %copy-start.2) | copy-done | bytes 2097176
  120.6 1.9 %convolution_convert_fusion = bf16[384,1024]{1,0:T(8,128)(2,1)} fusion(bf16[384,1024]{0,1:T(8,128)(2,1)S(1)} %fusion.4, bf16[1024,1024]{1,0:T(8,128)(2,1)S(1)} %copy-done.2), kind=kOutput, calls=%fused_computation.12 | convolution fusion | flops 805699584 | bytes 3670016 | tf_op jit(solution)/shard_map/dot_general | solution.py:63
  (11 shorter events, 0.1 us)
Async XLA Ops:
  0.0 4.7 %copy-start = (bf16[1024,1024]{1,0:T(8,128)(2,1)S(1)}, bf16[1024,1024]{1,0:T(8,128)(2,1)}, u32[]{:S(2)}) copy-start(bf16[1024,1024]{1,0:T(8,128)(2,1)} %param.10) | copy-start | bytes 6291460
  2.2 15.0 %collective-permute-start = (f32[16]{0:T(128)S(1)}, f32[16]{0:T(128)S(1)}, u32[]{:S(2)}, u32[]{:S(2)}) collective-permute-start(f32[16]{0:T(128)S(1)} %slice_reduce_fusion.1), channel_id=1, source_target_pairs={{0,1},{1,2},{2,3},{3,4},{4,5},{5,6},{6,7},{7,8},{8,9},{9,10},{10,1... | collective-permute-start | bytes 200 | tf_op jit(solution)/shard_map/ppermute | solution.py:21
  9.4 6.3 %copy-start.1 = (bf16[384,1024]{0,1:T(8,128)(2,1)}, bf16[384,1024]{0,1:T(8,128)(2,1)S(1)}, u32[]{:S(2)}) copy-start(bf16[384,1024]{0,1:T(8,128)(2,1)S(1)} %copy.26) | copy-start | bytes 2359300
  17.2 7.8 %collective-permute-start.1 = (f32[16]{0:T(128)S(1)}, f32[16]{0:T(128)S(1)}, u32[]{:S(2)}, u32[]{:S(2)}) collective-permute-start(f32[16]{0:T(128)S(1)} %add.65), channel_id=1, source_target_pairs={{0,2},{1,3},{2,4},{3,5},{4,6},{5,7},{6,8},{7,9},{8,10},{9,11},{10,... | collective-permute-start | bytes 200 | tf_op jit(solution)/shard_map/ppermute | solution.py:21
  21.7 8.7 %collective-permute-start.4 = (f32[16,64,64]{2,1,0:T(8,128)S(1)}, f32[16,64,64]{2,1,0:T(8,128)S(1)}, u32[]{:S(2)}, u32[]{:S(2)}) collective-permute-start(f32[16,64,64]{2,1,0:T(8,128)S(1)} %fusion.6), channel_id=1, source_target_pairs={{0,1},{1,2},{2,3},{3,4},{4,5},{5,6},{6,7},{7,8},{8,9},{9,10},{10,1... | collective-permute-start | bytes 786440 | tf_op jit(solution)/shard_map/ppermute | solution.py:21
  25.1 5.3 %collective-permute-start.2 = (f32[16]{0:T(128)S(1)}, f32[16]{0:T(128)S(1)}, u32[]{:S(2)}, u32[]{:S(2)}) collective-permute-start(f32[16]{0:T(128)S(1)} %get-tuple-element.7), channel_id=1, source_target_pairs={{0,4},{1,5},{2,6},{3,7},{4,8},{5,9},{6,10},{7,11},{8,12},{9,13},{1... | collective-permute-start | bytes 200 | tf_op jit(solution)/shard_map/ppermute | solution.py:21
  30.4 22.3 %copy-start.4 = (bf16[1024,1024]{1,0:T(8,128)(2,1)S(1)}, bf16[1024,1024]{1,0:T(8,128)(2,1)}, u32[]{:S(2)}) copy-start(bf16[1024,1024]{1,0:T(8,128)(2,1)} %param.9) | copy-start | bytes 6291460
  30.4 22.3 %copy-start.5 = (bf16[384,1024]{1,0:T(8,128)(2,1)S(1)}, bf16[384,1024]{1,0:T(8,128)(2,1)}, u32[]{:S(2)}) copy-start(bf16[384,1024]{1,0:T(8,128)(2,1)} %param.7) | copy-start | bytes 2359300
  30.6 16.1 %collective-permute-start.5 = (f32[16,64,64]{2,1,0:T(8,128)S(1)}, f32[16,64,64]{2,1,0:T(8,128)S(1)}, u32[]{:S(2)}, u32[]{:S(2)}) collective-permute-start(f32[16,64,64]{2,1,0:T(8,128)S(1)} %multiply_add_fusion.6), channel_id=1, source_target_pairs={{0,2},{1,3},{2,4},{3,5},{4,6},{5,7},{6,8},{7,9},{8,10},{9,11},{10,... | collective-permute-start | bytes 786440 | tf_op jit(solution)/shard_map/ppermute | solution.py:21
  46.8 16.1 %collective-permute-start.6 = (f32[16,64,64]{2,1,0:T(8,128)S(1)}, f32[16,64,64]{2,1,0:T(8,128)S(1)}, u32[]{:S(2)}, u32[]{:S(2)}) collective-permute-start(f32[16,64,64]{2,1,0:T(8,128)S(1)} %multiply_add_fusion.4), channel_id=1, source_target_pairs={{0,4},{1,5},{2,6},{3,7},{4,8},{5,9},{6,10},{7,11},{8,12},{9,13},{1... | collective-permute-start | bytes 786440 | tf_op jit(solution)/shard_map/ppermute | solution.py:21
  63.9 30.2 %collective-permute-start.7 = (f32[16,64,64]{2,1,0:T(8,128)}, f32[16,64,64]{2,1,0:T(8,128)}, u32[]{:S(2)}, u32[]{:S(2)}) collective-permute-start(f32[16,64,64]{2,1,0:T(8,128)} %get-tuple-element.9), channel_id=1, source_target_pairs={{0,8},{1,9},{2,10},{3,11},{4,12},{5,13},{6,14},{7,15},{8,16},{9,17... | collective-permute-start | bytes 786440 | tf_op jit(solution)/shard_map/ppermute | solution.py:21
  83.9 10.2 %collective-permute-start.3 = (f32[16]{0:T(128)S(1)}, f32[16]{0:T(128)S(1)}, u32[]{:S(2)}, u32[]{:S(2)}) collective-permute-start(f32[16]{0:T(128)S(1)} %get-tuple-element.5), channel_id=1, source_target_pairs={{0,8},{1,9},{2,10},{3,11},{4,12},{5,13},{6,14},{7,15},{8,16},{9,17... | collective-permute-start | bytes 200 | tf_op jit(solution)/shard_map/ppermute | solution.py:21
  96.1 19.1 %collective-permute-start.8 = (f32[16,64,64]{2,1,0:T(8,128)}, f32[16,64,64]{2,1,0:T(8,128)S(1)}, u32[]{:S(2)}, u32[]{:S(2)}) collective-permute-start(f32[16,64,64]{2,1,0:T(8,128)} %multiply_add_fusion), channel_id=1, source_target_pairs={{0,16},{1,17},{2,18},{3,19},{4,20},{5,21},{6,22},{7,23},{8,24},{9,... | collective-permute-start | bytes 786440 | tf_op jit(solution)/shard_map/ppermute | solution.py:21
  118.3 0.7 copy-start.3
  119.0 1.6 %copy-start.2 = (bf16[1024,1024]{1,0:T(8,128)(2,1)S(1)}, bf16[1024,1024]{1,0:T(8,128)(2,1)}, u32[]{:S(2)}) copy-start(bf16[1024,1024]{1,0:T(8,128)(2,1)} %param.13) | copy-start | bytes 6291460

commit v2 on v1

--- a/solution.py
+++ b/solution.py
@@ -6,24 +6,26 @@
 AXES = ("outer", "inner")
 
 
-def combine(earlier, later):
-    g_e, s_e = earlier
-    g_l, s_l = later
-    return (g_e + g_l, jnp.exp(g_l)[:, None, None] * s_e + s_l)
+def combine(earlier, later, heads):
+    body = earlier.shape[0] - 8
+    scale = jnp.concatenate(
+        [jnp.repeat(jnp.exp(later[body, :heads]), body // heads), jnp.ones((8,), later.dtype)]
+    )
+    return scale[:, None] * earlier + later
 
 
-def exclusive_scan(own, count):
-    before = (jnp.zeros_like(own[0]), jnp.zeros_like(own[1]))
+def exclusive_scan(own, count, heads):
+    before = jnp.zeros_like(own)
     through = own
     shift = 1
     while shift < count:
         perm = [(i, i + shift) for i in range(count - shift)]
-        got = jax.tree.map(lambda part: lax.ppermute(part, AXES, perm), through)
-        before = combine(got, before)
+        got = lax.ppermute(through, AXES, perm)
+        before = combine(got, before, heads)
         shift *= 2
         if shift < count:
-            through = combine(before, own)
-    return before[1]
+            through = combine(before, own, heads)
+    return before[:-8]
 
 
 def shards(count, tokens, log_decay, query_weight, key_weight, value_weight, norm_gain, output_weight):
@@ -38,7 +40,11 @@
     last = cum[-1]
     scaled = (keys.astype(f32) * jnp.exp(last[None, :] - cum)[:, :, None]).astype(jnp.bfloat16)
     local = jnp.einsum("thd,the->hde", scaled, value_rows, preferred_element_type=f32)
-    incoming = exclusive_scan((last, local), count)
+    lanes = 128
+    packed = jnp.concatenate(
+        [local.reshape(-1, lanes), jnp.zeros((8, lanes), f32).at[0, :heads].set(last)], axis=0
+    )
+    incoming = exclusive_scan(packed, count, heads).reshape(local.shape)
 
     queries = jax.nn.silu(jnp.dot(tokens, query_weight, preferred_element_type=f32)).astype(jnp.bfloat16)
     queries = queries.reshape(rows, heads, -1)

time: 123 us -> 89 us (0.72)
  starting transfers between devices: 58.8 us -> 32.6 us
  waiting for transfers between devices: 26.7 us -> 7.46 us
  other arithmetic: 4.76 us -> 11.3 us
  local copies, waits for them, and re-layouts: 9.23 us -> 12.4 us
  matrix products: 22.7 us -> 24.3 us
    ppermute x9 -> x5, starting transfers between devices: 58.8 us -> 32.6 us  [exclusive_scan(): got = lax.ppermute(through, AXES, perm)]
    ppermute x9 -> x5, waiting for transfers between devices: 26.7 us -> 7.46 us  [exclusive_scan(): got = lax.ppermute(through, AXES, perm)]
    add x7 -> x5, other arithmetic: 3.31 us -> 8.43 us  [combine(): return scale[:, None] * earlier + later]
    dot_general x1, matrix products: 2.07 us -> 3.86 us  [shards(): jnp.dot(tokens, query_weight, preferred_element_type=f32)]
    reshape x1 -> x7, local copies, waits for them, and re-layouts: 0.89 us -> 2.67 us  [the longest x1 1.17 us: shards(): local.reshape(-1, lanes)]
  transfers between devices with their start and end apart: 9 -> 5, of which waited for: 5 -> 4; matrix products, arithmetic and copies ran while one was open for 20% -> 16% of each run, Pallas kernels for 0% -> 0%
where the time goes in v2:
time: 89 us; the launch traced here: 88.2 us
  starting transfers between devices  32.6 us (37%)
  matrix products  24.3 us (27%)
  local copies, waits for them, and re-layouts  12.4 us (14%)
  other arithmetic  11.3 us (13%)
  waiting for transfers between devices  7.46 us (8%)
    ppermute x5, starting transfers between devices, exclusive_scan(): got = lax.ppermute(through, AXES, perm)  32.6 us
    add x5, other arithmetic, combine(): return scale[:, None] * earlier + later  8.43 us
    ppermute x5, waiting for transfers between devices, exclusive_scan(): got = lax.ppermute(through, AXES, perm)  7.46 us
    dot_general x1, matrix products, shards(): jnp.einsum('hts,shd->thd', weights, value_rows, preferred_element_type=f32)  6.86 us
    dot_general x1, matrix products, shards(): jnp.dot(tokens, query_weight, preferred_element_type=f32)  3.86 us
    dot_general x1, matrix products, shards(): jnp.dot(tokens, value_weight, preferred_element_type=f32)  3.71 us
    dot_general x1, matrix products, shards(): jnp.dot(tokens, key_weight, preferred_element_type=f32)  3.17 us
    dot_general x1, matrix products, shards(): jnp.einsum('thd,hde->the', qfloat, incoming, precision=lax.Precision.HIGH...  2.45 us
  transfers between devices with their start and end apart: 5, of which 4 were waited for; matrix products, arithmetic and copies ran while one was open for 16% of the time, Pallas kernels for 0%

profile of v2, /device:TPU:0, one launch (start us, length us, event | category | flops | bytes accessed | tf_op | source)
XLA Modules:
  0.0 88.2 jit_solution(18124090492705844697)
XLA Ops:
  0.0 0.9 %copy_bitcast_fusion.1 = f32[16,3,128]{2,0,1:T(8,128)S(1)} fusion(f32[384,16]{0,1:T(8,128)} %param.10), kind=kLoop, calls=%fused_computation.30 | loop fusion | bytes 49152 | tf_op jit(solution)/shard_map/reshape.34
  0.9 0.9 reduce-window.6
  1.7 0.2 slice_reduce_fusion
  1.9 0.1 fusion.13
  2.0 0.2 fusion.14
  2.2 0.1 copy.32
  2.3 0.1 bitcast_exponential_fusion
  2.4 3.2 %multiply_convert_fusion.3 = bf16[384,1024]{1,0:T(8,128)(2,1)} fusion(bf16[384,1024]{1,0:T(8,128)(2,1)} %param.9, bf16[1024,1024]{1,0:T(8,128)(2,1)S(1)} %copy-done), kind=kOutput, calls=%fused_computation.10 | convolution fusion | flops 807272448 | bytes 3670016 | tf_op jit(solution)/shard_map/dot_general | solution.py:35
  5.6 1.5 %copy.26 = bf16[384,1024]{0,1:T(8,128)(2,1)S(1)} copy(bf16[384,1024]{1,0:T(8,128)(2,1)} %multiply_convert_fusion.3) | data formatting | bytes 1572864 | tf_op jit(solution)/shard_map/convert_element_type | solution.py:35
  7.1 3.7 %convolution_convert_fusion.1 = bf16[384,1024]{1,0:T(8,128)(2,1)} fusion(bf16[384,1024]{1,0:T(8,128)(2,1)} %param.9, bf16[1024,1024]{1,0:T(8,128)(2,1)} %param.13), kind=kOutput, calls=%fused_computation.13 | convolution fusion | flops 805699584 | bytes 3670016 | tf_op jit(solution)/shard_map/dot_general | solution.py:36
  10.8 2.3 %copy.24 = bf16[384,1024]{0,1:T(8,128)(2,1)} copy(bf16[384,1024]{1,0:T(8,128)(2,1)} %convolution_convert_fusion.1) | data formatting | bytes 1572864 | tf_op jit(solution)/shard_map/convert_element_type | solution.py:36
  13.1 2.3 %fusion.6 = f32[16,64,64]{2,1,0:T(8,128)} fusion(bf16[384,16,64]{0,2,1:T(8,128)(2,1)} %bitcast.60, bf16[384,16,64]{0,2,1:T(8,128)(2,1)S(1)} %bitcast.58, f32[384,16]{0,1:T(8,128)S(1)} %get-tuple-element.24), kind=kOutput, calls=%fused_computation.14 | convolution fusion | flops 51511296 | bytes 1859584 | tf_op jit(solution)/shard_map/thd,the->hde/dot_general | solution.py:42
  15.4 1.2 %reshape.128 = f32[512,128]{1,0:T(8,128)S(1)} reshape(f32[16,64,64]{2,1,0:T(8,128)} %fusion.6) | data formatting | bytes 524288 | tf_op jit(solution)/shard_map/reshape | solution.py:45
  16.6 0.7 select_maximum_fusion
  17.3 2.4 %collective-permute-start = (f32[520,128]{1,0:T(8,128)}, f32[520,128]{1,0:T(8,128)S(1)}, u32[]{:S(2)}, u32[]{:S(2)}) collective-permute-start(f32[520,128]{1,0:T(8,128)} %select_maximum_fusion), channel_id=1, source_target_pairs={{0,1},{1,2},{2,3},{3,4},{4,5},{5,6},{6,7},{7,8},{8,9},{9,10},{10,1... | collective-permute-start | bytes 798728 | tf_op jit(solution)/shard_map/ppermute | solution.py:23
  19.7 0.1 broadcast_in_dim.31
  19.8 0.1 reshape.130
  19.9 1.2 %collective-permute-done = f32[520,128]{1,0:T(8,128)S(1)} collective-permute-done((f32[520,128]{1,0:T(8,128)}, f32[520,128]{1,0:T(8,128)S(1)}, u32[]{:S(2)}, u32[]{:S(2)}) %collective-permute-start) | collective-permute-done | bytes 266272 | tf_op jit(solution)/shard_map/ppermute | solution.py:23
  21.1 0.8 multiply_add_fusion.6
  21.9 9.8 %collective-permute-start.1 = (f32[520,128]{1,0:T(8,128)}, f32[520,128]{1,0:T(8,128)}, u32[]{:S(2)}, u32[]{:S(2)}) collective-permute-start(f32[520,128]{1,0:T(8,128)} %multiply_add_fusion.6), channel_id=1, source_target_pairs={{0,2},{1,3},{2,4},{3,5},{4,6},{5,7},{6,8},{7,9},{8,10},{9,11},{10,... | collective-permute-start | bytes 798728 | tf_op jit(solution)/shard_map/ppermute | solution.py:23
  31.7 3.9 %multiply_convert_fusion.4 = bf16[384,1024]{1,0:T(8,128)(2,1)} fusion(bf16[384,1024]{1,0:T(8,128)(2,1)} %param.9, bf16[1024,1024]{1,0:T(8,128)(2,1)} %param.11), kind=kOutput, calls=%fused_computation.11 | convolution fusion | flops 807272448 | bytes 3670016 | tf_op jit(solution)/shard_map/dot_general | solution.py:49
  35.6 0.1 broadcast_in_dim.30
  35.7 0.1 reshape.129
  35.8 0.7 collective-permute-done.1
  36.5 1.9 %multiply_add_fusion.4 = (f32[520,128]{1,0:T(8,128)}, f32[520,128]{1,0:T(8,128)S(1)}) fusion(f32[520]{0:T(1024)S(1)} %concatenate.25, f32[1,16]{1,0:T(1,128)S(1)} %copy.32, f32[512,128]{1,0:T(8,128)S(1)} %reshape.128, f32[520,128]{1,0:T(8,128)} %copy-done.4, f32[520,128]{1,0:T(8,128)} %collective-permute-done.1, f32[520]{0:T(1024)S(1)} %concatenate.24), kind=kLoop, calls=%fused_computation.24 | loop fusion | flops 465920 | bytes 1331328 | tf_op jit(solution)/shard_map/add | solution.py:14
  38.4 6.1 %collective-permute-start.2 = (f32[520,128]{1,0:T(8,128)}, f32[520,128]{1,0:T(8,128)}, u32[]{:S(2)}, u32[]{:S(2)}) collective-permute-start(f32[520,128]{1,0:T(8,128)} %get-tuple-element.21), channel_id=1, source_target_pairs={{0,4},{1,5},{2,6},{3,7},{4,8},{5,9},{6,10},{7,11},{8,12},{9,13},{1... | collective-permute-start | bytes 798728 | tf_op jit(solution)/shard_map/ppermute | solution.py:23
  44.5 0.7 iota_compare_fusion
  45.2 2.3 %copy.25 = bf16[384,1024]{0,1:T(8,128)(2,1)} copy(bf16[384,1024]{1,0:T(8,128)(2,1)} %multiply_convert_fusion.4) | data formatting | bytes 1572864 | tf_op jit(solution)/shard_map/convert_element_type | solution.py:49
  47.5 0.1 broadcast_in_dim.56
  47.6 0.1 reshape.131
  47.7 0.7 collective-permute-done.2
  48.4 1.9 %multiply_add_fusion.2 = (f32[520,128]{1,0:T(8,128)}, f32[520,128]{1,0:T(8,128)S(1)}) fusion(f32[520]{0:T(1024)S(1)} %concatenate.25, f32[1,16]{1,0:T(1,128)S(1)} %copy.32, f32[512,128]{1,0:T(8,128)S(1)} %reshape.128, f32[520,128]{1,0:T(8,128)} %copy-done.3, f32[520,128]{1,0:T(8,128)} %collective-permute-done.2, f32[520]{0:T(1024)S(1)} %concatenate.26), kind=kLoop, calls=%fused_computation.22 | loop fusion | flops 465920 | bytes 1331328 | tf_op jit(solution)/shard_map/add | solution.py:14
  50.3 11.6 %collective-permute-start.3 = (f32[520,128]{1,0:T(8,128)}, f32[520,128]{1,0:T(8,128)}, u32[]{:S(2)}, u32[]{:S(2)}) collective-permute-start(f32[520,128]{1,0:T(8,128)} %get-tuple-element.19), channel_id=1, source_target_pairs={{0,8},{1,9},{2,10},{3,11},{4,12},{5,13},{6,14},{7,15},{8,16},{9,17... | collective-permute-start | bytes 798728 | tf_op jit(solution)/shard_map/ppermute | solution.py:23
  61.9 6.9 %fusion = f32[16,64,384]{2,1,0:T(8,128)} fusion(bf16[384,16,64]{0,2,1:T(8,128)(2,1)} %bitcast.61, f32[16,384]{1,0:T(8,128)S(1)} %get-tuple-element.28, pred[384,384]{1,0:T(8,128)(4,1)} %iota_compare_fusion, bf16[384,16,64]{0,2,1:T(8,128)(2,1)} %bitcast.62, bf16[384,16,64]{0,2,1:T(8,128)(2,1)S(1)} %bitcast.59), kind=kOutput, calls=%fused_computation.1 | convolution fusion | flops 615776256 | bytes 4104192 | tf_op jit(solution)/shard_map/hts,shd->thd/dot_general | solution.py:59
  68.8 0.1 broadcast_in_dim.57
  68.8 0.1 reshape.132
  68.9 1.9 %multiply_add_fusion = (f32[520,128]{1,0:T(8,128)}, f32[520,128]{1,0:T(8,128)S(1)}) fusion(f32[520]{0:T(1024)S(1)} %concatenate.25, f32[1,16]{1,0:T(1,128)S(1)} %copy.32, f32[512,128]{1,0:T(8,128)S(1)} %reshape.128, f32[520,128]{1,0:T(8,128)S(1)} %get-tuple-element.20, f32[520,128]{1,0:T(8,128)} %collective-permute-done.3, f32[520]{0:T(1024)S(1)} %concatenate.27), kind=kLoop, calls=%fused_computation.20 | loop fusion | flops 465920 | bytes 1331328 | tf_op jit(solution)/shard_map/add | solution.py:14
  70.9 2.7 %collective-permute-start.4 = (f32[520,128]{1,0:T(8,128)}, f32[520,128]{1,0:T(8,128)S(1)}, u32[]{:S(2)}, u32[]{:S(2)}) collective-permute-start(f32[520,128]{1,0:T(8,128)} %get-tuple-element.17), channel_id=1, source_target_pairs={{0,16},{1,17},{2,18},{3,19},{4,20},{5,21},{6,22},{7,23},{8,24},{9,... | collective-permute-start | bytes 798728 | tf_op jit(solution)/shard_map/ppermute | solution.py:23
  73.7 0.1 reshape.133
  73.8 4.8 %collective-permute-done.4 = f32[520,128]{1,0:T(8,128)S(1)} collective-permute-done((f32[520,128]{1,0:T(8,128)}, f32[520,128]{1,0:T(8,128)S(1)}, u32[]{:S(2)}, u32[]{:S(2)}) %collective-permute-start.4) | collective-permute-done | bytes 266272 | tf_op jit(solution)/shard_map/ppermute | solution.py:23
  78.6 1.8 %slice_add_fusion = f32[512,128]{1,0:T(8,128)} fusion(f32[520,128]{1,0:T(8,128)} %copy-done.5, f32[520,128]{1,0:T(8,128)S(1)} %collective-permute-done.4, f32[512]{0:T(512)S(1)} %pad_slice_fusion), kind=kLoop, calls=%fused_computation.27 | loop fusion | flops 131072 | bytes 788480 | tf_op jit(solution)/shard_map/add | solution.py:14
  80.4 1.1 %reshape.134 = f32[16,64,64]{2,1,0:T(8,128)S(1)} reshape(f32[512,128]{1,0:T(8,128)} %slice_add_fusion) | data formatting | bytes 524288 | tf_op jit(solution)/shard_map/reshape | solution.py:47
  81.5 2.5 %multiply_reduce_fusion = (f32[384,16]{0,1:T(8,128)S(1)}, f32[384,16,64]{0,2,1:T(8,128)S(1)}) fusion(f32[384,16]{0,1:T(8,128)S(1)} %get-tuple-element.23, f32[16,64,64]{2,1,0:T(8,128)S(1)} %reshape.134, bf16[384,16,64]{0,2,1:T(8,128)(2,1)S(1)} %bitcast.63, f32[16,64,384]{2,1,0:T(8,128)} %fusion), kind=kOutput, calls=%fused_computation.8 | convolution fusion | flops 303556608 | bytes 4243456 | tf_op jit(solution)/shard_map/thd,hde->the/dot_general | solution.py:63
  84.0 0.1 broadcast_multiply_fusion
  84.2 0.5 copy-done.6
  84.7 0.2 fusion.4
  84.9 1.4 %copy-done.2 = bf16[1024,1024]{1,0:T(8,128)(2,1)S(1)} copy-done((bf16[1024,1024]{1,0:T(8,128)(2,1)S(1)}, bf16[1024,1024]{1,0:T(8,128)(2,1)}, u32[]{:S(2)}) %copy-start.2) | copy-done | bytes 2097176
  86.3 1.9 %convolution_convert_fusion = bf16[384,1024]{1,0:T(8,128)(2,1)} fusion(bf16[384,1024]{0,1:T(8,128)(2,1)S(1)} %fusion.4, bf16[1024,1024]{1,0:T(8,128)(2,1)S(1)} %copy-done.2), kind=kOutput, calls=%fused_computation.12 | convolution fusion | flops 805699584 | bytes 3670016 | tf_op jit(solution)/shard_map/dot_general | solution.py:69
  (26 shorter events, 0.2 us)
Async XLA Ops:
  0.0 2.4 %copy-start = (bf16[1024,1024]{1,0:T(8,128)(2,1)S(1)}, bf16[1024,1024]{1,0:T(8,128)(2,1)}, u32[]{:S(2)}) copy-start(bf16[1024,1024]{1,0:T(8,128)(2,1)} %param.12) | copy-start | bytes 6291460
  17.3 3.7 %collective-permute-start = (f32[520,128]{1,0:T(8,128)}, f32[520,128]{1,0:T(8,128)S(1)}, u32[]{:S(2)}, u32[]{:S(2)}) collective-permute-start(f32[520,128]{1,0:T(8,128)} %select_maximum_fusion), channel_id=1, source_target_pairs={{0,1},{1,2},{2,3},{3,4},{4,5},{5,6},{6,7},{7,8},{8,9},{9,10},{10,1... | collective-permute-start | bytes 798728 | tf_op jit(solution)/shard_map/ppermute | solution.py:23
  21.1 14.5 %copy-start.4 = (f32[520,128]{1,0:T(8,128)}, f32[520,128]{1,0:T(8,128)S(1)}, u32[]{:S(2)}) copy-start(f32[520,128]{1,0:T(8,128)S(1)} %collective-permute-done) | copy-start | bytes 798724
  21.9 14.6 %collective-permute-start.1 = (f32[520,128]{1,0:T(8,128)}, f32[520,128]{1,0:T(8,128)}, u32[]{:S(2)}, u32[]{:S(2)}) collective-permute-start(f32[520,128]{1,0:T(8,128)} %multiply_add_fusion.6), channel_id=1, source_target_pairs={{0,2},{1,3},{2,4},{3,5},{4,6},{5,7},{6,8},{7,9},{8,10},{9,11},{10,... | collective-permute-start | bytes 798728 | tf_op jit(solution)/shard_map/ppermute | solution.py:23
  38.4 9.3 %copy-start.3 = (f32[520,128]{1,0:T(8,128)}, f32[520,128]{1,0:T(8,128)S(1)}, u32[]{:S(2)}) copy-start(f32[520,128]{1,0:T(8,128)S(1)} %get-tuple-element.22) | copy-start | bytes 798724
  38.4 10.0 %collective-permute-start.2 = (f32[520,128]{1,0:T(8,128)}, f32[520,128]{1,0:T(8,128)}, u32[]{:S(2)}, u32[]{:S(2)}) collective-permute-start(f32[520,128]{1,0:T(8,128)} %get-tuple-element.21), channel_id=1, source_target_pairs={{0,4},{1,5},{2,6},{3,7},{4,8},{5,9},{6,10},{7,11},{8,12},{9,13},{1... | collective-permute-start | bytes 798728 | tf_op jit(solution)/shard_map/ppermute | solution.py:23
  50.3 18.6 %collective-permute-start.3 = (f32[520,128]{1,0:T(8,128)}, f32[520,128]{1,0:T(8,128)}, u32[]{:S(2)}, u32[]{:S(2)}) collective-permute-start(f32[520,128]{1,0:T(8,128)} %get-tuple-element.19), channel_id=1, source_target_pairs={{0,8},{1,9},{2,10},{3,11},{4,12},{5,13},{6,14},{7,15},{8,16},{9,17... | collective-permute-start | bytes 798728 | tf_op jit(solution)/shard_map/ppermute | solution.py:23
  68.8 12.7 %copy-start.1 = (bf16[384,1024]{0,1:T(8,128)(2,1)S(1)}, bf16[384,1024]{0,1:T(8,128)(2,1)}, u32[]{:S(2)}) copy-start(bf16[384,1024]{0,1:T(8,128)(2,1)} %copy.25) | copy-start | bytes 2359300
  70.9 2.7 %copy-start.5 = (f32[520,128]{1,0:T(8,128)}, f32[520,128]{1,0:T(8,128)S(1)}, u32[]{:S(2)}) copy-start(f32[520,128]{1,0:T(8,128)S(1)} %get-tuple-element.18) | copy-start | bytes 798724
  70.9 7.8 %collective-permute-start.4 = (f32[520,128]{1,0:T(8,128)}, f32[520,128]{1,0:T(8,128)S(1)}, u32[]{:S(2)}, u32[]{:S(2)}) collective-permute-start(f32[520,128]{1,0:T(8,128)} %get-tuple-element.17), channel_id=1, source_target_pairs={{0,16},{1,17},{2,18},{3,19},{4,20},{5,21},{6,22},{7,23},{8,24},{9,... | collective-permute-start | bytes 798728 | tf_op jit(solution)/shard_map/ppermute | solution.py:23
  84.0 0.7 copy-start.6
  84.7 1.6 %copy-start.2 = (bf16[1024,1024]{1,0:T(8,128)(2,1)S(1)}, bf16[1024,1024]{1,0:T(8,128)(2,1)}, u32[]{:S(2)}) copy-start(bf16[1024,1024]{1,0:T(8,128)(2,1)} %param.15) | copy-start | bytes 6291460

commit v3 on v2

--- a/solution.py
+++ b/solution.py
@@ -14,18 +14,46 @@
     return scale[:, None] * earlier + later
 
 
+def half_of(whole, half, heads):
+    body = whole.shape[0] - 8
+    part = heads // 2
+    rows = body // 2
+    states = jnp.where(half == 0, whole[:rows], whole[rows:body])
+    logs = jnp.where(half == 0, whole[body, :part], whole[body, part:heads])
+    return jnp.concatenate([states, jnp.zeros((8, whole.shape[1]), whole.dtype).at[0, :part].set(logs)])
+
+
+def join_halves(first, second, heads):
+    body = first.shape[0] - 8
+    part = heads // 2
+    logs = jnp.concatenate([first[body, :part], second[body, :part]])
+    tail = jnp.zeros((8, first.shape[1]), first.dtype).at[0, :heads].set(logs)
+    return jnp.concatenate([first[:body], second[:body], tail])
+
+
 def exclusive_scan(own, count, heads):
-    before = jnp.zeros_like(own)
-    through = own
-    shift = 1
-    while shift < count:
-        perm = [(i, i + shift) for i in range(count - shift)]
+    flat = lax.axis_index(AXES)
+    core = flat % 2
+    chip = flat // 2
+    chips = count // 2
+    partner = [(i, i ^ 1) for i in range(count)]
+    other = lax.ppermute(own, AXES, partner)
+    pooled = jnp.where(core == 0, combine(own, other, heads), combine(other, own, heads))
+    through = half_of(pooled, core, heads)
+    before = jnp.zeros_like(through)
+    bit = 1
+    while bit < chips:
+        perm = [(i, i ^ (2 * bit)) for i in range(count)]
         got = lax.ppermute(through, AXES, perm)
-        before = combine(got, before, heads)
-        shift *= 2
-        if shift < count:
-            through = combine(before, own, heads)
-    return before[:-8]
+        lower = (chip & bit) != 0
+        before = jnp.where(lower, combine(got, before, heads // 2), before)
+        bit *= 2
+        if bit < chips:
+            through = jnp.where(lower, combine(got, through, heads // 2), combine(through, got, heads // 2))
+    swapped = lax.ppermute(before, AXES, partner)
+    whole = jnp.where(core == 0, join_halves(before, swapped, heads), join_halves(swapped, before, heads))
+    whole = jnp.where(core == 0, whole, combine(whole, other, heads))
+    return whole[:-8]
 
 
 def shards(count, tokens, log_decay, query_weight, key_weight, value_weight, norm_gain, output_weight):

time: 89 us -> 74.2 us (0.83)
  starting transfers between devices: 32.6 us -> 8.86 us
  waiting for transfers between devices: 7.46 us -> 17.9 us
  other arithmetic: 11.3 us -> 8.46 us
  local copies, waits for them, and re-layouts: 12.4 us -> 13.9 us
    ppermute x5 -> x4, starting transfers between devices: 32.6 us -> 8.3 us  [exclusive_scan(): got = lax.ppermute(through, AXES, perm)]
    ppermute x5 -> x4, waiting for transfers between devices: 7.46 us -> 16.5 us  [exclusive_scan(): got = lax.ppermute(through, AXES, perm)]
    add x5 -> x0, other arithmetic: 8.43 us -> none  [combine(): return scale[:, None] * earlier + later]
    select_n x0 -> x7, other arithmetic: none -> 4.21 us  [the longest x3 2.19 us: exclusive_scan(): jnp.where(lower, combine(got, through, heads // 2), combine(through, got,...]
    ppermute x0 -> x2, waiting for transfers between devices: none -> 1.33 us  [the longest x1 1.33 us: exclusive_scan(): swapped = lax.ppermute(before, AXES, partner)]
    unnamed x15 -> x13, local copies, waits for them, and re-layouts: 2.01 us -> 2.5 us
  transfers between devices with their start and end apart: 5 -> 6, of which waited for: 4 -> 5; matrix products, arithmetic and copies ran while one was open for 16% -> 21% of each run, Pallas kernels for 0% -> 0%
where the time goes in v3:
time: 74.2 us; the launch traced here: 73.5 us
  matrix products  24.3 us (33%)
  waiting for transfers between devices  17.9 us (24%)
  local copies, waits for them, and re-layouts  13.9 us (19%)
  starting transfers between devices  8.86 us (12%)
  other arithmetic  8.46 us (11%)
    ppermute x4, waiting for transfers between devices, exclusive_scan(): got = lax.ppermute(through, AXES, perm)  16.5 us
    ppermute x4, starting transfers between devices, exclusive_scan(): got = lax.ppermute(through, AXES, perm)  8.3 us
    dot_general x1, matrix products, shards(): jnp.einsum('hts,shd->thd', weights, value_rows, preferred_element_type=f32)  6.85 us
    dot_general x1, matrix products, shards(): jnp.dot(tokens, query_weight, preferred_element_type=f32)  3.86 us
    dot_general x1, matrix products, shards(): jnp.dot(tokens, value_weight, preferred_element_type=f32)  3.71 us
    dot_general x1, matrix products, shards(): jnp.dot(tokens, key_weight, preferred_element_type=f32)  3.16 us
    unnamed x13, local copies, waits for them, and re-layouts  2.5 us
    dot_general x1, matrix products, shards(): jnp.einsum('thd,hde->the', qfloat, incoming, precision=lax.Precision.HIGH...  2.46 us
  transfers between devices with their start and end apart: 6, of which 5 were waited for; matrix products, arithmetic and copies ran while one was open for 21% of the time, Pallas kernels for 0%

profile of v3, /device:TPU:0, one launch (start us, length us, event | category | flops | bytes accessed | tf_op | source)
XLA Modules:
  0.0 73.5 jit_solution(16139337752380428676)
XLA Ops:
  0.0 0.9 %copy_bitcast_fusion.1 = f32[16,3,128]{2,0,1:T(8,128)S(1)} fusion(f32[384,16]{0,1:T(8,128)} %param.16), kind=kLoop, calls=%fused_computation.41 | loop fusion | bytes 49152 | tf_op jit(solution)/shard_map/reshape.98
  0.9 0.9 %reduce-window.6 = f32[16,3,128]{2,0,1:T(8,128)S(1)} reduce-window(f32[16,3,128]{2,0,1:T(8,128)S(1)} %copy_bitcast_fusion.1, f32[]{:T(128)} %constant.126.clone.1), window={size=1x1x128 pad=0_0x0_0x127_0}, to_apply=%region_0.1 | reduce-window | flops 780288 | bytes 49156 | tf_op jit(solution)/shard_map/reduce-window
  1.7 0.2 slice_reduce_fusion
  2.0 0.2 slice_reduce_fusion.1
  2.3 0.7 bitcast_exponential_fusion
  3.0 3.2 %multiply_convert_fusion.3 = bf16[384,1024]{1,0:T(8,128)(2,1)} fusion(bf16[384,1024]{1,0:T(8,128)(2,1)} %param.15, bf16[1024,1024]{1,0:T(8,128)(2,1)S(1)} %copy-done), kind=kOutput, calls=%fused_computation.10 | convolution fusion | flops 807272448 | bytes 3670016 | tf_op jit(solution)/shard_map/dot_general | solution.py:63
  6.1 1.5 %copy.26 = bf16[384,1024]{0,1:T(8,128)(2,1)S(1)} copy(bf16[384,1024]{1,0:T(8,128)(2,1)} %multiply_convert_fusion.3) | data formatting | bytes 1572864 | tf_op jit(solution)/shard_map/convert_element_type | solution.py:63
  7.6 3.7 %convolution_convert_fusion.1 = bf16[384,1024]{1,0:T(8,128)(2,1)} fusion(bf16[384,1024]{1,0:T(8,128)(2,1)} %param.15, bf16[1024,1024]{1,0:T(8,128)(2,1)} %param.19), kind=kOutput, calls=%fused_computation.13 | convolution fusion | flops 805699584 | bytes 3670016 | tf_op jit(solution)/shard_map/dot_general | solution.py:64
  11.3 2.3 %copy.24 = bf16[384,1024]{0,1:T(8,128)(2,1)} copy(bf16[384,1024]{1,0:T(8,128)(2,1)} %convolution_convert_fusion.1) | data formatting | bytes 1572864 | tf_op jit(solution)/shard_map/convert_element_type | solution.py:64
  13.6 2.3 %fusion.6 = f32[16,64,64]{2,1,0:T(8,128)} fusion(bf16[384,16,64]{0,2,1:T(8,128)(2,1)} %bitcast.80, bf16[384,16,64]{0,2,1:T(8,128)(2,1)S(1)} %bitcast.78, f32[384,16]{0,1:T(8,128)S(1)} %get-tuple-element.62), kind=kOutput, calls=%fused_computation.14 | convolution fusion | flops 51511296 | bytes 1859584 | tf_op jit(solution)/shard_map/thd,the->hde/dot_general | solution.py:70
  16.0 1.2 %reshape.235 = f32[512,128]{1,0:T(8,128)S(1)} reshape(f32[16,64,64]{2,1,0:T(8,128)} %fusion.6) | data formatting | bytes 524288 | tf_op jit(solution)/shard_map/reshape | solution.py:73
  17.2 0.7 select_maximum_fusion
  17.9 0.5 collective-permute-start
  18.4 0.7 iota_compare_fusion
  19.1 3.9 %multiply_convert_fusion.4 = bf16[384,1024]{1,0:T(8,128)(2,1)} fusion(bf16[384,1024]{1,0:T(8,128)(2,1)} %param.15, bf16[1024,1024]{1,0:T(8,128)(2,1)} %param.17), kind=kOutput, calls=%fused_computation.11 | convolution fusion | flops 807272448 | bytes 3670016 | tf_op jit(solution)/shard_map/dot_general | solution.py:77
  22.9 2.3 %copy.25 = bf16[384,1024]{0,1:T(8,128)(2,1)} copy(bf16[384,1024]{1,0:T(8,128)(2,1)} %multiply_convert_fusion.4) | data formatting | bytes 1572864 | tf_op jit(solution)/shard_map/convert_element_type | solution.py:77
  25.2 6.9 %fusion = f32[16,64,384]{2,1,0:T(8,128)} fusion(bf16[384,16,64]{0,2,1:T(8,128)(2,1)} %bitcast.81, f32[16,384]{1,0:T(8,128)S(1)} %get-tuple-element.66, pred[384,384]{1,0:T(8,128)(4,1)} %iota_compare_fusion, bf16[384,16,64]{0,2,1:T(8,128)(2,1)} %bitcast.82, bf16[384,16,64]{0,2,1:T(8,128)(2,1)S(1)} %bitcast.79), kind=kOutput, calls=%fused_computation.1 | convolution fusion | flops 615776256 | bytes 4104192 | tf_op jit(solution)/shard_map/hts,shd->thd/dot_general | solution.py:87
  32.2 0.1 reshape.237
  32.3 0.1 reshape.236
  32.4 0.2 add_select_fusion
  32.8 2.6 %collective-permute-start.1 = (f32[264,128]{1,0:T(8,128)S(1)}, f32[264,128]{1,0:T(8,128)S(1)}, u32[]{:S(2)}, u32[]{:S(2)}) collective-permute-start(f32[264,128]{1,0:T(8,128)S(1)} %select_maximum_fusion.1), channel_id=1, source_target_pairs={{0,2},{1,3},{2,0},{3,1},{4,6},{5,7},{6,4},{7,5},{8,10},{9,11},{10,... | collective-permute-start | bytes 405512 | tf_op jit(solution)/shard_map/ppermute | solution.py:47
  35.4 0.6 iota_compare_fusion.1
  36.1 0.1 reshape.239
  36.2 3.4 %collective-permute-done.1 = f32[264,128]{1,0:T(8,128)S(1)} collective-permute-done((f32[264,128]{1,0:T(8,128)S(1)}, f32[264,128]{1,0:T(8,128)S(1)}, u32[]{:S(2)}, u32[]{:S(2)}) %collective-permute-start.1) | collective-permute-done | bytes 135200 | tf_op jit(solution)/shard_map/ppermute | solution.py:47
  39.7 0.1 reshape.240
  39.8 0.1 add_select_fusion.6
  40.0 2.8 %collective-permute-start.2 = (f32[264,128]{1,0:T(8,128)S(1)}, f32[264,128]{1,0:T(8,128)S(1)}, u32[]{:S(2)}, u32[]{:S(2)}) collective-permute-start(f32[264,128]{1,0:T(8,128)S(1)} %get-tuple-element.59), channel_id=1, source_target_pairs={{0,4},{1,5},{2,6},{3,7},{4,0},{5,1},{6,2},{7,3},{8,12},{9,13},{10,... | collective-permute-start | bytes 405512 | tf_op jit(solution)/shard_map/ppermute | solution.py:47
  42.9 0.1 reshape.242
  43.0 0.1 reshape.238
  43.1 6.1 %collective-permute-done.2 = f32[264,128]{1,0:T(8,128)S(1)} collective-permute-done((f32[264,128]{1,0:T(8,128)S(1)}, f32[264,128]{1,0:T(8,128)S(1)}, u32[]{:S(2)}, u32[]{:S(2)}) %collective-permute-start.2) | collective-permute-done | bytes 135200 | tf_op jit(solution)/shard_map/ppermute | solution.py:47
  49.4 0.2 add_select_fusion.5
  49.6 1.4 %collective-permute-start.3 = (f32[264,128]{1,0:T(8,128)S(1)}, f32[264,128]{1,0:T(8,128)S(1)}, u32[]{:S(2)}, u32[]{:S(2)}) collective-permute-start(f32[264,128]{1,0:T(8,128)S(1)} %get-tuple-element.57), channel_id=1, source_target_pairs={{0,8},{1,9},{2,10},{3,11},{4,12},{5,13},{6,14},{7,15},{8,0},{9,1},... | collective-permute-start | bytes 405512 | tf_op jit(solution)/shard_map/ppermute | solution.py:47
  51.4 3.3 %collective-permute-done.3 = f32[264,128]{1,0:T(8,128)S(1)} collective-permute-done((f32[264,128]{1,0:T(8,128)S(1)}, f32[264,128]{1,0:T(8,128)S(1)}, u32[]{:S(2)}, u32[]{:S(2)}) %collective-permute-start.3) | collective-permute-done | bytes 135200 | tf_op jit(solution)/shard_map/ppermute | solution.py:47
  54.8 0.1 reshape.246
  54.9 0.5 copy-done.4
  55.4 1.9 %add_select_fusion.4 = (f32[264,128]{1,0:T(8,128)}, f32[264,128]{1,0:T(8,128)S(1)}) fusion(f32[264,128]{1,0:T(8,128)} %copy-done.4, f32[264,128]{1,0:T(8,128)S(1)} %get-tuple-element.57, f32[264]{0:T(512)S(1)} %concatenate.72, f32[264]{0:T(512)S(1)} %concatenate.71, pred[]{:T(512)S(6)} %ne.27, f32[264,128]{1,0:T(8,128)} %copy-done.3, f32[264]{0:T(512)S(1)} %concatenate.67), kind=kLoop, calls=%fused_computation.35 | loop fusion | flops 270336 | bytes 679009 | tf_op jit(solution)/shard_map/jit(_where)/select_n | solution.py:52
  57.2 1.4 %collective-permute-start.4 = (f32[264,128]{1,0:T(8,128)}, f32[264,128]{1,0:T(8,128)S(1)}, u32[]{:S(2)}, u32[]{:S(2)}) collective-permute-start(f32[264,128]{1,0:T(8,128)} %get-tuple-element.55), channel_id=1, source_target_pairs={{0,16},{1,17},{2,18},{3,19},{4,20},{5,21},{6,22},{7,23},{8,24},{9,... | collective-permute-start | bytes 405512 | tf_op jit(solution)/shard_map/ppermute | solution.py:47
  58.8 3.6 %collective-permute-done.4 = f32[264,128]{1,0:T(8,128)S(1)} collective-permute-done((f32[264,128]{1,0:T(8,128)}, f32[264,128]{1,0:T(8,128)S(1)}, u32[]{:S(2)}, u32[]{:S(2)}) %collective-permute-start.4) | collective-permute-done | bytes 135200 | tf_op jit(solution)/shard_map/ppermute | solution.py:47
  62.5 0.1 add_select_fusion.1
  62.7 1.3 %collective-permute-done.5 = f32[264,128]{1,0:T(8,128)S(1)} collective-permute-done((f32[264,128]{1,0:T(8,128)S(1)}, f32[264,128]{1,0:T(8,128)S(1)}, u32[]{:S(2)}, u32[]{:S(2)}) %collective-permute-start.5) | collective-permute-done | bytes 135200 | tf_op jit(solution)/shard_map/ppermute | solution.py:53
  64.1 1.7 %fusion.8 = f32[512,128]{1,0:T(8,128)} fusion(f32[520,128]{1,0:T(8,128)S(1)} %collective-permute-done, f32[1,16]{1,0:T(1,128)S(1)} %get-tuple-element.68, f32[256,128]{1,0:T(8,128)S(1)} %slice.170, f32[256,128]{1,0:T(8,128)S(1)} %slice.171, f32[1,16]{1,0:T(1,128)S(1)} %get-tuple-element.67, pred[520,128]{1,0:T(8,128)(4,1)} %iota_compare_fusion.1, ...), kind=kLoop, calls=%fused_computation.22 | loop fusion | flops 655360 | bytes 854145 | tf_op jit(solution)/shard_map/jit(_where)/select_n | solution.py:55
  65.8 1.1 %reshape.249 = f32[16,64,64]{2,1,0:T(8,128)S(1)} reshape(f32[512,128]{1,0:T(8,128)} %fusion.8) | data formatting | bytes 524288 | tf_op jit(solution)/shard_map/reshape | solution.py:75
  66.9 2.5 %multiply_reduce_fusion = (f32[384,16]{0,1:T(8,128)S(1)}, f32[384,16,64]{0,2,1:T(8,128)S(1)}) fusion(f32[384,16]{0,1:T(8,128)} %get-tuple-element.61, f32[16,64,64]{2,1,0:T(8,128)S(1)} %reshape.249, bf16[384,16,64]{0,2,1:T(8,128)(2,1)S(1)} %bitcast.83, f32[16,64,384]{2,1,0:T(8,128)} %fusion), kind=kOutput, calls=%fused_computation.8 | convolution fusion | flops 303556608 | bytes 4243456 | tf_op jit(solution)/shard_map/thd,hde->the/dot_general | solution.py:91
  69.4 0.1 broadcast_multiply_fusion
  69.5 0.5 copy-done.5
  70.1 0.2 fusion.4
  70.3 1.4 %copy-done.2 = bf16[1024,1024]{1,0:T(8,128)(2,1)S(1)} copy-done((bf16[1024,1024]{1,0:T(8,128)(2,1)S(1)}, bf16[1024,1024]{1,0:T(8,128)(2,1)}, u32[]{:S(2)}) %copy-start.2) | copy-done | bytes 2097176
  71.7 1.9 %convolution_convert_fusion = bf16[384,1024]{1,0:T(8,128)(2,1)} fusion(bf16[384,1024]{0,1:T(8,128)(2,1)S(1)} %fusion.4, bf16[1024,1024]{1,0:T(8,128)(2,1)S(1)} %copy-done.2), kind=kOutput, calls=%fused_computation.12 | convolution fusion | flops 805699584 | bytes 3670016 | tf_op jit(solution)/shard_map/dot_general | solution.py:97
  (59 shorter events, 1.7 us)
Async XLA Ops:
  0.0 3.0 %copy-start = (bf16[1024,1024]{1,0:T(8,128)(2,1)S(1)}, bf16[1024,1024]{1,0:T(8,128)(2,1)}, u32[]{:S(2)}) copy-start(bf16[1024,1024]{1,0:T(8,128)(2,1)} %param.18) | copy-start | bytes 6291460
  17.9 14.4 %collective-permute-start = (f32[520,128]{1,0:T(8,128)}, f32[520,128]{1,0:T(8,128)S(1)}, u32[]{:S(2)}, u32[]{:S(2)}) collective-permute-start(f32[520,128]{1,0:T(8,128)} %select_maximum_fusion), channel_id=1, source_target_pairs={{0,1},{1,0},{2,3},{3,2},{4,5},{5,4},{6,7},{7,6},{8,9},{9,8},{10,11... | collective-permute-start | bytes 798728 | tf_op jit(solution)/shard_map/ppermute | solution.py:40
  32.8 6.9 %collective-permute-start.1 = (f32[264,128]{1,0:T(8,128)S(1)}, f32[264,128]{1,0:T(8,128)S(1)}, u32[]{:S(2)}, u32[]{:S(2)}) collective-permute-start(f32[264,128]{1,0:T(8,128)S(1)} %select_maximum_fusion.1), channel_id=1, source_target_pairs={{0,2},{1,3},{2,0},{3,1},{4,6},{5,7},{6,4},{7,5},{8,10},{9,11},{10,... | collective-permute-start | bytes 405512 | tf_op jit(solution)/shard_map/ppermute | solution.py:47
  40.0 9.3 %collective-permute-start.2 = (f32[264,128]{1,0:T(8,128)S(1)}, f32[264,128]{1,0:T(8,128)S(1)}, u32[]{:S(2)}, u32[]{:S(2)}) collective-permute-start(f32[264,128]{1,0:T(8,128)S(1)} %get-tuple-element.59), channel_id=1, source_target_pairs={{0,4},{1,5},{2,6},{3,7},{4,0},{5,1},{6,2},{7,3},{8,12},{9,13},{10,... | collective-permute-start | bytes 405512 | tf_op jit(solution)/shard_map/ppermute | solution.py:47
  49.6 5.3 %copy-start.3 = (f32[264,128]{1,0:T(8,128)}, f32[264,128]{1,0:T(8,128)S(1)}, u32[]{:S(2)}) copy-start(f32[264,128]{1,0:T(8,128)S(1)} %get-tuple-element.58) | copy-start | bytes 405508
  49.6 5.1 %collective-permute-start.3 = (f32[264,128]{1,0:T(8,128)S(1)}, f32[264,128]{1,0:T(8,128)S(1)}, u32[]{:S(2)}, u32[]{:S(2)}) collective-permute-start(f32[264,128]{1,0:T(8,128)S(1)} %get-tuple-element.57), channel_id=1, source_target_pairs={{0,8},{1,9},{2,10},{3,11},{4,12},{5,13},{6,14},{7,15},{8,0},{9,1},... | collective-permute-start | bytes 405512 | tf_op jit(solution)/shard_map/ppermute | solution.py:47
  54.7 0.7 copy-start.4
  55.4 11.5 %copy-start.1 = (bf16[384,1024]{0,1:T(8,128)(2,1)S(1)}, bf16[384,1024]{0,1:T(8,128)(2,1)}, u32[]{:S(2)}) copy-start(bf16[384,1024]{0,1:T(8,128)(2,1)} %copy.25) | copy-start | bytes 2359300
  57.2 5.2 %collective-permute-start.4 = (f32[264,128]{1,0:T(8,128)}, f32[264,128]{1,0:T(8,128)S(1)}, u32[]{:S(2)}, u32[]{:S(2)}) collective-permute-start(f32[264,128]{1,0:T(8,128)} %get-tuple-element.55), channel_id=1, source_target_pairs={{0,16},{1,17},{2,18},{3,19},{4,20},{5,21},{6,22},{7,23},{8,24},{9,... | collective-permute-start | bytes 405512 | tf_op jit(solution)/shard_map/ppermute | solution.py:47
  62.6 1.4 %collective-permute-start.5 = (f32[264,128]{1,0:T(8,128)S(1)}, f32[264,128]{1,0:T(8,128)S(1)}, u32[]{:S(2)}, u32[]{:S(2)}) collective-permute-start(f32[264,128]{1,0:T(8,128)S(1)} %add_select_fusion.1), channel_id=1, source_target_pairs={{0,1},{1,0},{2,3},{3,2},{4,5},{5,4},{6,7},{7,6},{8,9},{9,8},{10,11... | collective-permute-start | bytes 405512 | tf_op jit(solution)/shard_map/ppermute | solution.py:53
  69.4 0.7 copy-start.5
  70.1 1.6 %copy-start.2 = (bf16[1024,1024]{1,0:T(8,128)(2,1)S(1)}, bf16[1024,1024]{1,0:T(8,128)(2,1)}, u32[]{:S(2)}) copy-start(bf16[1024,1024]{1,0:T(8,128)(2,1)} %param.21) | copy-start | bytes 6291460

commit v4 on v3

--- a/solution.py
+++ b/solution.py
@@ -41,10 +41,12 @@
     pooled = jnp.where(core == 0, combine(own, other, heads), combine(other, own, heads))
     through = half_of(pooled, core, heads)
     before = jnp.zeros_like(through)
+    received = []
     bit = 1
     while bit < chips:
         perm = [(i, i ^ (2 * bit)) for i in range(count)]
         got = lax.ppermute(through, AXES, perm)
+        received.append(got)
         lower = (chip & bit) != 0
         before = jnp.where(lower, combine(got, before, heads // 2), before)
         bit *= 2
@@ -53,7 +55,7 @@
     swapped = lax.ppermute(before, AXES, partner)
     whole = jnp.where(core == 0, join_halves(before, swapped, heads), join_halves(swapped, before, heads))
     whole = jnp.where(core == 0, whole, combine(whole, other, heads))
-    return whole[:-8]
+    return whole[:-8], received
 
 
 def shards(count, tokens, log_decay, query_weight, key_weight, value_weight, norm_gain, output_weight):
@@ -72,9 +74,13 @@
     packed = jnp.concatenate(
         [local.reshape(-1, lanes), jnp.zeros((8, lanes), f32).at[0, :heads].set(last)], axis=0
     )
-    incoming = exclusive_scan(packed, count, heads).reshape(local.shape)
+    incoming, received = exclusive_scan(packed, count, heads)
+    incoming = incoming.reshape(local.shape)
+    gate = lambda value, round_: lax.optimization_barrier((value, received[min(round_, len(received) - 1)]))[0]
 
-    queries = jax.nn.silu(jnp.dot(tokens, query_weight, preferred_element_type=f32)).astype(jnp.bfloat16)
+    queries = jax.nn.silu(
+        jnp.dot(gate(tokens, 0), query_weight, preferred_element_type=f32)
+    ).astype(jnp.bfloat16)
     queries = queries.reshape(rows, heads, -1)
     t_idx = lax.broadcasted_iota(jnp.int32, (rows, rows), 0)
     s_idx = lax.broadcasted_iota(jnp.int32, (rows, rows), 1)
@@ -82,9 +88,16 @@
     cum_h = cum.T
     diff = jnp.where(lower, cum_h[:, :, None] - cum_h[:, None, :], 0.0)
     decay = jnp.where(lower, jnp.exp(diff), 0.0)
-    scores = jnp.einsum("thd,shd->hts", queries, keys, preferred_element_type=f32)
-    weights = (scores * decay).astype(jnp.bfloat16)
-    intra = jnp.einsum("hts,shd->thd", weights, value_rows, preferred_element_type=f32)
+    parts = []
+    half = heads // 2
+    for part in range(2):
+        pick = slice(part * half, (part + 1) * half)
+        scores = jnp.einsum(
+            "thd,shd->hts", gate(queries[:, pick], part + 1), keys[:, pick], preferred_element_type=f32
+        )
+        weights = (scores * decay[pick]).astype(jnp.bfloat16)
+        parts.append(jnp.einsum("hts,shd->thd", weights, value_rows[:, pick], preferred_element_type=f32))
+    intra = jnp.concatenate(parts, axis=1)
 
     qfloat = queries.astype(f32)
     inter = (

time: 74.2 us -> 71.6 us (0.965)
  waiting for transfers between devices: 17.9 us -> 4.23 us
  local copies, waits for them, and re-layouts: 13.9 us -> 17.8 us
  other arithmetic: 8.46 us -> 12.3 us
  matrix products: 24.3 us -> 27.2 us
    ppermute x4, waiting for transfers between devices: 16.5 us -> 2.9 us  [exclusive_scan(): got = lax.ppermute(through, AXES, perm)]
    select_n x0 -> x1, other arithmetic: none -> 4.57 us  [shards(): decay = jnp.where(lower, jnp.exp(diff), 0.0)]
    dot_general x2 -> x3, matrix products: 10.7 us -> 14.3 us  [the longest x2 10.4 us: shards(): jnp.einsum('hts,shd->thd', weights, value_rows[:, pick], preferred_elemen...]
    concatenate x11, local copies, waits for them, and re-layouts: 0.07 us -> 2.98 us  [combine(): jnp.concatenate([jnp.repeat(jnp.exp(later[body, :heads]), body // heads),...]
    select_n x1 -> x3, other arithmetic: 0.1 us -> 1.98 us  [exclusive_scan(): before = jnp.where(lower, combine(got, before, heads // 2), before)]
    slice x1 -> x2, local copies, waits for them, and re-layouts: 0.01 us -> 1.49 us  [the longest x1 0.96 us: shards(): queries[:, pick]]
    reshape x11, local copies, waits for them, and re-layouts: 0.89 us -> 2.16 us  [combine(): jnp.repeat(jnp.exp(later[body, :heads]), body // heads)]
    unnamed x13 -> x17, local copies, waits for them, and re-layouts: 2.5 us -> 1.33 us
  transfers between devices with their start and end apart: 6 -> 6, of which waited for: 5 -> 2; matrix products, arithmetic and copies ran while one was open for 21% -> 36% of each run, Pallas kernels for 0% -> 0%
where the time goes in v4:
time: 71.6 us; the launch traced here: 70.9 us
  matrix products  27.2 us (38%)
  local copies, waits for them, and re-layouts  17.8 us (25%)
  other arithmetic  12.3 us (17%)
  starting transfers between devices  9.12 us (13%)
  waiting for transfers between devices  4.23 us (6%)
    dot_general x2, matrix products, shards(): jnp.einsum('hts,shd->thd', weights, value_rows[:, pick], preferred_elemen...  10.4 us
    ppermute x4, starting transfers between devices, exclusive_scan(): got = lax.ppermute(through, AXES, perm)  8.5 us
    select_n x1, other arithmetic, shards(): decay = jnp.where(lower, jnp.exp(diff), 0.0)  4.57 us
    dot_general x1, matrix products, shards(): jnp.dot(tokens, value_weight, preferred_element_type=f32)  3.97 us
    dot_general x1, matrix products, shards(): jnp.dot(gate(tokens, 0), query_weight, preferred_element_type=f32)  3.86 us
    dot_general x1, matrix products, shards(): jnp.dot(tokens, key_weight, preferred_element_type=f32)  3.17 us
    concatenate x11, local copies, waits for them, and re-layouts, combine(): jnp.concatenate([jnp.repeat(jnp.exp(later[body, :heads]), body // heads),...  2.98 us
    ppermute x4, waiting for transfers between devices, exclusive_scan(): got = lax.ppermute(through, AXES, perm)  2.9 us
  transfers between devices with their start and end apart: 6, of which 2 were waited for; matrix products, arithmetic and copies ran while one was open for 36% of the time, Pallas kernels for 0%

profile of v4, /device:TPU:0, one launch (start us, length us, event | category | flops | bytes accessed | tf_op | source)
XLA Modules:
  0.0 70.9 jit_solution(1451257873200911799)
XLA Ops:
  0.0 0.9 %copy_bitcast_fusion.1 = f32[16,3,128]{2,0,1:T(8,128)S(1)} fusion(f32[384,16]{0,1:T(8,128)} %param.16), kind=kLoop, calls=%fused_computation.50 | loop fusion | bytes 49152 | tf_op jit(solution)/shard_map/reshape.98
  0.9 0.9 %reduce-window.6 = f32[16,3,128]{2,0,1:T(8,128)S(1)} reduce-window(f32[16,3,128]{2,0,1:T(8,128)S(1)} %copy_bitcast_fusion.1, f32[]{:T(128)} %constant.132.clone.1), window={size=1x1x128 pad=0_0x0_0x127_0}, to_apply=%region_0.1 | reduce-window | flops 780288 | bytes 49156 | tf_op jit(solution)/shard_map/reduce-window
  1.7 0.2 slice_reduce_fusion
  2.0 0.2 slice_reduce_fusion.1
  2.3 0.7 bitcast_exponential_fusion
  3.0 3.2 %multiply_convert_fusion.2 = bf16[384,1024]{1,0:T(8,128)(2,1)} fusion(bf16[384,1024]{1,0:T(8,128)(2,1)} %param.15, bf16[1024,1024]{1,0:T(8,128)(2,1)S(1)} %copy-done), kind=kOutput, calls=%fused_computation.16 | convolution fusion | flops 807272448 | bytes 3670016 | tf_op jit(solution)/shard_map/dot_general | solution.py:65
  6.2 1.5 %copy.26 = bf16[384,1024]{0,1:T(8,128)(2,1)S(1)} copy(bf16[384,1024]{1,0:T(8,128)(2,1)} %multiply_convert_fusion.2) | data formatting | bytes 1572864 | tf_op jit(solution)/shard_map/convert_element_type | solution.py:65
  7.7 4.0 %convolution_convert_fusion.1 = bf16[384,1024]{1,0:T(8,128)(2,1)} fusion(bf16[384,1024]{1,0:T(8,128)(2,1)} %param.15, bf16[1024,1024]{1,0:T(8,128)(2,1)} %param.19), kind=kOutput, calls=%fused_computation.18 | convolution fusion | flops 805699584 | bytes 3670016 | tf_op jit(solution)/shard_map/dot_general | solution.py:66
  11.6 2.3 %copy.25 = bf16[384,1024]{0,1:T(8,128)(2,1)} copy(bf16[384,1024]{1,0:T(8,128)(2,1)} %convolution_convert_fusion.1) | data formatting | bytes 1572864 | tf_op jit(solution)/shard_map/convert_element_type | solution.py:66
  13.9 1.5 %fusion.17 = f32[16,64,64]{2,1,0:T(8,128)S(1)} fusion(bf16[384,16,64]{0,2,1:T(8,128)(2,1)} %bitcast.86, bf16[384,16,64]{0,2,1:T(8,128)(2,1)S(1)} %bitcast.83, f32[384,16]{0,1:T(8,128)S(1)} %get-tuple-element.70), kind=kOutput, calls=%fused_computation.21 | convolution fusion | flops 51511296 | bytes 1859584 | tf_op jit(solution)/shard_map/thd,the->hde/dot_general | solution.py:72
  15.5 0.1 reshape.234
  15.7 0.6 collective-permute-start
  16.3 0.1 reshape.236
  16.4 4.6 %exponential_select_fusion = f32[16,384,384]{2,1,0:T(8,128)} fusion(f32[16,384]{1,0:T(8,128)S(1)} %get-tuple-element.74, pred[384,384]{1,0:T(8,128)(4,1)S(1)} %iota_compare_fusion), kind=kLoop, calls=%fused_computation | loop fusion | flops 7077888 | bytes 9609216 | tf_op jit(solution)/shard_map/jit(_where)/select_n | solution.py:90
  21.2 0.2 add_select_fusion
  21.5 2.7 %collective-permute-start.1 = (f32[264,128]{1,0:T(8,128)S(1)}, f32[264,128]{1,0:T(8,128)S(1)}, u32[]{:S(2)}, u32[]{:S(2)}) collective-permute-start(f32[264,128]{1,0:T(8,128)S(1)} %select_maximum_fusion.1), channel_id=1, source_target_pairs={{0,2},{1,3},{2,0},{3,1},{4,6},{5,7},{6,4},{7,5},{8,10},{9,11},{10,... | collective-permute-start | bytes 405512 | tf_op jit(solution)/shard_map/ppermute | solution.py:48
  24.2 0.6 iota_compare_fusion.1
  25.0 0.5 pad_slice_fusion
  25.5 2.9 %collective-permute-done.1 = f32[264,128]{1,0:T(8,128)S(1)} collective-permute-done((f32[264,128]{1,0:T(8,128)S(1)}, f32[264,128]{1,0:T(8,128)S(1)}, u32[]{:S(2)}, u32[]{:S(2)}) %collective-permute-start.1) | collective-permute-done | bytes 135200 | tf_op jit(solution)/shard_map/ppermute | solution.py:48
  28.6 0.1 broadcast_select_fusion
  28.7 2.8 %collective-permute-start.2 = (f32[264,128]{1,0:T(8,128)S(1)}, f32[264,128]{1,0:T(8,128)S(1)}, u32[]{:S(2)}, u32[]{:S(2)}) collective-permute-start(f32[264,128]{1,0:T(8,128)S(1)} %get-tuple-element.68), channel_id=1, source_target_pairs={{0,4},{1,5},{2,6},{3,7},{4,0},{5,1},{6,2},{7,3},{8,12},{9,13},{10,... | collective-permute-start | bytes 405512 | tf_op jit(solution)/shard_map/ppermute | solution.py:48
  31.7 0.5 concatenate.72
  32.4 0.5 concatenate.69
  32.9 3.9 %multiply_convert_fusion = bf16[384,1024]{1,0:T(8,128)(2,1)} fusion(bf16[384,1024]{1,0:T(8,128)(2,1)} %param.15, bf16[1024,1024]{1,0:T(8,128)(2,1)} %param.17), kind=kOutput, calls=%fused_computation.14 | convolution fusion | flops 807272448 | bytes 3670016 | tf_op jit(solution)/shard_map/dot_general | solution.py:82
  36.8 1.5 %copy.30 = bf16[384,1024]{0,1:T(8,128)(2,1)S(1)} copy(bf16[384,1024]{1,0:T(8,128)(2,1)} %multiply_convert_fusion) | data formatting | bytes 1572864 | tf_op jit(solution)/shard_map/convert_element_type | solution.py:83
  38.3 1.0 %fusion.37 = (bf16[384,8,64]{0,2,1:T(8,128)(2,1)}, bf16[384,8,64]{0,2,1:T(8,128)(2,1)}) fusion(bf16[384,16,64]{0,2,1:T(8,128)(2,1)S(1)} %bitcast.81), kind=kLoop, calls=%fused_computation.83 | loop fusion | bytes 1572864 | tf_op jit(solution)/shard_map/slice | solution.py:96
  39.3 0.7 broadcast_in_dim.81
  39.9 1.4 %reshape.241 = f32[256]{0:T(256)} reshape(f32[8,32]{1,0:T(8,128)} %broadcast_in_dim.81) | data formatting | bytes 2048 | tf_op jit(solution)/shard_map/reshape | solution.py:12
  41.3 0.7 concatenate.70
  42.0 1.7 %add_select_fusion.3 = (f32[264,128]{1,0:T(8,128)S(1)}, f32[264,128]{1,0:T(8,128)}) fusion(f32[264,128]{1,0:T(8,128)S(1)} %get-tuple-element.67, f32[264,128]{1,0:T(8,128)} %copy-done.4, f32[264]{0:T(512)} %concatenate.72, pred[]{:T(512)S(6)} %ne.27, f32[264,128]{1,0:T(8,128)S(1)} %get-tuple-element.68, f32[264]{0:T(512)S(1)} %concatenate.70, f32[264]{0:T(512)} %concatenate.69), kind=kLoop, calls=%fused_computation.41 | loop fusion | flops 270336 | bytes 679009 | tf_op jit(solution)/shard_map/jit(_where)/select_n | solution.py:51
  43.7 0.7 fusion.28
  44.4 1.5 %collective-permute-start.3 = (f32[264,128]{1,0:T(8,128)}, f32[264,128]{1,0:T(8,128)S(1)}, u32[]{:S(2)}, u32[]{:S(2)}) collective-permute-start(f32[264,128]{1,0:T(8,128)} %get-tuple-element.66), channel_id=1, source_target_pairs={{0,8},{1,9},{2,10},{3,11},{4,12},{5,13},{6,14},{7,15},{8,0},{9,1},... | collective-permute-start | bytes 405512 | tf_op jit(solution)/shard_map/ppermute | solution.py:48
  46.0 0.6 concatenate.75
  46.6 5.2 %fusion.14 = f32[384,8,64]{0,2,1:T(8,128)} fusion(bf16[384,16,64]{0,2,1:T(8,128)(2,1)} %bitcast.87, f32[16,384,384]{2,1,0:T(8,128)} %exponential_select_fusion, bf16[384,8,64]{0,2,1:T(8,128)(2,1)} %get-tuple-element.57, bf16[384,16,64]{0,2,1:T(8,128)(2,1)} %bitcast.84), kind=kOutput, calls=%fused_computation.20 | convolution fusion | flops 304349184 | bytes 7077888 | tf_op jit(solution)/shard_map/hts,shd->thd/dot_general | solution.py:99
  52.0 0.6 concatenate.73
  52.7 1.7 %add_select_fusion.4 = (f32[264,128]{1,0:T(8,128)}, f32[264,128]{1,0:T(8,128)S(1)}) fusion(f32[264,128]{1,0:T(8,128)S(1)} %collective-permute-done.3, f32[264,128]{1,0:T(8,128)} %get-tuple-element.66, f32[264]{0:T(512)S(1)} %concatenate.76, f32[264]{0:T(512)} %concatenate.75, pred[]{:T(512)S(6)} %ne.29, f32[264,128]{1,0:T(8,128)S(1)} %get-tuple-element.65, ...), kind=kLoop, calls=%fused_computation.44 | loop fusion | flops 270336 | bytes 679009 | tf_op jit(solution)/shard_map/jit(_where)/select_n | solution.py:54
  54.4 1.5 %collective-permute-start.4 = (f32[264,128]{1,0:T(8,128)}, f32[264,128]{1,0:T(8,128)S(1)}, u32[]{:S(2)}, u32[]{:S(2)}) collective-permute-start(f32[264,128]{1,0:T(8,128)} %get-tuple-element.63), channel_id=1, source_target_pairs={{0,16},{1,17},{2,18},{3,19},{4,20},{5,21},{6,22},{7,23},{8,24},{9,... | collective-permute-start | bytes 405512 | tf_op jit(solution)/shard_map/ppermute | solution.py:48
  56.0 5.2 %fusion.11 = f32[384,8,64]{0,2,1:T(8,128)} fusion(bf16[384,16,64]{0,2,1:T(8,128)(2,1)} %bitcast.88, f32[16,384,384]{2,1,0:T(8,128)} %exponential_select_fusion, bf16[384,8,64]{0,2,1:T(8,128)(2,1)} %get-tuple-element.58, bf16[384,16,64]{0,2,1:T(8,128)(2,1)} %bitcast.85), kind=kOutput, calls=%fused_computation.19 | convolution fusion | flops 304349184 | bytes 7077888 | tf_op jit(solution)/shard_map/hts,shd->thd/dot_general | solution.py:99
  61.4 0.1 add_select_fusion.1
  61.6 1.3 %collective-permute-done.5 = f32[264,128]{1,0:T(8,128)S(1)} collective-permute-done((f32[264,128]{1,0:T(8,128)S(1)}, f32[264,128]{1,0:T(8,128)S(1)}, u32[]{:S(2)}, u32[]{:S(2)}) %collective-permute-start.5) | collective-permute-done | bytes 135200 | tf_op jit(solution)/shard_map/ppermute | solution.py:55
  63.0 0.9 %fusion.23 = f32[512,128]{1,0:T(8,128)} fusion(f32[520,128]{1,0:T(8,128)S(1)} %collective-permute-done, f32[1,16]{1,0:T(1,128)S(1)} %get-tuple-element.76, f32[256,128]{1,0:T(8,128)S(1)} %slice.208, f32[256,128]{1,0:T(8,128)S(1)} %slice.209, f32[1,16]{1,0:T(1,128)S(1)} %get-tuple-element.75, pred[520,128]{1,0:T(8,128)(4,1)S(1)} %copy-done.3, ...), kind=kLoop, calls=%fused_computation.31 | loop fusion | flops 655360 | bytes 854145 | tf_op jit(solution)/shard_map/jit(_where)/select_n | solution.py:57
  63.9 1.1 %reshape.249 = f32[16,64,64]{2,1,0:T(8,128)S(1)} reshape(f32[512,128]{1,0:T(8,128)} %fusion.23) | data formatting | bytes 524288 | tf_op jit(solution)/shard_map/reshape | solution.py:78
  65.0 2.4 %multiply_reduce_fusion = (f32[384,16]{0,1:T(8,128)S(1)}, f32[384,16,64]{0,2,1:T(8,128)S(1)}) fusion(f32[384,16]{0,1:T(8,128)S(1)} %copy-done.5, f32[16,64,64]{2,1,0:T(8,128)S(1)} %reshape.249, bf16[384,16,64]{0,2,1:T(8,128)(2,1)S(1)} %bitcast.82, f32[384,8,64]{0,2,1:T(8,128)} %fusion.11, f32[384,8,64]{0,2,1:T(8,128)} %fusion.14), kind=kOutput, calls=%fused_computation.13 | convolution fusion | flops 303949824 | bytes 4243456 | tf_op jit(solution)/shard_map/thd,hde->the/dot_general | solution.py:104
  67.5 0.1 broadcast_multiply_fusion
  67.6 0.5 copy-done.7
  68.1 0.2 fusion.10
  68.3 0.7 %copy-done.2 = bf16[1024,1024]{1,0:T(8,128)(2,1)S(1)} copy-done((bf16[1024,1024]{1,0:T(8,128)(2,1)S(1)}, bf16[1024,1024]{1,0:T(8,128)(2,1)}, u32[]{:S(2)}) %copy-start.2) | copy-done | bytes 2097176
  69.0 1.9 %convolution_convert_fusion = bf16[384,1024]{1,0:T(8,128)(2,1)} fusion(bf16[384,1024]{0,1:T(8,128)(2,1)S(1)} %fusion.10, bf16[1024,1024]{1,0:T(8,128)(2,1)S(1)} %copy-done.2), kind=kOutput, calls=%fused_computation.17 | convolution fusion | flops 805699584 | bytes 3670016 | tf_op jit(solution)/shard_map/dot_general | solution.py:110
  (66 shorter events, 2.1 us)
Async XLA Ops:
  0.0 3.0 %copy-start = (bf16[1024,1024]{1,0:T(8,128)(2,1)S(1)}, bf16[1024,1024]{1,0:T(8,128)(2,1)}, u32[]{:S(2)}) copy-start(bf16[1024,1024]{1,0:T(8,128)(2,1)} %param.18) | copy-start | bytes 6291460
  7.6 6.3 %copy-start.1 = (bf16[384,1024]{0,1:T(8,128)(2,1)}, bf16[384,1024]{0,1:T(8,128)(2,1)S(1)}, u32[]{:S(2)}) copy-start(bf16[384,1024]{0,1:T(8,128)(2,1)S(1)} %copy.26) | copy-start | bytes 2359300
  15.7 5.4 %collective-permute-start = (f32[520,128]{1,0:T(8,128)S(1)}, f32[520,128]{1,0:T(8,128)S(1)}, u32[]{:S(2)}, u32[]{:S(2)}) collective-permute-start(f32[520,128]{1,0:T(8,128)S(1)} %select_maximum_fusion), channel_id=1, source_target_pairs={{0,1},{1,0},{2,3},{3,2},{4,5},{5,4},{6,7},{7,6},{8,9},{9,8},{10,11... | collective-permute-start | bytes 798728 | tf_op jit(solution)/shard_map/ppermute | solution.py:40
  21.5 6.9 %collective-permute-start.1 = (f32[264,128]{1,0:T(8,128)S(1)}, f32[264,128]{1,0:T(8,128)S(1)}, u32[]{:S(2)}, u32[]{:S(2)}) collective-permute-start(f32[264,128]{1,0:T(8,128)S(1)} %select_maximum_fusion.1), channel_id=1, source_target_pairs={{0,2},{1,3},{2,0},{3,1},{4,6},{5,7},{6,4},{7,5},{8,10},{9,11},{10,... | collective-permute-start | bytes 405512 | tf_op jit(solution)/shard_map/ppermute | solution.py:48
  28.7 10.5 %collective-permute-start.2 = (f32[264,128]{1,0:T(8,128)S(1)}, f32[264,128]{1,0:T(8,128)S(1)}, u32[]{:S(2)}, u32[]{:S(2)}) collective-permute-start(f32[264,128]{1,0:T(8,128)S(1)} %get-tuple-element.68), channel_id=1, source_target_pairs={{0,4},{1,5},{2,6},{3,7},{4,0},{5,1},{6,2},{7,3},{8,12},{9,13},{10,... | collective-permute-start | bytes 405512 | tf_op jit(solution)/shard_map/ppermute | solution.py:48
  39.3 2.0 %copy-start.4 = (f32[264,128]{1,0:T(8,128)}, f32[264,128]{1,0:T(8,128)S(1)}, u32[]{:S(2)}) copy-start(f32[264,128]{1,0:T(8,128)S(1)} %collective-permute-done.2) | copy-start | bytes 405508
  44.4 8.2 %collective-permute-start.3 = (f32[264,128]{1,0:T(8,128)}, f32[264,128]{1,0:T(8,128)S(1)}, u32[]{:S(2)}, u32[]{:S(2)}) collective-permute-start(f32[264,128]{1,0:T(8,128)} %get-tuple-element.66), channel_id=1, source_target_pairs={{0,8},{1,9},{2,10},{3,11},{4,12},{5,13},{6,14},{7,15},{8,0},{9,1},... | collective-permute-start | bytes 405512 | tf_op jit(solution)/shard_map/ppermute | solution.py:48
  54.4 6.9 %collective-permute-start.4 = (f32[264,128]{1,0:T(8,128)}, f32[264,128]{1,0:T(8,128)S(1)}, u32[]{:S(2)}, u32[]{:S(2)}) collective-permute-start(f32[264,128]{1,0:T(8,128)} %get-tuple-element.63), channel_id=1, source_target_pairs={{0,16},{1,17},{2,18},{3,19},{4,20},{5,21},{6,22},{7,23},{8,24},{9,... | collective-permute-start | bytes 405512 | tf_op jit(solution)/shard_map/ppermute | solution.py:48
  56.0 7.0 %copy-start.3 = (pred[520,128]{1,0:T(8,128)(4,1)S(1)}, pred[520,128]{1,0:T(8,128)(4,1)}, u32[]{:S(2)}) copy-start(pred[520,128]{1,0:T(8,128)(4,1)} %iota_compare_fusion.1) | copy-start | bytes 199684
  56.0 7.0 %copy-start.6 = (f32[512]{0:T(512)S(1)}, f32[512]{0:T(512)}, u32[]{:S(2)}) copy-start(f32[512]{0:T(512)} %pad_slice_fusion) | copy-start | bytes 6148
  61.2 3.8 %copy-start.5 = (f32[384,16]{0,1:T(8,128)S(1)}, f32[384,16]{0,1:T(8,128)}, u32[]{:S(2)}) copy-start(f32[384,16]{0,1:T(8,128)} %get-tuple-element.69) | copy-start | bytes 73732
  61.5 1.4 %collective-permute-start.5 = (f32[264,128]{1,0:T(8,128)S(1)}, f32[264,128]{1,0:T(8,128)S(1)}, u32[]{:S(2)}, u32[]{:S(2)}) collective-permute-start(f32[264,128]{1,0:T(8,128)S(1)} %add_select_fusion.1), channel_id=1, source_target_pairs={{0,1},{1,0},{2,3},{3,2},{4,5},{5,4},{6,7},{7,6},{8,9},{9,8},{10,11... | collective-permute-start | bytes 405512 | tf_op jit(solution)/shard_map/ppermute | solution.py:55
  67.4 0.7 copy-start.7
  67.5 1.6 %copy-start.2 = (bf16[1024,1024]{1,0:T(8,128)(2,1)S(1)}, bf16[1024,1024]{1,0:T(8,128)(2,1)}, u32[]{:S(2)}) copy-start(bf16[1024,1024]{1,0:T(8,128)(2,1)} %param.21) | copy-start | bytes 6291460

commit v5 on v4

--- a/solution.py
+++ b/solution.py
@@ -1,9 +1,65 @@
+import functools
+
 import jax
 import jax.numpy as jnp
 from jax import lax
+from jax.experimental import pallas as pl
 from jax.sharding import PartitionSpec as P
 
 AXES = ("outer", "inner")
+
+LANES = 128
+
+
+def intra_kernel(q_ref, k_ref, v_ref, cum_ref, cum_t_ref, o_ref, *, head_dim):
+    f32 = jnp.float32
+    pair = pl.program_id(0)
+    group = LANES // head_dim
+    rows = q_ref.shape[0]
+    heads = cum_ref.shape[1]
+    q = q_ref[...]
+    k = k_ref[...]
+    v = v_ref[...]
+    lane_head = lax.broadcasted_iota(jnp.int32, q.shape, 1) // head_dim
+    t_i = lax.broadcasted_iota(jnp.int32, (rows, rows), 0)
+    s_i = lax.broadcasted_iota(jnp.int32, (rows, rows), 1)
+    lower = s_i <= t_i
+    cum = cum_ref[...]
+    cum_t = cum_t_ref[...]
+    col_head = lax.broadcasted_iota(jnp.int32, cum.shape, 1)
+    row_head = lax.broadcasted_iota(jnp.int32, cum_t.shape, 0)
+    out = None
+    for j in range(group):
+        head = pair * group + j
+        mine = lane_head == j
+        q_j = jnp.where(mine, q, jnp.zeros_like(q))
+        scores = lax.dot_general(q_j, k, (((1,), (1,)), ((), ())), preferred_element_type=f32)
+        col = jnp.sum(jnp.where(col_head == head, cum, 0.0), axis=1, keepdims=True)
+        row = jnp.sum(jnp.where(row_head == head, cum_t, 0.0), axis=0, keepdims=True)
+        diff = jnp.where(lower, col - row, 0.0)
+        decay = jnp.where(lower, jnp.exp(diff), 0.0)
+        weights = (scores * decay).astype(jnp.bfloat16)
+        o_j = jnp.dot(weights, v, preferred_element_type=f32)
+        out = o_j if out is None else jnp.where(mine, o_j, out)
+    o_ref[...] = out
+
+
+def intra_attention(queries, keys, value_rows, cum, head_dim):
+    rows, width = queries.shape
+    heads = cum.shape[1]
+    block = pl.BlockSpec((rows, LANES), lambda p: (0, p))
+    whole = lambda shape: pl.BlockSpec(shape, lambda p: (0, 0))
+    flops = 4 * rows * rows * LANES * (LANES // head_dim) * (width // LANES)
+    return pl.pallas_call(
+        functools.partial(intra_kernel, head_dim=head_dim),
+        grid=(width // LANES,),
+        in_specs=[block, block, block, whole((rows, heads)), whole((heads, rows))],
+        out_specs=block,
+        out_shape=jax.ShapeDtypeStruct((rows, width), jnp.float32),
+        cost_estimate=pl.CostEstimate(
+            flops=flops, transcendentals=rows * rows * heads, bytes_accessed=rows * width * 10
+        ),
+    )(queries, keys, value_rows, cum, cum.T)
 
 
 def combine(earlier, later, heads):
@@ -81,23 +137,10 @@
     queries = jax.nn.silu(
         jnp.dot(gate(tokens, 0), query_weight, preferred_element_type=f32)
     ).astype(jnp.bfloat16)
+    intra = intra_attention(
+        gate(queries, 1), keys.reshape(rows, -1), value_rows.reshape(rows, -1), cum, keys.shape[-1]
+    ).reshape(rows, heads, -1)
     queries = queries.reshape(rows, heads, -1)
-    t_idx = lax.broadcasted_iota(jnp.int32, (rows, rows), 0)
-    s_idx = lax.broadcasted_iota(jnp.int32, (rows, rows), 1)
-    lower = (s_idx <= t_idx)[None]
-    cum_h = cum.T
-    diff = jnp.where(lower, cum_h[:, :, None] - cum_h[:, None, :], 0.0)
-    decay = jnp.where(lower, jnp.exp(diff), 0.0)
-    parts = []
-    half = heads // 2
-    for part in range(2):
-        pick = slice(part * half, (part + 1) * half)
-        scores = jnp.einsum(
-            "thd,shd->hts", gate(queries[:, pick], part + 1), keys[:, pick], preferred_element_type=f32
-        )
-        weights = (scores * decay[pick]).astype(jnp.bfloat16)
-        parts.append(jnp.einsum("hts,shd->thd", weights, value_rows[:, pick], preferred_element_type=f32))
-    intra = jnp.concatenate(parts, axis=1)
 
     qfloat = queries.astype(f32)
     inter = (

time: 71.6 us -> 73.6 us (1.028)
  matrix products: 27.2 us -> 15.2 us
  Pallas kernels: 0 us -> 8.19 us
  local copies, waits for them, and re-layouts: 17.8 us -> 24.5 us
  other arithmetic: 12.3 us -> 7.87 us
  waiting for transfers between devices: 4.23 us -> 6.98 us
    dot_general x2 -> x0, matrix products: 10.4 us -> none  [shards(): jnp.einsum('hts,shd->thd', weights, value_rows[:, pick], preferred_elemen...]
    pallas_call x0 -> x1, Pallas kernels: none -> 8.19 us  [intra_attention(): pl.pallas_call(functools.partial(intra_kernel, head_dim=head_dim), grid=(...]
    select_n x1 -> x0, other arithmetic: 4.57 us -> none  [shards(): decay = jnp.where(lower, jnp.exp(diff), 0.0)]
    pallas_call x0 -> x1, local copies, waits for them, and re-layouts: none -> 3.07 us  [intra_attention(): pl.pallas_call(functools.partial(intra_kernel, head_dim=head_dim), grid=(...]
    ppermute x4, waiting for transfers between devices: 2.9 us -> 5.32 us  [exclusive_scan(): got = lax.ppermute(through, AXES, perm)]
    dot_general x1, matrix products: 3.97 us -> 1.9 us  [shards(): jnp.dot(tokens, value_weight, preferred_element_type=f32)]
    select_n x3 -> x2, other arithmetic: 1.98 us -> 0.25 us  [exclusive_scan(): before = jnp.where(lower, combine(got, before, heads // 2), before)]
    reshape x11, local copies, waits for them, and re-layouts: 2.16 us -> 3.34 us  [combine(): jnp.repeat(jnp.exp(later[body, :heads]), body // heads)]
  transfers between devices with their start and end apart: 6 -> 6, of which waited for: 2 -> 4; matrix products, arithmetic and copies ran while one was open for 36% -> 20% of each run, Pallas kernels for 0% -> 11%
where the time goes in v5:
time: 73.6 us; the launch traced here: 72.6 us
  local copies, waits for them, and re-layouts  24.5 us (33%)
  matrix products  15.2 us (21%)
  starting transfers between devices  9.52 us (13%)
  Pallas kernels  8.19 us (11%)
  other arithmetic  7.87 us (11%)
  waiting for transfers between devices  6.98 us (9%)
    ppermute x4, starting transfers between devices, exclusive_scan(): got = lax.ppermute(through, AXES, perm)  8.9 us
    pallas_call x1, Pallas kernels, intra_attention(): pl.pallas_call(functools.partial(intra_kernel, head_dim=head_dim), grid=(...  8.19 us
    ppermute x4, waiting for transfers between devices, exclusive_scan(): got = lax.ppermute(through, AXES, perm)  5.32 us
    dot_general x1, matrix products, shards(): jnp.dot(gate(tokens, 0), query_weight, preferred_element_type=f32)  3.86 us
    concatenate x11, local copies, waits for them, and re-layouts, combine(): jnp.concatenate([jnp.repeat(jnp.exp(later[body, :heads]), body // heads),...  3.72 us
    reshape x11, local copies, waits for them, and re-layouts, combine(): jnp.repeat(jnp.exp(later[body, :heads]), body // heads)  3.34 us
    dot_general x1, matrix products, shards(): jnp.dot(tokens, key_weight, preferred_element_type=f32)  3.33 us
    pallas_call x1, local copies, waits for them, and re-layouts, intra_attention(): pl.pallas_call(functools.partial(intra_kernel, head_dim=head_dim), grid=(...  3.07 us
  transfers between devices with their start and end apart: 6, of which 4 were waited for; matrix products, arithmetic and copies ran while one was open for 20% of the time, Pallas kernels for 11%

profile of v5, /device:TPU:0, one launch (start us, length us, event | category | flops | bytes accessed | tf_op | source)
XLA Modules:
  0.0 72.6 jit_solution(17462869671403310275)
XLA Ops:
  0.0 0.9 %copy_bitcast_fusion.1 = f32[16,3,128]{2,0,1:T(8,128)S(1)} fusion(f32[384,16]{0,1:T(8,128)} %param.16), kind=kLoop, calls=%fused_computation.37 | loop fusion | bytes 49152 | tf_op jit(solution)/shard_map/reshape.99
  0.9 0.9 %reduce-window.6 = f32[16,3,128]{2,0,1:T(8,128)S(1)} reduce-window(f32[16,3,128]{2,0,1:T(8,128)S(1)} %copy_bitcast_fusion.1, f32[]{:T(128)} %constant.132.clone.1), window={size=1x1x128 pad=0_0x0_0x127_0}, to_apply=%region_0.1 | reduce-window | flops 780288 | bytes 49156 | tf_op jit(solution)/shard_map/reduce-window
  1.7 0.2 slice_reduce_fusion
  2.2 0.5 copy-done.9
  2.6 0.7 %bitcast_exponential_fusion.1 = (f32[384,16]{1,0:T(8,128)}, f32[384,16]{1,0:T(8,128)S(1)}) fusion(f32[16,384]{0,1:T(8,128)S(1)} %copy.29, f32[16]{0:T(128)S(1)} %get-tuple-element.61), kind=kLoop, calls=%fused_computation.67 | loop fusion | flops 6144 | bytes 73792 | tf_op jit(solution)/shard_map/exp | solution.py:148
  3.5 3.3 %multiply_convert_fusion.2.k_ref = bf16[384,1024]{1,0:T(8,128)(2,1)} fusion(bf16[384,1024]{1,0:T(8,128)(2,1)} %param.15, bf16[1024,1024]{1,0:T(8,128)(2,1)S(1)} %copy-done), kind=kOutput, calls=%fused_computation.7 | convolution fusion | flops 807272448 | bytes 3670016 | tf_op jit(solution)/shard_map/dot_general | solution.py:121
  6.8 1.9 %convolution_convert_fusion.1.v_ref = bf16[384,1024]{1,0:T(8,128)(2,1)} fusion(bf16[384,1024]{1,0:T(8,128)(2,1)S(1)} %copy-done.12, bf16[1024,1024]{1,0:T(8,128)(2,1)S(1)} %copy-done.11), kind=kOutput, calls=%fused_computation.9 | convolution fusion | flops 805699584 | bytes 3670016 | tf_op jit(solution)/shard_map/dot_general | solution.py:122
  8.7 1.5 %copy.32 = bf16[384,1024]{0,1:T(8,128)(2,1)S(1)} copy(bf16[384,1024]{1,0:T(8,128)(2,1)} %convolution_convert_fusion.1.v_ref) | data formatting | bytes 1572864 | tf_op jit(solution)/shard_map/convert_element_type | solution.py:122
  10.2 2.6 %copy.26 = f32[384,1024]{0,1:T(8,128)} copy(bf16[384,1024]{1,0:T(8,128)(2,1)} %multiply_convert_fusion.2.k_ref) | data formatting | bytes 2359296 | tf_op jit(solution)/shard_map/convert_element_type | solution.py:127
  12.8 1.8 %fusion.2 = f32[16,64,64]{2,1,0:T(8,128)S(1)} fusion(bf16[384,16,64]{0,2,1:T(8,128)(2,1)S(1)} %bitcast.71, f32[384,16,64]{0,2,1:T(8,128)} %bitcast.70, f32[384,16]{0,1:T(8,128)S(1)} %copy.31), kind=kOutput, calls=%fused_computation.10 | convolution fusion | flops 51118080 | bytes 2646016 | tf_op jit(solution)/shard_map/thd,the->hde/dot_general | solution.py:128
  14.8 0.6 collective-permute-start
  15.3 0.7 bitcast_exponential_fusion
  16.2 0.3 collective-permute-done
  16.7 0.2 add_select_fusion
  17.0 3.0 %collective-permute-start.1 = (f32[264,128]{1,0:T(8,128)S(1)}, f32[264,128]{1,0:T(8,128)S(1)}, u32[]{:S(2)}, u32[]{:S(2)}) collective-permute-start(f32[264,128]{1,0:T(8,128)S(1)} %select_maximum_fusion.1), channel_id=1, source_target_pairs={{0,2},{1,3},{2,0},{3,1},{4,6},{5,7},{6,4},{7,5},{8,10},{9,11},{10,... | collective-permute-start | bytes 405512 | tf_op jit(solution)/shard_map/ppermute | solution.py:104
  20.0 0.7 iota_compare_fusion
  20.6 0.7 copy.36
  21.5 0.6 pad_slice_fusion
  22.1 1.8 %collective-permute-done.1 = f32[264,128]{1,0:T(8,128)S(1)} collective-permute-done((f32[264,128]{1,0:T(8,128)S(1)}, f32[264,128]{1,0:T(8,128)S(1)}, u32[]{:S(2)}, u32[]{:S(2)}) %collective-permute-start.1) | collective-permute-done | bytes 135200 | tf_op jit(solution)/shard_map/ppermute | solution.py:104
  24.2 2.8 %collective-permute-start.2 = (f32[264,128]{1,0:T(8,128)S(1)}, f32[264,128]{1,0:T(8,128)S(1)}, u32[]{:S(2)}, u32[]{:S(2)}) collective-permute-start(f32[264,128]{1,0:T(8,128)S(1)} %get-tuple-element.68), channel_id=1, source_target_pairs={{0,4},{1,5},{2,6},{3,7},{4,0},{5,1},{6,2},{7,3},{8,12},{9,13},{10,... | collective-permute-start | bytes 405512 | tf_op jit(solution)/shard_map/ppermute | solution.py:104
  27.0 3.9 %multiply_convert_fusion.q_ref = bf16[384,1024]{1,0:T(8,128)(2,1)} fusion(bf16[384,1024]{1,0:T(8,128)(2,1)} %param.15, bf16[1024,1024]{1,0:T(8,128)(2,1)} %param.17), kind=kOutput, calls=%fused_computation.5 | convolution fusion | flops 807272448 | bytes 3670016 | tf_op jit(solution)/shard_map/dot_general | solution.py:138
  31.0 0.6 concatenate.68
  31.8 0.6 concatenate.66
  32.4 1.5 %copy.34 = bf16[384,1024]{0,1:T(8,128)(2,1)S(1)} copy(bf16[384,1024]{1,0:T(8,128)(2,1)} %multiply_convert_fusion.q_ref) | data formatting | bytes 1572864 | tf_op jit(solution)/shard_map/convert_element_type | solution.py:139
  33.9 0.7 broadcast_in_dim.61
  34.6 1.3 %reshape.217 = f32[256]{0:T(256)} reshape(f32[8,32]{1,0:T(8,128)} %broadcast_in_dim.61) | data formatting | bytes 2048 | tf_op jit(solution)/shard_map/reshape | solution.py:68
  35.9 0.7 concatenate.69
  36.5 1.1 %add_select_fusion.5 = (f32[264,128]{1,0:T(8,128)S(1)}, f32[264,128]{1,0:T(8,128)S(1)}) fusion(f32[264,128]{1,0:T(8,128)} %copy-done.7, f32[264,128]{1,0:T(8,128)S(1)} %get-tuple-element.68, f32[264]{0:T(512)S(1)} %concatenate.69, f32[264]{0:T(512)} %concatenate.68, pred[]{:T(512)S(6)} %ne.29, f32[264,128]{1,0:T(8,128)S(1)} %get-tuple-element.67, ...), kind=kLoop, calls=%fused_computation.32 | loop fusion | flops 270336 | bytes 679009 | tf_op jit(solution)/shard_map/jit(_where)/select_n | solution.py:110
  37.7 1.5 %collective-permute-start.3 = (f32[264,128]{1,0:T(8,128)S(1)}, f32[264,128]{1,0:T(8,128)S(1)}, u32[]{:S(2)}, u32[]{:S(2)}) collective-permute-start(f32[264,128]{1,0:T(8,128)S(1)} %get-tuple-element.65), channel_id=1, source_target_pairs={{0,8},{1,9},{2,10},{3,11},{4,12},{5,13},{6,14},{7,15},{8,0},{9,1},... | collective-permute-start | bytes 405512 | tf_op jit(solution)/shard_map/ppermute | solution.py:104
  39.4 0.6 concatenate.71
  40.1 0.6 concatenate.67
  40.7 8.2 %shard_map.73 = f32[384,1024]{1,0:T(8,128)} custom-call(bf16[384,1024]{1,0:T(8,128)(2,1)} %multiply_convert_fusion.q_ref, bf16[384,1024]{1,0:T(8,128)(2,1)} %multiply_convert_fusion.2.k_ref, bf16[384,1024]{1,0:T(8,128)(2,1)} %convolution_convert_fusion.1.v_ref, f32[384,16]{1,0:T(8,128)} %bitcast.75, f32[16,384]{1,0:T(8,128)} %copy-done.9), custom_call_target="tpu_custom_call" | custom-call | flops 1207959552 | bytes 3932160 | tf_op jit(solution)/shard_map/pallas_call | solution.py:53
  48.9 3.1 %copy.33 = f32[384,1024]{0,1:T(8,128)} copy(f32[384,1024]{1,0:T(8,128)} %shard_map.73) | data formatting | bytes 3145728 | tf_op jit(solution)/shard_map/pallas_call | solution.py:53
  52.0 0.7 broadcast_in_dim.64
  52.7 1.3 %reshape.220 = f32[256]{0:T(256)} reshape(f32[8,32]{1,0:T(8,128)} %broadcast_in_dim.64) | data formatting | bytes 2048 | tf_op jit(solution)/shard_map/reshape | solution.py:68
  54.0 0.6 concatenate.72
  54.6 1.7 %add_select_fusion.4 = (f32[264,128]{1,0:T(8,128)}, f32[264,128]{1,0:T(8,128)S(1)}) fusion(f32[264,128]{1,0:T(8,128)} %copy-done.6, f32[264,128]{1,0:T(8,128)S(1)} %get-tuple-element.65, f32[264]{0:T(512)S(1)} %concatenate.72, f32[264]{0:T(512)} %concatenate.71, pred[]{:T(512)S(6)} %ne.28, f32[264,128]{1,0:T(8,128)S(1)} %copy-done.5, f32[264]{0:T(512)} %concatenate.67), kind=kLoop, calls=%fused_computation.31 | loop fusion | flops 270336 | bytes 679009 | tf_op jit(solution)/shard_map/jit(_where)/select_n | solution.py:110
  56.3 1.5 %collective-permute-start.4 = (f32[264,128]{1,0:T(8,128)}, f32[264,128]{1,0:T(8,128)S(1)}, u32[]{:S(2)}, u32[]{:S(2)}) collective-permute-start(f32[264,128]{1,0:T(8,128)} %get-tuple-element.63), channel_id=1, source_target_pairs={{0,16},{1,17},{2,18},{3,19},{4,20},{5,21},{6,22},{7,23},{8,24},{9,... | collective-permute-start | bytes 405512 | tf_op jit(solution)/shard_map/ppermute | solution.py:104
  58.0 3.5 %collective-permute-done.4 = f32[264,128]{1,0:T(8,128)S(1)} collective-permute-done((f32[264,128]{1,0:T(8,128)}, f32[264,128]{1,0:T(8,128)S(1)}, u32[]{:S(2)}, u32[]{:S(2)}) %collective-permute-start.4) | collective-permute-done | bytes 135200 | tf_op jit(solution)/shard_map/ppermute | solution.py:104
  61.8 1.3 %collective-permute-done.5 = f32[264,128]{1,0:T(8,128)S(1)} collective-permute-done((f32[264,128]{1,0:T(8,128)S(1)}, f32[264,128]{1,0:T(8,128)S(1)}, u32[]{:S(2)}, u32[]{:S(2)}) %collective-permute-start.5) | collective-permute-done | bytes 135200 | tf_op jit(solution)/shard_map/ppermute | solution.py:111
  63.2 1.7 %fusion.4 = f32[512,128]{1,0:T(8,128)} fusion(f32[520,128]{1,0:T(8,128)S(1)} %collective-permute-done, f32[1,16]{1,0:T(1,128)S(1)} %get-tuple-element.70, f32[256,128]{1,0:T(8,128)S(1)} %slice.170, f32[256,128]{1,0:T(8,128)S(1)} %slice.171, f32[1,16]{1,0:T(1,128)S(1)} %get-tuple-element.69, pred[520,128]{1,0:T(8,128)(4,1)} %iota_compare_fusion, ...), kind=kLoop, calls=%fused_computation.17 | loop fusion | flops 655360 | bytes 854145 | tf_op jit(solution)/shard_map/jit(_where)/select_n | solution.py:113
  64.9 1.1 %reshape.223 = f32[16,64,64]{2,1,0:T(8,128)S(1)} reshape(f32[512,128]{1,0:T(8,128)} %fusion.4) | data formatting | bytes 524288 | tf_op jit(solution)/shard_map/reshape | solution.py:134
  66.0 2.5 %multiply_reduce_fusion = (f32[384,16]{0,1:T(8,128)S(1)}, f32[384,16,64]{0,2,1:T(8,128)S(1)}) fusion(f32[384,16,64]{0,2,1:T(8,128)} %bitcast.69, f32[384,16]{0,1:T(8,128)S(1)} %copy-done.8, f32[16,64,64]{2,1,0:T(8,128)S(1)} %reshape.223, bf16[384,16,64]{0,2,1:T(8,128)(2,1)S(1)} %bitcast.72), kind=kOutput, calls=%fused_computation.4 | convolution fusion | flops 303556608 | bytes 4243456 | tf_op jit(solution)/shard_map/thd,hde->the/dot_general | solution.py:147
  68.5 0.1 broadcast_multiply_fusion
  68.6 0.5 copy-done.10
  69.2 0.2 fusion
  69.4 1.4 %copy-done.1 = bf16[1024,1024]{1,0:T(8,128)(2,1)S(1)} copy-done((bf16[1024,1024]{1,0:T(8,128)(2,1)S(1)}, bf16[1024,1024]{1,0:T(8,128)(2,1)}, u32[]{:S(2)}) %copy-start.1) | copy-done | bytes 2097176
  70.8 1.9 %convolution_convert_fusion = bf16[384,1024]{1,0:T(8,128)(2,1)} fusion(bf16[384,1024]{0,1:T(8,128)(2,1)S(1)} %fusion, bf16[1024,1024]{1,0:T(8,128)(2,1)S(1)} %copy-done.1), kind=kOutput, calls=%fused_computation.8 | convolution fusion | flops 805699584 | bytes 3670016 | tf_op jit(solution)/shard_map/dot_general | solution.py:153
  (75 shorter events, 2.5 us)
Async XLA Ops:
  0.0 3.5 %copy-start = (bf16[1024,1024]{1,0:T(8,128)(2,1)S(1)}, bf16[1024,1024]{1,0:T(8,128)(2,1)}, u32[]{:S(2)}) copy-start(bf16[1024,1024]{1,0:T(8,128)(2,1)} %param.18) | copy-start | bytes 6291460
  2.0 0.6 copy-start.9
  2.2 4.6 %copy-start.2 = (f32[16,384]{0,1:T(8,128)}, f32[16,384]{0,1:T(8,128)S(1)}, u32[]{:S(2)}) copy-start(f32[16,384]{0,1:T(8,128)S(1)} %copy.29) | copy-start | bytes 73732
  3.5 3.4 %copy-start.11 = (bf16[1024,1024]{1,0:T(8,128)(2,1)S(1)}, bf16[1024,1024]{1,0:T(8,128)(2,1)}, u32[]{:S(2)}) copy-start(bf16[1024,1024]{1,0:T(8,128)(2,1)} %param.19) | copy-start | bytes 6291460
  3.5 3.4 %copy-start.12 = (bf16[384,1024]{1,0:T(8,128)(2,1)S(1)}, bf16[384,1024]{1,0:T(8,128)(2,1)}, u32[]{:S(2)}) copy-start(bf16[384,1024]{1,0:T(8,128)(2,1)} %param.15) | copy-start | bytes 2359300
  14.6 6.1 %copy-start.3 = (f32[384,16]{1,0:T(8,128)S(1)}, f32[384,16]{1,0:T(8,128)}, u32[]{:S(2)}) copy-start(f32[384,16]{1,0:T(8,128)} %get-tuple-element.59) | copy-start | bytes 73732
  14.8 1.7 %collective-permute-start = (f32[520,128]{1,0:T(8,128)S(1)}, f32[520,128]{1,0:T(8,128)S(1)}, u32[]{:S(2)}, u32[]{:S(2)}) collective-permute-start(f32[520,128]{1,0:T(8,128)S(1)} %select_maximum_fusion), channel_id=1, source_target_pairs={{0,1},{1,0},{2,3},{3,2},{4,5},{5,4},{6,7},{7,6},{8,9},{9,8},{10,11... | collective-permute-start | bytes 798728 | tf_op jit(solution)/shard_map/ppermute | solution.py:96
  17.0 6.9 %collective-permute-start.1 = (f32[264,128]{1,0:T(8,128)S(1)}, f32[264,128]{1,0:T(8,128)S(1)}, u32[]{:S(2)}, u32[]{:S(2)}) collective-permute-start(f32[264,128]{1,0:T(8,128)S(1)} %select_maximum_fusion.1), channel_id=1, source_target_pairs={{0,2},{1,3},{2,0},{3,1},{4,6},{5,7},{6,4},{7,5},{8,10},{9,11},{10,... | collective-permute-start | bytes 405512 | tf_op jit(solution)/shard_map/ppermute | solution.py:104
  24.2 9.7 %collective-permute-start.2 = (f32[264,128]{1,0:T(8,128)S(1)}, f32[264,128]{1,0:T(8,128)S(1)}, u32[]{:S(2)}, u32[]{:S(2)}) collective-permute-start(f32[264,128]{1,0:T(8,128)S(1)} %get-tuple-element.68), channel_id=1, source_target_pairs={{0,4},{1,5},{2,6},{3,7},{4,0},{5,1},{6,2},{7,3},{8,12},{9,13},{10,... | collective-permute-start | bytes 405512 | tf_op jit(solution)/shard_map/ppermute | solution.py:104
  33.9 2.0 %copy-start.7 = (f32[264,128]{1,0:T(8,128)}, f32[264,128]{1,0:T(8,128)S(1)}, u32[]{:S(2)}) copy-start(f32[264,128]{1,0:T(8,128)S(1)} %collective-permute-done.2) | copy-start | bytes 405508
  37.6 1.6 %copy-start.4 = (f32[264,128]{1,0:T(8,128)}, f32[264,128]{1,0:T(8,128)S(1)}, u32[]{:S(2)}) copy-start(f32[264,128]{1,0:T(8,128)S(1)} %get-tuple-element.66) | copy-start | bytes 405508
  37.7 14.3 %collective-permute-start.3 = (f32[264,128]{1,0:T(8,128)S(1)}, f32[264,128]{1,0:T(8,128)S(1)}, u32[]{:S(2)}, u32[]{:S(2)}) collective-permute-start(f32[264,128]{1,0:T(8,128)S(1)} %get-tuple-element.65), channel_id=1, source_target_pairs={{0,8},{1,9},{2,10},{3,11},{4,12},{5,13},{6,14},{7,15},{8,0},{9,1},... | collective-permute-start | bytes 405512 | tf_op jit(solution)/shard_map/ppermute | solution.py:104
  48.9 5.7 %copy-start.5 = (f32[264,128]{1,0:T(8,128)S(1)}, f32[264,128]{1,0:T(8,128)}, u32[]{:S(2)}) copy-start(f32[264,128]{1,0:T(8,128)} %copy-done.4) | copy-start | bytes 405508
  52.0 2.0 %copy-start.6 = (f32[264,128]{1,0:T(8,128)}, f32[264,128]{1,0:T(8,128)S(1)}, u32[]{:S(2)}) copy-start(f32[264,128]{1,0:T(8,128)S(1)} %collective-permute-done.3) | copy-start | bytes 405508
  56.3 9.7 %copy-start.8 = (f32[384,16]{0,1:T(8,128)S(1)}, f32[384,16]{0,1:T(8,128)}, u32[]{:S(2)}) copy-start(f32[384,16]{0,1:T(8,128)} %copy.36) | copy-start | bytes 73732
  56.3 5.2 %collective-permute-start.4 = (f32[264,128]{1,0:T(8,128)}, f32[264,128]{1,0:T(8,128)S(1)}, u32[]{:S(2)}, u32[]{:S(2)}) collective-permute-start(f32[264,128]{1,0:T(8,128)} %get-tuple-element.63), channel_id=1, source_target_pairs={{0,16},{1,17},{2,18},{3,19},{4,20},{5,21},{6,22},{7,23},{8,24},{9,... | collective-permute-start | bytes 405512 | tf_op jit(solution)/shard_map/ppermute | solution.py:104
  61.7 1.4 %collective-permute-start.5 = (f32[264,128]{1,0:T(8,128)S(1)}, f32[264,128]{1,0:T(8,128)S(1)}, u32[]{:S(2)}, u32[]{:S(2)}) collective-permute-start(f32[264,128]{1,0:T(8,128)S(1)} %add_select_fusion.1), channel_id=1, source_target_pairs={{0,1},{1,0},{2,3},{3,2},{4,5},{5,4},{6,7},{7,6},{8,9},{9,8},{10,11... | collective-permute-start | bytes 405512 | tf_op jit(solution)/shard_map/ppermute | solution.py:111
  68.5 0.7 copy-start.10
  69.2 1.6 %copy-start.1 = (bf16[1024,1024]{1,0:T(8,128)(2,1)S(1)}, bf16[1024,1024]{1,0:T(8,128)(2,1)}, u32[]{:S(2)}) copy-start(bf16[1024,1024]{1,0:T(8,128)(2,1)} %param.21) | copy-start | bytes 6291460

commit v6 on v5

--- a/solution.py
+++ b/solution.py
@@ -62,40 +62,23 @@
     )(queries, keys, value_rows, cum, cum.T)
 
 
-def combine(earlier, later, heads):
-    body = earlier.shape[0] - 8
-    scale = jnp.concatenate(
-        [jnp.repeat(jnp.exp(later[body, :heads]), body // heads), jnp.ones((8,), later.dtype)]
-    )
-    return scale[:, None] * earlier + later
+def combine(earlier, later):
+    body = earlier.shape[1] - 8
+    row = lax.broadcasted_iota(jnp.int32, earlier.shape, 1)
+    scale = jnp.where(row < body, jnp.exp(later[:, body : body + 1, :]), 1.0)
+    return scale * earlier + later
 
 
-def half_of(whole, half, heads):
-    body = whole.shape[0] - 8
-    part = heads // 2
-    rows = body // 2
-    states = jnp.where(half == 0, whole[:rows], whole[rows:body])
-    logs = jnp.where(half == 0, whole[body, :part], whole[body, part:heads])
-    return jnp.concatenate([states, jnp.zeros((8, whole.shape[1]), whole.dtype).at[0, :part].set(logs)])
-
-
-def join_halves(first, second, heads):
-    body = first.shape[0] - 8
-    part = heads // 2
-    logs = jnp.concatenate([first[body, :part], second[body, :part]])
-    tail = jnp.zeros((8, first.shape[1]), first.dtype).at[0, :heads].set(logs)
-    return jnp.concatenate([first[:body], second[:body], tail])
-
-
-def exclusive_scan(own, count, heads):
+def exclusive_scan(own, count):
     flat = lax.axis_index(AXES)
     core = flat % 2
     chip = flat // 2
     chips = count // 2
+    half = own.shape[0] // 2
     partner = [(i, i ^ 1) for i in range(count)]
     other = lax.ppermute(own, AXES, partner)
-    pooled = jnp.where(core == 0, combine(own, other, heads), combine(other, own, heads))
-    through = half_of(pooled, core, heads)
+    pooled = jnp.where(core == 0, combine(own, other), combine(other, own))
+    through = jnp.where(core == 0, pooled[:half], pooled[half:])
     before = jnp.zeros_like(through)
     received = []
     bit = 1
@@ -104,14 +87,16 @@
         got = lax.ppermute(through, AXES, perm)
         received.append(got)
         lower = (chip & bit) != 0
-        before = jnp.where(lower, combine(got, before, heads // 2), before)
+        before = jnp.where(lower, combine(got, before), before)
         bit *= 2
         if bit < chips:
-            through = jnp.where(lower, combine(got, through, heads // 2), combine(through, got, heads // 2))
+            through = jnp.where(lower, combine(got, through), combine(through, got))
     swapped = lax.ppermute(before, AXES, partner)
-    whole = jnp.where(core == 0, join_halves(before, swapped, heads), join_halves(swapped, before, heads))
-    whole = jnp.where(core == 0, whole, combine(whole, other, heads))
-    return whole[:-8], received
+    whole = jnp.where(
+        core == 0, jnp.concatenate([before, swapped]), jnp.concatenate([swapped, before])
+    )
+    whole = jnp.where(core == 0, whole, combine(whole, other))
+    return whole[:, :-8], received
 
 
 def shards(count, tokens, log_decay, query_weight, key_weight, value_weight, norm_gain, output_weight):
@@ -126,12 +111,15 @@
     last = cum[-1]
     scaled = (keys.astype(f32) * jnp.exp(last[None, :] - cum)[:, :, None]).astype(jnp.bfloat16)
     local = jnp.einsum("thd,the->hde", scaled, value_rows, preferred_element_type=f32)
-    lanes = 128
-    packed = jnp.concatenate(
-        [local.reshape(-1, lanes), jnp.zeros((8, lanes), f32).at[0, :heads].set(last)], axis=0
-    )
-    incoming, received = exclusive_scan(packed, count, heads)
-    incoming = incoming.reshape(local.shape)
+    dim = local.shape[-1]
+    group = LANES // dim
+    pairs = heads // group
+    side = local.reshape(pairs, group, dim, dim).transpose(0, 2, 1, 3).reshape(pairs, dim, LANES)
+    logs = jnp.broadcast_to(jnp.repeat(last.reshape(pairs, group), dim, axis=1)[:, None, :], (pairs, 8, LANES))
+    logs = jnp.where(lax.broadcasted_iota(jnp.int32, logs.shape, 1) == 0, logs, 0.0)
+    packed = jnp.concatenate([side, logs], axis=1)
+    incoming, received = exclusive_scan(packed, count)
+    incoming = incoming.reshape(pairs, dim, group, dim).transpose(0, 2, 1, 3).reshape(local.shape)
     gate = lambda value, round_: lax.optimization_barrier((value, received[min(round_, len(received) - 1)]))[0]
 
     queries = jax.nn.silu(

time: 73.6 us -> 66.8 us (0.908)
  waiting for transfers between devices: 6.98 us -> 19.3 us
  local copies, waits for them, and re-layouts: 24.5 us -> 14.1 us
  other arithmetic: 7.87 us -> 2.94 us
  matrix products: 15.2 us -> 12 us
    ppermute x4, waiting for transfers between devices: 5.32 us -> 18.2 us  [exclusive_scan(): got = lax.ppermute(through, AXES, perm)]
    select_n x7 -> x8, other arithmetic: 4.98 us -> 0.8 us  [the longest x2 0.25 us: exclusive_scan(): through = jnp.where(lower, combine(got, through), combine(through, got))]
    concatenate x11 -> x0, local copies, waits for them, and re-layouts: 3.72 us -> none  [combine(): jnp.concatenate([jnp.repeat(jnp.exp(later[body, :heads]), body // heads),...]
    reshape x13 -> x3, local copies, waits for them, and re-layouts: 4.56 us -> 1.59 us  [the longest x11 3.34 us: combine(): jnp.repeat(jnp.exp(later[body, :heads]), body // heads)]
    dot_general x1, matrix products: 3.86 us -> 2.03 us  [shards(): jnp.dot(gate(tokens, 0), query_weight, preferred_element_type=f32)]
    broadcast_in_dim x11 -> x2, local copies, waits for them, and re-layouts: 1.96 us -> 0.15 us  [the longest x1 0.08 us: shards(): jnp.broadcast_to(jnp.repeat(last.reshape(pairs, group), dim, axis=1)[:, N...]
    dot_general x1, matrix products: 2.46 us -> 1.04 us  [shards(): jnp.einsum('thd,hde->the', qfloat, incoming, precision=lax.Precision.HIGH...]
    ppermute x1, waiting for transfers between devices: 1.33 us -> 0.01 us  [exclusive_scan(): swapped = lax.ppermute(before, AXES, partner)]
  transfers between devices with their start and end apart: 6 -> 6, of which waited for: 4 -> 5; matrix products, arithmetic and copies ran while one was open for 20% -> 10% of each run, Pallas kernels for 11% -> 12%
where the time goes in v6:
time: 66.8 us; the launch traced here: 66.2 us
  waiting for transfers between devices  19.3 us (29%)
  local copies, waits for them, and re-layouts  14.1 us (21%)
  matrix products  12 us (18%)
  starting transfers between devices  9.35 us (14%)
  Pallas kernels  8.21 us (12%)
  other arithmetic  2.94 us (4%)
    ppermute x4, waiting for transfers between devices, exclusive_scan(): got = lax.ppermute(through, AXES, perm)  18.2 us
    ppermute x4, starting transfers between devices, exclusive_scan(): got = lax.ppermute(through, AXES, perm)  8.73 us
    pallas_call x1, Pallas kernels, intra_attention(): pl.pallas_call(functools.partial(intra_kernel, head_dim=head_dim), grid=(...  8.21 us
    dot_general x1, matrix products, shards(): jnp.dot(tokens, key_weight, preferred_element_type=f32)  3.33 us
    unnamed x22, local copies, waits for them, and re-layouts  3.06 us
    pallas_call x1, local copies, waits for them, and re-layouts, intra_attention(): pl.pallas_call(functools.partial(intra_kernel, head_dim=head_dim), grid=(...  3.04 us
    convert_element_type x1, local copies, waits for them, and re-layouts, shards(): keys.astype(f32) * jnp.exp(last[None, :] - cum)[:, :, None]  2.56 us
    dot_general x1, matrix products, shards(): jnp.dot(gate(tokens, 0), query_weight, preferred_element_type=f32)  2.03 us
  transfers between devices with their start and end apart: 6, of which 5 were waited for; matrix products, arithmetic and copies ran while one was open for 10% of the time, Pallas kernels for 12%

profile of v6, /device:TPU:0, one launch (start us, length us, event | category | flops | bytes accessed | tf_op | source)
XLA Modules:
  0.0 66.2 jit_solution(10268153875494852651)
XLA Ops:
  0.0 0.9 %copy_bitcast_fusion.2 = f32[16,3,128]{2,0,1:T(8,128)S(1)} fusion(f32[384,16]{0,1:T(8,128)} %param.8), kind=kLoop, calls=%fused_computation.33 | loop fusion | bytes 49152 | tf_op jit(solution)/shard_map/reshape
  0.9 0.9 %reduce-window.6 = f32[16,3,128]{2,0,1:T(8,128)S(1)} reduce-window(f32[16,3,128]{2,0,1:T(8,128)S(1)} %copy_bitcast_fusion.2, f32[]{:T(128)} %constant.54.clone.1), window={size=1x1x128 pad=0_0x0_0x127_0}, to_apply=%region_0.1 | reduce-window | flops 780288 | bytes 49156 | tf_op jit(solution)/shard_map/reduce-window
  1.7 0.2 slice_reduce_fusion
  1.9 0.1 copy_bitcast_fusion.1.cum_t_ref
  2.0 0.1 copy.30
  2.2 0.1 reshape_squeeze.3
  2.3 0.1 broadcast_in_dim.129
  2.4 0.1 broadcast_in_dim.130
  2.4 0.7 %bitcast_exponential_fusion = (f32[384,16]{1,0:T(8,128)}, f32[384,16]{1,0:T(8,128)S(1)}) fusion(f32[16,384]{0,1:T(8,128)S(1)} %copy.30, f32[16]{0:T(128)S(1)} %get-tuple-element.13), kind=kLoop, calls=%fused_computation.53 | loop fusion | flops 6144 | bytes 73792 | tf_op jit(solution)/shard_map/exp | solution.py:136
  3.2 0.1 copy.32
  3.3 3.3 %multiply_convert_fusion.2.k_ref = bf16[384,1024]{1,0:T(8,128)(2,1)} fusion(bf16[384,1024]{1,0:T(8,128)(2,1)} %param.7, bf16[1024,1024]{1,0:T(8,128)(2,1)S(1)} %copy-done), kind=kOutput, calls=%fused_computation.7 | convolution fusion | flops 807272448 | bytes 3670016 | tf_op jit(solution)/shard_map/dot_general | solution.py:106
  6.6 1.9 %convolution_convert_fusion.1.v_ref = bf16[384,1024]{1,0:T(8,128)(2,1)} fusion(bf16[384,1024]{1,0:T(8,128)(2,1)S(1)} %copy-done.9, bf16[1024,1024]{1,0:T(8,128)(2,1)S(1)} %copy-done.7), kind=kOutput, calls=%fused_computation.9 | convolution fusion | flops 805699584 | bytes 3670016 | tf_op jit(solution)/shard_map/dot_general | solution.py:107
  8.5 1.5 %copy.33 = bf16[384,1024]{0,1:T(8,128)(2,1)S(1)} copy(bf16[384,1024]{1,0:T(8,128)(2,1)} %convolution_convert_fusion.1.v_ref) | data formatting | bytes 1572864 | tf_op jit(solution)/shard_map/convert_element_type | solution.py:107
  10.0 2.6 %copy.27 = f32[384,1024]{0,1:T(8,128)} copy(bf16[384,1024]{1,0:T(8,128)(2,1)} %multiply_convert_fusion.2.k_ref) | data formatting | bytes 2359296 | tf_op jit(solution)/shard_map/convert_element_type | solution.py:112
  12.5 1.8 %fusion.2 = f32[16,64,64]{2,1,0:T(8,128)S(1)} fusion(bf16[384,16,64]{0,2,1:T(8,128)(2,1)S(1)} %bitcast.58, f32[384,16,64]{0,2,1:T(8,128)} %bitcast.57, f32[384,16]{0,1:T(8,128)S(1)} %copy.32), kind=kOutput, calls=%fused_computation.10 | convolution fusion | flops 51118080 | bytes 2646016 | tf_op jit(solution)/shard_map/thd,the->hde/dot_general | solution.py:113
  14.4 0.4 copy.47
  14.8 0.3 reshape.51
  15.1 0.1 broadcast_select_fusion.1
  15.2 0.6 collective-permute-start
  15.8 0.1 copy.39
  15.9 1.1 %collective-permute-done = f32[8,72,128]{2,1,0:T(8,128)S(1)} collective-permute-done((f32[8,72,128]{2,1,0:T(8,128)S(1)}, f32[8,72,128]{2,1,0:T(8,128)S(1)}, u32[]{:S(2)}, u32[]{:S(2)}) %collective-permute-start) | collective-permute-done | bytes 294944 | tf_op jit(solution)/shard_map/ppermute | solution.py:79
  17.0 0.1 fusion.5
  17.2 3.0 %collective-permute-start.1 = (f32[4,72,128]{2,1,0:T(8,128)S(1)}, f32[4,72,128]{2,1,0:T(8,128)S(1)}, u32[]{:S(2)}, u32[]{:S(2)}) collective-permute-start(f32[4,72,128]{2,1,0:T(8,128)S(1)} %slice_select_fusion), channel_id=1, source_target_pairs={{0,2},{1,3},{2,0},{3,1},{4,6},{5,7},{6,4},{7,5},{8,10},{9,11},{10,... | collective-permute-start | bytes 442376 | tf_op jit(solution)/shard_map/ppermute | solution.py:87
  20.2 4.1 %collective-permute-done.1 = f32[4,72,128]{2,1,0:T(8,128)S(1)} collective-permute-done((f32[4,72,128]{2,1,0:T(8,128)S(1)}, f32[4,72,128]{2,1,0:T(8,128)S(1)}, u32[]{:S(2)}, u32[]{:S(2)}) %collective-permute-start.1) | collective-permute-done | bytes 147488 | tf_op jit(solution)/shard_map/ppermute | solution.py:87
  24.3 0.1 broadcast_select_fusion
  24.4 2.8 %collective-permute-start.2 = (f32[4,72,128]{2,1,0:T(8,128)S(1)}, f32[4,72,128]{2,1,0:T(8,128)S(1)}, u32[]{:S(2)}, u32[]{:S(2)}) collective-permute-start(f32[4,72,128]{2,1,0:T(8,128)S(1)} %get-tuple-element.20), channel_id=1, source_target_pairs={{0,4},{1,5},{2,6},{3,7},{4,0},{5,1},{6,2},{7,3},{8,12},{9,13},{10,... | collective-permute-start | bytes 442376 | tf_op jit(solution)/shard_map/ppermute | solution.py:87
  27.3 6.6 %collective-permute-done.2 = f32[4,72,128]{2,1,0:T(8,128)S(1)} collective-permute-done((f32[4,72,128]{2,1,0:T(8,128)S(1)}, f32[4,72,128]{2,1,0:T(8,128)S(1)}, u32[]{:S(2)}, u32[]{:S(2)}) %collective-permute-start.2) | collective-permute-done | bytes 147488 | tf_op jit(solution)/shard_map/ppermute | solution.py:87
  33.9 0.1 add_select_fusion.4
  34.0 1.4 %collective-permute-start.3 = (f32[4,72,128]{2,1,0:T(8,128)S(1)}, f32[4,72,128]{2,1,0:T(8,128)S(1)}, u32[]{:S(2)}, u32[]{:S(2)}) collective-permute-start(f32[4,72,128]{2,1,0:T(8,128)S(1)} %get-tuple-element.17), channel_id=1, source_target_pairs={{0,8},{1,9},{2,10},{3,11},{4,12},{5,13},{6,14},{7,15},{8,0},{9,1},... | collective-permute-start | bytes 442376 | tf_op jit(solution)/shard_map/ppermute | solution.py:87
  35.5 3.8 %collective-permute-done.3 = f32[4,72,128]{2,1,0:T(8,128)S(1)} collective-permute-done((f32[4,72,128]{2,1,0:T(8,128)S(1)}, f32[4,72,128]{2,1,0:T(8,128)S(1)}, u32[]{:S(2)}, u32[]{:S(2)}) %collective-permute-start.3) | collective-permute-done | bytes 147488 | tf_op jit(solution)/shard_map/ppermute | solution.py:87
  39.3 0.1 add_select_fusion.3
  39.4 1.5 %collective-permute-start.4 = (f32[4,72,128]{2,1,0:T(8,128)S(1)}, f32[4,72,128]{2,1,0:T(8,128)S(1)}, u32[]{:S(2)}, u32[]{:S(2)}) collective-permute-start(f32[4,72,128]{2,1,0:T(8,128)S(1)} %get-tuple-element.15), channel_id=1, source_target_pairs={{0,16},{1,17},{2,18},{3,19},{4,20},{5,21},{6,22},{7,23},{8,24},{9,... | collective-permute-start | bytes 442376 | tf_op jit(solution)/shard_map/ppermute | solution.py:87
  40.9 3.7 %collective-permute-done.4 = f32[4,72,128]{2,1,0:T(8,128)S(1)} collective-permute-done((f32[4,72,128]{2,1,0:T(8,128)S(1)}, f32[4,72,128]{2,1,0:T(8,128)S(1)}, u32[]{:S(2)}, u32[]{:S(2)}) %collective-permute-start.4) | collective-permute-done | bytes 147488 | tf_op jit(solution)/shard_map/ppermute | solution.py:87
  44.6 0.1 add_select_fusion
  44.7 0.1 collective-permute-start.5
  44.8 2.0 %multiply_convert_fusion.q_ref = bf16[384,1024]{1,0:T(8,128)(2,1)} fusion(bf16[384,1024]{1,0:T(8,128)(2,1)S(1)} %copy-done.10, bf16[1024,1024]{1,0:T(8,128)(2,1)S(1)} %copy-done.8), kind=kOutput, calls=%fused_computation.5 | convolution fusion | flops 807272448 | bytes 3670016 | tf_op jit(solution)/shard_map/dot_general | solution.py:126
  46.8 1.5 %copy.37 = bf16[384,1024]{0,1:T(8,128)(2,1)S(1)} copy(bf16[384,1024]{1,0:T(8,128)(2,1)} %multiply_convert_fusion.q_ref) | data formatting | bytes 1572864 | tf_op jit(solution)/shard_map/convert_element_type | solution.py:127
  48.3 8.2 %shard_map.73 = f32[384,1024]{1,0:T(8,128)} custom-call(bf16[384,1024]{1,0:T(8,128)(2,1)} %multiply_convert_fusion.q_ref, bf16[384,1024]{1,0:T(8,128)(2,1)} %multiply_convert_fusion.2.k_ref, bf16[384,1024]{1,0:T(8,128)(2,1)} %convolution_convert_fusion.1.v_ref, f32[384,16]{1,0:T(8,128)} %bitcast.64, f32[16,384]{1,0:T(8,128)} %copy-done.5), custom_call_target="tpu_custom_call" | custom-call | flops 1207959552 | bytes 3932160 | tf_op jit(solution)/shard_map/pallas_call | solution.py:53
  56.5 3.0 %copy.35 = f32[384,1024]{0,1:T(8,128)} copy(f32[384,1024]{1,0:T(8,128)} %shard_map.73) | data formatting | bytes 3145728 | tf_op jit(solution)/shard_map/pallas_call | solution.py:53
  59.6 0.1 fusion.7
  59.7 0.1 fusion.8
  59.9 1.1 %copy-done.1 = f32[384,1024]{0,1:T(8,128)S(1)} copy-done((f32[384,1024]{0,1:T(8,128)S(1)}, f32[384,1024]{0,1:T(8,128)}, u32[]{:S(2)}) %copy-start.1) | copy-done | bytes 1572888
  61.0 1.0 %multiply_reduce_fusion = (f32[384,16]{0,1:T(8,128)S(1)}, f32[384,16,64]{0,2,1:T(8,128)S(1)}) fusion(f32[384,16,64]{0,2,1:T(8,128)S(1)} %bitcast.56, f32[384,16]{0,1:T(8,128)S(1)} %copy.39, f32[16,64,64]{2,1,0:T(8,128)S(1)} %bitcast.60, bf16[384,16,64]{0,2,1:T(8,128)(2,1)S(1)} %bitcast.59), kind=kOutput, calls=%fused_computation.4 | convolution fusion | flops 303556608 | bytes 4243456 | tf_op jit(solution)/shard_map/thd,hde->the/dot_general | solution.py:135
  62.0 0.1 broadcast_multiply_fusion
  62.2 0.5 copy-done.6
  62.7 0.2 fusion
  62.9 1.4 %copy-done.2 = bf16[1024,1024]{1,0:T(8,128)(2,1)S(1)} copy-done((bf16[1024,1024]{1,0:T(8,128)(2,1)S(1)}, bf16[1024,1024]{1,0:T(8,128)(2,1)}, u32[]{:S(2)}) %copy-start.2) | copy-done | bytes 2097176
  64.3 1.9 %convolution_convert_fusion = bf16[384,1024]{1,0:T(8,128)(2,1)} fusion(bf16[384,1024]{0,1:T(8,128)(2,1)S(1)} %fusion, bf16[1024,1024]{1,0:T(8,128)(2,1)S(1)} %copy-done.2), kind=kOutput, calls=%fused_computation.8 | convolution fusion | flops 805699584 | bytes 3670016 | tf_op jit(solution)/shard_map/dot_general | solution.py:141
  (38 shorter events, 0.3 us)
Async XLA Ops:
  0.0 3.3 %copy-start = (bf16[1024,1024]{1,0:T(8,128)(2,1)S(1)}, bf16[1024,1024]{1,0:T(8,128)(2,1)}, u32[]{:S(2)}) copy-start(bf16[1024,1024]{1,0:T(8,128)(2,1)} %param.10) | copy-start | bytes 6291460
  2.0 4.6 %copy-start.5 = (f32[16,384]{1,0:T(8,128)}, f32[16,384]{1,0:T(8,128)S(1)}, u32[]{:S(2)}) copy-start(f32[16,384]{1,0:T(8,128)S(1)} %copy_bitcast_fusion.1.cum_t_ref) | copy-start | bytes 73732
  2.2 4.4 %copy-start.3 = (f32[16,384]{0,1:T(8,128)}, f32[16,384]{0,1:T(8,128)S(1)}, u32[]{:S(2)}) copy-start(f32[16,384]{0,1:T(8,128)S(1)} %copy.30) | copy-start | bytes 73732
  3.3 3.4 %copy-start.7 = (bf16[1024,1024]{1,0:T(8,128)(2,1)S(1)}, bf16[1024,1024]{1,0:T(8,128)(2,1)}, u32[]{:S(2)}) copy-start(bf16[1024,1024]{1,0:T(8,128)(2,1)} %param.11) | copy-start | bytes 6291460
  3.3 3.4 %copy-start.9 = (bf16[384,1024]{1,0:T(8,128)(2,1)S(1)}, bf16[384,1024]{1,0:T(8,128)(2,1)}, u32[]{:S(2)}) copy-start(bf16[384,1024]{1,0:T(8,128)(2,1)} %param.7) | copy-start | bytes 2359300
  14.4 1.4 %copy-start.4 = (f32[384,16]{1,0:T(8,128)S(1)}, f32[384,16]{1,0:T(8,128)}, u32[]{:S(2)}) copy-start(f32[384,16]{1,0:T(8,128)} %get-tuple-element.11) | copy-start | bytes 73732
  15.2 1.8 %collective-permute-start = (f32[8,72,128]{2,1,0:T(8,128)S(1)}, f32[8,72,128]{2,1,0:T(8,128)S(1)}, u32[]{:S(2)}, u32[]{:S(2)}) collective-permute-start(f32[8,72,128]{2,1,0:T(8,128)S(1)} %pad_maximum_fusion.1), channel_id=1, source_target_pairs={{0,1},{1,0},{2,3},{3,2},{4,5},{5,4},{6,7},{7,6},{8,9},{9,8},{10,11... | collective-permute-start | bytes 884744 | tf_op jit(solution)/shard_map/ppermute | solution.py:79
  17.1 27.7 %copy-start.8 = (bf16[1024,1024]{1,0:T(8,128)(2,1)S(1)}, bf16[1024,1024]{1,0:T(8,128)(2,1)}, u32[]{:S(2)}) copy-start(bf16[1024,1024]{1,0:T(8,128)(2,1)} %param.9) | copy-start | bytes 6291460
  17.1 27.6 %copy-start.10 = (bf16[384,1024]{1,0:T(8,128)(2,1)S(1)}, bf16[384,1024]{1,0:T(8,128)(2,1)}, u32[]{:S(2)}) copy-start(bf16[384,1024]{1,0:T(8,128)(2,1)} %param.7) | copy-start | bytes 2359300
  17.2 7.1 %collective-permute-start.1 = (f32[4,72,128]{2,1,0:T(8,128)S(1)}, f32[4,72,128]{2,1,0:T(8,128)S(1)}, u32[]{:S(2)}, u32[]{:S(2)}) collective-permute-start(f32[4,72,128]{2,1,0:T(8,128)S(1)} %slice_select_fusion), channel_id=1, source_target_pairs={{0,2},{1,3},{2,0},{3,1},{4,6},{5,7},{6,4},{7,5},{8,10},{9,11},{10,... | collective-permute-start | bytes 442376 | tf_op jit(solution)/shard_map/ppermute | solution.py:87
  24.4 9.4 %collective-permute-start.2 = (f32[4,72,128]{2,1,0:T(8,128)S(1)}, f32[4,72,128]{2,1,0:T(8,128)S(1)}, u32[]{:S(2)}, u32[]{:S(2)}) collective-permute-start(f32[4,72,128]{2,1,0:T(8,128)S(1)} %get-tuple-element.20), channel_id=1, source_target_pairs={{0,4},{1,5},{2,6},{3,7},{4,0},{5,1},{6,2},{7,3},{8,12},{9,13},{10,... | collective-permute-start | bytes 442376 | tf_op jit(solution)/shard_map/ppermute | solution.py:87
  34.0 5.2 %collective-permute-start.3 = (f32[4,72,128]{2,1,0:T(8,128)S(1)}, f32[4,72,128]{2,1,0:T(8,128)S(1)}, u32[]{:S(2)}, u32[]{:S(2)}) collective-permute-start(f32[4,72,128]{2,1,0:T(8,128)S(1)} %get-tuple-element.17), channel_id=1, source_target_pairs={{0,8},{1,9},{2,10},{3,11},{4,12},{5,13},{6,14},{7,15},{8,0},{9,1},... | collective-permute-start | bytes 442376 | tf_op jit(solution)/shard_map/ppermute | solution.py:87
  39.4 5.2 %collective-permute-start.4 = (f32[4,72,128]{2,1,0:T(8,128)S(1)}, f32[4,72,128]{2,1,0:T(8,128)S(1)}, u32[]{:S(2)}, u32[]{:S(2)}) collective-permute-start(f32[4,72,128]{2,1,0:T(8,128)S(1)} %get-tuple-element.15), channel_id=1, source_target_pairs={{0,16},{1,17},{2,18},{3,19},{4,20},{5,21},{6,22},{7,23},{8,24},{9,... | collective-permute-start | bytes 442376 | tf_op jit(solution)/shard_map/ppermute | solution.py:87
  44.7 14.9 %collective-permute-start.5 = (f32[4,72,128]{2,1,0:T(8,128)S(1)}, f32[4,72,128]{2,1,0:T(8,128)S(1)}, u32[]{:S(2)}, u32[]{:S(2)}) collective-permute-start(f32[4,72,128]{2,1,0:T(8,128)S(1)} %add_select_fusion), channel_id=1, source_target_pairs={{0,1},{1,0},{2,3},{3,2},{4,5},{5,4},{6,7},{7,6},{8,9},{9,8},{10,11... | collective-permute-start | bytes 442376 | tf_op jit(solution)/shard_map/ppermute | solution.py:94
  59.6 1.4 %copy-start.1 = (f32[384,1024]{0,1:T(8,128)S(1)}, f32[384,1024]{0,1:T(8,128)}, u32[]{:S(2)}) copy-start(f32[384,1024]{0,1:T(8,128)} %copy.35) | copy-start | bytes 4718596
  62.0 0.7 %copy-start.6 = (f32[1024]{0:T(1024)S(1)}, f32[1024]{0:T(1024)}, u32[]{:S(2)}) copy-start(f32[1024]{0:T(1024)} %param.12) | copy-start | bytes 12292
  62.7 1.6 %copy-start.2 = (bf16[1024,1024]{1,0:T(8,128)(2,1)S(1)}, bf16[1024,1024]{1,0:T(8,128)(2,1)}, u32[]{:S(2)}) copy-start(bf16[1024,1024]{1,0:T(8,128)(2,1)} %param.13) | copy-start | bytes 6291460

commit v7 on v6

--- a/solution.py
+++ b/solution.py
@@ -6,17 +6,17 @@
 from jax.experimental import pallas as pl
 from jax.sharding import PartitionSpec as P
 
+
 AXES = ("outer", "inner")
 
 LANES = 128
 
 
-def intra_kernel(q_ref, k_ref, v_ref, cum_ref, cum_t_ref, o_ref, *, head_dim):
+def intra_kernel(q_ref, k_ref, v_ref, cum_ref, cum_t_ref, o_ref, *, head_dim, first):
     f32 = jnp.float32
-    pair = pl.program_id(0)
+    pair = pl.program_id(0) + first
     group = LANES // head_dim
     rows = q_ref.shape[0]
-    heads = cum_ref.shape[1]
     q = q_ref[...]
     k = k_ref[...]
     v = v_ref[...]
@@ -44,20 +44,24 @@
     o_ref[...] = out
 
 
-def intra_attention(queries, keys, value_rows, cum, head_dim):
-    rows, width = queries.shape
+def intra_attention(queries, keys, value_rows, cum, head_dim, first, stop):
+    rows, _ = queries.shape
     heads = cum.shape[1]
-    block = pl.BlockSpec((rows, LANES), lambda p: (0, p))
+    block = pl.BlockSpec((rows, LANES), lambda p: (0, p + first))
+    out_block = pl.BlockSpec((rows, LANES), lambda p: (0, p))
     whole = lambda shape: pl.BlockSpec(shape, lambda p: (0, 0))
-    flops = 4 * rows * rows * LANES * (LANES // head_dim) * (width // LANES)
+    steps = stop - first
+    flops = 4 * rows * rows * LANES * (LANES // head_dim) * steps
     return pl.pallas_call(
-        functools.partial(intra_kernel, head_dim=head_dim),
-        grid=(width // LANES,),
+        functools.partial(intra_kernel, head_dim=head_dim, first=first),
+        grid=(steps,),
         in_specs=[block, block, block, whole((rows, heads)), whole((heads, rows))],
-        out_specs=block,
-        out_shape=jax.ShapeDtypeStruct((rows, width), jnp.float32),
+        out_specs=out_block,
+        out_shape=jax.ShapeDtypeStruct((rows, steps * LANES), jnp.float32),
         cost_estimate=pl.CostEstimate(
-            flops=flops, transcendentals=rows * rows * heads, bytes_accessed=rows * width * 10
+            flops=flops,
+            transcendentals=rows * rows * steps * (LANES // head_dim),
+            bytes_accessed=rows * steps * LANES * 10,
         ),
     )(queries, keys, value_rows, cum, cum.T)
 
@@ -99,7 +103,7 @@
     return whole[:, :-8], received
 
 
-def shards(count, tokens, log_decay, query_weight, key_weight, value_weight, norm_gain, output_weight):
+def layer(count, tokens, log_decay, query_weight, key_weight, value_weight, norm_gain, output_weight):
     rows = tokens.shape[0]
     heads = log_decay.shape[1]
     f32 = jnp.float32
@@ -118,16 +122,17 @@
     logs = jnp.broadcast_to(jnp.repeat(last.reshape(pairs, group), dim, axis=1)[:, None, :], (pairs, 8, LANES))
     logs = jnp.where(lax.broadcasted_iota(jnp.int32, logs.shape, 1) == 0, logs, 0.0)
     packed = jnp.concatenate([side, logs], axis=1)
-    incoming, received = exclusive_scan(packed, count)
+    incoming, _ = exclusive_scan(packed, count)
     incoming = incoming.reshape(pairs, dim, group, dim).transpose(0, 2, 1, 3).reshape(local.shape)
-    gate = lambda value, round_: lax.optimization_barrier((value, received[min(round_, len(received) - 1)]))[0]
-
     queries = jax.nn.silu(
-        jnp.dot(gate(tokens, 0), query_weight, preferred_element_type=f32)
+        jnp.dot(tokens, query_weight, preferred_element_type=f32)
     ).astype(jnp.bfloat16)
-    intra = intra_attention(
-        gate(queries, 1), keys.reshape(rows, -1), value_rows.reshape(rows, -1), cum, keys.shape[-1]
-    ).reshape(rows, heads, -1)
+    flat_k, flat_v = keys.reshape(rows, -1), value_rows.reshape(rows, -1)
+    blocks = flat_k.shape[1] // LANES
+    parts = []
+    for first, stop in ((0, blocks // 2), (blocks // 2, blocks)):
+        parts.append(intra_attention(queries, flat_k, flat_v, cum, dim, first, stop))
+    intra = jnp.concatenate(parts, axis=1).reshape(rows, heads, -1)
     queries = queries.reshape(rows, heads, -1)
 
     qfloat = queries.astype(f32)
@@ -145,5 +150,5 @@
     count = mesh.shape["outer"] * mesh.shape["inner"]
     in_specs = (P(AXES, None), P(AXES, None), P(), P(), P(), P(), P())
     out_specs = P(AXES, None)
-    body = lambda *args: shards(count, *args)
+    body = lambda *args: layer(count, *args)
     return jax.shard_map(body, mesh=mesh, in_specs=in_specs, out_specs=out_specs, check_vma=False)

time: 66.8 us -> 72.7 us (1.088)
  other arithmetic: 2.94 us -> 6.88 us
  matrix products: 12 us -> 14.8 us
  local copies, waits for them, and re-layouts: 14.1 us -> 12.7 us
  Pallas kernels: 8.21 us -> 9.59 us
    concatenate x0 -> x1, local copies, waits for them, and re-layouts: none -> 3.07 us  [layer(): intra = jnp.concatenate(parts, axis=1).reshape(rows, heads, -1)]
    pallas_call x1 -> x0, local copies, waits for them, and re-layouts: 3.04 us -> none  [intra_attention(): pl.pallas_call(functools.partial(intra_kernel, head_dim=head_dim), grid=(...]
    dot_general x6, matrix products: 12 us -> 14.8 us  [the longest x1 3.86 us: layer(): jnp.dot(tokens, query_weight, preferred_element_type=f32)]
    concatenate x2 -> x3, other arithmetic: 0.07 us -> 2.05 us  [the longest x1 1.29 us: layer(): intra = jnp.concatenate(parts, axis=1).reshape(rows, heads, -1)]
    pallas_call x1 -> x2, Pallas kernels: 8.21 us -> 9.59 us  [intra_attention(): pl.pallas_call(functools.partial(intra_kernel, head_dim=head_dim, first=f...]
    select_n x1, other arithmetic: 0.11 us -> 1.4 us  [exclusive_scan(): whole = jnp.where(core == 0, whole, combine(whole, other))]
    ppermute x1, waiting for transfers between devices: 1.08 us -> 0.01 us  [exclusive_scan(): other = lax.ppermute(own, AXES, partner)]
    unnamed x22 -> x24, local copies, waits for them, and re-layouts: 3.06 us -> 2.22 us
  transfers between devices with their start and end apart: 6 -> 6, of which waited for: 5 -> 4; matrix products, arithmetic and copies ran while one was open for 10% -> 13% of each run, Pallas kernels for 12% -> 13%
where the time goes in v7:
time: 72.7 us; the launch traced here: 72 us
  waiting for transfers between devices  19 us (26%)
  matrix products  14.8 us (20%)
  local copies, waits for them, and re-layouts  12.7 us (17%)
  Pallas kernels  9.59 us (13%)
  starting transfers between devices  8.87 us (12%)
  other arithmetic  6.88 us (9%)
    ppermute x4, waiting for transfers between devices, exclusive_scan(): got = lax.ppermute(through, AXES, perm)  19 us
    pallas_call x2, Pallas kernels, intra_attention(): pl.pallas_call(functools.partial(intra_kernel, head_dim=head_dim, first=f...  9.59 us
    ppermute x4, starting transfers between devices, exclusive_scan(): got = lax.ppermute(through, AXES, perm)  8.37 us
    dot_general x1, matrix products, layer(): jnp.dot(tokens, query_weight, preferred_element_type=f32)  3.86 us
    dot_general x1, matrix products, layer(): jnp.dot(tokens, value_weight, preferred_element_type=f32)  3.71 us
    concatenate x1, local copies, waits for them, and re-layouts, layer(): intra = jnp.concatenate(parts, axis=1).reshape(rows, heads, -1)  3.07 us
    dot_general x1, matrix products, layer(): jnp.dot(tokens, key_weight, preferred_element_type=f32)  2.31 us
    convert_element_type x1, local copies, waits for them, and re-layouts, layer(): jnp.dot(tokens, value_weight, preferred_element_type=f32)  2.29 us
  transfers between devices with their start and end apart: 6, of which 4 were waited for; matrix products, arithmetic and copies ran while one was open for 13% of the time, Pallas kernels for 13%

profile of v7, /device:TPU:0, one launch (start us, length us, event | category | flops | bytes accessed | tf_op | source)
XLA Modules:
  0.0 72.0 jit_solution(8273004559021334983)
XLA Ops:
  0.0 0.9 %copy_bitcast_fusion.2 = f32[16,3,128]{2,0,1:T(8,128)S(1)} fusion(f32[384,16]{0,1:T(8,128)} %param.8), kind=kLoop, calls=%fused_computation.34 | loop fusion | bytes 49152 | tf_op jit(solution)/shard_map/reshape
  0.9 0.9 %reduce-window.6 = f32[16,3,128]{2,0,1:T(8,128)S(1)} reduce-window(f32[16,3,128]{2,0,1:T(8,128)S(1)} %copy_bitcast_fusion.2, f32[]{:T(128)} %constant.47.clone.1), window={size=1x1x128 pad=0_0x0_0x127_0}, to_apply=%region_0.1 | reduce-window | flops 780288 | bytes 49156 | tf_op jit(solution)/shard_map/reduce-window
  1.7 0.2 slice_reduce_fusion
  1.9 0.1 copy_bitcast_fusion.1.cum_t_ref
  2.0 0.1 copy.30
  2.2 0.7 %bitcast_exponential_fusion = (f32[384,16]{1,0:T(8,128)}, f32[384,16]{1,0:T(8,128)S(1)}) fusion(f32[16,384]{0,1:T(8,128)S(1)} %copy.30, f32[16]{0:T(128)S(1)} %get-tuple-element.9), kind=kLoop, calls=%fused_computation.54 | loop fusion | flops 6144 | bytes 73792 | tf_op jit(solution)/shard_map/exp | solution.py:141
  2.9 0.1 copy.34
  3.0 2.3 %multiply_convert_fusion.1.k_ref = bf16[384,1024]{1,0:T(8,128)(2,1)S(1)} fusion(bf16[384,1024]{1,0:T(8,128)(2,1)} %param.7, bf16[1024,1024]{1,0:T(8,128)(2,1)S(1)} %copy-done), kind=kOutput, calls=%fused_computation.7 | convolution fusion | flops 807272448 | bytes 3670016 | tf_op jit(solution)/shard_map/dot_general | solution.py:110
  5.4 1.4 %copy.32 = f32[384,1024]{0,1:T(8,128)} copy(bf16[384,1024]{1,0:T(8,128)(2,1)S(1)} %multiply_convert_fusion.1.k_ref) | data formatting | bytes 2359296 | tf_op jit(solution)/shard_map/convert_element_type | solution.py:116
  6.8 3.7 %convolution_convert_fusion.1.v_ref = bf16[384,1024]{1,0:T(8,128)(2,1)} fusion(bf16[384,1024]{1,0:T(8,128)(2,1)} %param.7, bf16[1024,1024]{1,0:T(8,128)(2,1)} %param.11), kind=kOutput, calls=%fused_computation.10 | convolution fusion | flops 805699584 | bytes 3670016 | tf_op jit(solution)/shard_map/dot_general | solution.py:111
  10.5 2.3 %copy.35 = bf16[384,1024]{0,1:T(8,128)(2,1)} copy(bf16[384,1024]{1,0:T(8,128)(2,1)} %convolution_convert_fusion.1.v_ref) | data formatting | bytes 1572864 | tf_op jit(solution)/shard_map/convert_element_type | solution.py:111
  12.8 2.0 %fusion.2 = f32[16,64,64]{2,1,0:T(8,128)S(1)} fusion(bf16[384,16,64]{0,2,1:T(8,128)(2,1)} %bitcast.61, f32[384,16,64]{0,2,1:T(8,128)} %bitcast.57, f32[384,16]{0,1:T(8,128)S(1)} %copy.34), kind=kOutput, calls=%fused_computation.11 | convolution fusion | flops 51118080 | bytes 2646016 | tf_op jit(solution)/shard_map/thd,the->hde/dot_general | solution.py:117
  14.8 0.4 copy.48
  15.2 0.3 reshape.52
  15.5 0.1 reshape_squeeze.3
  15.7 0.1 broadcast_in_dim.130
  15.8 0.1 broadcast_select_fusion.1
  15.8 0.7 %pad_maximum_fusion.2 = f32[8,72,128]{2,1,0:T(8,128)} fusion(f32[8,8,128]{2,1,0:T(8,128)S(1)} %broadcast_select_fusion.1, f32[8,64,128]{2,1,0:T(8,128)S(1)} %reshape.52), kind=kLoop, calls=%fused_computation.22 | loop fusion | flops 73728 | bytes 589824 | tf_op jit(solution)/shard_map/concatenate | solution.py:124
  16.6 0.5 collective-permute-start
  17.1 3.9 %multiply_convert_fusion.2.q_ref = bf16[384,1024]{1,0:T(8,128)(2,1)} fusion(bf16[384,1024]{1,0:T(8,128)(2,1)} %param.7, bf16[1024,1024]{1,0:T(8,128)(2,1)} %param.9), kind=kOutput, calls=%fused_computation.8 | convolution fusion | flops 807272448 | bytes 3670016 | tf_op jit(solution)/shard_map/dot_general | solution.py:128
  20.9 4.8 %shard_map.73 = f32[384,512]{1,0:T(8,128)} custom-call(bf16[384,1024]{1,0:T(8,128)(2,1)} %multiply_convert_fusion.2.q_ref, bf16[384,1024]{1,0:T(8,128)(2,1)} %copy-done.1, bf16[384,1024]{1,0:T(8,128)(2,1)} %convolution_convert_fusion.1.v_ref, f32[384,16]{1,0:T(8,128)} %bitcast.59, f32[16,384]{1,0:T(8,128)} %copy-done.10), custom_call_target="tpu_custom_call" | custom-call | flops 603979776 | bytes 1966080 | tf_op jit(solution)/shard_map/pallas_call | solution.py:55
  25.8 1.2 %copy.38 = bf16[384,1024]{0,1:T(8,128)(2,1)} copy(bf16[384,1024]{1,0:T(8,128)(2,1)S(1)} %copy-done.2) | data formatting | bytes 1572864 | tf_op jit(solution)/shard_map/convert_element_type | solution.py:129
  26.9 4.8 %shard_map.74 = f32[384,512]{1,0:T(8,128)} custom-call(bf16[384,1024]{1,0:T(8,128)(2,1)} %multiply_convert_fusion.2.q_ref, bf16[384,1024]{1,0:T(8,128)(2,1)} %copy-done.1, bf16[384,1024]{1,0:T(8,128)(2,1)} %convolution_convert_fusion.1.v_ref, f32[384,16]{1,0:T(8,128)} %bitcast.60, f32[16,384]{1,0:T(8,128)} %copy-done.10), custom_call_target="tpu_custom_call" | custom-call | flops 603979776 | bytes 1966080 | tf_op jit(solution)/shard_map/pallas_call | solution.py:55
  31.7 0.1 fusion.5
  31.9 2.6 %collective-permute-start.1 = (f32[4,72,128]{2,1,0:T(8,128)S(1)}, f32[4,72,128]{2,1,0:T(8,128)S(1)}, u32[]{:S(2)}, u32[]{:S(2)}) collective-permute-start(f32[4,72,128]{2,1,0:T(8,128)S(1)} %slice_select_fusion), channel_id=1, source_target_pairs={{0,2},{1,3},{2,0},{3,1},{4,6},{5,7},{6,4},{7,5},{8,10},{9,11},{10,... | collective-permute-start | bytes 442376 | tf_op jit(solution)/shard_map/ppermute | solution.py:91
  34.6 4.5 %collective-permute-done.1 = f32[4,72,128]{2,1,0:T(8,128)S(1)} collective-permute-done((f32[4,72,128]{2,1,0:T(8,128)S(1)}, f32[4,72,128]{2,1,0:T(8,128)S(1)}, u32[]{:S(2)}, u32[]{:S(2)}) %collective-permute-start.1) | collective-permute-done | bytes 147488 | tf_op jit(solution)/shard_map/ppermute | solution.py:91
  39.1 0.1 add_select_fusion.5
  39.2 2.8 %collective-permute-start.2 = (f32[4,72,128]{2,1,0:T(8,128)S(1)}, f32[4,72,128]{2,1,0:T(8,128)S(1)}, u32[]{:S(2)}, u32[]{:S(2)}) collective-permute-start(f32[4,72,128]{2,1,0:T(8,128)S(1)} %get-tuple-element.15), channel_id=1, source_target_pairs={{0,4},{1,5},{2,6},{3,7},{4,0},{5,1},{6,2},{7,3},{8,12},{9,13},{10,... | collective-permute-start | bytes 442376 | tf_op jit(solution)/shard_map/ppermute | solution.py:91
  42.0 7.0 %collective-permute-done.2 = f32[4,72,128]{2,1,0:T(8,128)S(1)} collective-permute-done((f32[4,72,128]{2,1,0:T(8,128)S(1)}, f32[4,72,128]{2,1,0:T(8,128)S(1)}, u32[]{:S(2)}, u32[]{:S(2)}) %collective-permute-start.2) | collective-permute-done | bytes 147488 | tf_op jit(solution)/shard_map/ppermute | solution.py:91
  49.0 0.1 add_select_fusion.4
  49.1 1.4 %collective-permute-start.3 = (f32[4,72,128]{2,1,0:T(8,128)S(1)}, f32[4,72,128]{2,1,0:T(8,128)S(1)}, u32[]{:S(2)}, u32[]{:S(2)}) collective-permute-start(f32[4,72,128]{2,1,0:T(8,128)S(1)} %get-tuple-element.13), channel_id=1, source_target_pairs={{0,8},{1,9},{2,10},{3,11},{4,12},{5,13},{6,14},{7,15},{8,0},{9,1},... | collective-permute-start | bytes 442376 | tf_op jit(solution)/shard_map/ppermute | solution.py:91
  50.6 3.7 %collective-permute-done.3 = f32[4,72,128]{2,1,0:T(8,128)S(1)} collective-permute-done((f32[4,72,128]{2,1,0:T(8,128)S(1)}, f32[4,72,128]{2,1,0:T(8,128)S(1)}, u32[]{:S(2)}, u32[]{:S(2)}) %collective-permute-start.3) | collective-permute-done | bytes 147488 | tf_op jit(solution)/shard_map/ppermute | solution.py:91
  54.4 0.1 add_select_fusion.3
  54.5 1.5 %collective-permute-start.4 = (f32[4,72,128]{2,1,0:T(8,128)S(1)}, f32[4,72,128]{2,1,0:T(8,128)S(1)}, u32[]{:S(2)}, u32[]{:S(2)}) collective-permute-start(f32[4,72,128]{2,1,0:T(8,128)S(1)} %get-tuple-element.11), channel_id=1, source_target_pairs={{0,16},{1,17},{2,18},{3,19},{4,20},{5,21},{6,22},{7,23},{8,24},{9,... | collective-permute-start | bytes 442376 | tf_op jit(solution)/shard_map/ppermute | solution.py:91
  56.0 3.7 %collective-permute-done.4 = f32[4,72,128]{2,1,0:T(8,128)S(1)} collective-permute-done((f32[4,72,128]{2,1,0:T(8,128)S(1)}, f32[4,72,128]{2,1,0:T(8,128)S(1)}, u32[]{:S(2)}, u32[]{:S(2)}) %collective-permute-start.4) | collective-permute-done | bytes 147488 | tf_op jit(solution)/shard_map/ppermute | solution.py:91
  59.7 0.8 %add_select_fusion = f32[4,72,128]{2,1,0:T(8,128)} fusion(f32[4,72,128]{2,1,0:T(8,128)S(1)} %get-tuple-element.12, f32[4,72,128]{2,1,0:T(8,128)S(1)} %collective-permute-done.4, f32[4,128]{1,0:T(4,128)S(1)} %bitcast.74, pred[72]{0:T(512)(128)(4,1)S(1)} %iota_compare_fusion.1, pred[]{:T(512)S(6)} %ne.26), kind=kLoop, calls=%fused_computation.24 | loop fusion | flops 147456 | bytes 444489 | tf_op jit(solution)/shard_map/jit(_where)/select_n | solution.py:94
  60.5 1.3 %pad_maximum_fusion = f32[384,1024]{1,0:T(8,128)} fusion(f32[384,512]{1,0:T(8,128)S(1)} %copy-done.6, f32[384,512]{1,0:T(8,128)S(1)} %copy-done.5), kind=kLoop, calls=%fused_computation | loop fusion | flops 393216 | bytes 3145728 | tf_op jit(solution)/shard_map/concatenate | solution.py:135
  61.8 3.1 %copy.31 = f32[384,1024]{0,1:T(8,128)} copy(f32[384,1024]{1,0:T(8,128)} %pad_maximum_fusion) | data formatting | bytes 3145728 | tf_op jit(solution)/shard_map/concatenate | solution.py:135
  64.8 0.1 copy.40
  64.9 1.4 %fusion.7 = f32[8,72,128]{2,1,0:T(8,128)S(1)} fusion(f32[8,72,128]{2,1,0:T(8,128)S(1)} %collective-permute-done, f32[4,72,128]{2,1,0:T(8,128)} %collective-permute-done.5, f32[4,72,128]{2,1,0:T(8,128)} %add_select_fusion, f32[8,128]{1,0:T(8,128)S(1)} %bitcast.67, pred[72]{0:T(512)(128)(4,1)S(1)} %iota_compare_fusion.1, pred[]{:T(512)S(6)} %eq.15), kind=kLoop, calls=%fused_computation.21 | loop fusion | flops 516096 | bytes 888905 | tf_op jit(solution)/shard_map/jit(_where)/select_n | solution.py:102
  66.3 0.1 fusion.8
  66.5 0.3 copy-done.3
  66.8 1.0 %multiply_reduce_fusion = (f32[384,16]{0,1:T(8,128)S(1)}, f32[384,16,64]{0,2,1:T(8,128)S(1)}) fusion(f32[384,16,64]{0,2,1:T(8,128)S(1)} %bitcast.56, f32[384,16]{0,1:T(8,128)S(1)} %copy.40, f32[16,64,64]{2,1,0:T(8,128)S(1)} %bitcast.63, bf16[384,16,64]{0,2,1:T(8,128)(2,1)S(1)} %bitcast.62), kind=kOutput, calls=%fused_computation.5 | convolution fusion | flops 303556608 | bytes 4243456 | tf_op jit(solution)/shard_map/thd,hde->the/dot_general | solution.py:140
  67.9 0.1 broadcast_multiply_fusion
  68.0 0.5 copy-done.11
  68.6 0.2 fusion
  68.8 1.4 %copy-done.8 = bf16[1024,1024]{1,0:T(8,128)(2,1)S(1)} copy-done((bf16[1024,1024]{1,0:T(8,128)(2,1)S(1)}, bf16[1024,1024]{1,0:T(8,128)(2,1)}, u32[]{:S(2)}) %copy-start.8) | copy-done | bytes 2097176
  70.1 1.9 %convolution_convert_fusion = bf16[384,1024]{1,0:T(8,128)(2,1)} fusion(bf16[384,1024]{0,1:T(8,128)(2,1)S(1)} %fusion, bf16[1024,1024]{1,0:T(8,128)(2,1)S(1)} %copy-done.8), kind=kOutput, calls=%fused_computation.9 | convolution fusion | flops 805699584 | bytes 3670016 | tf_op jit(solution)/shard_map/dot_general | solution.py:146
  (42 shorter events, 0.3 us)
Async XLA Ops:
  0.0 3.0 %copy-start = (bf16[1024,1024]{1,0:T(8,128)(2,1)S(1)}, bf16[1024,1024]{1,0:T(8,128)(2,1)}, u32[]{:S(2)}) copy-start(bf16[1024,1024]{1,0:T(8,128)(2,1)} %param.10) | copy-start | bytes 6291460
  2.0 3.3 %copy-start.10 = (f32[16,384]{1,0:T(8,128)}, f32[16,384]{1,0:T(8,128)S(1)}, u32[]{:S(2)}) copy-start(f32[16,384]{1,0:T(8,128)S(1)} %copy_bitcast_fusion.1.cum_t_ref) | copy-start | bytes 73732
  2.2 3.2 %copy-start.4 = (f32[16,384]{0,1:T(8,128)}, f32[16,384]{0,1:T(8,128)S(1)}, u32[]{:S(2)}) copy-start(f32[16,384]{0,1:T(8,128)S(1)} %copy.30) | copy-start | bytes 73732
  5.3 5.1 %copy-start.1 = (bf16[384,1024]{1,0:T(8,128)(2,1)}, bf16[384,1024]{1,0:T(8,128)(2,1)S(1)}, u32[]{:S(2)}) copy-start(bf16[384,1024]{1,0:T(8,128)(2,1)S(1)} %multiply_convert_fusion.1.k_ref) | copy-start | bytes 2359300
  16.6 15.1 %collective-permute-start = (f32[8,72,128]{2,1,0:T(8,128)}, f32[8,72,128]{2,1,0:T(8,128)S(1)}, u32[]{:S(2)}, u32[]{:S(2)}) collective-permute-start(f32[8,72,128]{2,1,0:T(8,128)} %pad_maximum_fusion.2), channel_id=1, source_target_pairs={{0,1},{1,0},{2,3},{3,2},{4,5},{5,4},{6,7},{7,6},{8,9},{9,8},{10,11... | collective-permute-start | bytes 884744 | tf_op jit(solution)/shard_map/ppermute | solution.py:83
  20.9 4.8 %copy-start.2 = (bf16[384,1024]{1,0:T(8,128)(2,1)S(1)}, bf16[384,1024]{1,0:T(8,128)(2,1)}, u32[]{:S(2)}) copy-start(bf16[384,1024]{1,0:T(8,128)(2,1)} %multiply_convert_fusion.2.q_ref) | copy-start | bytes 2359300
  31.9 28.6 %copy-start.5 = (f32[384,512]{1,0:T(8,128)S(1)}, f32[384,512]{1,0:T(8,128)}, u32[]{:S(2)}) copy-start(f32[384,512]{1,0:T(8,128)} %shard_map.73) | copy-start | bytes 2359300
  31.9 28.6 %copy-start.6 = (f32[384,512]{1,0:T(8,128)S(1)}, f32[384,512]{1,0:T(8,128)}, u32[]{:S(2)}) copy-start(f32[384,512]{1,0:T(8,128)} %shard_map.74) | copy-start | bytes 2359300
  31.9 7.2 %collective-permute-start.1 = (f32[4,72,128]{2,1,0:T(8,128)S(1)}, f32[4,72,128]{2,1,0:T(8,128)S(1)}, u32[]{:S(2)}, u32[]{:S(2)}) collective-permute-start(f32[4,72,128]{2,1,0:T(8,128)S(1)} %slice_select_fusion), channel_id=1, source_target_pairs={{0,2},{1,3},{2,0},{3,1},{4,6},{5,7},{6,4},{7,5},{8,10},{9,11},{10,... | collective-permute-start | bytes 442376 | tf_op jit(solution)/shard_map/ppermute | solution.py:91
  39.2 9.8 %collective-permute-start.2 = (f32[4,72,128]{2,1,0:T(8,128)S(1)}, f32[4,72,128]{2,1,0:T(8,128)S(1)}, u32[]{:S(2)}, u32[]{:S(2)}) collective-permute-start(f32[4,72,128]{2,1,0:T(8,128)S(1)} %get-tuple-element.15), channel_id=1, source_target_pairs={{0,4},{1,5},{2,6},{3,7},{4,0},{5,1},{6,2},{7,3},{8,12},{9,13},{10,... | collective-permute-start | bytes 442376 | tf_op jit(solution)/shard_map/ppermute | solution.py:91
  49.1 5.2 %collective-permute-start.3 = (f32[4,72,128]{2,1,0:T(8,128)S(1)}, f32[4,72,128]{2,1,0:T(8,128)S(1)}, u32[]{:S(2)}, u32[]{:S(2)}) collective-permute-start(f32[4,72,128]{2,1,0:T(8,128)S(1)} %get-tuple-element.13), channel_id=1, source_target_pairs={{0,8},{1,9},{2,10},{3,11},{4,12},{5,13},{6,14},{7,15},{8,0},{9,1},... | collective-permute-start | bytes 442376 | tf_op jit(solution)/shard_map/ppermute | solution.py:91
  54.5 5.2 %collective-permute-start.4 = (f32[4,72,128]{2,1,0:T(8,128)S(1)}, f32[4,72,128]{2,1,0:T(8,128)S(1)}, u32[]{:S(2)}, u32[]{:S(2)}) collective-permute-start(f32[4,72,128]{2,1,0:T(8,128)S(1)} %get-tuple-element.11), channel_id=1, source_target_pairs={{0,16},{1,17},{2,18},{3,19},{4,20},{5,21},{6,22},{7,23},{8,24},{9,... | collective-permute-start | bytes 442376 | tf_op jit(solution)/shard_map/ppermute | solution.py:91
  60.5 4.5 %collective-permute-start.5 = (f32[4,72,128]{2,1,0:T(8,128)}, f32[4,72,128]{2,1,0:T(8,128)}, u32[]{:S(2)}, u32[]{:S(2)}) collective-permute-start(f32[4,72,128]{2,1,0:T(8,128)} %add_select_fusion), channel_id=1, source_target_pairs={{0,1},{1,0},{2,3},{3,2},{4,5},{5,4},{6,7},{7,6},{8,9},{9,8},{10,11... | collective-permute-start | bytes 442376 | tf_op jit(solution)/shard_map/ppermute | solution.py:98
  61.8 3.1 %copy-start.9 = (f32[384,16]{1,0:T(8,128)S(1)}, f32[384,16]{1,0:T(8,128)}, u32[]{:S(2)}) copy-start(f32[384,16]{1,0:T(8,128)} %get-tuple-element.7) | copy-start | bytes 73732
  64.8 1.7 %copy-start.7 = (bf16[384,1024]{0,1:T(8,128)(2,1)S(1)}, bf16[384,1024]{0,1:T(8,128)(2,1)}, u32[]{:S(2)}) copy-start(bf16[384,1024]{0,1:T(8,128)(2,1)} %copy.38) | copy-start | bytes 2359300
  64.9 1.9 %copy-start.3 = (f32[384,1024]{0,1:T(8,128)S(1)}, f32[384,1024]{0,1:T(8,128)}, u32[]{:S(2)}) copy-start(f32[384,1024]{0,1:T(8,128)} %copy.31) | copy-start | bytes 4718596
  67.9 0.7 copy-start.11
  68.5 1.6 %copy-start.8 = (bf16[1024,1024]{1,0:T(8,128)(2,1)S(1)}, bf16[1024,1024]{1,0:T(8,128)(2,1)}, u32[]{:S(2)}) copy-start(bf16[1024,1024]{1,0:T(8,128)(2,1)} %param.13) | copy-start | bytes 6291460

commit v8 on v7

v8 whole, which is shorter than its diff:
```python
import functools

import jax
import jax.numpy as jnp
from jax import lax
from jax.experimental import pallas as pl
from jax.sharding import PartitionSpec as P


AXES = ("outer", "inner")

LANES = 128


def intra_kernel(q_ref, k_ref, v_ref, cum_ref, cum_t_ref, *rest, head_dim, first):
    o_ref = rest[-1]
    f32 = jnp.float32
    pair = pl.program_id(0) + first
    group = LANES // head_dim
    rows = q_ref.shape[0]
    q = q_ref[...]
    k = k_ref[...]
    v = v_ref[...]
    lane_head = lax.broadcasted_iota(jnp.int32, q.shape, 1) // head_dim
    t_i = lax.broadcasted_iota(jnp.int32, (rows, rows), 0)
    s_i = lax.broadcasted_iota(jnp.int32, (rows, rows), 1)
    lower = s_i <= t_i
    cum = cum_ref[...]
    cum_t = cum_t_ref[...]
    col_head = lax.broadcasted_iota(jnp.int32, cum.shape, 1)
    row_head = lax.broadcasted_iota(jnp.int32, cum_t.shape, 0)
    out = None
    for j in range(group):
        head = pair * group + j
        mine = lane_head == j
        q_j = jnp.where(mine, q, jnp.zeros_like(q))
        scores = lax.dot_general(q_j, k, (((1,), (1,)), ((), ())), preferred_element_type=f32)
        col = jnp.sum(jnp.where(col_head == head, cum, 0.0), axis=1, keepdims=True)
        row = jnp.sum(jnp.where(row_head == head, cum_t, 0.0), axis=0, keepdims=True)
        diff = jnp.where(lower, col - row, 0.0)
        decay = jnp.where(lower, jnp.exp(diff), 0.0)
        weights = (scores * decay).astype(jnp.bfloat16)
        o_j = jnp.dot(weights, v, preferred_element_type=f32)
        out = o_j if out is None else jnp.where(mine, o_j, out)
    o_ref[...] = out


def intra_attention(queries, keys, value_rows, cum, head_dim, first, stop, into=None):
    rows, width = queries.shape
    heads = cum.shape[1]
    block = pl.BlockSpec((rows, LANES), lambda p: (0, p + first))
    out_block = block
    extra = () if into is None else (into,)
    extra_specs = [] if into is None else [pl.BlockSpec(memory_space=pl.ANY)]
    whole = lambda shape: pl.BlockSpec(shape, lambda p: (0, 0))
    steps = stop - first
    flops = 4 * rows * rows * LANES * (LANES // head_dim) * steps
    return pl.pallas_call(
        functools.partial(intra_kernel, head_dim=head_dim, first=first),
        grid=(steps,),
        in_specs=[block, block, block, whole((rows, heads)), whole((heads, rows))] + extra_specs,
        out_specs=out_block,
        out_shape=jax.ShapeDtypeStruct((rows, width), jnp.float32),
        input_output_aliases={} if into is None else {5: 0},
        cost_estimate=pl.CostEstimate(
            flops=flops,
            transcendentals=rows * rows * steps * (LANES // head_dim),
            bytes_accessed=rows * steps * LANES * 10,
        ),
    )(queries, keys, value_rows, cum, cum.T, *extra)


def head_column(table, head):
    lane = lax.broadcasted_iota(jnp.int32, table.shape, 1)
    return jnp.sum(jnp.where(lane == head, table, 0.0), axis=1, keepdims=True)


def local_kernel(k_ref, v_ref, cum_ref, o_ref, *, head_dim):
    f32 = jnp.float32
    pair = pl.program_id(0)
    group = LANES // head_dim
    rows = k_ref.shape[0]
    cum = cum_ref[...]
    lane_head = lax.broadcasted_iota(jnp.int32, (rows, LANES), 1) // head_dim
    weight = jnp.zeros((rows, LANES), f32)
    logs = jnp.zeros((1, LANES), f32)
    for j in range(group):
        col = head_column(cum, pair * group + j)
        last = col[rows - 1 :, :]
        weight = jnp.where(lane_head == j, jnp.exp(last - col), weight)
        logs = jnp.where(lane_head[:1] == j, last, logs)
    scaled = (k_ref[...].astype(f32) * weight).astype(jnp.bfloat16)
    state = lax.dot_general(scaled, v_ref[...], (((0,), (0,)), ((), ())), preferred_element_type=f32)
    lane = lax.broadcasted_iota(jnp.int32, (head_dim, LANES), 1) // head_dim
    packed = state[:head_dim]
    for j in range(1, group):
        packed = jnp.where(lane == j, state[j * head_dim : (j + 1) * head_dim], packed)
    o_ref[0, :head_dim, :] = packed
    tail_row = lax.broadcasted_iota(jnp.int32, (8, LANES), 0)
    o_ref[0, head_dim:, :] = jnp.where(tail_row == 0, jnp.broadcast_to(logs, (8, LANES)), 0.0)


def local_states(keys, value_rows, cum, head_dim):
    rows, width = keys.shape
    heads = cum.shape[1]
    pairs = width // LANES
    block = pl.BlockSpec((rows, LANES), lambda p: (0, p))
    return pl.pallas_call(
        functools.partial(local_kernel, head_dim=head_dim),
        grid=(pairs,),
        in_specs=[block, block, pl.BlockSpec((rows, heads), lambda p: (0, 0))],
        out_specs=pl.BlockSpec((1, head_dim + 8, LANES), lambda p: (p, 0, 0)),
        out_shape=jax.ShapeDtypeStruct((pairs, head_dim + 8, LANES), jnp.float32),
        cost_estimate=pl.CostEstimate(
            flops=2 * rows * LANES * LANES * pairs, transcendentals=rows * heads, bytes_accessed=rows * width * 4
        ),
    )(keys, value_rows, cum)


def finish_kernel(q_ref, intra_ref, state_ref, cum_ref, gain_ref, o_ref, *, head_dim):
    f32 = jnp.float32
    bf16 = jnp.bfloat16
    pair = pl.program_id(0)
    group = LANES // head_dim
    rows = q_ref.shape[0]
    state = state_ref[0, :head_dim, :]
    tall = jnp.concatenate([state] * group, axis=0)
    r_head = lax.broadcasted_iota(jnp.int32, (LANES, LANES), 0) // head_dim
    c_head = lax.broadcasted_iota(jnp.int32, (LANES, LANES), 1) // head_dim
    block = jnp.where(r_head == c_head, tall, 0.0)
    q = q_ref[...]
    inter = jnp.zeros((rows, LANES), f32)
    rest = block
    for _ in range(3):
        part = rest.astype(bf16)
        inter = inter + jnp.dot(q, part, preferred_element_type=f32)
        rest = rest - part.astype(f32)
    cum = cum_ref[...]
    lane_head = lax.broadcasted_iota(jnp.int32, (rows, LANES), 1) // head_dim
    growth = jnp.zeros((rows, LANES), f32)
    for j in range(group):
        growth = jnp.where(lane_head == j, jnp.exp(head_column(cum, pair * group + j)), growth)
    attended = intra_ref[...] + inter * growth
    square = attended * attended
    scale = jnp.zeros((rows, LANES), f32)
    for j in range(group):
        mean = jnp.sum(jnp.where(lane_head == j, square, 0.0), axis=1, keepdims=True) / head_dim
        scale = jnp.where(lane_head == j, lax.rsqrt(mean + 1e-05), scale)
    o_ref[...] = (attended * scale * gain_ref[...]).astype(bf16)


def finish(queries, intra, states, cum, norm_gain, head_dim):
    rows, width = queries.shape
    heads = cum.shape[1]
    pairs = width // LANES
    block = pl.BlockSpec((rows, LANES), lambda p: (0, p))
    return pl.pallas_call(
        functools.partial(finish_kernel, head_dim=head_dim),
        grid=(pairs,),
        in_specs=[
            block,
            block,
            pl.BlockSpec((1,) + states.shape[1:], lambda p: (p, 0, 0)),
            pl.BlockSpec((rows, heads), lambda p: (0, 0)),
            pl.BlockSpec((1, LANES), lambda p: (0, p)),
        ],
        out_specs=block,
        out_shape=jax.ShapeDtypeStruct((rows, width), jnp.bfloat16),
        cost_estimate=pl.CostEstimate(
            flops=6 * rows * LANES * LANES * pairs, transcendentals=rows * heads * 2, bytes_accessed=rows * width * 8
        ),
    )(queries, intra, states, cum, norm_gain.reshape(1, width))


def combine(earlier, later):
    body = earlier.shape[1] - 8
    row = lax.broadcasted_iota(jnp.int32, earlier.shape, 1)
    scale = jnp.where(row < body, jnp.exp(later[:, body : body + 1, :]), 1.0)
    return scale * earlier + later


def exclusive_scan(own, count):
    flat = lax.axis_index(AXES)
    core = flat % 2
    chip = flat // 2
    chips = count // 2
    half = own.shape[0] // 2
    partner = [(i, i ^ 1) for i in range(count)]
    other = lax.ppermute(own, AXES, partner)
    pooled = jnp.where(core == 0, combine(own, other), combine(other, own))
    through = jnp.where(core == 0, pooled[:half], pooled[half:])
    before = jnp.zeros_like(through)
    received = []
    bit = 1
    while bit < chips:
        perm = [(i, i ^ (2 * bit)) for i in range(count)]
        got = lax.ppermute(through, AXES, perm)
        received.append(got)
        lower = (chip & bit) != 0
        before = jnp.where(lower, combine(got, before), before)
        bit *= 2
        if bit < chips:
            through = jnp.where(lower, combine(got, through), combine(through, got))
    swapped = lax.ppermute(before, AXES, partner)
    whole = jnp.where(
        core == 0, jnp.concatenate([before, swapped]), jnp.concatenate([swapped, before])
    )
    whole = jnp.where(core == 0, whole, combine(whole, other))
    return whole, received


def layer(count, tokens, log_decay, query_weight, key_weight, value_weight, norm_gain, output_weight):
    f32 = jnp.float32
    bf16 = jnp.bfloat16
    heads = log_decay.shape[1]
    dim = key_weight.shape[1] // heads
    keys = jax.nn.silu(jnp.dot(tokens, key_weight, preferred_element_type=f32)).astype(bf16)
    value_rows = jnp.dot(tokens, value_weight, preferred_element_type=f32).astype(bf16)
    cum = jnp.cumsum(log_decay, axis=0)
    packed = local_states(keys, value_rows, cum, dim)
    incoming, _ = exclusive_scan(packed, count)

    queries = jax.nn.silu(jnp.dot(tokens, query_weight, preferred_element_type=f32)).astype(bf16)
    blocks = keys.shape[1] // LANES
    intra = None
    for first, stop in ((0, blocks // 2), (blocks // 2, blocks)):
        intra = intra_attention(queries, keys, value_rows, cum, dim, first, stop, intra)
    normalized_output = finish(queries, intra, incoming, cum, norm_gain, dim)
    return jnp.dot(normalized_output, output_weight, preferred_element_type=f32).astype(bf16)


def solution(mesh):
    count = mesh.shape["outer"] * mesh.shape["inner"]
    in_specs = (P(AXES, None), P(AXES, None), P(), P(), P(), P(), P())
    out_specs = P(AXES, None)
    body = lambda *args: layer(count, *args)
    return jax.shard_map(body, mesh=mesh, in_specs=in_specs, out_specs=out_specs, check_vma=False)
```

time: 72.7 us -> 70.9 us (0.975)
  Pallas kernels: 9.59 us -> 23.5 us
  local copies, waits for them, and re-layouts: 12.7 us -> 4.14 us
  matrix products: 14.8 us -> 10.8 us
  other arithmetic: 6.88 us -> 3.37 us
    pallas_call x0 -> x2, Pallas kernels: none -> 13.9 us  [the longest x1 7.29 us: finish(): pl.pallas_call(functools.partial(finish_kernel, head_dim=head_dim), grid=...]
    dot_general x3 -> x1, matrix products: 6.76 us -> 1.86 us  [layer(): jnp.dot(tokens, value_weight, preferred_element_type=f32).astype(bf16)]
    convert_element_type x3 -> x0, local copies, waits for them, and re-layouts: 4.88 us -> none  [the longest x1 2.29 us: layer(): jnp.dot(tokens, value_weight, preferred_element_type=f32)]
    concatenate x1 -> x0, local copies, waits for them, and re-layouts: 3.07 us -> none  [layer(): intra = jnp.concatenate(parts, axis=1).reshape(rows, heads, -1)]
    concatenate x3 -> x0, other arithmetic: 2.05 us -> none  [the longest x1 1.29 us: layer(): intra = jnp.concatenate(parts, axis=1).reshape(rows, heads, -1)]
    dot_general x1, matrix products: 3.86 us -> 2.03 us  [layer(): jnp.dot(tokens, query_weight, preferred_element_type=f32)]
    dot_general x1, matrix products: 1.88 us -> 3.7 us  [layer(): jnp.dot(normalized_output, output_weight, preferred_element_type=f32)]
    reshape x3 -> x1, local copies, waits for them, and re-layouts: 1.59 us -> 0.01 us
  transfers between devices with their start and end apart: 6 -> 6, of which waited for: 4 -> 5; matrix products, arithmetic and copies ran while one was open for 13% -> 5% of each run, Pallas kernels for 13% -> 14%
where the time goes in v8:
time: 70.9 us; the launch traced here: 70 us
  Pallas kernels  23.5 us (33%)
  waiting for transfers between devices  18.9 us (27%)
  matrix products  10.8 us (15%)
  starting transfers between devices  9.27 us (13%)
  local copies, waits for them, and re-layouts  4.14 us (6%)
  other arithmetic  3.37 us (5%)
    ppermute x4, waiting for transfers between devices, exclusive_scan(): got = lax.ppermute(through, AXES, perm)  18.3 us
    pallas_call x2, Pallas kernels, intra_attention(): pl.pallas_call(functools.partial(intra_kernel, head_dim=head_dim, first=f...  9.54 us
    ppermute x4, starting transfers between devices, exclusive_scan(): got = lax.ppermute(through, AXES, perm)  8.7 us
    pallas_call x1, Pallas kernels, finish(): pl.pallas_call(functools.partial(finish_kernel, head_dim=head_dim), grid=...  7.29 us
    pallas_call x1, Pallas kernels, local_states(): pl.pallas_call(functools.partial(local_kernel, head_dim=head_dim), grid=(...  6.65 us
    dot_general x1, matrix products, layer(): jnp.dot(normalized_output, output_weight, preferred_element_type=f32)  3.7 us
    dot_general x1, matrix products, layer(): jnp.dot(tokens, key_weight, preferred_element_type=f32)  3.16 us
    dot_general x1, matrix products, layer(): jnp.dot(tokens, query_weight, preferred_element_type=f32)  2.03 us
  transfers between devices with their start and end apart: 6, of which 5 were waited for; matrix products, arithmetic and copies ran while one was open for 5% of the time, Pallas kernels for 14%

profile of v8, /device:TPU:0, one launch (start us, length us, event | category | flops | bytes accessed | tf_op | source)
XLA Modules:
  0.0 70.0 jit_solution(16241515805278171318)
XLA Ops:
  0.0 0.0 copy-start
  0.0 0.0 copy-start.5
  0.0 0.0 copy-start.3
  0.0 1.6 %copy-done = bf16[1024,1024]{1,0:T(8,128)(2,1)S(1)} copy-done((bf16[1024,1024]{1,0:T(8,128)(2,1)S(1)}, bf16[1024,1024]{1,0:T(8,128)(2,1)}, u32[]{:S(2)}) %copy-start) | copy-done | bytes 2097176
  1.6 3.2 %multiply_convert_fusion.k_ref = bf16[384,1024]{1,0:T(8,128)(2,1)} fusion(bf16[384,1024]{1,0:T(8,128)(2,1)} %param.7, bf16[1024,1024]{1,0:T(8,128)(2,1)S(1)} %copy-done), kind=kOutput, calls=%fused_computation | convolution fusion | flops 807272448 | bytes 3670016 | tf_op jit(solution)/shard_map/dot_general | solution.py:217
  4.8 0.0 copy-done.5
  4.8 0.0 copy-done.3
  4.8 0.0 copy-start.2
  4.8 1.9 %convolution_convert_fusion.1.v_ref = bf16[384,1024]{1,0:T(8,128)(2,1)} fusion(bf16[384,1024]{1,0:T(8,128)(2,1)S(1)} %copy-done.5, bf16[1024,1024]{1,0:T(8,128)(2,1)S(1)} %copy-done.3), kind=kOutput, calls=%fused_computation.3 | convolution fusion | flops 805699584 | bytes 3670016 | tf_op jit(solution)/shard_map/dot_general | solution.py:218
  6.6 0.0 copy-done.2
  6.6 0.9 %reduce-window.6 = f32[16,3,128]{2,0,1:T(8,128)S(1)} reduce-window(f32[16,3,128]{2,0,1:T(8,128)S(1)} %copy_bitcast_fusion, f32[]{:T(128)} %constant.42.clone.1), window={size=1x1x128 pad=0_0x0_0x127_0}, to_apply=%region_0.1 | reduce-window | flops 780288 | bytes 49156 | tf_op jit(solution)/shard_map/reduce-window
  7.5 0.2 slice_reduce_fusion
  7.7 0.1 broadcast_add_fusion
  7.8 0.8 %copy.14 = f32[16,3,128]{0,2,1:T(8,128)} copy(f32[16,3,128]{2,0,1:T(8,128)S(1)} %broadcast_add_fusion) | data formatting | bytes 49152 | tf_op jit(solution)/shard_map/reduce_window_sum
  8.6 6.6 %shard_map.75 = f32[8,72,128]{2,1,0:T(8,128)} custom-call(bf16[384,1024]{1,0:T(8,128)(2,1)} %multiply_convert_fusion.k_ref, bf16[384,1024]{1,0:T(8,128)(2,1)} %convolution_convert_fusion.1.v_ref, f32[384,16]{1,0:T(8,128)} %bitcast.30), custom_call_target="tpu_custom_call" | custom-call | flops 100663296 | bytes 1572864 | tf_op jit(solution)/shard_map/pallas_call | solution.py:108
  15.2 0.5 collective-permute-start
  15.7 0.8 %slice_exponential_fusion = f32[8,1,128]{2,1,0:T(1,128)S(1)} fusion(f32[8,72,128]{2,1,0:T(8,128)} %shard_map.75), kind=kLoop, calls=%fused_computation.22 | loop fusion | bytes 8192 | tf_op jit(solution)/shard_map/exp | solution.py:178
  16.5 0.6 collective-permute-done
  17.2 1.1 %fusion.1 = f32[8,72,128]{2,1,0:T(8,128)S(1)} fusion(f32[8,72,128]{2,1,0:T(8,128)S(1)} %collective-permute-done, f32[8,72,128]{2,1,0:T(8,128)} %shard_map.75, f32[8,128]{1,0:T(8,128)S(1)} %bitcast.37, f32[8,128]{1,0:T(8,128)S(1)} %bitcast.35, pred[72]{0:T(512)(128)(4,1)S(1)} %iota_compare_fusion, pred[]{:T(512)S(6)} %eq.4), kind=kLoop, calls=%fused_computation.7 | loop fusion | flops 516096 | bytes 893001 | tf_op jit(solution)/shard_map/jit(_where)/select_n | solution.py:190
  18.3 0.0 copy-start.4
  18.3 0.0 copy-start.6
  18.3 3.0 %collective-permute-start.1 = (f32[4,72,128]{2,1,0:T(8,128)S(1)}, f32[4,72,128]{2,1,0:T(8,128)S(1)}, u32[]{:S(2)}, u32[]{:S(2)}) collective-permute-start(f32[4,72,128]{2,1,0:T(8,128)S(1)} %slice_select_fusion), channel_id=1, source_target_pairs={{0,2},{1,3},{2,0},{3,1},{4,6},{5,7},{6,4},{7,5},{8,10},{9,11},{10,... | collective-permute-start | bytes 442376 | tf_op jit(solution)/shard_map/ppermute | solution.py:197
  21.3 4.1 %collective-permute-done.1 = f32[4,72,128]{2,1,0:T(8,128)S(1)} collective-permute-done((f32[4,72,128]{2,1,0:T(8,128)S(1)}, f32[4,72,128]{2,1,0:T(8,128)S(1)}, u32[]{:S(2)}, u32[]{:S(2)}) %collective-permute-start.1) | collective-permute-done | bytes 147488 | tf_op jit(solution)/shard_map/ppermute | solution.py:197
  25.5 0.1 add_select_fusion.5
  25.6 2.8 %collective-permute-start.2 = (f32[4,72,128]{2,1,0:T(8,128)S(1)}, f32[4,72,128]{2,1,0:T(8,128)S(1)}, u32[]{:S(2)}, u32[]{:S(2)}) collective-permute-start(f32[4,72,128]{2,1,0:T(8,128)S(1)} %get-tuple-element.9), channel_id=1, source_target_pairs={{0,4},{1,5},{2,6},{3,7},{4,0},{5,1},{6,2},{7,3},{8,12},{9,13},{10,... | collective-permute-start | bytes 442376 | tf_op jit(solution)/shard_map/ppermute | solution.py:197
  28.4 6.6 %collective-permute-done.2 = f32[4,72,128]{2,1,0:T(8,128)S(1)} collective-permute-done((f32[4,72,128]{2,1,0:T(8,128)S(1)}, f32[4,72,128]{2,1,0:T(8,128)S(1)}, u32[]{:S(2)}, u32[]{:S(2)}) %collective-permute-start.2) | collective-permute-done | bytes 147488 | tf_op jit(solution)/shard_map/ppermute | solution.py:197
  35.0 0.1 add_select_fusion.4
  35.2 1.4 %collective-permute-start.3 = (f32[4,72,128]{2,1,0:T(8,128)S(1)}, f32[4,72,128]{2,1,0:T(8,128)S(1)}, u32[]{:S(2)}, u32[]{:S(2)}) collective-permute-start(f32[4,72,128]{2,1,0:T(8,128)S(1)} %get-tuple-element.7), channel_id=1, source_target_pairs={{0,8},{1,9},{2,10},{3,11},{4,12},{5,13},{6,14},{7,15},{8,0},{9,1},... | collective-permute-start | bytes 442376 | tf_op jit(solution)/shard_map/ppermute | solution.py:197
  36.6 3.8 %collective-permute-done.3 = f32[4,72,128]{2,1,0:T(8,128)S(1)} collective-permute-done((f32[4,72,128]{2,1,0:T(8,128)S(1)}, f32[4,72,128]{2,1,0:T(8,128)S(1)}, u32[]{:S(2)}, u32[]{:S(2)}) %collective-permute-start.3) | collective-permute-done | bytes 147488 | tf_op jit(solution)/shard_map/ppermute | solution.py:197
  40.4 0.1 add_select_fusion.3
  40.5 1.5 %collective-permute-start.4 = (f32[4,72,128]{2,1,0:T(8,128)S(1)}, f32[4,72,128]{2,1,0:T(8,128)S(1)}, u32[]{:S(2)}, u32[]{:S(2)}) collective-permute-start(f32[4,72,128]{2,1,0:T(8,128)S(1)} %get-tuple-element.5), channel_id=1, source_target_pairs={{0,16},{1,17},{2,18},{3,19},{4,20},{5,21},{6,22},{7,23},{8,24},{9,... | collective-permute-start | bytes 442376 | tf_op jit(solution)/shard_map/ppermute | solution.py:197
  42.0 3.7 %collective-permute-done.4 = f32[4,72,128]{2,1,0:T(8,128)S(1)} collective-permute-done((f32[4,72,128]{2,1,0:T(8,128)S(1)}, f32[4,72,128]{2,1,0:T(8,128)S(1)}, u32[]{:S(2)}, u32[]{:S(2)}) %collective-permute-start.4) | collective-permute-done | bytes 147488 | tf_op jit(solution)/shard_map/ppermute | solution.py:197
  45.7 0.1 add_select_fusion
  45.8 0.0 copy-start.1
  45.8 0.1 collective-permute-start.5
  45.9 0.0 copy-done.4
  45.9 0.0 copy-done.6
  45.9 2.0 %multiply_convert_fusion.1.q_ref = bf16[384,1024]{1,0:T(8,128)(2,1)} fusion(bf16[384,1024]{1,0:T(8,128)(2,1)S(1)} %copy-done.6, bf16[1024,1024]{1,0:T(8,128)(2,1)S(1)} %copy-done.4), kind=kOutput, calls=%fused_computation.1 | convolution fusion | flops 807272448 | bytes 3670016 | tf_op jit(solution)/shard_map/dot_general | solution.py:223
  48.0 0.0 copy-done.1
  48.0 0.7 %copy.16.cum_t_ref = f32[16,384]{1,0:T(8,128)} copy(f32[16,384]{0,1:T(8,128)S(1)} %bitcast.34) | data formatting | bytes 49152 | tf_op jit(solution)/shard_map/reduce_window_sum
  48.7 4.8 %shard_map.73.rest_0_ = f32[384,1024]{1,0:T(8,128)} custom-call(bf16[384,1024]{1,0:T(8,128)(2,1)} %multiply_convert_fusion.1.q_ref, bf16[384,1024]{1,0:T(8,128)(2,1)} %multiply_convert_fusion.k_ref, bf16[384,1024]{1,0:T(8,128)(2,1)} %convolution_convert_fusion.1.v_ref, f32[384,16]{1,0:T(8,128)} %bitcast.31, f32[16,384]{1,0:T(8,128)} %copy.16.cum_t_ref), custom_call_target="tpu_custom_call" | custom-call | flops 603979776 | bytes 1966080 | tf_op jit(solution)/shard_map/pallas_call | solution.py:58
  53.4 4.8 %shard_map.74.intra_ref = f32[384,1024]{1,0:T(8,128)} custom-call(bf16[384,1024]{1,0:T(8,128)(2,1)} %multiply_convert_fusion.1.q_ref, bf16[384,1024]{1,0:T(8,128)(2,1)} %multiply_convert_fusion.k_ref, bf16[384,1024]{1,0:T(8,128)(2,1)} %convolution_convert_fusion.1.v_ref, f32[384,16]{1,0:T(8,128)} %bitcast.32, ...), custom_call_target="tpu_custom_call", output_to_operand_aliasing={{}: (5, {})} | custom-call | flops 603979776 | bytes 1966080 | tf_op jit(solution)/shard_map/pallas_call | solution.py:58
  58.2 0.0 collective-permute-done.5
  58.2 0.8 %fusion.3.state_ref = f32[8,72,128]{2,1,0:T(8,128)} fusion(f32[8,72,128]{2,1,0:T(8,128)S(1)} %collective-permute-done, f32[4,72,128]{2,1,0:T(8,128)S(1)} %collective-permute-done.5, f32[4,72,128]{2,1,0:T(8,128)S(1)} %add_select_fusion, f32[8,128]{1,0:T(8,128)S(1)} %bitcast.36, pred[72]{0:T(512)(128)(4,1)S(1)} %iota_compare_fusion, pred[]{:T(512)S(6)} %eq.4), kind=kLoop, calls=%fused_computation.9 | loop fusion | flops 516096 | bytes 888905 | tf_op jit(solution)/shard_map/jit(_where)/select_n | solution.py:208
  59.0 7.3 %shard_map.76 = bf16[384,1024]{1,0:T(8,128)(2,1)} custom-call(bf16[384,1024]{1,0:T(8,128)(2,1)} %multiply_convert_fusion.1.q_ref, f32[384,1024]{1,0:T(8,128)} %shard_map.74.intra_ref, f32[8,72,128]{2,1,0:T(8,128)} %fusion.3.state_ref, f32[384,16]{1,0:T(8,128)} %bitcast.33, f32[1,1024]{1,0:T(1,128)} %bitcast.48), custom_call_target="tpu_custom_call" | custom-call | flops 301989888 | bytes 3145728 | tf_op jit(solution)/shard_map/pallas_call | solution.py:157
  66.3 3.7 %convolution_convert_fusion = bf16[384,1024]{1,0:T(8,128)(2,1)} fusion(bf16[384,1024]{1,0:T(8,128)(2,1)} %shard_map.76, bf16[1024,1024]{1,0:T(8,128)(2,1)} %param.13), kind=kOutput, calls=%fused_computation.2 | convolution fusion | flops 805699584 | bytes 3670016 | tf_op jit(solution)/shard_map/dot_general | solution.py:229
  (13 shorter events, 0.1 us)
Async XLA Ops:
  0.0 1.6 %copy-start = (bf16[1024,1024]{1,0:T(8,128)(2,1)S(1)}, bf16[1024,1024]{1,0:T(8,128)(2,1)}, u32[]{:S(2)}) copy-start(bf16[1024,1024]{1,0:T(8,128)(2,1)} %param.10) | copy-start | bytes 6291460
  0.0 4.8 %copy-start.5 = (bf16[384,1024]{1,0:T(8,128)(2,1)S(1)}, bf16[384,1024]{1,0:T(8,128)(2,1)}, u32[]{:S(2)}) copy-start(bf16[384,1024]{1,0:T(8,128)(2,1)} %param.7) | copy-start | bytes 2359300
  0.0 4.8 %copy-start.3 = (bf16[1024,1024]{1,0:T(8,128)(2,1)S(1)}, bf16[1024,1024]{1,0:T(8,128)(2,1)}, u32[]{:S(2)}) copy-start(bf16[1024,1024]{1,0:T(8,128)(2,1)} %param.11) | copy-start | bytes 6291460
  4.8 1.9 %copy-start.2 = (f32[384,16]{0,1:T(8,128)S(1)}, f32[384,16]{0,1:T(8,128)}, u32[]{:S(2)}) copy-start(f32[384,16]{0,1:T(8,128)} %param.8) | copy-start | bytes 73732
  15.2 1.9 %collective-permute-start = (f32[8,72,128]{2,1,0:T(8,128)}, f32[8,72,128]{2,1,0:T(8,128)S(1)}, u32[]{:S(2)}, u32[]{:S(2)}) collective-permute-start(f32[8,72,128]{2,1,0:T(8,128)} %shard_map.75), channel_id=1, source_target_pairs={{0,1},{1,0},{2,3},{3,2},{4,5},{5,4},{6,7},{7,6},{8,9},{9,8},{10,11... | collective-permute-start | bytes 884744 | tf_op jit(solution)/shard_map/ppermute | solution.py:189
  18.3 27.7 %copy-start.4 = (bf16[1024,1024]{1,0:T(8,128)(2,1)S(1)}, bf16[1024,1024]{1,0:T(8,128)(2,1)}, u32[]{:S(2)}) copy-start(bf16[1024,1024]{1,0:T(8,128)(2,1)} %param.9) | copy-start | bytes 6291460
  18.3 27.7 %copy-start.6 = (bf16[384,1024]{1,0:T(8,128)(2,1)S(1)}, bf16[384,1024]{1,0:T(8,128)(2,1)}, u32[]{:S(2)}) copy-start(bf16[384,1024]{1,0:T(8,128)(2,1)} %param.7) | copy-start | bytes 2359300
  18.3 7.2 %collective-permute-start.1 = (f32[4,72,128]{2,1,0:T(8,128)S(1)}, f32[4,72,128]{2,1,0:T(8,128)S(1)}, u32[]{:S(2)}, u32[]{:S(2)}) collective-permute-start(f32[4,72,128]{2,1,0:T(8,128)S(1)} %slice_select_fusion), channel_id=1, source_target_pairs={{0,2},{1,3},{2,0},{3,1},{4,6},{5,7},{6,4},{7,5},{8,10},{9,11},{10,... | collective-permute-start | bytes 442376 | tf_op jit(solution)/shard_map/ppermute | solution.py:197
  25.6 9.4 %collective-permute-start.2 = (f32[4,72,128]{2,1,0:T(8,128)S(1)}, f32[4,72,128]{2,1,0:T(8,128)S(1)}, u32[]{:S(2)}, u32[]{:S(2)}) collective-permute-start(f32[4,72,128]{2,1,0:T(8,128)S(1)} %get-tuple-element.9), channel_id=1, source_target_pairs={{0,4},{1,5},{2,6},{3,7},{4,0},{5,1},{6,2},{7,3},{8,12},{9,13},{10,... | collective-permute-start | bytes 442376 | tf_op jit(solution)/shard_map/ppermute | solution.py:197
  35.2 5.2 %collective-permute-start.3 = (f32[4,72,128]{2,1,0:T(8,128)S(1)}, f32[4,72,128]{2,1,0:T(8,128)S(1)}, u32[]{:S(2)}, u32[]{:S(2)}) collective-permute-start(f32[4,72,128]{2,1,0:T(8,128)S(1)} %get-tuple-element.7), channel_id=1, source_target_pairs={{0,8},{1,9},{2,10},{3,11},{4,12},{5,13},{6,14},{7,15},{8,0},{9,1},... | collective-permute-start | bytes 442376 | tf_op jit(solution)/shard_map/ppermute | solution.py:197
  40.5 5.2 %collective-permute-start.4 = (f32[4,72,128]{2,1,0:T(8,128)S(1)}, f32[4,72,128]{2,1,0:T(8,128)S(1)}, u32[]{:S(2)}, u32[]{:S(2)}) collective-permute-start(f32[4,72,128]{2,1,0:T(8,128)S(1)} %get-tuple-element.5), channel_id=1, source_target_pairs={{0,16},{1,17},{2,18},{3,19},{4,20},{5,21},{6,22},{7,23},{8,24},{9,... | collective-permute-start | bytes 442376 | tf_op jit(solution)/shard_map/ppermute | solution.py:197
  45.8 2.1 %copy-start.1 = (f32[16,3,128]{0,2,1:T(8,128)S(1)}, f32[16,3,128]{0,2,1:T(8,128)}, u32[]{:S(2)}) copy-start(f32[16,3,128]{0,2,1:T(8,128)} %copy.14) | copy-start | bytes 73732
  45.8 12.4 %collective-permute-start.5 = (f32[4,72,128]{2,1,0:T(8,128)S(1)}, f32[4,72,128]{2,1,0:T(8,128)S(1)}, u32[]{:S(2)}, u32[]{:S(2)}) collective-permute-start(f32[4,72,128]{2,1,0:T(8,128)S(1)} %add_select_fusion), channel_id=1, source_target_pairs={{0,1},{1,0},{2,3},{3,2},{4,5},{5,4},{6,7},{7,6},{8,9},{9,8},{10,11... | collective-permute-start | bytes 442376 | tf_op jit(solution)/shard_map/ppermute | solution.py:204

commit v9 on v8

--- a/solution.py
+++ b/solution.py
@@ -10,6 +10,7 @@
 AXES = ("outer", "inner")
 
 LANES = 128
+PER_STEP = 4
 
 
 def intra_kernel(q_ref, k_ref, v_ref, cum_ref, cum_t_ref, *rest, head_dim, first):
@@ -76,8 +77,14 @@
 
 
 def local_kernel(k_ref, v_ref, cum_ref, o_ref, *, head_dim):
-    f32 = jnp.float32
-    pair = pl.program_id(0)
+    for step in range(o_ref.shape[0]):
+        local_pair(k_ref, v_ref, cum_ref, o_ref, head_dim, step)
+
+
+def local_pair(k_ref, v_ref, cum_ref, o_ref, head_dim, step):
+    f32 = jnp.float32
+    pair = pl.program_id(0) * o_ref.shape[0] + step
+    cols = pl.ds(step * LANES, LANES)
     group = LANES // head_dim
     rows = k_ref.shape[0]
     cum = cum_ref[...]
@@ -89,27 +96,28 @@
         last = col[rows - 1 :, :]
         weight = jnp.where(lane_head == j, jnp.exp(last - col), weight)
         logs = jnp.where(lane_head[:1] == j, last, logs)
-    scaled = (k_ref[...].astype(f32) * weight).astype(jnp.bfloat16)
-    state = lax.dot_general(scaled, v_ref[...], (((0,), (0,)), ((), ())), preferred_element_type=f32)
+    scaled = (k_ref[:, cols].astype(f32) * weight).astype(jnp.bfloat16)
+    state = lax.dot_general(scaled, v_ref[:, cols], (((0,), (0,)), ((), ())), preferred_element_type=f32)
     lane = lax.broadcasted_iota(jnp.int32, (head_dim, LANES), 1) // head_dim
     packed = state[:head_dim]
     for j in range(1, group):
         packed = jnp.where(lane == j, state[j * head_dim : (j + 1) * head_dim], packed)
-    o_ref[0, :head_dim, :] = packed
+    o_ref[step, :head_dim, :] = packed
     tail_row = lax.broadcasted_iota(jnp.int32, (8, LANES), 0)
-    o_ref[0, head_dim:, :] = jnp.where(tail_row == 0, jnp.broadcast_to(logs, (8, LANES)), 0.0)
+    o_ref[step, head_dim:, :] = jnp.where(tail_row == 0, jnp.broadcast_to(logs, (8, LANES)), 0.0)
 
 
 def local_states(keys, value_rows, cum, head_dim):
     rows, width = keys.shape
     heads = cum.shape[1]
     pairs = width // LANES
-    block = pl.BlockSpec((rows, LANES), lambda p: (0, p))
+    per = PER_STEP if pairs % PER_STEP == 0 else 1
+    block = pl.BlockSpec((rows, per * LANES), lambda p: (0, p))
     return pl.pallas_call(
         functools.partial(local_kernel, head_dim=head_dim),
-        grid=(pairs,),
+        grid=(pairs // per,),
         in_specs=[block, block, pl.BlockSpec((rows, heads), lambda p: (0, 0))],
-        out_specs=pl.BlockSpec((1, head_dim + 8, LANES), lambda p: (p, 0, 0)),
+        out_specs=pl.BlockSpec((per, head_dim + 8, LANES), lambda p: (p, 0, 0)),
         out_shape=jax.ShapeDtypeStruct((pairs, head_dim + 8, LANES), jnp.float32),
         cost_estimate=pl.CostEstimate(
             flops=2 * rows * LANES * LANES * pairs, transcendentals=rows * heads, bytes_accessed=rows * width * 4
@@ -118,17 +126,23 @@
 
 
 def finish_kernel(q_ref, intra_ref, state_ref, cum_ref, gain_ref, o_ref, *, head_dim):
+    for step in range(state_ref.shape[0]):
+        finish_pair(q_ref, intra_ref, state_ref, cum_ref, gain_ref, o_ref, head_dim, step)
+
+
+def finish_pair(q_ref, intra_ref, state_ref, cum_ref, gain_ref, o_ref, head_dim, step):
     f32 = jnp.float32
     bf16 = jnp.bfloat16
-    pair = pl.program_id(0)
+    pair = pl.program_id(0) * state_ref.shape[0] + step
+    cols = pl.ds(step * LANES, LANES)
     group = LANES // head_dim
     rows = q_ref.shape[0]
-    state = state_ref[0, :head_dim, :]
+    state = state_ref[step, :head_dim, :]
     tall = jnp.concatenate([state] * group, axis=0)
     r_head = lax.broadcasted_iota(jnp.int32, (LANES, LANES), 0) // head_dim
     c_head = lax.broadcasted_iota(jnp.int32, (LANES, LANES), 1) // head_dim
     block = jnp.where(r_head == c_head, tall, 0.0)
-    q = q_ref[...]
+    q = q_ref[:, cols]
     inter = jnp.zeros((rows, LANES), f32)
     rest = block
     for _ in range(3):
@@ -140,29 +154,30 @@
     growth = jnp.zeros((rows, LANES), f32)
     for j in range(group):
         growth = jnp.where(lane_head == j, jnp.exp(head_column(cum, pair * group + j)), growth)
-    attended = intra_ref[...] + inter * growth
+    attended = intra_ref[:, cols] + inter * growth
     square = attended * attended
     scale = jnp.zeros((rows, LANES), f32)
     for j in range(group):
         mean = jnp.sum(jnp.where(lane_head == j, square, 0.0), axis=1, keepdims=True) / head_dim
         scale = jnp.where(lane_head == j, lax.rsqrt(mean + 1e-05), scale)
-    o_ref[...] = (attended * scale * gain_ref[...]).astype(bf16)
+    o_ref[:, cols] = (attended * scale * gain_ref[:, cols]).astype(bf16)
 
 
 def finish(queries, intra, states, cum, norm_gain, head_dim):
     rows, width = queries.shape
     heads = cum.shape[1]
     pairs = width // LANES
-    block = pl.BlockSpec((rows, LANES), lambda p: (0, p))
+    per = PER_STEP if pairs % PER_STEP == 0 else 1
+    block = pl.BlockSpec((rows, per * LANES), lambda p: (0, p))
     return pl.pallas_call(
         functools.partial(finish_kernel, head_dim=head_dim),
-        grid=(pairs,),
+        grid=(pairs // per,),
         in_specs=[
             block,
             block,
-            pl.BlockSpec((1,) + states.shape[1:], lambda p: (p, 0, 0)),
+            pl.BlockSpec((per,) + states.shape[1:], lambda p: (p, 0, 0)),
             pl.BlockSpec((rows, heads), lambda p: (0, 0)),
-            pl.BlockSpec((1, LANES), lambda p: (0, p)),
+            pl.BlockSpec((1, per * LANES), lambda p: (0, p)),
         ],
         out_specs=block,
         out_shape=jax.ShapeDtypeStruct((rows, width), jnp.bfloat16),

time: 70.9 us -> 65 us (0.917)
  Pallas kernels: 23.5 us -> 17.9 us
    pallas_call x1, Pallas kernels: 6.65 us -> 3.53 us  [local_states(): pl.pallas_call(functools.partial(local_kernel, head_dim=head_dim), grid=(...]
    pallas_call x1, Pallas kernels: 7.29 us -> 4.83 us  [finish(): pl.pallas_call(functools.partial(finish_kernel, head_dim=head_dim), grid=...]
  transfers between devices with their start and end apart: 6 -> 6, of which waited for: 5 -> 5; matrix products, arithmetic and copies ran while one was open for 5% -> 5% of each run, Pallas kernels for 14% -> 15%
where the time goes in v9:
time: 65 us; the launch traced here: 64.5 us
  waiting for transfers between devices  18.9 us (29%)
  Pallas kernels  17.9 us (28%)
  matrix products  10.8 us (17%)
  starting transfers between devices  9.27 us (14%)
  local copies, waits for them, and re-layouts  4.14 us (6%)
  other arithmetic  3.37 us (5%)
    ppermute x4, waiting for transfers between devices, exclusive_scan(): got = lax.ppermute(through, AXES, perm)  18.3 us
    pallas_call x2, Pallas kernels, intra_attention(): pl.pallas_call(functools.partial(intra_kernel, head_dim=head_dim, first=f...  9.53 us
    ppermute x4, starting transfers between devices, exclusive_scan(): got = lax.ppermute(through, AXES, perm)  8.7 us
    pallas_call x1, Pallas kernels, finish(): pl.pallas_call(functools.partial(finish_kernel, head_dim=head_dim), grid=...  4.83 us
    dot_general x1, matrix products, layer(): jnp.dot(normalized_output, output_weight, preferred_element_type=f32)  3.7 us
    pallas_call x1, Pallas kernels, local_states(): pl.pallas_call(functools.partial(local_kernel, head_dim=head_dim), grid=(...  3.53 us
    dot_general x1, matrix products, layer(): jnp.dot(tokens, key_weight, preferred_element_type=f32)  3.16 us
    dot_general x1, matrix products, layer(): jnp.dot(tokens, query_weight, preferred_element_type=f32)  2.03 us
  transfers between devices with their start and end apart: 6, of which 5 were waited for; matrix products, arithmetic and copies ran while one was open for 5% of the time, Pallas kernels for 15%

profile of v9, /device:TPU:0, one launch (start us, length us, event | category | flops | bytes accessed | tf_op | source)
XLA Modules:
  0.0 64.5 jit_solution(8914957141715443146)
XLA Ops:
  0.0 0.0 copy-start
  0.0 0.0 copy-start.5
  0.0 0.0 copy-start.3
  0.0 1.6 %copy-done = bf16[1024,1024]{1,0:T(8,128)(2,1)S(1)} copy-done((bf16[1024,1024]{1,0:T(8,128)(2,1)S(1)}, bf16[1024,1024]{1,0:T(8,128)(2,1)}, u32[]{:S(2)}) %copy-start) | copy-done | bytes 2097176
  1.6 3.2 %multiply_convert_fusion.k_ref = bf16[384,1024]{1,0:T(8,128)(2,1)} fusion(bf16[384,1024]{1,0:T(8,128)(2,1)} %param.7, bf16[1024,1024]{1,0:T(8,128)(2,1)S(1)} %copy-done), kind=kOutput, calls=%fused_computation | convolution fusion | flops 807272448 | bytes 3670016 | tf_op jit(solution)/shard_map/dot_general | solution.py:232
  4.8 0.0 copy-done.5
  4.8 0.0 copy-done.3
  4.8 0.0 copy-start.2
  4.8 1.9 %convolution_convert_fusion.1.v_ref = bf16[384,1024]{1,0:T(8,128)(2,1)} fusion(bf16[384,1024]{1,0:T(8,128)(2,1)S(1)} %copy-done.5, bf16[1024,1024]{1,0:T(8,128)(2,1)S(1)} %copy-done.3), kind=kOutput, calls=%fused_computation.3 | convolution fusion | flops 805699584 | bytes 3670016 | tf_op jit(solution)/shard_map/dot_general | solution.py:233
  6.6 0.0 copy-done.2
  6.6 0.9 %reduce-window.6 = f32[16,3,128]{2,0,1:T(8,128)S(1)} reduce-window(f32[16,3,128]{2,0,1:T(8,128)S(1)} %copy_bitcast_fusion, f32[]{:T(128)} %constant.42.clone.1), window={size=1x1x128 pad=0_0x0_0x127_0}, to_apply=%region_0.1 | reduce-window | flops 780288 | bytes 49156 | tf_op jit(solution)/shard_map/reduce-window
  7.5 0.2 slice_reduce_fusion
  7.7 0.1 broadcast_add_fusion
  7.8 0.8 %copy.14 = f32[16,3,128]{0,2,1:T(8,128)} copy(f32[16,3,128]{2,0,1:T(8,128)S(1)} %broadcast_add_fusion) | data formatting | bytes 49152 | tf_op jit(solution)/shard_map/reduce_window_sum
  8.6 3.5 %shard_map.75 = f32[8,72,128]{2,1,0:T(8,128)} custom-call(bf16[384,1024]{1,0:T(8,128)(2,1)} %multiply_convert_fusion.k_ref, bf16[384,1024]{1,0:T(8,128)(2,1)} %convolution_convert_fusion.1.v_ref, f32[384,16]{1,0:T(8,128)} %bitcast.30), custom_call_target="tpu_custom_call" | custom-call | flops 100663296 | bytes 1572864 | tf_op jit(solution)/shard_map/pallas_call | solution.py:116
  12.1 0.5 collective-permute-start
  12.6 0.8 %slice_exponential_fusion = f32[8,1,128]{2,1,0:T(1,128)S(1)} fusion(f32[8,72,128]{2,1,0:T(8,128)} %shard_map.75), kind=kLoop, calls=%fused_computation.22 | loop fusion | bytes 8192 | tf_op jit(solution)/shard_map/exp | solution.py:193
  13.4 0.6 collective-permute-done
  14.0 1.1 %fusion.1 = f32[8,72,128]{2,1,0:T(8,128)S(1)} fusion(f32[8,72,128]{2,1,0:T(8,128)S(1)} %collective-permute-done, f32[8,72,128]{2,1,0:T(8,128)} %shard_map.75, f32[8,128]{1,0:T(8,128)S(1)} %bitcast.37, f32[8,128]{1,0:T(8,128)S(1)} %bitcast.35, pred[72]{0:T(512)(128)(4,1)S(1)} %iota_compare_fusion, pred[]{:T(512)S(6)} %eq.4), kind=kLoop, calls=%fused_computation.7 | loop fusion | flops 516096 | bytes 893001 | tf_op jit(solution)/shard_map/jit(_where)/select_n | solution.py:205
  15.2 0.0 copy-start.4
  15.2 0.0 copy-start.6
  15.2 3.0 %collective-permute-start.1 = (f32[4,72,128]{2,1,0:T(8,128)S(1)}, f32[4,72,128]{2,1,0:T(8,128)S(1)}, u32[]{:S(2)}, u32[]{:S(2)}) collective-permute-start(f32[4,72,128]{2,1,0:T(8,128)S(1)} %slice_select_fusion), channel_id=1, source_target_pairs={{0,2},{1,3},{2,0},{3,1},{4,6},{5,7},{6,4},{7,5},{8,10},{9,11},{10,... | collective-permute-start | bytes 442376 | tf_op jit(solution)/shard_map/ppermute | solution.py:212
  18.2 4.1 %collective-permute-done.1 = f32[4,72,128]{2,1,0:T(8,128)S(1)} collective-permute-done((f32[4,72,128]{2,1,0:T(8,128)S(1)}, f32[4,72,128]{2,1,0:T(8,128)S(1)}, u32[]{:S(2)}, u32[]{:S(2)}) %collective-permute-start.1) | collective-permute-done | bytes 147488 | tf_op jit(solution)/shard_map/ppermute | solution.py:212
  22.4 0.1 add_select_fusion.5
  22.5 2.8 %collective-permute-start.2 = (f32[4,72,128]{2,1,0:T(8,128)S(1)}, f32[4,72,128]{2,1,0:T(8,128)S(1)}, u32[]{:S(2)}, u32[]{:S(2)}) collective-permute-start(f32[4,72,128]{2,1,0:T(8,128)S(1)} %get-tuple-element.9), channel_id=1, source_target_pairs={{0,4},{1,5},{2,6},{3,7},{4,0},{5,1},{6,2},{7,3},{8,12},{9,13},{10,... | collective-permute-start | bytes 442376 | tf_op jit(solution)/shard_map/ppermute | solution.py:212
  25.3 6.6 %collective-permute-done.2 = f32[4,72,128]{2,1,0:T(8,128)S(1)} collective-permute-done((f32[4,72,128]{2,1,0:T(8,128)S(1)}, f32[4,72,128]{2,1,0:T(8,128)S(1)}, u32[]{:S(2)}, u32[]{:S(2)}) %collective-permute-start.2) | collective-permute-done | bytes 147488 | tf_op jit(solution)/shard_map/ppermute | solution.py:212
  31.9 0.1 add_select_fusion.4
  32.1 1.4 %collective-permute-start.3 = (f32[4,72,128]{2,1,0:T(8,128)S(1)}, f32[4,72,128]{2,1,0:T(8,128)S(1)}, u32[]{:S(2)}, u32[]{:S(2)}) collective-permute-start(f32[4,72,128]{2,1,0:T(8,128)S(1)} %get-tuple-element.7), channel_id=1, source_target_pairs={{0,8},{1,9},{2,10},{3,11},{4,12},{5,13},{6,14},{7,15},{8,0},{9,1},... | collective-permute-start | bytes 442376 | tf_op jit(solution)/shard_map/ppermute | solution.py:212
  33.5 3.8 %collective-permute-done.3 = f32[4,72,128]{2,1,0:T(8,128)S(1)} collective-permute-done((f32[4,72,128]{2,1,0:T(8,128)S(1)}, f32[4,72,128]{2,1,0:T(8,128)S(1)}, u32[]{:S(2)}, u32[]{:S(2)}) %collective-permute-start.3) | collective-permute-done | bytes 147488 | tf_op jit(solution)/shard_map/ppermute | solution.py:212
  37.3 0.1 add_select_fusion.3
  37.4 1.5 %collective-permute-start.4 = (f32[4,72,128]{2,1,0:T(8,128)S(1)}, f32[4,72,128]{2,1,0:T(8,128)S(1)}, u32[]{:S(2)}, u32[]{:S(2)}) collective-permute-start(f32[4,72,128]{2,1,0:T(8,128)S(1)} %get-tuple-element.5), channel_id=1, source_target_pairs={{0,16},{1,17},{2,18},{3,19},{4,20},{5,21},{6,22},{7,23},{8,24},{9,... | collective-permute-start | bytes 442376 | tf_op jit(solution)/shard_map/ppermute | solution.py:212
  38.9 3.7 %collective-permute-done.4 = f32[4,72,128]{2,1,0:T(8,128)S(1)} collective-permute-done((f32[4,72,128]{2,1,0:T(8,128)S(1)}, f32[4,72,128]{2,1,0:T(8,128)S(1)}, u32[]{:S(2)}, u32[]{:S(2)}) %collective-permute-start.4) | collective-permute-done | bytes 147488 | tf_op jit(solution)/shard_map/ppermute | solution.py:212
  42.6 0.1 add_select_fusion
  42.7 0.0 copy-start.1
  42.7 0.1 collective-permute-start.5
  42.8 0.0 copy-done.4
  42.8 0.0 copy-done.6
  42.8 2.0 %multiply_convert_fusion.1.q_ref = bf16[384,1024]{1,0:T(8,128)(2,1)} fusion(bf16[384,1024]{1,0:T(8,128)(2,1)S(1)} %copy-done.6, bf16[1024,1024]{1,0:T(8,128)(2,1)S(1)} %copy-done.4), kind=kOutput, calls=%fused_computation.1 | convolution fusion | flops 807272448 | bytes 3670016 | tf_op jit(solution)/shard_map/dot_general | solution.py:238
  44.9 0.0 copy-done.1
  44.9 0.7 %copy.16.cum_t_ref = f32[16,384]{1,0:T(8,128)} copy(f32[16,384]{0,1:T(8,128)S(1)} %bitcast.34) | data formatting | bytes 49152 | tf_op jit(solution)/shard_map/reduce_window_sum
  45.6 4.8 %shard_map.73.rest_0_ = f32[384,1024]{1,0:T(8,128)} custom-call(bf16[384,1024]{1,0:T(8,128)(2,1)} %multiply_convert_fusion.1.q_ref, bf16[384,1024]{1,0:T(8,128)(2,1)} %multiply_convert_fusion.k_ref, bf16[384,1024]{1,0:T(8,128)(2,1)} %convolution_convert_fusion.1.v_ref, f32[384,16]{1,0:T(8,128)} %bitcast.31, f32[16,384]{1,0:T(8,128)} %copy.16.cum_t_ref), custom_call_target="tpu_custom_call" | custom-call | flops 603979776 | bytes 1966080 | tf_op jit(solution)/shard_map/pallas_call | solution.py:59
  50.3 4.8 %shard_map.74.intra_ref = f32[384,1024]{1,0:T(8,128)} custom-call(bf16[384,1024]{1,0:T(8,128)(2,1)} %multiply_convert_fusion.1.q_ref, bf16[384,1024]{1,0:T(8,128)(2,1)} %multiply_convert_fusion.k_ref, bf16[384,1024]{1,0:T(8,128)(2,1)} %convolution_convert_fusion.1.v_ref, f32[384,16]{1,0:T(8,128)} %bitcast.32, ...), custom_call_target="tpu_custom_call", output_to_operand_aliasing={{}: (5, {})} | custom-call | flops 603979776 | bytes 1966080 | tf_op jit(solution)/shard_map/pallas_call | solution.py:59
  55.1 0.0 collective-permute-done.5
  55.1 0.8 %fusion.3.state_ref = f32[8,72,128]{2,1,0:T(8,128)} fusion(f32[8,72,128]{2,1,0:T(8,128)S(1)} %collective-permute-done, f32[4,72,128]{2,1,0:T(8,128)S(1)} %collective-permute-done.5, f32[4,72,128]{2,1,0:T(8,128)S(1)} %add_select_fusion, f32[8,128]{1,0:T(8,128)S(1)} %bitcast.36, pred[72]{0:T(512)(128)(4,1)S(1)} %iota_compare_fusion, pred[]{:T(512)S(6)} %eq.4), kind=kLoop, calls=%fused_computation.9 | loop fusion | flops 516096 | bytes 888905 | tf_op jit(solution)/shard_map/jit(_where)/select_n | solution.py:223
  55.9 4.8 %shard_map.76 = bf16[384,1024]{1,0:T(8,128)(2,1)} custom-call(bf16[384,1024]{1,0:T(8,128)(2,1)} %multiply_convert_fusion.1.q_ref, f32[384,1024]{1,0:T(8,128)} %shard_map.74.intra_ref, f32[8,72,128]{2,1,0:T(8,128)} %fusion.3.state_ref, f32[384,16]{1,0:T(8,128)} %bitcast.33, f32[1,1024]{1,0:T(1,128)} %bitcast.48), custom_call_target="tpu_custom_call" | custom-call | flops 301989888 | bytes 3145728 | tf_op jit(solution)/shard_map/pallas_call | solution.py:172
  60.8 3.7 %convolution_convert_fusion = bf16[384,1024]{1,0:T(8,128)(2,1)} fusion(bf16[384,1024]{1,0:T(8,128)(2,1)} %shard_map.76, bf16[1024,1024]{1,0:T(8,128)(2,1)} %param.13), kind=kOutput, calls=%fused_computation.2 | convolution fusion | flops 805699584 | bytes 3670016 | tf_op jit(solution)/shard_map/dot_general | solution.py:244
  (13 shorter events, 0.1 us)
Async XLA Ops:
  0.0 1.6 %copy-start = (bf16[1024,1024]{1,0:T(8,128)(2,1)S(1)}, bf16[1024,1024]{1,0:T(8,128)(2,1)}, u32[]{:S(2)}) copy-start(bf16[1024,1024]{1,0:T(8,128)(2,1)} %param.10) | copy-start | bytes 6291460
  0.0 4.8 %copy-start.5 = (bf16[384,1024]{1,0:T(8,128)(2,1)S(1)}, bf16[384,1024]{1,0:T(8,128)(2,1)}, u32[]{:S(2)}) copy-start(bf16[384,1024]{1,0:T(8,128)(2,1)} %param.7) | copy-start | bytes 2359300
  0.0 4.8 %copy-start.3 = (bf16[1024,1024]{1,0:T(8,128)(2,1)S(1)}, bf16[1024,1024]{1,0:T(8,128)(2,1)}, u32[]{:S(2)}) copy-start(bf16[1024,1024]{1,0:T(8,128)(2,1)} %param.11) | copy-start | bytes 6291460
  4.8 1.9 %copy-start.2 = (f32[384,16]{0,1:T(8,128)S(1)}, f32[384,16]{0,1:T(8,128)}, u32[]{:S(2)}) copy-start(f32[384,16]{0,1:T(8,128)} %param.8) | copy-start | bytes 73732
  12.1 1.9 %collective-permute-start = (f32[8,72,128]{2,1,0:T(8,128)}, f32[8,72,128]{2,1,0:T(8,128)S(1)}, u32[]{:S(2)}, u32[]{:S(2)}) collective-permute-start(f32[8,72,128]{2,1,0:T(8,128)} %shard_map.75), channel_id=1, source_target_pairs={{0,1},{1,0},{2,3},{3,2},{4,5},{5,4},{6,7},{7,6},{8,9},{9,8},{10,11... | collective-permute-start | bytes 884744 | tf_op jit(solution)/shard_map/ppermute | solution.py:204
  15.2 27.7 %copy-start.4 = (bf16[1024,1024]{1,0:T(8,128)(2,1)S(1)}, bf16[1024,1024]{1,0:T(8,128)(2,1)}, u32[]{:S(2)}) copy-start(bf16[1024,1024]{1,0:T(8,128)(2,1)} %param.9) | copy-start | bytes 6291460
  15.2 27.7 %copy-start.6 = (bf16[384,1024]{1,0:T(8,128)(2,1)S(1)}, bf16[384,1024]{1,0:T(8,128)(2,1)}, u32[]{:S(2)}) copy-start(bf16[384,1024]{1,0:T(8,128)(2,1)} %param.7) | copy-start | bytes 2359300
  15.2 7.2 %collective-permute-start.1 = (f32[4,72,128]{2,1,0:T(8,128)S(1)}, f32[4,72,128]{2,1,0:T(8,128)S(1)}, u32[]{:S(2)}, u32[]{:S(2)}) collective-permute-start(f32[4,72,128]{2,1,0:T(8,128)S(1)} %slice_select_fusion), channel_id=1, source_target_pairs={{0,2},{1,3},{2,0},{3,1},{4,6},{5,7},{6,4},{7,5},{8,10},{9,11},{10,... | collective-permute-start | bytes 442376 | tf_op jit(solution)/shard_map/ppermute | solution.py:212
  22.5 9.4 %collective-permute-start.2 = (f32[4,72,128]{2,1,0:T(8,128)S(1)}, f32[4,72,128]{2,1,0:T(8,128)S(1)}, u32[]{:S(2)}, u32[]{:S(2)}) collective-permute-start(f32[4,72,128]{2,1,0:T(8,128)S(1)} %get-tuple-element.9), channel_id=1, source_target_pairs={{0,4},{1,5},{2,6},{3,7},{4,0},{5,1},{6,2},{7,3},{8,12},{9,13},{10,... | collective-permute-start | bytes 442376 | tf_op jit(solution)/shard_map/ppermute | solution.py:212
  32.1 5.2 %collective-permute-start.3 = (f32[4,72,128]{2,1,0:T(8,128)S(1)}, f32[4,72,128]{2,1,0:T(8,128)S(1)}, u32[]{:S(2)}, u32[]{:S(2)}) collective-permute-start(f32[4,72,128]{2,1,0:T(8,128)S(1)} %get-tuple-element.7), channel_id=1, source_target_pairs={{0,8},{1,9},{2,10},{3,11},{4,12},{5,13},{6,14},{7,15},{8,0},{9,1},... | collective-permute-start | bytes 442376 | tf_op jit(solution)/shard_map/ppermute | solution.py:212
  37.4 5.2 %collective-permute-start.4 = (f32[4,72,128]{2,1,0:T(8,128)S(1)}, f32[4,72,128]{2,1,0:T(8,128)S(1)}, u32[]{:S(2)}, u32[]{:S(2)}) collective-permute-start(f32[4,72,128]{2,1,0:T(8,128)S(1)} %get-tuple-element.5), channel_id=1, source_target_pairs={{0,16},{1,17},{2,18},{3,19},{4,20},{5,21},{6,22},{7,23},{8,24},{9,... | collective-permute-start | bytes 442376 | tf_op jit(solution)/shard_map/ppermute | solution.py:212
  42.7 2.1 %copy-start.1 = (f32[16,3,128]{0,2,1:T(8,128)S(1)}, f32[16,3,128]{0,2,1:T(8,128)}, u32[]{:S(2)}) copy-start(f32[16,3,128]{0,2,1:T(8,128)} %copy.14) | copy-start | bytes 73732
  42.7 12.4 %collective-permute-start.5 = (f32[4,72,128]{2,1,0:T(8,128)S(1)}, f32[4,72,128]{2,1,0:T(8,128)S(1)}, u32[]{:S(2)}, u32[]{:S(2)}) collective-permute-start(f32[4,72,128]{2,1,0:T(8,128)S(1)} %add_select_fusion), channel_id=1, source_target_pairs={{0,1},{1,0},{2,3},{3,2},{4,5},{5,4},{6,7},{7,6},{8,9},{9,8},{10,11... | collective-permute-start | bytes 442376 | tf_op jit(solution)/shard_map/ppermute | solution.py:219

commit v10 on v9

--- a/solution.py
+++ b/solution.py
@@ -76,11 +76,6 @@
     return jnp.sum(jnp.where(lane == head, table, 0.0), axis=1, keepdims=True)
 
 
-def local_kernel(k_ref, v_ref, cum_ref, o_ref, *, head_dim):
-    for step in range(o_ref.shape[0]):
-        local_pair(k_ref, v_ref, cum_ref, o_ref, head_dim, step)
-
-
 def local_pair(k_ref, v_ref, cum_ref, o_ref, head_dim, step):
     f32 = jnp.float32
     pair = pl.program_id(0) * o_ref.shape[0] + step
@@ -107,22 +102,40 @@
     o_ref[step, head_dim:, :] = jnp.where(tail_row == 0, jnp.broadcast_to(logs, (8, LANES)), 0.0)
 
 
-def local_states(keys, value_rows, cum, head_dim):
-    rows, width = keys.shape
+def project_kernel(x_ref, wk_ref, wv_ref, cum_ref, k_ref, v_ref, o_ref, *, head_dim):
+    f32 = jnp.float32
+    x = x_ref[...]
+    key_sum = jnp.dot(x, wk_ref[...], preferred_element_type=f32)
+    k_ref[...] = (key_sum / (1.0 + jnp.exp(-key_sum))).astype(jnp.bfloat16)
+    v_ref[...] = jnp.dot(x, wv_ref[...], preferred_element_type=f32).astype(jnp.bfloat16)
+    for step in range(o_ref.shape[0]):
+        local_pair(k_ref, v_ref, cum_ref, o_ref, head_dim, step)
+
+
+def project_keys_values(tokens, key_weight, value_weight, cum, head_dim):
+    rows, depth = tokens.shape
+    width = key_weight.shape[1]
     heads = cum.shape[1]
     pairs = width // LANES
-    per = PER_STEP if pairs % PER_STEP == 0 else 1
+    per = 2 if pairs % 2 == 0 else 1
     block = pl.BlockSpec((rows, per * LANES), lambda p: (0, p))
+    weights = pl.BlockSpec((depth, per * LANES), lambda p: (0, p))
     return pl.pallas_call(
-        functools.partial(local_kernel, head_dim=head_dim),
+        functools.partial(project_kernel, head_dim=head_dim),
         grid=(pairs // per,),
-        in_specs=[block, block, pl.BlockSpec((rows, heads), lambda p: (0, 0))],
-        out_specs=pl.BlockSpec((per, head_dim + 8, LANES), lambda p: (p, 0, 0)),
-        out_shape=jax.ShapeDtypeStruct((pairs, head_dim + 8, LANES), jnp.float32),
+        in_specs=[pl.BlockSpec((rows, depth), lambda p: (0, 0)), weights, weights, pl.BlockSpec((rows, heads), lambda p: (0, 0))],
+        out_specs=[block, block, pl.BlockSpec((per, head_dim + 8, LANES), lambda p: (p, 0, 0))],
+        out_shape=[
+            jax.ShapeDtypeStruct((rows, width), jnp.bfloat16),
+            jax.ShapeDtypeStruct((rows, width), jnp.bfloat16),
+            jax.ShapeDtypeStruct((pairs, head_dim + 8, LANES), jnp.float32),
+        ],
         cost_estimate=pl.CostEstimate(
-            flops=2 * rows * LANES * LANES * pairs, transcendentals=rows * heads, bytes_accessed=rows * width * 4
+            flops=4 * rows * depth * width + 2 * rows * LANES * width,
+            transcendentals=rows * width + rows * heads,
+            bytes_accessed=2 * depth * width * 2 + rows * depth * 2 + rows * width * 4,
         ),
-    )(keys, value_rows, cum)
+    )(tokens, key_weight, value_weight, cum)
 
 
 def finish_kernel(q_ref, intra_ref, state_ref, cum_ref, gain_ref, o_ref, *, head_dim):
@@ -229,10 +242,8 @@
     bf16 = jnp.bfloat16
     heads = log_decay.shape[1]
     dim = key_weight.shape[1] // heads
-    keys = jax.nn.silu(jnp.dot(tokens, key_weight, preferred_element_type=f32)).astype(bf16)
-    value_rows = jnp.dot(tokens, value_weight, preferred_element_type=f32).astype(bf16)
     cum = jnp.cumsum(log_decay, axis=0)
-    packed = local_states(keys, value_rows, cum, dim)
+    keys, value_rows, packed = project_keys_values(tokens, key_weight, value_weight, cum, dim)
     incoming, _ = exclusive_scan(packed, count)
 
     queries = jax.nn.silu(jnp.dot(tokens, query_weight, preferred_element_type=f32)).astype(bf16)

time: 65 us -> 63.1 us (0.971)
  matrix products: 10.8 us -> 6.86 us
  Pallas kernels: 17.9 us -> 20.5 us
  local copies, waits for them, and re-layouts: 4.14 us -> 3.42 us
    dot_general x2 -> x0, matrix products: 5.02 us -> none  [the longest x1 3.16 us: layer(): jnp.dot(tokens, key_weight, preferred_element_type=f32)]
    pallas_call x1, Pallas kernels: 3.53 us -> 6.15 us  [project_keys_values(): pl.pallas_call(functools.partial(project_kernel, head_dim=head_dim), grid...]
    unnamed x14 -> x4, local copies, waits for them, and re-layouts: 1.61 us -> 0.01 us
    dot_general x1, matrix products: 2.03 us -> 3.16 us  [layer(): jnp.dot(tokens, query_weight, preferred_element_type=f32)]
    reshape x1, local copies, waits for them, and re-layouts: 0.01 us -> 0.89 us
  transfers between devices with their start and end apart: 6 -> 6, of which waited for: 5 -> 5; matrix products, arithmetic and copies ran while one was open for 5% -> 7% of each run, Pallas kernels for 15% -> 15%
where the time goes in v10:
time: 63.1 us; the launch traced here: 62.4 us
  Pallas kernels  20.5 us (32%)
  waiting for transfers between devices  18.9 us (30%)
  starting transfers between devices  9.3 us (15%)
  matrix products  6.86 us (11%)
  local copies, waits for them, and re-layouts  3.42 us (5%)
  other arithmetic  3.38 us (5%)
    ppermute x4, waiting for transfers between devices, exclusive_scan(): got = lax.ppermute(through, AXES, perm)  18.2 us
    pallas_call x2, Pallas kernels, intra_attention(): pl.pallas_call(functools.partial(intra_kernel, head_dim=head_dim, first=f...  9.52 us
    ppermute x4, starting transfers between devices, exclusive_scan(): got = lax.ppermute(through, AXES, perm)  8.74 us
    pallas_call x1, Pallas kernels, project_keys_values(): pl.pallas_call(functools.partial(project_kernel, head_dim=head_dim), grid...  6.15 us
    pallas_call x1, Pallas kernels, finish(): pl.pallas_call(functools.partial(finish_kernel, head_dim=head_dim), grid=...  4.84 us
    dot_general x1, matrix products, layer(): jnp.dot(normalized_output, output_weight, preferred_element_type=f32)  3.7 us
    dot_general x1, matrix products, layer(): jnp.dot(tokens, query_weight, preferred_element_type=f32)  3.16 us
    another operation x2, local copies, waits for them, and re-layouts  1.53 us
  transfers between devices with their start and end apart: 6, of which 5 were waited for; matrix products, arithmetic and copies ran while one was open for 7% of the time, Pallas kernels for 15%

profile of v10, /device:TPU:0, one launch (start us, length us, event | category | flops | bytes accessed | tf_op | source)
XLA Modules:
  0.0 62.4 jit_solution(16098105396809528348)
XLA Ops:
  0.0 0.0 copy-start
  0.0 0.9 %copy_bitcast_fusion = f32[16,3,128]{2,0,1:T(8,128)S(1)} fusion(f32[384,16]{0,1:T(8,128)} %param.8), kind=kLoop, calls=%fused_computation.17 | loop fusion | bytes 49152 | tf_op jit(solution)/shard_map/reshape
  0.9 0.9 %reduce-window.6 = f32[16,3,128]{2,0,1:T(8,128)S(1)} reduce-window(f32[16,3,128]{2,0,1:T(8,128)S(1)} %copy_bitcast_fusion, f32[]{:T(128)} %constant.41.clone.1), window={size=1x1x128 pad=0_0x0_0x127_0}, to_apply=%region_0.0 | reduce-window | flops 780288 | bytes 49156 | tf_op jit(solution)/shard_map/reduce-window
  1.7 0.2 slice_reduce_fusion
  1.9 0.1 broadcast_add_fusion
  2.0 0.8 %copy.14 = f32[16,3,128]{0,2,1:T(8,128)} copy(f32[16,3,128]{2,0,1:T(8,128)S(1)} %broadcast_add_fusion) | data formatting | bytes 49152 | tf_op jit(solution)/shard_map/reduce_window_sum
  2.8 6.1 %shard_map.73 = (bf16[384,1024]{1,0:T(8,128)(2,1)}, bf16[384,1024]{1,0:T(8,128)(2,1)}, f32[8,72,128]{2,1,0:T(8,128)}) custom-call(bf16[384,1024]{1,0:T(8,128)(2,1)} %x_ref.1, bf16[1024,1024]{1,0:T(8,128)(2,1)} %wk_ref.1, bf16[1024,1024]{1,0:T(8,128)(2,1)} %wv_ref.1, f32[384,16]{1,0:T(8,128)} %bitcast.26), custom_call_target="tpu_custom_call" | custom-call | flops 1711276032 | bytes 6553600 | tf_op jit(solution)/shard_map/pallas_call | solution.py:123
  9.0 0.5 collective-permute-start
  9.5 0.8 %slice_exponential_fusion.1 = f32[8,1,128]{2,1,0:T(1,128)S(1)} fusion(f32[8,72,128]{2,1,0:T(8,128)} %get-tuple-element.10), kind=kLoop, calls=%fused_computation.21 | loop fusion | bytes 8192 | tf_op jit(solution)/shard_map/exp | solution.py:206
  10.3 0.6 %collective-permute-done = f32[8,72,128]{2,1,0:T(8,128)S(1)} collective-permute-done((f32[8,72,128]{2,1,0:T(8,128)}, f32[8,72,128]{2,1,0:T(8,128)S(1)}, u32[]{:S(2)}, u32[]{:S(2)}) %collective-permute-start) | collective-permute-done | bytes 294944 | tf_op jit(solution)/shard_map/ppermute | solution.py:217
  10.9 1.1 %fusion.1 = f32[8,72,128]{2,1,0:T(8,128)S(1)} fusion(f32[8,72,128]{2,1,0:T(8,128)S(1)} %collective-permute-done, f32[8,72,128]{2,1,0:T(8,128)} %get-tuple-element.10, f32[8,128]{1,0:T(8,128)S(1)} %bitcast.33, f32[8,128]{1,0:T(8,128)S(1)} %bitcast.31, pred[72]{0:T(512)(128)(4,1)S(1)} %iota_compare_fusion, pred[]{:T(512)S(6)} %eq.4), kind=kLoop, calls=%fused_computation.5 | loop fusion | flops 516096 | bytes 893001 | tf_op jit(solution)/shard_map/jit(_where)/select_n | solution.py:218
  12.1 3.0 %collective-permute-start.1 = (f32[4,72,128]{2,1,0:T(8,128)S(1)}, f32[4,72,128]{2,1,0:T(8,128)S(1)}, u32[]{:S(2)}, u32[]{:S(2)}) collective-permute-start(f32[4,72,128]{2,1,0:T(8,128)S(1)} %slice_select_fusion), channel_id=1, source_target_pairs={{0,2},{1,3},{2,0},{3,1},{4,6},{5,7},{6,4},{7,5},{8,10},{9,11},{10,... | collective-permute-start | bytes 442376 | tf_op jit(solution)/shard_map/ppermute | solution.py:225
  15.1 4.1 %collective-permute-done.1 = f32[4,72,128]{2,1,0:T(8,128)S(1)} collective-permute-done((f32[4,72,128]{2,1,0:T(8,128)S(1)}, f32[4,72,128]{2,1,0:T(8,128)S(1)}, u32[]{:S(2)}, u32[]{:S(2)}) %collective-permute-start.1) | collective-permute-done | bytes 147488 | tf_op jit(solution)/shard_map/ppermute | solution.py:225
  19.2 0.1 add_select_fusion.5
  19.3 2.8 %collective-permute-start.2 = (f32[4,72,128]{2,1,0:T(8,128)S(1)}, f32[4,72,128]{2,1,0:T(8,128)S(1)}, u32[]{:S(2)}, u32[]{:S(2)}) collective-permute-start(f32[4,72,128]{2,1,0:T(8,128)S(1)} %get-tuple-element.15), channel_id=1, source_target_pairs={{0,4},{1,5},{2,6},{3,7},{4,0},{5,1},{6,2},{7,3},{8,12},{9,13},{10,... | collective-permute-start | bytes 442376 | tf_op jit(solution)/shard_map/ppermute | solution.py:225
  22.2 6.6 %collective-permute-done.2 = f32[4,72,128]{2,1,0:T(8,128)S(1)} collective-permute-done((f32[4,72,128]{2,1,0:T(8,128)S(1)}, f32[4,72,128]{2,1,0:T(8,128)S(1)}, u32[]{:S(2)}, u32[]{:S(2)}) %collective-permute-start.2) | collective-permute-done | bytes 147488 | tf_op jit(solution)/shard_map/ppermute | solution.py:225
  28.8 0.1 add_select_fusion.4
  28.9 1.4 %collective-permute-start.3 = (f32[4,72,128]{2,1,0:T(8,128)S(1)}, f32[4,72,128]{2,1,0:T(8,128)S(1)}, u32[]{:S(2)}, u32[]{:S(2)}) collective-permute-start(f32[4,72,128]{2,1,0:T(8,128)S(1)} %get-tuple-element.13), channel_id=1, source_target_pairs={{0,8},{1,9},{2,10},{3,11},{4,12},{5,13},{6,14},{7,15},{8,0},{9,1},... | collective-permute-start | bytes 442376 | tf_op jit(solution)/shard_map/ppermute | solution.py:225
  30.4 3.8 %collective-permute-done.3 = f32[4,72,128]{2,1,0:T(8,128)S(1)} collective-permute-done((f32[4,72,128]{2,1,0:T(8,128)S(1)}, f32[4,72,128]{2,1,0:T(8,128)S(1)}, u32[]{:S(2)}, u32[]{:S(2)}) %collective-permute-start.3) | collective-permute-done | bytes 147488 | tf_op jit(solution)/shard_map/ppermute | solution.py:225
  34.1 0.1 add_select_fusion.3
  34.3 1.5 %collective-permute-start.4 = (f32[4,72,128]{2,1,0:T(8,128)S(1)}, f32[4,72,128]{2,1,0:T(8,128)S(1)}, u32[]{:S(2)}, u32[]{:S(2)}) collective-permute-start(f32[4,72,128]{2,1,0:T(8,128)S(1)} %get-tuple-element.11), channel_id=1, source_target_pairs={{0,16},{1,17},{2,18},{3,19},{4,20},{5,21},{6,22},{7,23},{8,24},{9,... | collective-permute-start | bytes 442376 | tf_op jit(solution)/shard_map/ppermute | solution.py:225
  35.7 3.7 %collective-permute-done.4 = f32[4,72,128]{2,1,0:T(8,128)S(1)} collective-permute-done((f32[4,72,128]{2,1,0:T(8,128)S(1)}, f32[4,72,128]{2,1,0:T(8,128)S(1)}, u32[]{:S(2)}, u32[]{:S(2)}) %collective-permute-start.4) | collective-permute-done | bytes 147488 | tf_op jit(solution)/shard_map/ppermute | solution.py:225
  39.5 0.1 add_select_fusion
  39.6 0.0 copy-start.1
  39.6 0.1 collective-permute-start.5
  39.7 0.0 copy-done
  39.7 3.2 %multiply_convert_fusion.q_ref = bf16[384,1024]{1,0:T(8,128)(2,1)} fusion(bf16[384,1024]{1,0:T(8,128)(2,1)} %x_ref.1, bf16[1024,1024]{1,0:T(8,128)(2,1)S(1)} %copy-done), kind=kOutput, calls=%fused_computation | convolution fusion | flops 807272448 | bytes 3670016 | tf_op jit(solution)/shard_map/dot_general | solution.py:249
  42.8 0.0 copy-done.1
  42.8 0.7 %copy.16.cum_t_ref = f32[16,384]{1,0:T(8,128)} copy(f32[16,384]{0,1:T(8,128)S(1)} %bitcast.30) | data formatting | bytes 49152 | tf_op jit(solution)/shard_map/reduce_window_sum
  43.5 4.8 %shard_map.74.rest_0_ = f32[384,1024]{1,0:T(8,128)} custom-call(bf16[384,1024]{1,0:T(8,128)(2,1)} %multiply_convert_fusion.q_ref, bf16[384,1024]{1,0:T(8,128)(2,1)} %get-tuple-element.8.k_ref, bf16[384,1024]{1,0:T(8,128)(2,1)} %get-tuple-element.9.v_ref, f32[384,16]{1,0:T(8,128)} %bitcast.27, f32[16,384]{1,0:T(8,128)} %copy.16.cum_t_ref), custom_call_target="tpu_custom_call" | custom-call | flops 603979776 | bytes 1966080 | tf_op jit(solution)/shard_map/pallas_call | solution.py:59
  48.3 4.8 %shard_map.75.intra_ref = f32[384,1024]{1,0:T(8,128)} custom-call(bf16[384,1024]{1,0:T(8,128)(2,1)} %multiply_convert_fusion.q_ref, bf16[384,1024]{1,0:T(8,128)(2,1)} %get-tuple-element.8.k_ref, bf16[384,1024]{1,0:T(8,128)(2,1)} %get-tuple-element.9.v_ref, f32[384,16]{1,0:T(8,128)} %bitcast.28, ...), custom_call_target="tpu_custom_call", output_to_operand_aliasing={{}: (5, {})} | custom-call | flops 603979776 | bytes 1966080 | tf_op jit(solution)/shard_map/pallas_call | solution.py:59
  53.1 0.0 collective-permute-done.5
  53.1 0.8 %fusion.3.state_ref = f32[8,72,128]{2,1,0:T(8,128)} fusion(f32[8,72,128]{2,1,0:T(8,128)S(1)} %collective-permute-done, f32[4,72,128]{2,1,0:T(8,128)S(1)} %collective-permute-done.5, f32[4,72,128]{2,1,0:T(8,128)S(1)} %add_select_fusion, f32[8,128]{1,0:T(8,128)S(1)} %bitcast.32, pred[72]{0:T(512)(128)(4,1)S(1)} %iota_compare_fusion, pred[]{:T(512)S(6)} %eq.4), kind=kLoop, calls=%fused_computation.7 | loop fusion | flops 516096 | bytes 888905 | tf_op jit(solution)/shard_map/jit(_where)/select_n | solution.py:236
  53.9 4.8 %shard_map.76 = bf16[384,1024]{1,0:T(8,128)(2,1)} custom-call(bf16[384,1024]{1,0:T(8,128)(2,1)} %multiply_convert_fusion.q_ref, f32[384,1024]{1,0:T(8,128)} %shard_map.75.intra_ref, f32[8,72,128]{2,1,0:T(8,128)} %fusion.3.state_ref, f32[384,16]{1,0:T(8,128)} %bitcast.29, f32[1,1024]{1,0:T(1,128)} %bitcast.44), custom_call_target="tpu_custom_call" | custom-call | flops 301989888 | bytes 3145728 | tf_op jit(solution)/shard_map/pallas_call | solution.py:185
  58.7 3.7 %convolution_convert_fusion = bf16[384,1024]{1,0:T(8,128)(2,1)} fusion(bf16[384,1024]{1,0:T(8,128)(2,1)} %shard_map.76, bf16[1024,1024]{1,0:T(8,128)(2,1)} %param.13), kind=kOutput, calls=%fused_computation.1 | convolution fusion | flops 805699584 | bytes 3670016 | tf_op jit(solution)/shard_map/dot_general | solution.py:255
  (12 shorter events, 0.1 us)
Async XLA Ops:
  0.0 39.7 %copy-start = (bf16[1024,1024]{1,0:T(8,128)(2,1)S(1)}, bf16[1024,1024]{1,0:T(8,128)(2,1)}, u32[]{:S(2)}) copy-start(bf16[1024,1024]{1,0:T(8,128)(2,1)} %param.9) | copy-start | bytes 6291460
  9.0 1.9 %collective-permute-start = (f32[8,72,128]{2,1,0:T(8,128)}, f32[8,72,128]{2,1,0:T(8,128)S(1)}, u32[]{:S(2)}, u32[]{:S(2)}) collective-permute-start(f32[8,72,128]{2,1,0:T(8,128)} %get-tuple-element.10), channel_id=1, source_target_pairs={{0,1},{1,0},{2,3},{3,2},{4,5},{5,4},{6,7},{7,6},{8,9},{9,8},{10,11... | collective-permute-start | bytes 884744 | tf_op jit(solution)/shard_map/ppermute | solution.py:217
  12.1 7.1 %collective-permute-start.1 = (f32[4,72,128]{2,1,0:T(8,128)S(1)}, f32[4,72,128]{2,1,0:T(8,128)S(1)}, u32[]{:S(2)}, u32[]{:S(2)}) collective-permute-start(f32[4,72,128]{2,1,0:T(8,128)S(1)} %slice_select_fusion), channel_id=1, source_target_pairs={{0,2},{1,3},{2,0},{3,1},{4,6},{5,7},{6,4},{7,5},{8,10},{9,11},{10,... | collective-permute-start | bytes 442376 | tf_op jit(solution)/shard_map/ppermute | solution.py:225
  19.3 9.4 %collective-permute-start.2 = (f32[4,72,128]{2,1,0:T(8,128)S(1)}, f32[4,72,128]{2,1,0:T(8,128)S(1)}, u32[]{:S(2)}, u32[]{:S(2)}) collective-permute-start(f32[4,72,128]{2,1,0:T(8,128)S(1)} %get-tuple-element.15), channel_id=1, source_target_pairs={{0,4},{1,5},{2,6},{3,7},{4,0},{5,1},{6,2},{7,3},{8,12},{9,13},{10,... | collective-permute-start | bytes 442376 | tf_op jit(solution)/shard_map/ppermute | solution.py:225
  28.9 5.2 %collective-permute-start.3 = (f32[4,72,128]{2,1,0:T(8,128)S(1)}, f32[4,72,128]{2,1,0:T(8,128)S(1)}, u32[]{:S(2)}, u32[]{:S(2)}) collective-permute-start(f32[4,72,128]{2,1,0:T(8,128)S(1)} %get-tuple-element.13), channel_id=1, source_target_pairs={{0,8},{1,9},{2,10},{3,11},{4,12},{5,13},{6,14},{7,15},{8,0},{9,1},... | collective-permute-start | bytes 442376 | tf_op jit(solution)/shard_map/ppermute | solution.py:225
  34.3 5.2 %collective-permute-start.4 = (f32[4,72,128]{2,1,0:T(8,128)S(1)}, f32[4,72,128]{2,1,0:T(8,128)S(1)}, u32[]{:S(2)}, u32[]{:S(2)}) collective-permute-start(f32[4,72,128]{2,1,0:T(8,128)S(1)} %get-tuple-element.11), channel_id=1, source_target_pairs={{0,16},{1,17},{2,18},{3,19},{4,20},{5,21},{6,22},{7,23},{8,24},{9,... | collective-permute-start | bytes 442376 | tf_op jit(solution)/shard_map/ppermute | solution.py:225
  39.6 3.3 %copy-start.1 = (f32[16,3,128]{0,2,1:T(8,128)S(1)}, f32[16,3,128]{0,2,1:T(8,128)}, u32[]{:S(2)}) copy-start(f32[16,3,128]{0,2,1:T(8,128)} %copy.14) | copy-start | bytes 73732
  39.6 13.5 %collective-permute-start.5 = (f32[4,72,128]{2,1,0:T(8,128)S(1)}, f32[4,72,128]{2,1,0:T(8,128)S(1)}, u32[]{:S(2)}, u32[]{:S(2)}) collective-permute-start(f32[4,72,128]{2,1,0:T(8,128)S(1)} %add_select_fusion), channel_id=1, source_target_pairs={{0,1},{1,0},{2,3},{3,2},{4,5},{5,4},{6,7},{7,6},{8,9},{9,8},{10,11... | collective-permute-start | bytes 442376 | tf_op jit(solution)/shard_map/ppermute | solution.py:232

commit v11 on v10

--- a/solution.py
+++ b/solution.py
@@ -4,6 +4,7 @@
 import jax.numpy as jnp
 from jax import lax
 from jax.experimental import pallas as pl
+from jax.experimental.pallas import tpu as pltpu
 from jax.sharding import PartitionSpec as P
 
 
@@ -138,9 +139,23 @@
     )(tokens, key_weight, value_weight, cum)
 
 
-def finish_kernel(q_ref, intra_ref, state_ref, cum_ref, gain_ref, o_ref, *, head_dim):
+def finish_kernel(q_ref, intra_ref, state_ref, cum_ref, gain_ref, w_ref, o_ref, normed_ref, acc_ref, *, head_dim):
     for step in range(state_ref.shape[0]):
-        finish_pair(q_ref, intra_ref, state_ref, cum_ref, gain_ref, o_ref, head_dim, step)
+        finish_pair(q_ref, intra_ref, state_ref, cum_ref, gain_ref, normed_ref, head_dim, step)
+    part = jnp.dot(normed_ref[...], w_ref[...], preferred_element_type=jnp.float32)
+    index = pl.program_id(0)
+
+    @pl.when(index == 0)
+    def _():
+        acc_ref[...] = part
+
+    @pl.when(index > 0)
+    def _():
+        acc_ref[...] += part
+
+    @pl.when(index == pl.num_programs(0) - 1)
+    def _():
+        o_ref[...] = acc_ref[...].astype(o_ref.dtype)
 
 
 def finish_pair(q_ref, intra_ref, state_ref, cum_ref, gain_ref, o_ref, head_dim, step):
@@ -176,10 +191,11 @@
     o_ref[:, cols] = (attended * scale * gain_ref[:, cols]).astype(bf16)
 
 
-def finish(queries, intra, states, cum, norm_gain, head_dim):
+def finish(queries, intra, states, cum, norm_gain, output_weight, head_dim):
     rows, width = queries.shape
     heads = cum.shape[1]
     pairs = width // LANES
+    out_width = output_weight.shape[1]
     per = PER_STEP if pairs % PER_STEP == 0 else 1
     block = pl.BlockSpec((rows, per * LANES), lambda p: (0, p))
     return pl.pallas_call(
@@ -191,13 +207,17 @@
             pl.BlockSpec((per,) + states.shape[1:], lambda p: (p, 0, 0)),
             pl.BlockSpec((rows, heads), lambda p: (0, 0)),
             pl.BlockSpec((1, per * LANES), lambda p: (0, p)),
+            pl.BlockSpec((per * LANES, out_width), lambda p: (p, 0)),
         ],
-        out_specs=block,
-        out_shape=jax.ShapeDtypeStruct((rows, width), jnp.bfloat16),
+        out_specs=pl.BlockSpec((rows, out_width), lambda p: (0, 0)),
+        out_shape=jax.ShapeDtypeStruct((rows, out_width), jnp.bfloat16),
+        scratch_shapes=[pltpu.VMEM((rows, per * LANES), jnp.bfloat16), pltpu.VMEM((rows, out_width), jnp.float32)],
         cost_estimate=pl.CostEstimate(
-            flops=6 * rows * LANES * LANES * pairs, transcendentals=rows * heads * 2, bytes_accessed=rows * width * 8
+            flops=6 * rows * LANES * LANES * pairs + 2 * rows * width * out_width,
+            transcendentals=rows * heads * 2,
+            bytes_accessed=rows * width * 8 + width * out_width * 2,
         ),
-    )(queries, intra, states, cum, norm_gain.reshape(1, width))
+    )(queries, intra, states, cum, norm_gain.reshape(1, width), output_weight)
 
 
 def combine(earlier, later):
@@ -251,8 +271,7 @@
     intra = None
     for first, stop in ((0, blocks // 2), (blocks // 2, blocks)):
         intra = intra_attention(queries, keys, value_rows, cum, dim, first, stop, intra)
-    normalized_output = finish(queries, intra, incoming, cum, norm_gain, dim)
-    return jnp.dot(normalized_output, output_weight, preferred_element_type=f32).astype(bf16)
+    return finish(queries, intra, incoming, cum, norm_gain, output_weight, dim)
 
 
 def solution(mesh):

time: 63.1 us -> 59.5 us (0.943)
  matrix products: 6.86 us -> 2.05 us
  Pallas kernels: 20.5 us -> 21.8 us
    dot_general x1 -> x0, matrix products: 3.7 us -> none  [layer(): jnp.dot(normalized_output, output_weight, preferred_element_type=f32)]
    pallas_call x1, Pallas kernels: 4.84 us -> 6.14 us  [finish(): pl.pallas_call(functools.partial(finish_kernel, head_dim=head_dim), grid=...]
    dot_general x1, matrix products: 3.16 us -> 2.05 us  [layer(): jnp.dot(tokens, query_weight, preferred_element_type=f32)]
  transfers between devices with their start and end apart: 6 -> 6, of which waited for: 5 -> 5; matrix products, arithmetic and copies ran while one was open for 7% -> 6% of each run, Pallas kernels for 15% -> 16%
where the time goes in v11:
time: 59.5 us; the launch traced here: 58.9 us
  Pallas kernels  21.8 us (37%)
  waiting for transfers between devices  18.9 us (32%)
  starting transfers between devices  9.28 us (16%)
  local copies, waits for them, and re-layouts  3.42 us (6%)
  other arithmetic  3.38 us (6%)
  matrix products  2.05 us (3%)
    ppermute x4, waiting for transfers between devices, exclusive_scan(): got = lax.ppermute(through, AXES, perm)  18.3 us
    pallas_call x2, Pallas kernels, intra_attention(): pl.pallas_call(functools.partial(intra_kernel, head_dim=head_dim, first=f...  9.52 us
    ppermute x4, starting transfers between devices, exclusive_scan(): got = lax.ppermute(through, AXES, perm)  8.72 us
    pallas_call x1, Pallas kernels, project_keys_values(): pl.pallas_call(functools.partial(project_kernel, head_dim=head_dim), grid...  6.15 us
    pallas_call x1, Pallas kernels, finish(): pl.pallas_call(functools.partial(finish_kernel, head_dim=head_dim), grid=...  6.14 us
    dot_general x1, matrix products, layer(): jnp.dot(tokens, query_weight, preferred_element_type=f32)  2.05 us
    another operation x2, local copies, waits for them, and re-layouts  1.52 us
  transfers between devices with their start and end apart: 6, of which 5 were waited for; matrix products, arithmetic and copies ran while one was open for 6% of the time, Pallas kernels for 16%

profile of v11, /device:TPU:0, one launch (start us, length us, event | category | flops | bytes accessed | tf_op | source)
XLA Modules:
  0.0 58.9 jit_solution(8964806822466879453)
XLA Ops:
  0.0 0.0 copy-start
  0.0 0.9 %copy_bitcast_fusion = f32[16,3,128]{2,0,1:T(8,128)S(1)} fusion(f32[384,16]{0,1:T(8,128)} %param.8), kind=kLoop, calls=%fused_computation.16 | loop fusion | bytes 49152 | tf_op jit(solution)/shard_map/reshape
  0.9 0.9 %reduce-window.6 = f32[16,3,128]{2,0,1:T(8,128)S(1)} reduce-window(f32[16,3,128]{2,0,1:T(8,128)S(1)} %copy_bitcast_fusion, f32[]{:T(128)} %constant.41.clone.1), window={size=1x1x128 pad=0_0x0_0x127_0}, to_apply=%region_0.0 | reduce-window | flops 780288 | bytes 49156 | tf_op jit(solution)/shard_map/reduce-window
  1.7 0.2 slice_reduce_fusion
  1.9 0.1 broadcast_add_fusion
  2.0 0.8 %copy.14 = f32[16,3,128]{0,2,1:T(8,128)} copy(f32[16,3,128]{2,0,1:T(8,128)S(1)} %broadcast_add_fusion) | data formatting | bytes 49152 | tf_op jit(solution)/shard_map/reduce_window_sum
  2.8 6.1 %shard_map.73 = (bf16[384,1024]{1,0:T(8,128)(2,1)}, bf16[384,1024]{1,0:T(8,128)(2,1)}, f32[8,72,128]{2,1,0:T(8,128)}) custom-call(bf16[384,1024]{1,0:T(8,128)(2,1)} %x_ref.1, bf16[1024,1024]{1,0:T(8,128)(2,1)} %wk_ref.1, bf16[1024,1024]{1,0:T(8,128)(2,1)} %wv_ref.1, f32[384,16]{1,0:T(8,128)} %bitcast.24), custom_call_target="tpu_custom_call" | custom-call | flops 1711276032 | bytes 6553600 | tf_op jit(solution)/shard_map/pallas_call | solution.py:124
  9.0 0.5 collective-permute-start
  9.5 0.8 %slice_exponential_fusion.1 = f32[8,1,128]{2,1,0:T(1,128)S(1)} fusion(f32[8,72,128]{2,1,0:T(8,128)} %get-tuple-element.10), kind=kLoop, calls=%fused_computation.20 | loop fusion | bytes 8192 | tf_op jit(solution)/shard_map/exp | solution.py:226
  10.3 0.6 %collective-permute-done = f32[8,72,128]{2,1,0:T(8,128)S(1)} collective-permute-done((f32[8,72,128]{2,1,0:T(8,128)}, f32[8,72,128]{2,1,0:T(8,128)S(1)}, u32[]{:S(2)}, u32[]{:S(2)}) %collective-permute-start) | collective-permute-done | bytes 294944 | tf_op jit(solution)/shard_map/ppermute | solution.py:237
  10.9 1.1 %fusion.1 = f32[8,72,128]{2,1,0:T(8,128)S(1)} fusion(f32[8,72,128]{2,1,0:T(8,128)S(1)} %collective-permute-done, f32[8,72,128]{2,1,0:T(8,128)} %get-tuple-element.10, f32[8,128]{1,0:T(8,128)S(1)} %bitcast.31, f32[8,128]{1,0:T(8,128)S(1)} %bitcast.29, pred[72]{0:T(512)(128)(4,1)S(1)} %iota_compare_fusion, pred[]{:T(512)S(6)} %eq.4), kind=kLoop, calls=%fused_computation.4 | loop fusion | flops 516096 | bytes 893001 | tf_op jit(solution)/shard_map/jit(_where)/select_n | solution.py:238
  12.0 0.0 copy-start.2
  12.1 3.0 %collective-permute-start.1 = (f32[4,72,128]{2,1,0:T(8,128)S(1)}, f32[4,72,128]{2,1,0:T(8,128)S(1)}, u32[]{:S(2)}, u32[]{:S(2)}) collective-permute-start(f32[4,72,128]{2,1,0:T(8,128)S(1)} %slice_select_fusion), channel_id=1, source_target_pairs={{0,2},{1,3},{2,0},{3,1},{4,6},{5,7},{6,4},{7,5},{8,10},{9,11},{10,... | collective-permute-start | bytes 442376 | tf_op jit(solution)/shard_map/ppermute | solution.py:245
  15.1 4.1 %collective-permute-done.1 = f32[4,72,128]{2,1,0:T(8,128)S(1)} collective-permute-done((f32[4,72,128]{2,1,0:T(8,128)S(1)}, f32[4,72,128]{2,1,0:T(8,128)S(1)}, u32[]{:S(2)}, u32[]{:S(2)}) %collective-permute-start.1) | collective-permute-done | bytes 147488 | tf_op jit(solution)/shard_map/ppermute | solution.py:245
  19.2 0.1 add_select_fusion.5
  19.3 2.8 %collective-permute-start.2 = (f32[4,72,128]{2,1,0:T(8,128)S(1)}, f32[4,72,128]{2,1,0:T(8,128)S(1)}, u32[]{:S(2)}, u32[]{:S(2)}) collective-permute-start(f32[4,72,128]{2,1,0:T(8,128)S(1)} %get-tuple-element.15), channel_id=1, source_target_pairs={{0,4},{1,5},{2,6},{3,7},{4,0},{5,1},{6,2},{7,3},{8,12},{9,13},{10,... | collective-permute-start | bytes 442376 | tf_op jit(solution)/shard_map/ppermute | solution.py:245
  22.2 6.6 %collective-permute-done.2 = f32[4,72,128]{2,1,0:T(8,128)S(1)} collective-permute-done((f32[4,72,128]{2,1,0:T(8,128)S(1)}, f32[4,72,128]{2,1,0:T(8,128)S(1)}, u32[]{:S(2)}, u32[]{:S(2)}) %collective-permute-start.2) | collective-permute-done | bytes 147488 | tf_op jit(solution)/shard_map/ppermute | solution.py:245
  28.8 0.1 add_select_fusion.4
  28.9 1.4 %collective-permute-start.3 = (f32[4,72,128]{2,1,0:T(8,128)S(1)}, f32[4,72,128]{2,1,0:T(8,128)S(1)}, u32[]{:S(2)}, u32[]{:S(2)}) collective-permute-start(f32[4,72,128]{2,1,0:T(8,128)S(1)} %get-tuple-element.13), channel_id=1, source_target_pairs={{0,8},{1,9},{2,10},{3,11},{4,12},{5,13},{6,14},{7,15},{8,0},{9,1},... | collective-permute-start | bytes 442376 | tf_op jit(solution)/shard_map/ppermute | solution.py:245
  30.4 3.8 %collective-permute-done.3 = f32[4,72,128]{2,1,0:T(8,128)S(1)} collective-permute-done((f32[4,72,128]{2,1,0:T(8,128)S(1)}, f32[4,72,128]{2,1,0:T(8,128)S(1)}, u32[]{:S(2)}, u32[]{:S(2)}) %collective-permute-start.3) | collective-permute-done | bytes 147488 | tf_op jit(solution)/shard_map/ppermute | solution.py:245
  34.1 0.1 add_select_fusion.3
  34.3 1.5 %collective-permute-start.4 = (f32[4,72,128]{2,1,0:T(8,128)S(1)}, f32[4,72,128]{2,1,0:T(8,128)S(1)}, u32[]{:S(2)}, u32[]{:S(2)}) collective-permute-start(f32[4,72,128]{2,1,0:T(8,128)S(1)} %get-tuple-element.11), channel_id=1, source_target_pairs={{0,16},{1,17},{2,18},{3,19},{4,20},{5,21},{6,22},{7,23},{8,24},{9,... | collective-permute-start | bytes 442376 | tf_op jit(solution)/shard_map/ppermute | solution.py:245
  35.8 3.7 %collective-permute-done.4 = f32[4,72,128]{2,1,0:T(8,128)S(1)} collective-permute-done((f32[4,72,128]{2,1,0:T(8,128)S(1)}, f32[4,72,128]{2,1,0:T(8,128)S(1)}, u32[]{:S(2)}, u32[]{:S(2)}) %collective-permute-start.4) | collective-permute-done | bytes 147488 | tf_op jit(solution)/shard_map/ppermute | solution.py:245
  39.5 0.1 add_select_fusion
  39.6 0.0 copy-start.1
  39.6 0.1 collective-permute-start.5
  39.7 0.0 copy-done
  39.7 0.0 copy-done.2
  39.7 2.0 %multiply_convert_fusion.q_ref = bf16[384,1024]{1,0:T(8,128)(2,1)} fusion(bf16[384,1024]{1,0:T(8,128)(2,1)S(1)} %copy-done.2, bf16[1024,1024]{1,0:T(8,128)(2,1)S(1)} %copy-done), kind=kOutput, calls=%fused_computation | convolution fusion | flops 807272448 | bytes 3670016 | tf_op jit(solution)/shard_map/dot_general | solution.py:269
  41.7 0.0 copy-done.1
  41.7 0.7 %copy.16.cum_t_ref = f32[16,384]{1,0:T(8,128)} copy(f32[16,384]{0,1:T(8,128)S(1)} %bitcast.28) | data formatting | bytes 49152 | tf_op jit(solution)/shard_map/reduce_window_sum
  42.5 4.8 %shard_map.74.rest_0_ = f32[384,1024]{1,0:T(8,128)} custom-call(bf16[384,1024]{1,0:T(8,128)(2,1)} %multiply_convert_fusion.q_ref, bf16[384,1024]{1,0:T(8,128)(2,1)} %get-tuple-element.8.k_ref, bf16[384,1024]{1,0:T(8,128)(2,1)} %get-tuple-element.9.v_ref, f32[384,16]{1,0:T(8,128)} %bitcast.25, f32[16,384]{1,0:T(8,128)} %copy.16.cum_t_ref), custom_call_target="tpu_custom_call" | custom-call | flops 603979776 | bytes 1966080 | tf_op jit(solution)/shard_map/pallas_call | solution.py:60
  47.2 4.8 %shard_map.75.intra_ref = f32[384,1024]{1,0:T(8,128)} custom-call(bf16[384,1024]{1,0:T(8,128)(2,1)} %multiply_convert_fusion.q_ref, bf16[384,1024]{1,0:T(8,128)(2,1)} %get-tuple-element.8.k_ref, bf16[384,1024]{1,0:T(8,128)(2,1)} %get-tuple-element.9.v_ref, f32[384,16]{1,0:T(8,128)} %bitcast.26, ...), custom_call_target="tpu_custom_call", output_to_operand_aliasing={{}: (5, {})} | custom-call | flops 603979776 | bytes 1966080 | tf_op jit(solution)/shard_map/pallas_call | solution.py:60
  52.0 0.0 collective-permute-done.5
  52.0 0.8 %fusion.3.state_ref = f32[8,72,128]{2,1,0:T(8,128)} fusion(f32[8,72,128]{2,1,0:T(8,128)S(1)} %collective-permute-done, f32[4,72,128]{2,1,0:T(8,128)S(1)} %collective-permute-done.5, f32[4,72,128]{2,1,0:T(8,128)S(1)} %add_select_fusion, f32[8,128]{1,0:T(8,128)S(1)} %bitcast.30, pred[72]{0:T(512)(128)(4,1)S(1)} %iota_compare_fusion, pred[]{:T(512)S(6)} %eq.4), kind=kLoop, calls=%fused_computation.6 | loop fusion | flops 516096 | bytes 888905 | tf_op jit(solution)/shard_map/jit(_where)/select_n | solution.py:256
  52.8 6.1 %shard_map.76 = bf16[384,1024]{1,0:T(8,128)(2,1)} custom-call(bf16[384,1024]{1,0:T(8,128)(2,1)} %multiply_convert_fusion.q_ref, f32[384,1024]{1,0:T(8,128)} %shard_map.75.intra_ref, f32[8,72,128]{2,1,0:T(8,128)} %fusion.3.state_ref, f32[384,16]{1,0:T(8,128)} %bitcast.27, f32[1,1024]{1,0:T(1,128)} %bitcast.42, bf16[1024,1024]{1,0:T(8,128)(2,1)} %w_ref.1), custom_call_target="tpu_custom_call" | custom-call | flops 1107296256 | bytes 5242880 | tf_op jit(solution)/shard_map/pallas_call | solution.py:201
  (12 shorter events, 0.1 us)
Async XLA Ops:
  0.0 39.7 %copy-start = (bf16[1024,1024]{1,0:T(8,128)(2,1)S(1)}, bf16[1024,1024]{1,0:T(8,128)(2,1)}, u32[]{:S(2)}) copy-start(bf16[1024,1024]{1,0:T(8,128)(2,1)} %param.9) | copy-start | bytes 6291460
  9.0 1.9 %collective-permute-start = (f32[8,72,128]{2,1,0:T(8,128)}, f32[8,72,128]{2,1,0:T(8,128)S(1)}, u32[]{:S(2)}, u32[]{:S(2)}) collective-permute-start(f32[8,72,128]{2,1,0:T(8,128)} %get-tuple-element.10), channel_id=1, source_target_pairs={{0,1},{1,0},{2,3},{3,2},{4,5},{5,4},{6,7},{7,6},{8,9},{9,8},{10,11... | collective-permute-start | bytes 884744 | tf_op jit(solution)/shard_map/ppermute | solution.py:237
  12.0 27.7 %copy-start.2 = (bf16[384,1024]{1,0:T(8,128)(2,1)S(1)}, bf16[384,1024]{1,0:T(8,128)(2,1)}, u32[]{:S(2)}) copy-start(bf16[384,1024]{1,0:T(8,128)(2,1)} %x_ref.1) | copy-start | bytes 2359300
  12.1 7.2 %collective-permute-start.1 = (f32[4,72,128]{2,1,0:T(8,128)S(1)}, f32[4,72,128]{2,1,0:T(8,128)S(1)}, u32[]{:S(2)}, u32[]{:S(2)}) collective-permute-start(f32[4,72,128]{2,1,0:T(8,128)S(1)} %slice_select_fusion), channel_id=1, source_target_pairs={{0,2},{1,3},{2,0},{3,1},{4,6},{5,7},{6,4},{7,5},{8,10},{9,11},{10,... | collective-permute-start | bytes 442376 | tf_op jit(solution)/shard_map/ppermute | solution.py:245
  19.3 9.4 %collective-permute-start.2 = (f32[4,72,128]{2,1,0:T(8,128)S(1)}, f32[4,72,128]{2,1,0:T(8,128)S(1)}, u32[]{:S(2)}, u32[]{:S(2)}) collective-permute-start(f32[4,72,128]{2,1,0:T(8,128)S(1)} %get-tuple-element.15), channel_id=1, source_target_pairs={{0,4},{1,5},{2,6},{3,7},{4,0},{5,1},{6,2},{7,3},{8,12},{9,13},{10,... | collective-permute-start | bytes 442376 | tf_op jit(solution)/shard_map/ppermute | solution.py:245
  28.9 5.2 %collective-permute-start.3 = (f32[4,72,128]{2,1,0:T(8,128)S(1)}, f32[4,72,128]{2,1,0:T(8,128)S(1)}, u32[]{:S(2)}, u32[]{:S(2)}) collective-permute-start(f32[4,72,128]{2,1,0:T(8,128)S(1)} %get-tuple-element.13), channel_id=1, source_target_pairs={{0,8},{1,9},{2,10},{3,11},{4,12},{5,13},{6,14},{7,15},{8,0},{9,1},... | collective-permute-start | bytes 442376 | tf_op jit(solution)/shard_map/ppermute | solution.py:245
  34.3 5.2 %collective-permute-start.4 = (f32[4,72,128]{2,1,0:T(8,128)S(1)}, f32[4,72,128]{2,1,0:T(8,128)S(1)}, u32[]{:S(2)}, u32[]{:S(2)}) collective-permute-start(f32[4,72,128]{2,1,0:T(8,128)S(1)} %get-tuple-element.11), channel_id=1, source_target_pairs={{0,16},{1,17},{2,18},{3,19},{4,20},{5,21},{6,22},{7,23},{8,24},{9,... | collective-permute-start | bytes 442376 | tf_op jit(solution)/shard_map/ppermute | solution.py:245
  39.6 2.2 %copy-start.1 = (f32[16,3,128]{0,2,1:T(8,128)S(1)}, f32[16,3,128]{0,2,1:T(8,128)}, u32[]{:S(2)}) copy-start(f32[16,3,128]{0,2,1:T(8,128)} %copy.14) | copy-start | bytes 73732
  39.6 12.4 %collective-permute-start.5 = (f32[4,72,128]{2,1,0:T(8,128)S(1)}, f32[4,72,128]{2,1,0:T(8,128)S(1)}, u32[]{:S(2)}, u32[]{:S(2)}) collective-permute-start(f32[4,72,128]{2,1,0:T(8,128)S(1)} %add_select_fusion), channel_id=1, source_target_pairs={{0,1},{1,0},{2,3},{3,2},{4,5},{5,4},{6,7},{7,6},{8,9},{9,8},{10,11... | collective-permute-start | bytes 442376 | tf_op jit(solution)/shard_map/ppermute | solution.py:252

commit v12 on v11

--- a/solution.py
+++ b/solution.py
@@ -47,7 +47,7 @@
     o_ref[...] = out
 
 
-def intra_attention(queries, keys, value_rows, cum, head_dim, first, stop, into=None):
+def intra_attention(queries, keys, value_rows, cum, cum_t, head_dim, first, stop, into=None):
     rows, width = queries.shape
     heads = cum.shape[1]
     block = pl.BlockSpec((rows, LANES), lambda p: (0, p + first))
@@ -69,7 +69,7 @@
             transcendentals=rows * rows * steps * (LANES // head_dim),
             bytes_accessed=rows * steps * LANES * 10,
         ),
-    )(queries, keys, value_rows, cum, cum.T, *extra)
+    )(queries, keys, value_rows, cum, cum_t, *extra)
 
 
 def head_column(table, head):
@@ -103,8 +103,24 @@
     o_ref[step, head_dim:, :] = jnp.where(tail_row == 0, jnp.broadcast_to(logs, (8, LANES)), 0.0)
 
 
-def project_kernel(x_ref, wk_ref, wv_ref, cum_ref, k_ref, v_ref, o_ref, *, head_dim):
-    f32 = jnp.float32
+def project_kernel(x_ref, wk_ref, wv_ref, g_ref, k_ref, v_ref, o_ref, cum_ref, cum_t_ref, *, head_dim):
+    f32 = jnp.float32
+    bf16 = jnp.bfloat16
+    rows = g_ref.shape[0]
+    t_i = lax.broadcasted_iota(jnp.int32, (rows, rows), 0)
+    s_i = lax.broadcasted_iota(jnp.int32, (rows, rows), 1)
+    lower = jnp.where(s_i <= t_i, 1.0, 0.0).astype(bf16)
+    upper = jnp.where(t_i <= s_i, 1.0, 0.0).astype(bf16)
+    rest = g_ref[...]
+    cum = jnp.zeros(cum_ref.shape, f32)
+    cum_t = jnp.zeros(cum_t_ref.shape, f32)
+    for _ in range(3):
+        part = rest.astype(bf16)
+        cum = cum + jnp.dot(lower, part, preferred_element_type=f32)
+        cum_t = cum_t + lax.dot_general(part, upper, (((0,), (0,)), ((), ())), preferred_element_type=f32)
+        rest = rest - part.astype(f32)
+    cum_ref[...] = cum
+    cum_t_ref[...] = cum_t
     x = x_ref[...]
     key_sum = jnp.dot(x, wk_ref[...], preferred_element_type=f32)
     k_ref[...] = (key_sum / (1.0 + jnp.exp(-key_sum))).astype(jnp.bfloat16)
@@ -113,10 +129,10 @@
         local_pair(k_ref, v_ref, cum_ref, o_ref, head_dim, step)
 
 
-def project_keys_values(tokens, key_weight, value_weight, cum, head_dim):
+def project_keys_values(tokens, key_weight, value_weight, log_decay, head_dim):
     rows, depth = tokens.shape
     width = key_weight.shape[1]
-    heads = cum.shape[1]
+    heads = log_decay.shape[1]
     pairs = width // LANES
     per = 2 if pairs % 2 == 0 else 1
     block = pl.BlockSpec((rows, per * LANES), lambda p: (0, p))
@@ -125,18 +141,26 @@
         functools.partial(project_kernel, head_dim=head_dim),
         grid=(pairs // per,),
         in_specs=[pl.BlockSpec((rows, depth), lambda p: (0, 0)), weights, weights, pl.BlockSpec((rows, heads), lambda p: (0, 0))],
-        out_specs=[block, block, pl.BlockSpec((per, head_dim + 8, LANES), lambda p: (p, 0, 0))],
+        out_specs=[
+            block,
+            block,
+            pl.BlockSpec((per, head_dim + 8, LANES), lambda p: (p, 0, 0)),
+            pl.BlockSpec((rows, heads), lambda p: (0, 0)),
+            pl.BlockSpec((heads, rows), lambda p: (0, 0)),
+        ],
         out_shape=[
             jax.ShapeDtypeStruct((rows, width), jnp.bfloat16),
             jax.ShapeDtypeStruct((rows, width), jnp.bfloat16),
             jax.ShapeDtypeStruct((pairs, head_dim + 8, LANES), jnp.float32),
+            jax.ShapeDtypeStruct((rows, heads), jnp.float32),
+            jax.ShapeDtypeStruct((heads, rows), jnp.float32),
         ],
         cost_estimate=pl.CostEstimate(
             flops=4 * rows * depth * width + 2 * rows * LANES * width,
             transcendentals=rows * width + rows * heads,
             bytes_accessed=2 * depth * width * 2 + rows * depth * 2 + rows * width * 4,
         ),
-    )(tokens, key_weight, value_weight, cum)
+    )(tokens, key_weight, value_weight, log_decay)
 
 
 def finish_kernel(q_ref, intra_ref, state_ref, cum_ref, gain_ref, w_ref, o_ref, normed_ref, acc_ref, *, head_dim):
@@ -262,15 +286,15 @@
     bf16 = jnp.bfloat16
     heads = log_decay.shape[1]
     dim = key_weight.shape[1] // heads
-    cum = jnp.cumsum(log_decay, axis=0)
-    keys, value_rows, packed = project_keys_values(tokens, key_weight, value_weight, cum, dim)
+    keys, value_rows, packed, cum, cum_t = project_keys_values(tokens, key_weight, value_weight, log_decay, dim)
     incoming, _ = exclusive_scan(packed, count)
 
     queries = jax.nn.silu(jnp.dot(tokens, query_weight, preferred_element_type=f32)).astype(bf16)
     blocks = keys.shape[1] // LANES
     intra = None
-    for first, stop in ((0, blocks // 2), (blocks // 2, blocks)):
-        intra = intra_attention(queries, keys, value_rows, cum, dim, first, stop, intra)
+    cuts = (0, blocks // 2, (3 * blocks) // 4, blocks)
+    for part in range(3):
+        intra = intra_attention(queries, keys, value_rows, cum, cum_t, dim, cuts[part], cuts[part + 1], intra)
     return finish(queries, intra, incoming, cum, norm_gain, output_weight, dim)
 
 

time: 59.5 us -> 60.1 us (1.010)
  Pallas kernels: 21.8 us -> 24.4 us
  other arithmetic: 3.38 us -> 2.41 us
  local copies, waits for them, and re-layouts: 3.42 us -> 2.55 us
    unnamed x6 -> x5, local copies, waits for them, and re-layouts: 0.01 us -> 1.71 us
    another operation x2 -> x0, local copies, waits for them, and re-layouts: 1.52 us -> none
    pallas_call x2 -> x3, Pallas kernels: 9.52 us -> 10.9 us  [intra_attention(): pl.pallas_call(functools.partial(intra_kernel, head_dim=head_dim, first=f...]
    pallas_call x1, Pallas kernels: 6.15 us -> 7.4 us  [project_keys_values(): pl.pallas_call(functools.partial(project_kernel, head_dim=head_dim), grid...]
    another operation x3 -> x0, other arithmetic: 0.97 us -> none
    reshape x1 -> x0, local copies, waits for them, and re-layouts: 0.89 us -> none
  transfers between devices with their start and end apart: 6 -> 6, of which waited for: 5 -> 5; matrix products, arithmetic and copies ran while one was open for 6% -> 5% of each run, Pallas kernels for 16% -> 18%
where the time goes in v12:
time: 60.1 us; the launch traced here: 59.7 us
  Pallas kernels  24.4 us (41%)
  waiting for transfers between devices  18.9 us (31%)
  starting transfers between devices  9.28 us (15%)
  local copies, waits for them, and re-layouts  2.55 us (4%)
  other arithmetic  2.41 us (4%)
  matrix products  2.04 us (3%)
    ppermute x4, waiting for transfers between devices, exclusive_scan(): got = lax.ppermute(through, AXES, perm)  18.2 us
    pallas_call x3, Pallas kernels, intra_attention(): pl.pallas_call(functools.partial(intra_kernel, head_dim=head_dim, first=f...  10.9 us
    ppermute x4, starting transfers between devices, exclusive_scan(): got = lax.ppermute(through, AXES, perm)  8.72 us
    pallas_call x1, Pallas kernels, project_keys_values(): pl.pallas_call(functools.partial(project_kernel, head_dim=head_dim), grid...  7.4 us
    pallas_call x1, Pallas kernels, finish(): pl.pallas_call(functools.partial(finish_kernel, head_dim=head_dim), grid=...  6.15 us
    dot_general x1, matrix products, layer(): jnp.dot(tokens, query_weight, preferred_element_type=f32)  2.04 us
    unnamed x5, local copies, waits for them, and re-layouts  1.71 us
  transfers between devices with their start and end apart: 6, of which 5 were waited for; matrix products, arithmetic and copies ran while one was open for 5% of the time, Pallas kernels for 18%

profile of v12, /device:TPU:0, one launch (start us, length us, event | category | flops | bytes accessed | tf_op | source)
XLA Modules:
  0.0 59.7 jit_solution(12156796759426636472)
XLA Ops:
  0.0 0.0 copy-start
  0.0 1.7 %copy.10.g_ref = f32[384,16]{1,0:T(8,128)} copy(f32[384,16]{0,1:T(8,128)} %param.8) | data formatting | bytes 49152 | tf_op args[1]
  1.7 7.4 %shard_map.73 = (bf16[384,1024]{1,0:T(8,128)(2,1)}, bf16[384,1024]{1,0:T(8,128)(2,1)}, f32[8,72,128]{2,1,0:T(8,128)}, f32[384,16]{1,0:T(8,128)}, f32[16,384]{1,0:T(8,128)}) custom-call(bf16[384,1024]{1,0:T(8,128)(2,1)} %x_ref.1, bf16[1024,1024]{1,0:T(8,128)(2,1)} %wk_ref.1, bf16[1024,1024]{1,0:T(8,128)(2,1)} %wv_ref.1, f32[384,16]{1,0:T(8,128)} %copy.10.g_ref), custom_call_target="tpu_custom_call" | custom-call | flops 1711276032 | bytes 6553600 | tf_op jit(solution)/shard_map/pallas_call | solution.py:140
  9.1 0.5 collective-permute-start
  9.6 0.8 %slice_exponential_fusion.1 = f32[8,1,128]{2,1,0:T(1,128)S(1)} fusion(f32[8,72,128]{2,1,0:T(8,128)} %get-tuple-element.14), kind=kLoop, calls=%fused_computation.17 | loop fusion | bytes 8192 | tf_op jit(solution)/shard_map/exp | solution.py:250
  10.4 0.6 %collective-permute-done = f32[8,72,128]{2,1,0:T(8,128)S(1)} collective-permute-done((f32[8,72,128]{2,1,0:T(8,128)}, f32[8,72,128]{2,1,0:T(8,128)S(1)}, u32[]{:S(2)}, u32[]{:S(2)}) %collective-permute-start) | collective-permute-done | bytes 294944 | tf_op jit(solution)/shard_map/ppermute | solution.py:261
  11.0 1.1 %fusion.1 = f32[8,72,128]{2,1,0:T(8,128)S(1)} fusion(f32[8,72,128]{2,1,0:T(8,128)S(1)} %collective-permute-done, f32[8,72,128]{2,1,0:T(8,128)} %get-tuple-element.14, f32[8,128]{1,0:T(8,128)S(1)} %bitcast.16, f32[8,128]{1,0:T(8,128)S(1)} %bitcast.14, pred[72]{0:T(512)(128)(4,1)S(1)} %iota_compare_fusion, pred[]{:T(512)S(6)} %eq.4), kind=kLoop, calls=%fused_computation.4 | loop fusion | flops 516096 | bytes 893001 | tf_op jit(solution)/shard_map/jit(_where)/select_n | solution.py:262
  12.1 0.0 copy-start.1
  12.2 3.0 %collective-permute-start.1 = (f32[4,72,128]{2,1,0:T(8,128)S(1)}, f32[4,72,128]{2,1,0:T(8,128)S(1)}, u32[]{:S(2)}, u32[]{:S(2)}) collective-permute-start(f32[4,72,128]{2,1,0:T(8,128)S(1)} %slice_select_fusion), channel_id=1, source_target_pairs={{0,2},{1,3},{2,0},{3,1},{4,6},{5,7},{6,4},{7,5},{8,10},{9,11},{10,... | collective-permute-start | bytes 442376 | tf_op jit(solution)/shard_map/ppermute | solution.py:269
  15.2 4.1 %collective-permute-done.1 = f32[4,72,128]{2,1,0:T(8,128)S(1)} collective-permute-done((f32[4,72,128]{2,1,0:T(8,128)S(1)}, f32[4,72,128]{2,1,0:T(8,128)S(1)}, u32[]{:S(2)}, u32[]{:S(2)}) %collective-permute-start.1) | collective-permute-done | bytes 147488 | tf_op jit(solution)/shard_map/ppermute | solution.py:269
  19.3 0.1 add_select_fusion.5
  19.4 2.8 %collective-permute-start.2 = (f32[4,72,128]{2,1,0:T(8,128)S(1)}, f32[4,72,128]{2,1,0:T(8,128)S(1)}, u32[]{:S(2)}, u32[]{:S(2)}) collective-permute-start(f32[4,72,128]{2,1,0:T(8,128)S(1)} %get-tuple-element.19), channel_id=1, source_target_pairs={{0,4},{1,5},{2,6},{3,7},{4,0},{5,1},{6,2},{7,3},{8,12},{9,13},{10,... | collective-permute-start | bytes 442376 | tf_op jit(solution)/shard_map/ppermute | solution.py:269
  22.3 6.6 %collective-permute-done.2 = f32[4,72,128]{2,1,0:T(8,128)S(1)} collective-permute-done((f32[4,72,128]{2,1,0:T(8,128)S(1)}, f32[4,72,128]{2,1,0:T(8,128)S(1)}, u32[]{:S(2)}, u32[]{:S(2)}) %collective-permute-start.2) | collective-permute-done | bytes 147488 | tf_op jit(solution)/shard_map/ppermute | solution.py:269
  28.9 0.1 add_select_fusion.4
  29.0 1.4 %collective-permute-start.3 = (f32[4,72,128]{2,1,0:T(8,128)S(1)}, f32[4,72,128]{2,1,0:T(8,128)S(1)}, u32[]{:S(2)}, u32[]{:S(2)}) collective-permute-start(f32[4,72,128]{2,1,0:T(8,128)S(1)} %get-tuple-element.17), channel_id=1, source_target_pairs={{0,8},{1,9},{2,10},{3,11},{4,12},{5,13},{6,14},{7,15},{8,0},{9,1},... | collective-permute-start | bytes 442376 | tf_op jit(solution)/shard_map/ppermute | solution.py:269
  30.5 3.8 %collective-permute-done.3 = f32[4,72,128]{2,1,0:T(8,128)S(1)} collective-permute-done((f32[4,72,128]{2,1,0:T(8,128)S(1)}, f32[4,72,128]{2,1,0:T(8,128)S(1)}, u32[]{:S(2)}, u32[]{:S(2)}) %collective-permute-start.3) | collective-permute-done | bytes 147488 | tf_op jit(solution)/shard_map/ppermute | solution.py:269
  34.3 0.1 add_select_fusion.3
  34.4 1.5 %collective-permute-start.4 = (f32[4,72,128]{2,1,0:T(8,128)S(1)}, f32[4,72,128]{2,1,0:T(8,128)S(1)}, u32[]{:S(2)}, u32[]{:S(2)}) collective-permute-start(f32[4,72,128]{2,1,0:T(8,128)S(1)} %get-tuple-element.15), channel_id=1, source_target_pairs={{0,16},{1,17},{2,18},{3,19},{4,20},{5,21},{6,22},{7,23},{8,24},{9,... | collective-permute-start | bytes 442376 | tf_op jit(solution)/shard_map/ppermute | solution.py:269
  35.9 3.7 %collective-permute-done.4 = f32[4,72,128]{2,1,0:T(8,128)S(1)} collective-permute-done((f32[4,72,128]{2,1,0:T(8,128)S(1)}, f32[4,72,128]{2,1,0:T(8,128)S(1)}, u32[]{:S(2)}, u32[]{:S(2)}) %collective-permute-start.4) | collective-permute-done | bytes 147488 | tf_op jit(solution)/shard_map/ppermute | solution.py:269
  39.6 0.1 add_select_fusion
  39.7 0.1 collective-permute-start.5
  39.8 0.0 copy-done
  39.8 0.0 copy-done.1
  39.8 2.0 %multiply_convert_fusion.q_ref = bf16[384,1024]{1,0:T(8,128)(2,1)} fusion(bf16[384,1024]{1,0:T(8,128)(2,1)S(1)} %copy-done.1, bf16[1024,1024]{1,0:T(8,128)(2,1)S(1)} %copy-done), kind=kOutput, calls=%fused_computation | convolution fusion | flops 807272448 | bytes 3670016 | tf_op jit(solution)/shard_map/dot_general | solution.py:292
  41.8 4.8 %shard_map.74.rest_0_ = f32[384,1024]{1,0:T(8,128)} custom-call(bf16[384,1024]{1,0:T(8,128)(2,1)} %multiply_convert_fusion.q_ref, bf16[384,1024]{1,0:T(8,128)(2,1)} %get-tuple-element.10.k_ref, bf16[384,1024]{1,0:T(8,128)(2,1)} %get-tuple-element.11.v_ref, f32[384,16]{1,0:T(8,128)} %get-tuple-element.12.cum_ref, f32[16,384]{1,0:T(8,128)} %get-tuple-element.13.cum_t_ref), custom_call_target="tpu_custom_call" | custom-call | flops 603979776 | bytes 1966080 | tf_op jit(solution)/shard_map/pallas_call | solution.py:60
  46.6 3.1 %shard_map.75.rest_0_ = f32[384,1024]{1,0:T(8,128)} custom-call(bf16[384,1024]{1,0:T(8,128)(2,1)} %multiply_convert_fusion.q_ref, bf16[384,1024]{1,0:T(8,128)(2,1)} %get-tuple-element.10.k_ref, bf16[384,1024]{1,0:T(8,128)(2,1)} %get-tuple-element.11.v_ref, f32[384,16]{1,0:T(8,128)} %get-tuple-element.12.cum_ref, ...), custom_call_target="tpu_custom_call", output_to_operand_aliasing={{}: (5, {})} | custom-call | flops 301989888 | bytes 983040 | tf_op jit(solution)/shard_map/pallas_call | solution.py:60
  49.7 3.1 %shard_map.76.intra_ref = f32[384,1024]{1,0:T(8,128)} custom-call(bf16[384,1024]{1,0:T(8,128)(2,1)} %multiply_convert_fusion.q_ref, bf16[384,1024]{1,0:T(8,128)(2,1)} %get-tuple-element.10.k_ref, bf16[384,1024]{1,0:T(8,128)(2,1)} %get-tuple-element.11.v_ref, f32[384,16]{1,0:T(8,128)} %get-tuple-element.12.cum_ref, ...), custom_call_target="tpu_custom_call", output_to_operand_aliasing={{}: (5, {})} | custom-call | flops 301989888 | bytes 983040 | tf_op jit(solution)/shard_map/pallas_call | solution.py:60
  52.7 0.0 collective-permute-done.5
  52.7 0.8 %fusion.3.state_ref = f32[8,72,128]{2,1,0:T(8,128)} fusion(f32[8,72,128]{2,1,0:T(8,128)S(1)} %collective-permute-done, f32[4,72,128]{2,1,0:T(8,128)S(1)} %collective-permute-done.5, f32[4,72,128]{2,1,0:T(8,128)S(1)} %add_select_fusion, f32[8,128]{1,0:T(8,128)S(1)} %bitcast.15, pred[72]{0:T(512)(128)(4,1)S(1)} %iota_compare_fusion, pred[]{:T(512)S(6)} %eq.4), kind=kLoop, calls=%fused_computation.6 | loop fusion | flops 516096 | bytes 888905 | tf_op jit(solution)/shard_map/jit(_where)/select_n | solution.py:280
  53.6 6.1 %shard_map.77 = bf16[384,1024]{1,0:T(8,128)(2,1)} custom-call(bf16[384,1024]{1,0:T(8,128)(2,1)} %multiply_convert_fusion.q_ref, f32[384,1024]{1,0:T(8,128)} %shard_map.76.intra_ref, f32[8,72,128]{2,1,0:T(8,128)} %fusion.3.state_ref, f32[384,16]{1,0:T(8,128)} %get-tuple-element.12.cum_ref, f32[1,1024]{1,0:T(1,128)} %bitcast.26, bf16[1024,1024]{1,0:T(8,128)(2,1)} %w_ref.1), custom_call_target="tpu_custom_call" | custom-call | flops 1107296256 | bytes 5242880 | tf_op jit(solution)/shard_map/pallas_call | solution.py:225
  (11 shorter events, 0.1 us)
Async XLA Ops:
  0.0 39.8 %copy-start = (bf16[1024,1024]{1,0:T(8,128)(2,1)S(1)}, bf16[1024,1024]{1,0:T(8,128)(2,1)}, u32[]{:S(2)}) copy-start(bf16[1024,1024]{1,0:T(8,128)(2,1)} %param.9) | copy-start | bytes 6291460
  9.1 1.9 %collective-permute-start = (f32[8,72,128]{2,1,0:T(8,128)}, f32[8,72,128]{2,1,0:T(8,128)S(1)}, u32[]{:S(2)}, u32[]{:S(2)}) collective-permute-start(f32[8,72,128]{2,1,0:T(8,128)} %get-tuple-element.14), channel_id=1, source_target_pairs={{0,1},{1,0},{2,3},{3,2},{4,5},{5,4},{6,7},{7,6},{8,9},{9,8},{10,11... | collective-permute-start | bytes 884744 | tf_op jit(solution)/shard_map/ppermute | solution.py:261
  12.1 27.6 %copy-start.1 = (bf16[384,1024]{1,0:T(8,128)(2,1)S(1)}, bf16[384,1024]{1,0:T(8,128)(2,1)}, u32[]{:S(2)}) copy-start(bf16[384,1024]{1,0:T(8,128)(2,1)} %x_ref.1) | copy-start | bytes 2359300
  12.2 7.1 %collective-permute-start.1 = (f32[4,72,128]{2,1,0:T(8,128)S(1)}, f32[4,72,128]{2,1,0:T(8,128)S(1)}, u32[]{:S(2)}, u32[]{:S(2)}) collective-permute-start(f32[4,72,128]{2,1,0:T(8,128)S(1)} %slice_select_fusion), channel_id=1, source_target_pairs={{0,2},{1,3},{2,0},{3,1},{4,6},{5,7},{6,4},{7,5},{8,10},{9,11},{10,... | collective-permute-start | bytes 442376 | tf_op jit(solution)/shard_map/ppermute | solution.py:269
  19.4 9.4 %collective-permute-start.2 = (f32[4,72,128]{2,1,0:T(8,128)S(1)}, f32[4,72,128]{2,1,0:T(8,128)S(1)}, u32[]{:S(2)}, u32[]{:S(2)}) collective-permute-start(f32[4,72,128]{2,1,0:T(8,128)S(1)} %get-tuple-element.19), channel_id=1, source_target_pairs={{0,4},{1,5},{2,6},{3,7},{4,0},{5,1},{6,2},{7,3},{8,12},{9,13},{10,... | collective-permute-start | bytes 442376 | tf_op jit(solution)/shard_map/ppermute | solution.py:269
  29.0 5.2 %collective-permute-start.3 = (f32[4,72,128]{2,1,0:T(8,128)S(1)}, f32[4,72,128]{2,1,0:T(8,128)S(1)}, u32[]{:S(2)}, u32[]{:S(2)}) collective-permute-start(f32[4,72,128]{2,1,0:T(8,128)S(1)} %get-tuple-element.17), channel_id=1, source_target_pairs={{0,8},{1,9},{2,10},{3,11},{4,12},{5,13},{6,14},{7,15},{8,0},{9,1},... | collective-permute-start | bytes 442376 | tf_op jit(solution)/shard_map/ppermute | solution.py:269
  34.4 5.2 %collective-permute-start.4 = (f32[4,72,128]{2,1,0:T(8,128)S(1)}, f32[4,72,128]{2,1,0:T(8,128)S(1)}, u32[]{:S(2)}, u32[]{:S(2)}) collective-permute-start(f32[4,72,128]{2,1,0:T(8,128)S(1)} %get-tuple-element.15), channel_id=1, source_target_pairs={{0,16},{1,17},{2,18},{3,19},{4,20},{5,21},{6,22},{7,23},{8,24},{9,... | collective-permute-start | bytes 442376 | tf_op jit(solution)/shard_map/ppermute | solution.py:269
  39.7 13.0 %collective-permute-start.5 = (f32[4,72,128]{2,1,0:T(8,128)S(1)}, f32[4,72,128]{2,1,0:T(8,128)S(1)}, u32[]{:S(2)}, u32[]{:S(2)}) collective-permute-start(f32[4,72,128]{2,1,0:T(8,128)S(1)} %add_select_fusion), channel_id=1, source_target_pairs={{0,1},{1,0},{2,3},{3,2},{4,5},{5,4},{6,7},{7,6},{8,9},{9,8},{10,11... | collective-permute-start | bytes 442376 | tf_op jit(solution)/shard_map/ppermute | solution.py:276

commit v13 on v12

--- a/solution.py
+++ b/solution.py
@@ -106,21 +106,25 @@
 def project_kernel(x_ref, wk_ref, wv_ref, g_ref, k_ref, v_ref, o_ref, cum_ref, cum_t_ref, *, head_dim):
     f32 = jnp.float32
     bf16 = jnp.bfloat16
-    rows = g_ref.shape[0]
-    t_i = lax.broadcasted_iota(jnp.int32, (rows, rows), 0)
-    s_i = lax.broadcasted_iota(jnp.int32, (rows, rows), 1)
-    lower = jnp.where(s_i <= t_i, 1.0, 0.0).astype(bf16)
-    upper = jnp.where(t_i <= s_i, 1.0, 0.0).astype(bf16)
-    rest = g_ref[...]
-    cum = jnp.zeros(cum_ref.shape, f32)
-    cum_t = jnp.zeros(cum_t_ref.shape, f32)
-    for _ in range(3):
-        part = rest.astype(bf16)
-        cum = cum + jnp.dot(lower, part, preferred_element_type=f32)
-        cum_t = cum_t + lax.dot_general(part, upper, (((0,), (0,)), ((), ())), preferred_element_type=f32)
-        rest = rest - part.astype(f32)
-    cum_ref[...] = cum
-    cum_t_ref[...] = cum_t
+
+    @pl.when(pl.program_id(0) == 0)
+    def _():
+        rows = g_ref.shape[1]
+        t_i = lax.broadcasted_iota(jnp.int32, (rows, rows), 0)
+        s_i = lax.broadcasted_iota(jnp.int32, (rows, rows), 1)
+        lower = jnp.where(s_i <= t_i, 1.0, 0.0).astype(bf16)
+        upper = jnp.where(t_i <= s_i, 1.0, 0.0).astype(bf16)
+        rest = g_ref[...]
+        cum = jnp.zeros(cum_ref.shape, f32)
+        cum_t = jnp.zeros(cum_t_ref.shape, f32)
+        for _ in range(3):
+            part = rest.astype(bf16)
+            cum = cum + lax.dot_general(lower, part, (((1,), (1,)), ((), ())), preferred_element_type=f32)
+            cum_t = cum_t + jnp.dot(part, upper, preferred_element_type=f32)
+            rest = rest - part.astype(f32)
+        cum_ref[...] = cum
+        cum_t_ref[...] = cum_t
+
     x = x_ref[...]
     key_sum = jnp.dot(x, wk_ref[...], preferred_element_type=f32)
     k_ref[...] = (key_sum / (1.0 + jnp.exp(-key_sum))).astype(jnp.bfloat16)
@@ -140,7 +144,12 @@
     return pl.pallas_call(
         functools.partial(project_kernel, head_dim=head_dim),
         grid=(pairs // per,),
-        in_specs=[pl.BlockSpec((rows, depth), lambda p: (0, 0)), weights, weights, pl.BlockSpec((rows, heads), lambda p: (0, 0))],
+        in_specs=[
+            pl.BlockSpec((rows, depth), lambda p: (0, 0)),
+            weights,
+            weights,
+            pl.BlockSpec((heads, rows), lambda p: (0, 0)),
+        ],
         out_specs=[
             block,
             block,
@@ -160,7 +169,7 @@
             transcendentals=rows * width + rows * heads,
             bytes_accessed=2 * depth * width * 2 + rows * depth * 2 + rows * width * 4,
         ),
-    )(tokens, key_weight, value_weight, log_decay)
+    )(tokens, key_weight, value_weight, log_decay.T)
 
 
 def finish_kernel(q_ref, intra_ref, state_ref, cum_ref, gain_ref, w_ref, o_ref, normed_ref, acc_ref, *, head_dim):

time: 60.1 us -> 57.8 us (0.962)
  local copies, waits for them, and re-layouts: 2.55 us -> 0.85 us
    unnamed x5 -> x4, local copies, waits for them, and re-layouts: 1.71 us -> 0.01 us
    pallas_call x1, Pallas kernels: 7.4 us -> 6.73 us  [project_keys_values(): pl.pallas_call(functools.partial(project_kernel, head_dim=head_dim), grid...]
  transfers between devices with their start and end apart: 6 -> 6, of which waited for: 5 -> 5; matrix products, arithmetic and copies ran while one was open for 5% -> 5% of each run, Pallas kernels for 18% -> 19%
where the time goes in v13:
time: 57.8 us; the launch traced here: 57.3 us
  Pallas kernels  23.8 us (41%)
  waiting for transfers between devices  18.9 us (33%)
  starting transfers between devices  9.28 us (16%)
  other arithmetic  2.41 us (4%)
  matrix products  2.03 us (4%)
  local copies, waits for them, and re-layouts  0.85 us (1%)
    ppermute x4, waiting for transfers between devices, exclusive_scan(): got = lax.ppermute(through, AXES, perm)  18.2 us
    pallas_call x3, Pallas kernels, intra_attention(): pl.pallas_call(functools.partial(intra_kernel, head_dim=head_dim, first=f...  10.9 us
    ppermute x4, starting transfers between devices, exclusive_scan(): got = lax.ppermute(through, AXES, perm)  8.72 us
    pallas_call x1, Pallas kernels, project_keys_values(): pl.pallas_call(functools.partial(project_kernel, head_dim=head_dim), grid...  6.73 us
    pallas_call x1, Pallas kernels, finish(): pl.pallas_call(functools.partial(finish_kernel, head_dim=head_dim), grid=...  6.15 us
    dot_general x1, matrix products, layer(): jnp.dot(tokens, query_weight, preferred_element_type=f32)  2.03 us
  transfers between devices with their start and end apart: 6, of which 5 were waited for; matrix products, arithmetic and copies ran while one was open for 5% of the time, Pallas kernels for 19%

profile of v13, /device:TPU:0, one launch (start us, length us, event | category | flops | bytes accessed | tf_op | source)
XLA Modules:
  0.0 57.3 jit_solution(2954562299196565566)
XLA Ops:
  0.0 0.0 copy-start
  0.0 6.7 %shard_map.73 = (bf16[384,1024]{1,0:T(8,128)(2,1)}, bf16[384,1024]{1,0:T(8,128)(2,1)}, f32[8,72,128]{2,1,0:T(8,128)}, f32[384,16]{1,0:T(8,128)}, f32[16,384]{1,0:T(8,128)}) custom-call(bf16[384,1024]{1,0:T(8,128)(2,1)} %x_ref.1, bf16[1024,1024]{1,0:T(8,128)(2,1)} %wk_ref.1, bf16[1024,1024]{1,0:T(8,128)(2,1)} %wv_ref.1, f32[16,384]{1,0:T(8,128)} %bitcast.28), custom_call_target="tpu_custom_call" | custom-call | flops 1711276032 | bytes 6553600 | tf_op jit(solution)/shard_map/pallas_call | solution.py:144
  6.7 0.5 collective-permute-start
  7.2 0.8 %slice_exponential_fusion.1 = f32[8,1,128]{2,1,0:T(1,128)S(1)} fusion(f32[8,72,128]{2,1,0:T(8,128)} %get-tuple-element.14), kind=kLoop, calls=%fused_computation.17 | loop fusion | bytes 8192 | tf_op jit(solution)/shard_map/exp | solution.py:259
  8.0 0.6 %collective-permute-done = f32[8,72,128]{2,1,0:T(8,128)S(1)} collective-permute-done((f32[8,72,128]{2,1,0:T(8,128)}, f32[8,72,128]{2,1,0:T(8,128)S(1)}, u32[]{:S(2)}, u32[]{:S(2)}) %collective-permute-start) | collective-permute-done | bytes 294944 | tf_op jit(solution)/shard_map/ppermute | solution.py:270
  8.7 1.1 %fusion.1 = f32[8,72,128]{2,1,0:T(8,128)S(1)} fusion(f32[8,72,128]{2,1,0:T(8,128)S(1)} %collective-permute-done, f32[8,72,128]{2,1,0:T(8,128)} %get-tuple-element.14, f32[8,128]{1,0:T(8,128)S(1)} %bitcast.17, f32[8,128]{1,0:T(8,128)S(1)} %bitcast.15, pred[72]{0:T(512)(128)(4,1)S(1)} %iota_compare_fusion, pred[]{:T(512)S(6)} %eq.4), kind=kLoop, calls=%fused_computation.4 | loop fusion | flops 516096 | bytes 893001 | tf_op jit(solution)/shard_map/jit(_where)/select_n | solution.py:271
  9.8 0.0 copy-start.1
  9.8 3.0 %collective-permute-start.1 = (f32[4,72,128]{2,1,0:T(8,128)S(1)}, f32[4,72,128]{2,1,0:T(8,128)S(1)}, u32[]{:S(2)}, u32[]{:S(2)}) collective-permute-start(f32[4,72,128]{2,1,0:T(8,128)S(1)} %slice_select_fusion), channel_id=1, source_target_pairs={{0,2},{1,3},{2,0},{3,1},{4,6},{5,7},{6,4},{7,5},{8,10},{9,11},{10,... | collective-permute-start | bytes 442376 | tf_op jit(solution)/shard_map/ppermute | solution.py:278
  12.8 4.1 %collective-permute-done.1 = f32[4,72,128]{2,1,0:T(8,128)S(1)} collective-permute-done((f32[4,72,128]{2,1,0:T(8,128)S(1)}, f32[4,72,128]{2,1,0:T(8,128)S(1)}, u32[]{:S(2)}, u32[]{:S(2)}) %collective-permute-start.1) | collective-permute-done | bytes 147488 | tf_op jit(solution)/shard_map/ppermute | solution.py:278
  17.0 0.1 add_select_fusion.5
  17.1 2.8 %collective-permute-start.2 = (f32[4,72,128]{2,1,0:T(8,128)S(1)}, f32[4,72,128]{2,1,0:T(8,128)S(1)}, u32[]{:S(2)}, u32[]{:S(2)}) collective-permute-start(f32[4,72,128]{2,1,0:T(8,128)S(1)} %get-tuple-element.19), channel_id=1, source_target_pairs={{0,4},{1,5},{2,6},{3,7},{4,0},{5,1},{6,2},{7,3},{8,12},{9,13},{10,... | collective-permute-start | bytes 442376 | tf_op jit(solution)/shard_map/ppermute | solution.py:278
  19.9 6.6 %collective-permute-done.2 = f32[4,72,128]{2,1,0:T(8,128)S(1)} collective-permute-done((f32[4,72,128]{2,1,0:T(8,128)S(1)}, f32[4,72,128]{2,1,0:T(8,128)S(1)}, u32[]{:S(2)}, u32[]{:S(2)}) %collective-permute-start.2) | collective-permute-done | bytes 147488 | tf_op jit(solution)/shard_map/ppermute | solution.py:278
  26.5 0.1 add_select_fusion.4
  26.7 1.4 %collective-permute-start.3 = (f32[4,72,128]{2,1,0:T(8,128)S(1)}, f32[4,72,128]{2,1,0:T(8,128)S(1)}, u32[]{:S(2)}, u32[]{:S(2)}) collective-permute-start(f32[4,72,128]{2,1,0:T(8,128)S(1)} %get-tuple-element.17), channel_id=1, source_target_pairs={{0,8},{1,9},{2,10},{3,11},{4,12},{5,13},{6,14},{7,15},{8,0},{9,1},... | collective-permute-start | bytes 442376 | tf_op jit(solution)/shard_map/ppermute | solution.py:278
  28.1 3.8 %collective-permute-done.3 = f32[4,72,128]{2,1,0:T(8,128)S(1)} collective-permute-done((f32[4,72,128]{2,1,0:T(8,128)S(1)}, f32[4,72,128]{2,1,0:T(8,128)S(1)}, u32[]{:S(2)}, u32[]{:S(2)}) %collective-permute-start.3) | collective-permute-done | bytes 147488 | tf_op jit(solution)/shard_map/ppermute | solution.py:278
  31.9 0.1 add_select_fusion.3
  32.0 1.5 %collective-permute-start.4 = (f32[4,72,128]{2,1,0:T(8,128)S(1)}, f32[4,72,128]{2,1,0:T(8,128)S(1)}, u32[]{:S(2)}, u32[]{:S(2)}) collective-permute-start(f32[4,72,128]{2,1,0:T(8,128)S(1)} %get-tuple-element.15), channel_id=1, source_target_pairs={{0,16},{1,17},{2,18},{3,19},{4,20},{5,21},{6,22},{7,23},{8,24},{9,... | collective-permute-start | bytes 442376 | tf_op jit(solution)/shard_map/ppermute | solution.py:278
  33.5 3.7 %collective-permute-done.4 = f32[4,72,128]{2,1,0:T(8,128)S(1)} collective-permute-done((f32[4,72,128]{2,1,0:T(8,128)S(1)}, f32[4,72,128]{2,1,0:T(8,128)S(1)}, u32[]{:S(2)}, u32[]{:S(2)}) %collective-permute-start.4) | collective-permute-done | bytes 147488 | tf_op jit(solution)/shard_map/ppermute | solution.py:278
  37.2 0.1 add_select_fusion
  37.3 0.1 collective-permute-start.5
  37.4 0.0 copy-done
  37.4 0.0 copy-done.1
  37.4 2.0 %multiply_convert_fusion.q_ref = bf16[384,1024]{1,0:T(8,128)(2,1)} fusion(bf16[384,1024]{1,0:T(8,128)(2,1)S(1)} %copy-done.1, bf16[1024,1024]{1,0:T(8,128)(2,1)S(1)} %copy-done), kind=kOutput, calls=%fused_computation | convolution fusion | flops 807272448 | bytes 3670016 | tf_op jit(solution)/shard_map/dot_general | solution.py:301
  39.5 4.8 %shard_map.74.rest_0_ = f32[384,1024]{1,0:T(8,128)} custom-call(bf16[384,1024]{1,0:T(8,128)(2,1)} %multiply_convert_fusion.q_ref, bf16[384,1024]{1,0:T(8,128)(2,1)} %get-tuple-element.10.k_ref, bf16[384,1024]{1,0:T(8,128)(2,1)} %get-tuple-element.11.v_ref, f32[384,16]{1,0:T(8,128)} %get-tuple-element.12.cum_ref, f32[16,384]{1,0:T(8,128)} %get-tuple-element.13.cum_t_ref), custom_call_target="tpu_custom_call" | custom-call | flops 603979776 | bytes 1966080 | tf_op jit(solution)/shard_map/pallas_call | solution.py:60
  44.2 3.1 %shard_map.75.rest_0_ = f32[384,1024]{1,0:T(8,128)} custom-call(bf16[384,1024]{1,0:T(8,128)(2,1)} %multiply_convert_fusion.q_ref, bf16[384,1024]{1,0:T(8,128)(2,1)} %get-tuple-element.10.k_ref, bf16[384,1024]{1,0:T(8,128)(2,1)} %get-tuple-element.11.v_ref, f32[384,16]{1,0:T(8,128)} %get-tuple-element.12.cum_ref, ...), custom_call_target="tpu_custom_call", output_to_operand_aliasing={{}: (5, {})} | custom-call | flops 301989888 | bytes 983040 | tf_op jit(solution)/shard_map/pallas_call | solution.py:60
  47.3 3.1 %shard_map.76.intra_ref = f32[384,1024]{1,0:T(8,128)} custom-call(bf16[384,1024]{1,0:T(8,128)(2,1)} %multiply_convert_fusion.q_ref, bf16[384,1024]{1,0:T(8,128)(2,1)} %get-tuple-element.10.k_ref, bf16[384,1024]{1,0:T(8,128)(2,1)} %get-tuple-element.11.v_ref, f32[384,16]{1,0:T(8,128)} %get-tuple-element.12.cum_ref, ...), custom_call_target="tpu_custom_call", output_to_operand_aliasing={{}: (5, {})} | custom-call | flops 301989888 | bytes 983040 | tf_op jit(solution)/shard_map/pallas_call | solution.py:60
  50.4 0.0 collective-permute-done.5
  50.4 0.8 %fusion.3.state_ref = f32[8,72,128]{2,1,0:T(8,128)} fusion(f32[8,72,128]{2,1,0:T(8,128)S(1)} %collective-permute-done, f32[4,72,128]{2,1,0:T(8,128)S(1)} %collective-permute-done.5, f32[4,72,128]{2,1,0:T(8,128)S(1)} %add_select_fusion, f32[8,128]{1,0:T(8,128)S(1)} %bitcast.16, pred[72]{0:T(512)(128)(4,1)S(1)} %iota_compare_fusion, pred[]{:T(512)S(6)} %eq.4), kind=kLoop, calls=%fused_computation.6 | loop fusion | flops 516096 | bytes 888905 | tf_op jit(solution)/shard_map/jit(_where)/select_n | solution.py:289
  51.2 6.1 %shard_map.77 = bf16[384,1024]{1,0:T(8,128)(2,1)} custom-call(bf16[384,1024]{1,0:T(8,128)(2,1)} %multiply_convert_fusion.q_ref, f32[384,1024]{1,0:T(8,128)} %shard_map.76.intra_ref, f32[8,72,128]{2,1,0:T(8,128)} %fusion.3.state_ref, f32[384,16]{1,0:T(8,128)} %get-tuple-element.12.cum_ref, f32[1,1024]{1,0:T(1,128)} %bitcast.27, bf16[1024,1024]{1,0:T(8,128)(2,1)} %w_ref.1), custom_call_target="tpu_custom_call" | custom-call | flops 1107296256 | bytes 5242880 | tf_op jit(solution)/shard_map/pallas_call | solution.py:234
  (11 shorter events, 0.1 us)
Async XLA Ops:
  0.0 37.4 %copy-start = (bf16[1024,1024]{1,0:T(8,128)(2,1)S(1)}, bf16[1024,1024]{1,0:T(8,128)(2,1)}, u32[]{:S(2)}) copy-start(bf16[1024,1024]{1,0:T(8,128)(2,1)} %param.9) | copy-start | bytes 6291460
  6.7 1.9 %collective-permute-start = (f32[8,72,128]{2,1,0:T(8,128)}, f32[8,72,128]{2,1,0:T(8,128)S(1)}, u32[]{:S(2)}, u32[]{:S(2)}) collective-permute-start(f32[8,72,128]{2,1,0:T(8,128)} %get-tuple-element.14), channel_id=1, source_target_pairs={{0,1},{1,0},{2,3},{3,2},{4,5},{5,4},{6,7},{7,6},{8,9},{9,8},{10,11... | collective-permute-start | bytes 884744 | tf_op jit(solution)/shard_map/ppermute | solution.py:270
  9.8 27.6 %copy-start.1 = (bf16[384,1024]{1,0:T(8,128)(2,1)S(1)}, bf16[384,1024]{1,0:T(8,128)(2,1)}, u32[]{:S(2)}) copy-start(bf16[384,1024]{1,0:T(8,128)(2,1)} %x_ref.1) | copy-start | bytes 2359300
  9.8 7.1 %collective-permute-start.1 = (f32[4,72,128]{2,1,0:T(8,128)S(1)}, f32[4,72,128]{2,1,0:T(8,128)S(1)}, u32[]{:S(2)}, u32[]{:S(2)}) collective-permute-start(f32[4,72,128]{2,1,0:T(8,128)S(1)} %slice_select_fusion), channel_id=1, source_target_pairs={{0,2},{1,3},{2,0},{3,1},{4,6},{5,7},{6,4},{7,5},{8,10},{9,11},{10,... | collective-permute-start | bytes 442376 | tf_op jit(solution)/shard_map/ppermute | solution.py:278
  17.1 9.4 %collective-permute-start.2 = (f32[4,72,128]{2,1,0:T(8,128)S(1)}, f32[4,72,128]{2,1,0:T(8,128)S(1)}, u32[]{:S(2)}, u32[]{:S(2)}) collective-permute-start(f32[4,72,128]{2,1,0:T(8,128)S(1)} %get-tuple-element.19), channel_id=1, source_target_pairs={{0,4},{1,5},{2,6},{3,7},{4,0},{5,1},{6,2},{7,3},{8,12},{9,13},{10,... | collective-permute-start | bytes 442376 | tf_op jit(solution)/shard_map/ppermute | solution.py:278
  26.7 5.2 %collective-permute-start.3 = (f32[4,72,128]{2,1,0:T(8,128)S(1)}, f32[4,72,128]{2,1,0:T(8,128)S(1)}, u32[]{:S(2)}, u32[]{:S(2)}) collective-permute-start(f32[4,72,128]{2,1,0:T(8,128)S(1)} %get-tuple-element.17), channel_id=1, source_target_pairs={{0,8},{1,9},{2,10},{3,11},{4,12},{5,13},{6,14},{7,15},{8,0},{9,1},... | collective-permute-start | bytes 442376 | tf_op jit(solution)/shard_map/ppermute | solution.py:278
  32.0 5.2 %collective-permute-start.4 = (f32[4,72,128]{2,1,0:T(8,128)S(1)}, f32[4,72,128]{2,1,0:T(8,128)S(1)}, u32[]{:S(2)}, u32[]{:S(2)}) collective-permute-start(f32[4,72,128]{2,1,0:T(8,128)S(1)} %get-tuple-element.15), channel_id=1, source_target_pairs={{0,16},{1,17},{2,18},{3,19},{4,20},{5,21},{6,22},{7,23},{8,24},{9,... | collective-permute-start | bytes 442376 | tf_op jit(solution)/shard_map/ppermute | solution.py:278
  37.3 13.0 %collective-permute-start.5 = (f32[4,72,128]{2,1,0:T(8,128)S(1)}, f32[4,72,128]{2,1,0:T(8,128)S(1)}, u32[]{:S(2)}, u32[]{:S(2)}) collective-permute-start(f32[4,72,128]{2,1,0:T(8,128)S(1)} %add_select_fusion), channel_id=1, source_target_pairs={{0,1},{1,0},{2,3},{3,2},{4,5},{5,4},{6,7},{7,6},{8,9},{9,8},{10,11... | collective-permute-start | bytes 442376 | tf_op jit(solution)/shard_map/ppermute | solution.py:285

commit v14 on v13

--- a/solution.py
+++ b/solution.py
@@ -77,9 +77,10 @@
     return jnp.sum(jnp.where(lane == head, table, 0.0), axis=1, keepdims=True)
 
 
-def local_pair(k_ref, v_ref, cum_ref, o_ref, head_dim, step):
-    f32 = jnp.float32
-    pair = pl.program_id(0) * o_ref.shape[0] + step
+def local_pair(k_ref, v_ref, cum_ref, o_ref, head_dim, step, pair=None):
+    f32 = jnp.float32
+    if pair is None:
+        pair = pl.program_id(0) * o_ref.shape[0] + step
     cols = pl.ds(step * LANES, LANES)
     group = LANES // head_dim
     rows = k_ref.shape[0]
@@ -103,11 +104,15 @@
     o_ref[step, head_dim:, :] = jnp.where(tail_row == 0, jnp.broadcast_to(logs, (8, LANES)), 0.0)
 
 
-def project_kernel(x_ref, wk_ref, wv_ref, g_ref, k_ref, v_ref, o_ref, cum_ref, cum_t_ref, *, head_dim):
+def project_kernel(
+    core_ref, x_ref, wk_ref, wv_ref, g_ref, k_ref, v_ref, send_ref, keep_ref, cum_ref, cum_t_ref, *, head_dim
+):
     f32 = jnp.float32
     bf16 = jnp.bfloat16
-
-    @pl.when(pl.program_id(0) == 0)
+    index = pl.program_id(0)
+    half = (index + 1 + core_ref[0]) % 2
+
+    @pl.when(index == 0)
     def _():
         rows = g_ref.shape[1]
         t_i = lax.broadcasted_iota(jnp.int32, (rows, rows), 0)
@@ -129,38 +134,50 @@
     key_sum = jnp.dot(x, wk_ref[...], preferred_element_type=f32)
     k_ref[...] = (key_sum / (1.0 + jnp.exp(-key_sum))).astype(jnp.bfloat16)
     v_ref[...] = jnp.dot(x, wv_ref[...], preferred_element_type=f32).astype(jnp.bfloat16)
-    for step in range(o_ref.shape[0]):
-        local_pair(k_ref, v_ref, cum_ref, o_ref, head_dim, step)
-
-
-def project_keys_values(tokens, key_weight, value_weight, log_decay, head_dim):
+    per = send_ref.shape[0]
+
+    @pl.when(index == 0)
+    def _():
+        for step in range(per):
+            local_pair(k_ref, v_ref, cum_ref, send_ref, head_dim, step, half * per + step)
+
+    @pl.when(index == 1)
+    def _():
+        for step in range(per):
+            local_pair(k_ref, v_ref, cum_ref, keep_ref, head_dim, step, half * per + step)
+
+
+def project_keys_values(tokens, key_weight, value_weight, log_decay, head_dim, core):
     rows, depth = tokens.shape
     width = key_weight.shape[1]
     heads = log_decay.shape[1]
     pairs = width // LANES
-    per = 2 if pairs % 2 == 0 else 1
-    block = pl.BlockSpec((rows, per * LANES), lambda p: (0, p))
-    weights = pl.BlockSpec((depth, per * LANES), lambda p: (0, p))
+    per = pairs // 2
+    columns = lambda p, core_ref: (0, (p + 1 + core_ref[0]) % 2)
+    whole = lambda shape: pl.BlockSpec(shape, lambda p, core_ref: (0,) * len(shape))
+    block = pl.BlockSpec((rows, per * LANES), columns)
+    weights = pl.BlockSpec((depth, per * LANES), columns)
+    half = jax.ShapeDtypeStruct((per, head_dim + 8, LANES), jnp.float32)
     return pl.pallas_call(
         functools.partial(project_kernel, head_dim=head_dim),
-        grid=(pairs // per,),
-        in_specs=[
-            pl.BlockSpec((rows, depth), lambda p: (0, 0)),
-            weights,
-            weights,
-            pl.BlockSpec((heads, rows), lambda p: (0, 0)),
-        ],
-        out_specs=[
-            block,
-            block,
-            pl.BlockSpec((per, head_dim + 8, LANES), lambda p: (p, 0, 0)),
-            pl.BlockSpec((rows, heads), lambda p: (0, 0)),
-            pl.BlockSpec((heads, rows), lambda p: (0, 0)),
-        ],
+        grid_spec=pltpu.PrefetchScalarGridSpec(
+            num_scalar_prefetch=1,
+            grid=(2,),
+            in_specs=[whole((rows, depth)), weights, weights, whole((heads, rows))],
+            out_specs=[
+                block,
+                block,
+                whole((per, head_dim + 8, LANES)),
+                whole((per, head_dim + 8, LANES)),
+                whole((rows, heads)),
+                whole((heads, rows)),
+            ],
+        ),
         out_shape=[
             jax.ShapeDtypeStruct((rows, width), jnp.bfloat16),
             jax.ShapeDtypeStruct((rows, width), jnp.bfloat16),
-            jax.ShapeDtypeStruct((pairs, head_dim + 8, LANES), jnp.float32),
+            half,
+            half,
             jax.ShapeDtypeStruct((rows, heads), jnp.float32),
             jax.ShapeDtypeStruct((heads, rows), jnp.float32),
         ],
@@ -169,7 +186,7 @@
             transcendentals=rows * width + rows * heads,
             bytes_accessed=2 * depth * width * 2 + rows * depth * 2 + rows * width * 4,
         ),
-    )(tokens, key_weight, value_weight, log_decay.T)
+    )(jnp.reshape(core, (1,)).astype(jnp.int32), tokens, key_weight, value_weight, log_decay.T)
 
 
 def finish_kernel(q_ref, intra_ref, state_ref, cum_ref, gain_ref, w_ref, o_ref, normed_ref, acc_ref, *, head_dim):
@@ -260,33 +277,30 @@
     return scale * earlier + later
 
 
-def exclusive_scan(own, count):
+def exclusive_scan(send, keep, count):
     flat = lax.axis_index(AXES)
     core = flat % 2
     chip = flat // 2
     chips = count // 2
-    half = own.shape[0] // 2
     partner = [(i, i ^ 1) for i in range(count)]
-    other = lax.ppermute(own, AXES, partner)
-    pooled = jnp.where(core == 0, combine(own, other), combine(other, own))
-    through = jnp.where(core == 0, pooled[:half], pooled[half:])
+    got = lax.ppermute(send, AXES, partner)
+    through = jnp.where(core == 0, combine(keep, got), combine(got, keep))
     before = jnp.zeros_like(through)
     received = []
     bit = 1
     while bit < chips:
         perm = [(i, i ^ (2 * bit)) for i in range(count)]
-        got = lax.ppermute(through, AXES, perm)
-        received.append(got)
+        exchanged = lax.ppermute(through, AXES, perm)
+        received.append(exchanged)
         lower = (chip & bit) != 0
-        before = jnp.where(lower, combine(got, before), before)
+        before = jnp.where(lower, combine(exchanged, before), before)
         bit *= 2
         if bit < chips:
-            through = jnp.where(lower, combine(got, through), combine(through, got))
-    swapped = lax.ppermute(before, AXES, partner)
+            through = jnp.where(lower, combine(exchanged, through), combine(through, exchanged))
+    back = lax.ppermute(jnp.where(core == 0, combine(before, keep), before), AXES, partner)
     whole = jnp.where(
-        core == 0, jnp.concatenate([before, swapped]), jnp.concatenate([swapped, before])
+        core == 0, jnp.concatenate([before, back]), jnp.concatenate([back, combine(before, got)])
     )
-    whole = jnp.where(core == 0, whole, combine(whole, other))
     return whole, received
 
 
@@ -295,8 +309,11 @@
     bf16 = jnp.bfloat16
     heads = log_decay.shape[1]
     dim = key_weight.shape[1] // heads
-    keys, value_rows, packed, cum, cum_t = project_keys_values(tokens, key_weight, value_weight, log_decay, dim)
-    incoming, _ = exclusive_scan(packed, count)
+    core = lax.axis_index(AXES) % 2
+    keys, value_rows, send, keep, cum, cum_t = project_keys_values(
+        tokens, key_weight, value_weight, log_decay, dim, core
+    )
+    incoming, _ = exclusive_scan(send, keep, count)
 
     queries = jax.nn.silu(jnp.dot(tokens, query_weight, preferred_element_type=f32)).astype(bf16)
     blocks = keys.shape[1] // LANES

time: 57.8 us -> 58.1 us (level)
    select_n x7 -> x6, other arithmetic: 2.4 us -> 2.29 us  [the longest x1 1.08 us: exclusive_scan(): through = jnp.where(core == 0, combine(keep, got), combine(got, keep))]
where the time goes in v14:
time: 58.1 us; the launch traced here: 57.8 us
  Pallas kernels  24.3 us (42%)
  waiting for transfers between devices  18.8 us (32%)
  starting transfers between devices  9.34 us (16%)
  other arithmetic  2.41 us (4%)
  matrix products  2.05 us (4%)
  local copies, waits for them, and re-layouts  0.8 us (1%)
    ppermute x4, waiting for transfers between devices, exclusive_scan(): exchanged = lax.ppermute(through, AXES, perm)  18.3 us
    pallas_call x3, Pallas kernels, intra_attention(): pl.pallas_call(functools.partial(intra_kernel, head_dim=head_dim, first=f...  10.9 us
    ppermute x4, starting transfers between devices, exclusive_scan(): exchanged = lax.ppermute(through, AXES, perm)  8.71 us
    pallas_call x1, Pallas kernels, project_keys_values(): pl.pallas_call(functools.partial(project_kernel, head_dim=head_dim), grid...  7.28 us
    pallas_call x1, Pallas kernels, finish(): pl.pallas_call(functools.partial(finish_kernel, head_dim=head_dim), grid=...  6.14 us
    dot_general x1, matrix products, layer(): jnp.dot(tokens, query_weight, preferred_element_type=f32)  2.05 us
  transfers between devices with their start and end apart: 6, of which 5 were waited for; matrix products, arithmetic and copies ran while one was open for 5% of the time, Pallas kernels for 19%

profile of v14, /device:TPU:0, one launch (start us, length us, event | category | flops | bytes accessed | tf_op | source)
XLA Modules:
  0.0 57.8 jit_solution(3056613916042822941)
XLA Ops:
  0.0 0.0 copy-start
  0.0 7.3 %shard_map.73 = (bf16[384,1024]{1,0:T(8,128)(2,1)}, bf16[384,1024]{1,0:T(8,128)(2,1)}, f32[4,72,128]{2,1,0:T(8,128)}, f32[4,72,128]{2,1,0:T(8,128)}, f32[384,16]{1,0:T(8,128)}, /*index=5*/f32[16,384]{1,0:T(8,128)}) custom-call(s32[1]{0:T(128)} %bitcast.core_ref, bf16[384,1024]{1,0:T(8,128)(2,1)} %x_ref.1, bf16[1024,1024]{1,0:T(8,128)(2,1)} %wk_ref.1, ...), custom_call_target="tpu_custom_call" | custom-call | flops 1711276032 | bytes 6553600 | tf_op jit(solution)/shard_map/pallas_call | solution.py:161
  7.3 0.6 collective-permute-start
  7.8 0.7 %slice_exponential_fusion.10 = f32[4,1,128]{2,1,0:T(1,128)S(1)} fusion(f32[4,72,128]{2,1,0:T(8,128)} %get-tuple-element.16), kind=kLoop, calls=%fused_computation.29 | loop fusion | bytes 4096 | tf_op jit(solution)/shard_map/exp | solution.py:276
  8.6 0.5 collective-permute-done
  9.1 0.0 copy-start.1
  9.1 1.1 %fusion.1 = f32[4,72,128]{2,1,0:T(8,128)S(1)} fusion(f32[4,72,128]{2,1,0:T(8,128)S(1)} %collective-permute-done, f32[4,72,128]{2,1,0:T(8,128)} %get-tuple-element.16, f32[4,128]{1,0:T(4,128)S(1)} %bitcast.16, f32[4,128]{1,0:T(4,128)S(1)} %bitcast.18, pred[72]{0:T(512)(128)(4,1)S(1)} %iota_compare_fusion, pred[]{:T(512)S(6)} %eq.8), kind=kLoop, calls=%fused_computation.10 | loop fusion | flops 258048 | bytes 446537 | tf_op jit(solution)/shard_map/jit(_where)/select_n | solution.py:287
  10.2 3.0 %collective-permute-start.1 = (f32[4,72,128]{2,1,0:T(8,128)S(1)}, f32[4,72,128]{2,1,0:T(8,128)S(1)}, u32[]{:S(2)}, u32[]{:S(2)}) collective-permute-start(f32[4,72,128]{2,1,0:T(8,128)S(1)} %fusion.1), channel_id=1, source_target_pairs={{0,2},{1,3},{2,0},{3,1},{4,6},{5,7},{6,4},{7,5},{8,10},{9,11},{10,... | collective-permute-start | bytes 442376 | tf_op jit(solution)/shard_map/ppermute | solution.py:293
  13.2 4.2 %collective-permute-done.1 = f32[4,72,128]{2,1,0:T(8,128)S(1)} collective-permute-done((f32[4,72,128]{2,1,0:T(8,128)S(1)}, f32[4,72,128]{2,1,0:T(8,128)S(1)}, u32[]{:S(2)}, u32[]{:S(2)}) %collective-permute-start.1) | collective-permute-done | bytes 147488 | tf_op jit(solution)/shard_map/ppermute | solution.py:293
  17.3 0.0 copy-start.2
  17.3 0.1 add_select_fusion.5
  17.5 2.8 %collective-permute-start.2 = (f32[4,72,128]{2,1,0:T(8,128)S(1)}, f32[4,72,128]{2,1,0:T(8,128)S(1)}, u32[]{:S(2)}, u32[]{:S(2)}) collective-permute-start(f32[4,72,128]{2,1,0:T(8,128)S(1)} %get-tuple-element.23), channel_id=1, source_target_pairs={{0,4},{1,5},{2,6},{3,7},{4,0},{5,1},{6,2},{7,3},{8,12},{9,13},{10,... | collective-permute-start | bytes 442376 | tf_op jit(solution)/shard_map/ppermute | solution.py:293
  20.3 6.6 %collective-permute-done.2 = f32[4,72,128]{2,1,0:T(8,128)S(1)} collective-permute-done((f32[4,72,128]{2,1,0:T(8,128)S(1)}, f32[4,72,128]{2,1,0:T(8,128)S(1)}, u32[]{:S(2)}, u32[]{:S(2)}) %collective-permute-start.2) | collective-permute-done | bytes 147488 | tf_op jit(solution)/shard_map/ppermute | solution.py:293
  26.9 0.1 add_select_fusion.4
  27.1 1.4 %collective-permute-start.3 = (f32[4,72,128]{2,1,0:T(8,128)S(1)}, f32[4,72,128]{2,1,0:T(8,128)S(1)}, u32[]{:S(2)}, u32[]{:S(2)}) collective-permute-start(f32[4,72,128]{2,1,0:T(8,128)S(1)} %get-tuple-element.21), channel_id=1, source_target_pairs={{0,8},{1,9},{2,10},{3,11},{4,12},{5,13},{6,14},{7,15},{8,0},{9,1},... | collective-permute-start | bytes 442376 | tf_op jit(solution)/shard_map/ppermute | solution.py:293
  28.5 3.8 %collective-permute-done.3 = f32[4,72,128]{2,1,0:T(8,128)S(1)} collective-permute-done((f32[4,72,128]{2,1,0:T(8,128)S(1)}, f32[4,72,128]{2,1,0:T(8,128)S(1)}, u32[]{:S(2)}, u32[]{:S(2)}) %collective-permute-start.3) | collective-permute-done | bytes 147488 | tf_op jit(solution)/shard_map/ppermute | solution.py:293
  32.3 0.1 add_select_fusion.3
  32.4 1.5 %collective-permute-start.4 = (f32[4,72,128]{2,1,0:T(8,128)S(1)}, f32[4,72,128]{2,1,0:T(8,128)S(1)}, u32[]{:S(2)}, u32[]{:S(2)}) collective-permute-start(f32[4,72,128]{2,1,0:T(8,128)S(1)} %get-tuple-element.19), channel_id=1, source_target_pairs={{0,16},{1,17},{2,18},{3,19},{4,20},{5,21},{6,22},{7,23},{8,24},{9,... | collective-permute-start | bytes 442376 | tf_op jit(solution)/shard_map/ppermute | solution.py:293
  33.9 3.7 %collective-permute-done.4 = f32[4,72,128]{2,1,0:T(8,128)S(1)} collective-permute-done((f32[4,72,128]{2,1,0:T(8,128)S(1)}, f32[4,72,128]{2,1,0:T(8,128)S(1)}, u32[]{:S(2)}, u32[]{:S(2)}) %collective-permute-start.4) | collective-permute-done | bytes 147488 | tf_op jit(solution)/shard_map/ppermute | solution.py:293
  37.6 0.1 fusion.2
  37.7 0.0 copy-done.1
  37.7 0.1 fusion.5
  37.8 0.1 collective-permute-start.5
  37.9 0.0 copy-done
  37.9 0.0 copy-done.2
  37.9 2.0 %multiply_convert_fusion.q_ref = bf16[384,1024]{1,0:T(8,128)(2,1)} fusion(bf16[384,1024]{1,0:T(8,128)(2,1)S(1)} %copy-done.2, bf16[1024,1024]{1,0:T(8,128)(2,1)S(1)} %copy-done), kind=kOutput, calls=%fused_computation | convolution fusion | flops 807272448 | bytes 3670016 | tf_op jit(solution)/shard_map/dot_general | solution.py:318
  40.0 4.8 %shard_map.74.rest_0_ = f32[384,1024]{1,0:T(8,128)} custom-call(bf16[384,1024]{1,0:T(8,128)(2,1)} %multiply_convert_fusion.q_ref, bf16[384,1024]{1,0:T(8,128)(2,1)} %get-tuple-element.11.k_ref, bf16[384,1024]{1,0:T(8,128)(2,1)} %get-tuple-element.12.v_ref, f32[384,16]{1,0:T(8,128)} %get-tuple-element.13.cum_ref, f32[16,384]{1,0:T(8,128)} %get-tuple-element.14.cum_t_ref), custom_call_target="tpu_custom_call" | custom-call | flops 603979776 | bytes 1966080 | tf_op jit(solution)/shard_map/pallas_call | solution.py:60
  44.8 3.1 %shard_map.75.rest_0_ = f32[384,1024]{1,0:T(8,128)} custom-call(bf16[384,1024]{1,0:T(8,128)(2,1)} %multiply_convert_fusion.q_ref, bf16[384,1024]{1,0:T(8,128)(2,1)} %get-tuple-element.11.k_ref, bf16[384,1024]{1,0:T(8,128)(2,1)} %get-tuple-element.12.v_ref, f32[384,16]{1,0:T(8,128)} %get-tuple-element.13.cum_ref, ...), custom_call_target="tpu_custom_call", output_to_operand_aliasing={{}: (5, {})} | custom-call | flops 301989888 | bytes 983040 | tf_op jit(solution)/shard_map/pallas_call | solution.py:60
  47.8 3.1 %shard_map.76.intra_ref = f32[384,1024]{1,0:T(8,128)} custom-call(bf16[384,1024]{1,0:T(8,128)(2,1)} %multiply_convert_fusion.q_ref, bf16[384,1024]{1,0:T(8,128)(2,1)} %get-tuple-element.11.k_ref, bf16[384,1024]{1,0:T(8,128)(2,1)} %get-tuple-element.12.v_ref, f32[384,16]{1,0:T(8,128)} %get-tuple-element.13.cum_ref, ...), custom_call_target="tpu_custom_call", output_to_operand_aliasing={{}: (5, {})} | custom-call | flops 301989888 | bytes 983040 | tf_op jit(solution)/shard_map/pallas_call | solution.py:60
  50.9 0.0 collective-permute-done.5
  50.9 0.7 %maximum_select_fusion.state_ref = f32[8,72,128]{2,1,0:T(8,128)} fusion(f32[4,72,128]{2,1,0:T(8,128)S(1)} %collective-permute-done.5, f32[4,72,128]{2,1,0:T(8,128)S(1)} %get-tuple-element.18, f32[4,72,128]{2,1,0:T(8,128)S(1)} %get-tuple-element.17, pred[]{:T(512)S(6)} %eq.8), kind=kLoop, calls=%fused_computation.1 | loop fusion | flops 221184 | bytes 737281 | tf_op jit(solution)/shard_map/jit(_where)/select_n | solution.py:301
  51.6 6.1 %shard_map.77 = bf16[384,1024]{1,0:T(8,128)(2,1)} custom-call(bf16[384,1024]{1,0:T(8,128)(2,1)} %multiply_convert_fusion.q_ref, f32[384,1024]{1,0:T(8,128)} %shard_map.76.intra_ref, f32[8,72,128]{2,1,0:T(8,128)} %maximum_select_fusion.state_ref, f32[384,16]{1,0:T(8,128)} %get-tuple-element.13.cum_ref, f32[1,1024]{1,0:T(1,128)} %bitcast.29, ...), custom_call_target="tpu_custom_call" | custom-call | flops 1107296256 | bytes 5242880 | tf_op jit(solution)/shard_map/pallas_call | solution.py:251
  (10 shorter events, 0.1 us)
Async XLA Ops:
  0.0 37.9 %copy-start = (bf16[1024,1024]{1,0:T(8,128)(2,1)S(1)}, bf16[1024,1024]{1,0:T(8,128)(2,1)}, u32[]{:S(2)}) copy-start(bf16[1024,1024]{1,0:T(8,128)(2,1)} %param.9) | copy-start | bytes 6291460
  7.3 1.8 %collective-permute-start = (f32[4,72,128]{2,1,0:T(8,128)}, f32[4,72,128]{2,1,0:T(8,128)S(1)}, u32[]{:S(2)}, u32[]{:S(2)}) collective-permute-start(f32[4,72,128]{2,1,0:T(8,128)} %get-tuple-element.15), channel_id=1, source_target_pairs={{0,1},{1,0},{2,3},{3,2},{4,5},{5,4},{6,7},{7,6},{8,9},{9,8},{10,11... | collective-permute-start | bytes 442376 | tf_op jit(solution)/shard_map/ppermute | solution.py:286
  9.1 28.7 %copy-start.1 = (f32[4,72,128]{2,1,0:T(8,128)S(1)}, f32[4,72,128]{2,1,0:T(8,128)}, u32[]{:S(2)}) copy-start(f32[4,72,128]{2,1,0:T(8,128)} %get-tuple-element.16) | copy-start | bytes 442372
  10.2 7.2 %collective-permute-start.1 = (f32[4,72,128]{2,1,0:T(8,128)S(1)}, f32[4,72,128]{2,1,0:T(8,128)S(1)}, u32[]{:S(2)}, u32[]{:S(2)}) collective-permute-start(f32[4,72,128]{2,1,0:T(8,128)S(1)} %fusion.1), channel_id=1, source_target_pairs={{0,2},{1,3},{2,0},{3,1},{4,6},{5,7},{6,4},{7,5},{8,10},{9,11},{10,... | collective-permute-start | bytes 442376 | tf_op jit(solution)/shard_map/ppermute | solution.py:293
  17.3 20.6 %copy-start.2 = (bf16[384,1024]{1,0:T(8,128)(2,1)S(1)}, bf16[384,1024]{1,0:T(8,128)(2,1)}, u32[]{:S(2)}) copy-start(bf16[384,1024]{1,0:T(8,128)(2,1)} %x_ref.1) | copy-start | bytes 2359300
  17.5 9.4 %collective-permute-start.2 = (f32[4,72,128]{2,1,0:T(8,128)S(1)}, f32[4,72,128]{2,1,0:T(8,128)S(1)}, u32[]{:S(2)}, u32[]{:S(2)}) collective-permute-start(f32[4,72,128]{2,1,0:T(8,128)S(1)} %get-tuple-element.23), channel_id=1, source_target_pairs={{0,4},{1,5},{2,6},{3,7},{4,0},{5,1},{6,2},{7,3},{8,12},{9,13},{10,... | collective-permute-start | bytes 442376 | tf_op jit(solution)/shard_map/ppermute | solution.py:293
  27.1 5.2 %collective-permute-start.3 = (f32[4,72,128]{2,1,0:T(8,128)S(1)}, f32[4,72,128]{2,1,0:T(8,128)S(1)}, u32[]{:S(2)}, u32[]{:S(2)}) collective-permute-start(f32[4,72,128]{2,1,0:T(8,128)S(1)} %get-tuple-element.21), channel_id=1, source_target_pairs={{0,8},{1,9},{2,10},{3,11},{4,12},{5,13},{6,14},{7,15},{8,0},{9,1},... | collective-permute-start | bytes 442376 | tf_op jit(solution)/shard_map/ppermute | solution.py:293
  32.4 5.2 %collective-permute-start.4 = (f32[4,72,128]{2,1,0:T(8,128)S(1)}, f32[4,72,128]{2,1,0:T(8,128)S(1)}, u32[]{:S(2)}, u32[]{:S(2)}) collective-permute-start(f32[4,72,128]{2,1,0:T(8,128)S(1)} %get-tuple-element.19), channel_id=1, source_target_pairs={{0,16},{1,17},{2,18},{3,19},{4,20},{5,21},{6,22},{7,23},{8,24},{9,... | collective-permute-start | bytes 442376 | tf_op jit(solution)/shard_map/ppermute | solution.py:293
  37.8 13.1 %collective-permute-start.5 = (f32[4,72,128]{2,1,0:T(8,128)S(1)}, f32[4,72,128]{2,1,0:T(8,128)S(1)}, u32[]{:S(2)}, u32[]{:S(2)}) collective-permute-start(f32[4,72,128]{2,1,0:T(8,128)S(1)} %fusion.5), channel_id=1, source_target_pairs={{0,1},{1,0},{2,3},{3,2},{4,5},{5,4},{6,7},{7,6},{8,9},{9,8},{10,11... | collective-permute-start | bytes 442376 | tf_op jit(solution)/shard_map/ppermute | solution.py:300

commit v15 on v13

--- a/solution.py
+++ b/solution.py
@@ -138,7 +138,7 @@
     width = key_weight.shape[1]
     heads = log_decay.shape[1]
     pairs = width // LANES
-    per = 2 if pairs % 2 == 0 else 1
+    per = PER_STEP if pairs % PER_STEP == 0 else 1
     block = pl.BlockSpec((rows, per * LANES), lambda p: (0, p))
     weights = pl.BlockSpec((depth, per * LANES), lambda p: (0, p))
     return pl.pallas_call(
@@ -210,17 +210,26 @@
         part = rest.astype(bf16)
         inter = inter + jnp.dot(q, part, preferred_element_type=f32)
         rest = rest - part.astype(f32)
-    cum = cum_ref[...]
-    lane_head = lax.broadcasted_iota(jnp.int32, (rows, LANES), 1) // head_dim
-    growth = jnp.zeros((rows, LANES), f32)
-    for j in range(group):
-        growth = jnp.where(lane_head == j, jnp.exp(head_column(cum, pair * group + j)), growth)
-    attended = intra_ref[:, cols] + inter * growth
+    heads = cum_ref.shape[1]
+    pick_h = lax.broadcasted_iota(jnp.int32, (heads, LANES), 0)
+    pick_l = lax.broadcasted_iota(jnp.int32, (heads, LANES), 1) // head_dim + pair * group
+    pick = jnp.where(pick_h == pick_l, 1.0, 0.0).astype(bf16)
+    rest = cum_ref[...]
+    lane_cum = jnp.zeros((rows, LANES), f32)
+    for _ in range(3):
+        part = rest.astype(bf16)
+        lane_cum = lane_cum + jnp.dot(part, pick, preferred_element_type=f32)
+        rest = rest - part.astype(f32)
+    attended = intra_ref[:, cols] + inter * jnp.exp(lane_cum)
     square = attended * attended
-    scale = jnp.zeros((rows, LANES), f32)
-    for j in range(group):
-        mean = jnp.sum(jnp.where(lane_head == j, square, 0.0), axis=1, keepdims=True) / head_dim
-        scale = jnp.where(lane_head == j, lax.rsqrt(mean + 1e-05), scale)
+    average = jnp.where(r_head == c_head, 1.0 / head_dim, 0.0).astype(bf16)
+    rest = square
+    mean = jnp.zeros((rows, LANES), f32)
+    for _ in range(3):
+        part = rest.astype(bf16)
+        mean = mean + jnp.dot(part, average, preferred_element_type=f32)
+        rest = rest - part.astype(f32)
+    scale = lax.rsqrt(mean + 1e-05)
     o_ref[:, cols] = (attended * scale * gain_ref[:, cols]).astype(bf16)
 
 
@@ -267,26 +276,24 @@
     chips = count // 2
     half = own.shape[0] // 2
     partner = [(i, i ^ 1) for i in range(count)]
-    other = lax.ppermute(own, AXES, partner)
-    pooled = jnp.where(core == 0, combine(own, other), combine(other, own))
-    through = jnp.where(core == 0, pooled[:half], pooled[half:])
+    got = lax.ppermute(jnp.where(core == 0, own[half:], own[:half]), AXES, partner)
+    through = jnp.where(core == 0, combine(own[:half], got), combine(got, own[half:]))
     before = jnp.zeros_like(through)
     received = []
     bit = 1
     while bit < chips:
         perm = [(i, i ^ (2 * bit)) for i in range(count)]
-        got = lax.ppermute(through, AXES, perm)
-        received.append(got)
+        exchanged = lax.ppermute(through, AXES, perm)
+        received.append(exchanged)
         lower = (chip & bit) != 0
-        before = jnp.where(lower, combine(got, before), before)
+        before = jnp.where(lower, combine(exchanged, before), before)
         bit *= 2
         if bit < chips:
-            through = jnp.where(lower, combine(got, through), combine(through, got))
-    swapped = lax.ppermute(before, AXES, partner)
+            through = jnp.where(lower, combine(exchanged, through), combine(through, exchanged))
+    back = lax.ppermute(jnp.where(core == 0, combine(before, own[:half]), before), AXES, partner)
     whole = jnp.where(
-        core == 0, jnp.concatenate([before, swapped]), jnp.concatenate([swapped, before])
+        core == 0, jnp.concatenate([before, back]), jnp.concatenate([back, combine(before, got)])
     )
-    whole = jnp.where(core == 0, whole, combine(whole, other))
     return whole, received
 
 

time: 57.8 us -> 59.1 us (1.022)
  other arithmetic: 2.41 us -> 3.42 us
  Pallas kernels: 23.8 us -> 24.5 us
    pallas_call x1, Pallas kernels: 6.15 us -> 7.6 us  [finish(): pl.pallas_call(functools.partial(finish_kernel, head_dim=head_dim), grid=...]
    select_n x7, other arithmetic: 2.4 us -> 3.3 us  [the longest x1 1.09 us: exclusive_scan(): jnp.where(core == 0, combine(own[:half], got), combine(got, own[half:]))]
    pallas_call x1, Pallas kernels: 6.73 us -> 5.97 us  [project_keys_values(): pl.pallas_call(functools.partial(project_kernel, head_dim=head_dim), grid...]
where the time goes in v15:
time: 59.1 us; the launch traced here: 58.7 us
  Pallas kernels  24.5 us (41%)
  waiting for transfers between devices  18.5 us (31%)
  starting transfers between devices  9.34 us (16%)
  other arithmetic  3.42 us (6%)
  matrix products  2.04 us (3%)
  local copies, waits for them, and re-layouts  0.82 us (1%)
    ppermute x4, waiting for transfers between devices, exclusive_scan(): exchanged = lax.ppermute(through, AXES, perm)  18.3 us
    pallas_call x3, Pallas kernels, intra_attention(): pl.pallas_call(functools.partial(intra_kernel, head_dim=head_dim, first=f...  10.9 us
    ppermute x4, starting transfers between devices, exclusive_scan(): exchanged = lax.ppermute(through, AXES, perm)  8.72 us
    pallas_call x1, Pallas kernels, finish(): pl.pallas_call(functools.partial(finish_kernel, head_dim=head_dim), grid=...  7.6 us
    pallas_call x1, Pallas kernels, project_keys_values(): pl.pallas_call(functools.partial(project_kernel, head_dim=head_dim), grid...  5.97 us
    dot_general x1, matrix products, layer(): jnp.dot(tokens, query_weight, preferred_element_type=f32)  2.04 us
  transfers between devices with their start and end apart: 6, of which 5 were waited for; matrix products, arithmetic and copies ran while one was open for 5% of the time, Pallas kernels for 19%

profile of v15, /device:TPU:0, one launch (start us, length us, event | category | flops | bytes accessed | tf_op | source)
XLA Modules:
  0.0 58.7 jit_solution(12545963940601923437)
XLA Ops:
  0.0 0.0 copy-start
  0.0 6.0 %shard_map.73 = (bf16[384,1024]{1,0:T(8,128)(2,1)}, bf16[384,1024]{1,0:T(8,128)(2,1)}, f32[8,72,128]{2,1,0:T(8,128)}, f32[384,16]{1,0:T(8,128)}, f32[16,384]{1,0:T(8,128)}) custom-call(bf16[384,1024]{1,0:T(8,128)(2,1)} %x_ref.1, bf16[1024,1024]{1,0:T(8,128)(2,1)} %wk_ref.1, bf16[1024,1024]{1,0:T(8,128)(2,1)} %wv_ref.1, f32[16,384]{1,0:T(8,128)} %bitcast.30), custom_call_target="tpu_custom_call" | custom-call | flops 1711276032 | bytes 6553600 | tf_op jit(solution)/shard_map/pallas_call | solution.py:144
  6.0 1.0 %slice_select_fusion = f32[4,72,128]{2,1,0:T(8,128)S(1)} fusion(f32[8,72,128]{2,1,0:T(8,128)} %get-tuple-element.14, pred[]{:T(512)S(6)} %eq.4), kind=kLoop, calls=%fused_computation.14 | loop fusion | flops 36864 | bytes 442369 | tf_op jit(solution)/shard_map/jit(_where)/select_n | solution.py:279
  7.0 0.6 collective-permute-start
  7.5 0.7 %slice_exponential_fusion.10 = (f32[4,1,128]{2,1,0:T(1,128)S(1)}, f32[4,1,128]{2,1,0:T(1,128)S(1)}) fusion(f32[8,72,128]{2,1,0:T(8,128)} %get-tuple-element.14), kind=kLoop, calls=%fused_computation.26 | loop fusion | bytes 8192 | tf_op jit(solution)/shard_map/exp | solution.py:268
  8.3 0.2 collective-permute-done
  8.5 1.1 %fusion.1 = f32[4,72,128]{2,1,0:T(8,128)S(1)} fusion(f32[4,72,128]{2,1,0:T(8,128)S(1)} %collective-permute-done, f32[8,72,128]{2,1,0:T(8,128)} %get-tuple-element.14, f32[4,128]{1,0:T(4,128)S(1)} %bitcast.26, f32[4,128]{1,0:T(4,128)S(1)} %bitcast.16, pred[72]{0:T(512)(128)(4,1)S(1)} %iota_compare_fusion, pred[]{:T(512)S(6)} %eq.4), kind=kLoop, calls=%fused_computation.8 | loop fusion | flops 258048 | bytes 593993 | tf_op jit(solution)/shard_map/jit(_where)/select_n | solution.py:280
  9.6 0.0 copy-start.1
  9.7 3.0 %collective-permute-start.1 = (f32[4,72,128]{2,1,0:T(8,128)S(1)}, f32[4,72,128]{2,1,0:T(8,128)S(1)}, u32[]{:S(2)}, u32[]{:S(2)}) collective-permute-start(f32[4,72,128]{2,1,0:T(8,128)S(1)} %fusion.1), channel_id=1, source_target_pairs={{0,2},{1,3},{2,0},{3,1},{4,6},{5,7},{6,4},{7,5},{8,10},{9,11},{10,... | collective-permute-start | bytes 442376 | tf_op jit(solution)/shard_map/ppermute | solution.py:286
  12.7 4.2 %collective-permute-done.1 = f32[4,72,128]{2,1,0:T(8,128)S(1)} collective-permute-done((f32[4,72,128]{2,1,0:T(8,128)S(1)}, f32[4,72,128]{2,1,0:T(8,128)S(1)}, u32[]{:S(2)}, u32[]{:S(2)}) %collective-permute-start.1) | collective-permute-done | bytes 147488 | tf_op jit(solution)/shard_map/ppermute | solution.py:286
  16.8 0.0 copy-start.2
  16.8 0.1 add_select_fusion.6
  16.9 2.8 %collective-permute-start.2 = (f32[4,72,128]{2,1,0:T(8,128)S(1)}, f32[4,72,128]{2,1,0:T(8,128)S(1)}, u32[]{:S(2)}, u32[]{:S(2)}) collective-permute-start(f32[4,72,128]{2,1,0:T(8,128)S(1)} %get-tuple-element.23), channel_id=1, source_target_pairs={{0,4},{1,5},{2,6},{3,7},{4,0},{5,1},{6,2},{7,3},{8,12},{9,13},{10,... | collective-permute-start | bytes 442376 | tf_op jit(solution)/shard_map/ppermute | solution.py:286
  19.8 6.6 %collective-permute-done.2 = f32[4,72,128]{2,1,0:T(8,128)S(1)} collective-permute-done((f32[4,72,128]{2,1,0:T(8,128)S(1)}, f32[4,72,128]{2,1,0:T(8,128)S(1)}, u32[]{:S(2)}, u32[]{:S(2)}) %collective-permute-start.2) | collective-permute-done | bytes 147488 | tf_op jit(solution)/shard_map/ppermute | solution.py:286
  26.4 0.1 add_select_fusion.5
  26.5 1.4 %collective-permute-start.3 = (f32[4,72,128]{2,1,0:T(8,128)S(1)}, f32[4,72,128]{2,1,0:T(8,128)S(1)}, u32[]{:S(2)}, u32[]{:S(2)}) collective-permute-start(f32[4,72,128]{2,1,0:T(8,128)S(1)} %get-tuple-element.21), channel_id=1, source_target_pairs={{0,8},{1,9},{2,10},{3,11},{4,12},{5,13},{6,14},{7,15},{8,0},{9,1},... | collective-permute-start | bytes 442376 | tf_op jit(solution)/shard_map/ppermute | solution.py:286
  28.0 3.8 %collective-permute-done.3 = f32[4,72,128]{2,1,0:T(8,128)S(1)} collective-permute-done((f32[4,72,128]{2,1,0:T(8,128)S(1)}, f32[4,72,128]{2,1,0:T(8,128)S(1)}, u32[]{:S(2)}, u32[]{:S(2)}) %collective-permute-start.3) | collective-permute-done | bytes 147488 | tf_op jit(solution)/shard_map/ppermute | solution.py:286
  31.8 0.1 add_select_fusion.4
  31.9 1.5 %collective-permute-start.4 = (f32[4,72,128]{2,1,0:T(8,128)S(1)}, f32[4,72,128]{2,1,0:T(8,128)S(1)}, u32[]{:S(2)}, u32[]{:S(2)}) collective-permute-start(f32[4,72,128]{2,1,0:T(8,128)S(1)} %get-tuple-element.19), channel_id=1, source_target_pairs={{0,16},{1,17},{2,18},{3,19},{4,20},{5,21},{6,22},{7,23},{8,24},{9,... | collective-permute-start | bytes 442376 | tf_op jit(solution)/shard_map/ppermute | solution.py:286
  33.4 3.7 %collective-permute-done.4 = f32[4,72,128]{2,1,0:T(8,128)S(1)} collective-permute-done((f32[4,72,128]{2,1,0:T(8,128)S(1)}, f32[4,72,128]{2,1,0:T(8,128)S(1)}, u32[]{:S(2)}, u32[]{:S(2)}) %collective-permute-start.4) | collective-permute-done | bytes 147488 | tf_op jit(solution)/shard_map/ppermute | solution.py:286
  37.1 0.1 fusion.2
  37.2 0.0 copy-done.1
  37.2 0.1 add_select_fusion.3
  37.3 0.1 collective-permute-start.5
  37.4 0.0 copy-done
  37.4 0.0 copy-done.2
  37.4 2.0 %multiply_convert_fusion.q_ref = bf16[384,1024]{1,0:T(8,128)(2,1)} fusion(bf16[384,1024]{1,0:T(8,128)(2,1)S(1)} %copy-done.2, bf16[1024,1024]{1,0:T(8,128)(2,1)S(1)} %copy-done), kind=kOutput, calls=%fused_computation | convolution fusion | flops 807272448 | bytes 3670016 | tf_op jit(solution)/shard_map/dot_general | solution.py:308
  39.5 4.8 %shard_map.74.rest_0_ = f32[384,1024]{1,0:T(8,128)} custom-call(bf16[384,1024]{1,0:T(8,128)(2,1)} %multiply_convert_fusion.q_ref, bf16[384,1024]{1,0:T(8,128)(2,1)} %get-tuple-element.10.k_ref, bf16[384,1024]{1,0:T(8,128)(2,1)} %get-tuple-element.11.v_ref, f32[384,16]{1,0:T(8,128)} %get-tuple-element.12.cum_ref, f32[16,384]{1,0:T(8,128)} %get-tuple-element.13.cum_t_ref), custom_call_target="tpu_custom_call" | custom-call | flops 603979776 | bytes 1966080 | tf_op jit(solution)/shard_map/pallas_call | solution.py:60
  44.2 3.1 %shard_map.75.rest_0_ = f32[384,1024]{1,0:T(8,128)} custom-call(bf16[384,1024]{1,0:T(8,128)(2,1)} %multiply_convert_fusion.q_ref, bf16[384,1024]{1,0:T(8,128)(2,1)} %get-tuple-element.10.k_ref, bf16[384,1024]{1,0:T(8,128)(2,1)} %get-tuple-element.11.v_ref, f32[384,16]{1,0:T(8,128)} %get-tuple-element.12.cum_ref, ...), custom_call_target="tpu_custom_call", output_to_operand_aliasing={{}: (5, {})} | custom-call | flops 301989888 | bytes 983040 | tf_op jit(solution)/shard_map/pallas_call | solution.py:60
  47.3 3.1 %shard_map.76.intra_ref = f32[384,1024]{1,0:T(8,128)} custom-call(bf16[384,1024]{1,0:T(8,128)(2,1)} %multiply_convert_fusion.q_ref, bf16[384,1024]{1,0:T(8,128)(2,1)} %get-tuple-element.10.k_ref, bf16[384,1024]{1,0:T(8,128)(2,1)} %get-tuple-element.11.v_ref, f32[384,16]{1,0:T(8,128)} %get-tuple-element.12.cum_ref, ...), custom_call_target="tpu_custom_call", output_to_operand_aliasing={{}: (5, {})} | custom-call | flops 301989888 | bytes 983040 | tf_op jit(solution)/shard_map/pallas_call | solution.py:60
  50.4 0.0 collective-permute-done.5
  50.4 0.7 %maximum_select_fusion.state_ref = f32[8,72,128]{2,1,0:T(8,128)} fusion(f32[4,72,128]{2,1,0:T(8,128)S(1)} %collective-permute-done.5, f32[4,72,128]{2,1,0:T(8,128)S(1)} %get-tuple-element.16, f32[4,72,128]{2,1,0:T(8,128)S(1)} %get-tuple-element.15, pred[]{:T(512)S(6)} %eq.4), kind=kLoop, calls=%fused_computation.1 | loop fusion | flops 221184 | bytes 737281 | tf_op jit(solution)/shard_map/jit(_where)/select_n | solution.py:294
  51.1 7.6 %shard_map.77 = bf16[384,1024]{1,0:T(8,128)(2,1)} custom-call(bf16[384,1024]{1,0:T(8,128)(2,1)} %multiply_convert_fusion.q_ref, f32[384,1024]{1,0:T(8,128)} %shard_map.76.intra_ref, f32[8,72,128]{2,1,0:T(8,128)} %maximum_select_fusion.state_ref, f32[384,16]{1,0:T(8,128)} %get-tuple-element.12.cum_ref, f32[1,1024]{1,0:T(1,128)} %bitcast.29, ...), custom_call_target="tpu_custom_call" | custom-call | flops 1107296256 | bytes 5242880 | tf_op jit(solution)/shard_map/pallas_call | solution.py:243
  (10 shorter events, 0.1 us)
Async XLA Ops:
  0.0 37.4 %copy-start = (bf16[1024,1024]{1,0:T(8,128)(2,1)S(1)}, bf16[1024,1024]{1,0:T(8,128)(2,1)}, u32[]{:S(2)}) copy-start(bf16[1024,1024]{1,0:T(8,128)(2,1)} %param.9) | copy-start | bytes 6291460
  7.0 1.6 %collective-permute-start = (f32[4,72,128]{2,1,0:T(8,128)S(1)}, f32[4,72,128]{2,1,0:T(8,128)S(1)}, u32[]{:S(2)}, u32[]{:S(2)}) collective-permute-start(f32[4,72,128]{2,1,0:T(8,128)S(1)} %slice_select_fusion), channel_id=1, source_target_pairs={{0,1},{1,0},{2,3},{3,2},{4,5},{5,4},{6,7},{7,6},{8,9},{9,8},{10,11... | collective-permute-start | bytes 442376 | tf_op jit(solution)/shard_map/ppermute | solution.py:279
  9.6 27.6 %copy-start.1 = (f32[8,72,128]{2,1,0:T(8,128)S(1)}, f32[8,72,128]{2,1,0:T(8,128)}, u32[]{:S(2)}) copy-start(f32[8,72,128]{2,1,0:T(8,128)} %get-tuple-element.14) | copy-start | bytes 884740
  9.7 7.2 %collective-permute-start.1 = (f32[4,72,128]{2,1,0:T(8,128)S(1)}, f32[4,72,128]{2,1,0:T(8,128)S(1)}, u32[]{:S(2)}, u32[]{:S(2)}) collective-permute-start(f32[4,72,128]{2,1,0:T(8,128)S(1)} %fusion.1), channel_id=1, source_target_pairs={{0,2},{1,3},{2,0},{3,1},{4,6},{5,7},{6,4},{7,5},{8,10},{9,11},{10,... | collective-permute-start | bytes 442376 | tf_op jit(solution)/shard_map/ppermute | solution.py:286
  16.8 20.6 %copy-start.2 = (bf16[384,1024]{1,0:T(8,128)(2,1)S(1)}, bf16[384,1024]{1,0:T(8,128)(2,1)}, u32[]{:S(2)}) copy-start(bf16[384,1024]{1,0:T(8,128)(2,1)} %x_ref.1) | copy-start | bytes 2359300
  16.9 9.4 %collective-permute-start.2 = (f32[4,72,128]{2,1,0:T(8,128)S(1)}, f32[4,72,128]{2,1,0:T(8,128)S(1)}, u32[]{:S(2)}, u32[]{:S(2)}) collective-permute-start(f32[4,72,128]{2,1,0:T(8,128)S(1)} %get-tuple-element.23), channel_id=1, source_target_pairs={{0,4},{1,5},{2,6},{3,7},{4,0},{5,1},{6,2},{7,3},{8,12},{9,13},{10,... | collective-permute-start | bytes 442376 | tf_op jit(solution)/shard_map/ppermute | solution.py:286
  26.5 5.2 %collective-permute-start.3 = (f32[4,72,128]{2,1,0:T(8,128)S(1)}, f32[4,72,128]{2,1,0:T(8,128)S(1)}, u32[]{:S(2)}, u32[]{:S(2)}) collective-permute-start(f32[4,72,128]{2,1,0:T(8,128)S(1)} %get-tuple-element.21), channel_id=1, source_target_pairs={{0,8},{1,9},{2,10},{3,11},{4,12},{5,13},{6,14},{7,15},{8,0},{9,1},... | collective-permute-start | bytes 442376 | tf_op jit(solution)/shard_map/ppermute | solution.py:286
  31.9 5.2 %collective-permute-start.4 = (f32[4,72,128]{2,1,0:T(8,128)S(1)}, f32[4,72,128]{2,1,0:T(8,128)S(1)}, u32[]{:S(2)}, u32[]{:S(2)}) collective-permute-start(f32[4,72,128]{2,1,0:T(8,128)S(1)} %get-tuple-element.19), channel_id=1, source_target_pairs={{0,16},{1,17},{2,18},{3,19},{4,20},{5,21},{6,22},{7,23},{8,24},{9,... | collective-permute-start | bytes 442376 | tf_op jit(solution)/shard_map/ppermute | solution.py:286
  37.3 13.1 %collective-permute-start.5 = (f32[4,72,128]{2,1,0:T(8,128)S(1)}, f32[4,72,128]{2,1,0:T(8,128)S(1)}, u32[]{:S(2)}, u32[]{:S(2)}) collective-permute-start(f32[4,72,128]{2,1,0:T(8,128)S(1)} %add_select_fusion.3), channel_id=1, source_target_pairs={{0,1},{1,0},{2,3},{3,2},{4,5},{5,4},{6,7},{7,6},{8,9},{9,8},{10,11... | collective-permute-start | bytes 442376 | tf_op jit(solution)/shard_map/ppermute | solution.py:293

commit v16 on v13

--- a/solution.py
+++ b/solution.py
@@ -138,7 +138,7 @@
     width = key_weight.shape[1]
     heads = log_decay.shape[1]
     pairs = width // LANES
-    per = 2 if pairs % 2 == 0 else 1
+    per = PER_STEP if pairs % PER_STEP == 0 else 1
     block = pl.BlockSpec((rows, per * LANES), lambda p: (0, p))
     weights = pl.BlockSpec((depth, per * LANES), lambda p: (0, p))
     return pl.pallas_call(
@@ -229,7 +229,7 @@
     heads = cum.shape[1]
     pairs = width // LANES
     out_width = output_weight.shape[1]
-    per = PER_STEP if pairs % PER_STEP == 0 else 1
+    per = 2 if pairs % 2 == 0 else 1
     block = pl.BlockSpec((rows, per * LANES), lambda p: (0, p))
     return pl.pallas_call(
         functools.partial(finish_kernel, head_dim=head_dim),
@@ -267,26 +267,24 @@
     chips = count // 2
     half = own.shape[0] // 2
     partner = [(i, i ^ 1) for i in range(count)]
-    other = lax.ppermute(own, AXES, partner)
-    pooled = jnp.where(core == 0, combine(own, other), combine(other, own))
-    through = jnp.where(core == 0, pooled[:half], pooled[half:])
+    got = lax.ppermute(jnp.where(core == 0, own[half:], own[:half]), AXES, partner)
+    through = jnp.where(core == 0, combine(own[:half], got), combine(got, own[half:]))
     before = jnp.zeros_like(through)
     received = []
     bit = 1
     while bit < chips:
         perm = [(i, i ^ (2 * bit)) for i in range(count)]
-        got = lax.ppermute(through, AXES, perm)
-        received.append(got)
+        exchanged = lax.ppermute(through, AXES, perm)
+        received.append(exchanged)
         lower = (chip & bit) != 0
-        before = jnp.where(lower, combine(got, before), before)
+        before = jnp.where(lower, combine(exchanged, before), before)
         bit *= 2
         if bit < chips:
-            through = jnp.where(lower, combine(got, through), combine(through, got))
-    swapped = lax.ppermute(before, AXES, partner)
+            through = jnp.where(lower, combine(exchanged, through), combine(through, exchanged))
+    back = lax.ppermute(jnp.where(core == 0, combine(before, own[:half]), before), AXES, partner)
     whole = jnp.where(
-        core == 0, jnp.concatenate([before, swapped]), jnp.concatenate([swapped, before])
+        core == 0, jnp.concatenate([before, back]), jnp.concatenate([back, combine(before, got)])
     )
-    whole = jnp.where(core == 0, whole, combine(whole, other))
     return whole, received
 
 

time: 57.8 us -> 58.4 us (1.010)
  other arithmetic: 2.41 us -> 3.42 us
    select_n x7, other arithmetic: 2.4 us -> 3.3 us  [the longest x1 1.09 us: exclusive_scan(): jnp.where(core == 0, combine(own[:half], got), combine(got, own[half:]))]
    pallas_call x1, Pallas kernels: 6.73 us -> 5.97 us  [project_keys_values(): pl.pallas_call(functools.partial(project_kernel, head_dim=head_dim), grid...]
    pallas_call x1, Pallas kernels: 6.15 us -> 6.82 us  [finish(): pl.pallas_call(functools.partial(finish_kernel, head_dim=head_dim), grid=...]
where the time goes in v16:
time: 58.4 us; the launch traced here: 58 us
  Pallas kernels  23.7 us (41%)
  waiting for transfers between devices  18.5 us (32%)
  starting transfers between devices  9.34 us (16%)
  other arithmetic  3.42 us (6%)
  matrix products  2.04 us (3%)
  local copies, waits for them, and re-layouts  0.82 us (1%)
    ppermute x4, waiting for transfers between devices, exclusive_scan(): exchanged = lax.ppermute(through, AXES, perm)  18.3 us
    pallas_call x3, Pallas kernels, intra_attention(): pl.pallas_call(functools.partial(intra_kernel, head_dim=head_dim, first=f...  10.9 us
    ppermute x4, starting transfers between devices, exclusive_scan(): exchanged = lax.ppermute(through, AXES, perm)  8.72 us
    pallas_call x1, Pallas kernels, finish(): pl.pallas_call(functools.partial(finish_kernel, head_dim=head_dim), grid=...  6.82 us
    pallas_call x1, Pallas kernels, project_keys_values(): pl.pallas_call(functools.partial(project_kernel, head_dim=head_dim), grid...  5.97 us
    dot_general x1, matrix products, layer(): jnp.dot(tokens, query_weight, preferred_element_type=f32)  2.04 us
  transfers between devices with their start and end apart: 6, of which 5 were waited for; matrix products, arithmetic and copies ran while one was open for 5% of the time, Pallas kernels for 19%

profile of v16, /device:TPU:0, one launch (start us, length us, event | category | flops | bytes accessed | tf_op | source)
XLA Modules:
  0.0 58.0 jit_solution(1604966652371289240)
XLA Ops:
  0.0 0.0 copy-start
  0.0 6.0 %shard_map.73 = (bf16[384,1024]{1,0:T(8,128)(2,1)}, bf16[384,1024]{1,0:T(8,128)(2,1)}, f32[8,72,128]{2,1,0:T(8,128)}, f32[384,16]{1,0:T(8,128)}, f32[16,384]{1,0:T(8,128)}) custom-call(bf16[384,1024]{1,0:T(8,128)(2,1)} %x_ref.1, bf16[1024,1024]{1,0:T(8,128)(2,1)} %wk_ref.1, bf16[1024,1024]{1,0:T(8,128)(2,1)} %wv_ref.1, f32[16,384]{1,0:T(8,128)} %bitcast.30), custom_call_target="tpu_custom_call" | custom-call | flops 1711276032 | bytes 6553600 | tf_op jit(solution)/shard_map/pallas_call | solution.py:144
  6.0 1.0 %slice_select_fusion = f32[4,72,128]{2,1,0:T(8,128)S(1)} fusion(f32[8,72,128]{2,1,0:T(8,128)} %get-tuple-element.14, pred[]{:T(512)S(6)} %eq.4), kind=kLoop, calls=%fused_computation.14 | loop fusion | flops 36864 | bytes 442369 | tf_op jit(solution)/shard_map/jit(_where)/select_n | solution.py:270
  7.0 0.6 collective-permute-start
  7.5 0.7 %slice_exponential_fusion.10 = (f32[4,1,128]{2,1,0:T(1,128)S(1)}, f32[4,1,128]{2,1,0:T(1,128)S(1)}) fusion(f32[8,72,128]{2,1,0:T(8,128)} %get-tuple-element.14), kind=kLoop, calls=%fused_computation.26 | loop fusion | bytes 8192 | tf_op jit(solution)/shard_map/exp | solution.py:259
  8.3 0.2 collective-permute-done
  8.5 1.1 %fusion.1 = f32[4,72,128]{2,1,0:T(8,128)S(1)} fusion(f32[4,72,128]{2,1,0:T(8,128)S(1)} %collective-permute-done, f32[8,72,128]{2,1,0:T(8,128)} %get-tuple-element.14, f32[4,128]{1,0:T(4,128)S(1)} %bitcast.26, f32[4,128]{1,0:T(4,128)S(1)} %bitcast.16, pred[72]{0:T(512)(128)(4,1)S(1)} %iota_compare_fusion, pred[]{:T(512)S(6)} %eq.4), kind=kLoop, calls=%fused_computation.8 | loop fusion | flops 258048 | bytes 593993 | tf_op jit(solution)/shard_map/jit(_where)/select_n | solution.py:271
  9.6 0.0 copy-start.1
  9.7 3.0 %collective-permute-start.1 = (f32[4,72,128]{2,1,0:T(8,128)S(1)}, f32[4,72,128]{2,1,0:T(8,128)S(1)}, u32[]{:S(2)}, u32[]{:S(2)}) collective-permute-start(f32[4,72,128]{2,1,0:T(8,128)S(1)} %fusion.1), channel_id=1, source_target_pairs={{0,2},{1,3},{2,0},{3,1},{4,6},{5,7},{6,4},{7,5},{8,10},{9,11},{10,... | collective-permute-start | bytes 442376 | tf_op jit(solution)/shard_map/ppermute | solution.py:277
  12.7 4.2 %collective-permute-done.1 = f32[4,72,128]{2,1,0:T(8,128)S(1)} collective-permute-done((f32[4,72,128]{2,1,0:T(8,128)S(1)}, f32[4,72,128]{2,1,0:T(8,128)S(1)}, u32[]{:S(2)}, u32[]{:S(2)}) %collective-permute-start.1) | collective-permute-done | bytes 147488 | tf_op jit(solution)/shard_map/ppermute | solution.py:277
  16.8 0.0 copy-start.2
  16.8 0.1 add_select_fusion.6
  16.9 2.8 %collective-permute-start.2 = (f32[4,72,128]{2,1,0:T(8,128)S(1)}, f32[4,72,128]{2,1,0:T(8,128)S(1)}, u32[]{:S(2)}, u32[]{:S(2)}) collective-permute-start(f32[4,72,128]{2,1,0:T(8,128)S(1)} %get-tuple-element.23), channel_id=1, source_target_pairs={{0,4},{1,5},{2,6},{3,7},{4,0},{5,1},{6,2},{7,3},{8,12},{9,13},{10,... | collective-permute-start | bytes 442376 | tf_op jit(solution)/shard_map/ppermute | solution.py:277
  19.8 6.6 %collective-permute-done.2 = f32[4,72,128]{2,1,0:T(8,128)S(1)} collective-permute-done((f32[4,72,128]{2,1,0:T(8,128)S(1)}, f32[4,72,128]{2,1,0:T(8,128)S(1)}, u32[]{:S(2)}, u32[]{:S(2)}) %collective-permute-start.2) | collective-permute-done | bytes 147488 | tf_op jit(solution)/shard_map/ppermute | solution.py:277
  26.4 0.1 add_select_fusion.5
  26.5 1.4 %collective-permute-start.3 = (f32[4,72,128]{2,1,0:T(8,128)S(1)}, f32[4,72,128]{2,1,0:T(8,128)S(1)}, u32[]{:S(2)}, u32[]{:S(2)}) collective-permute-start(f32[4,72,128]{2,1,0:T(8,128)S(1)} %get-tuple-element.21), channel_id=1, source_target_pairs={{0,8},{1,9},{2,10},{3,11},{4,12},{5,13},{6,14},{7,15},{8,0},{9,1},... | collective-permute-start | bytes 442376 | tf_op jit(solution)/shard_map/ppermute | solution.py:277
  28.0 3.8 %collective-permute-done.3 = f32[4,72,128]{2,1,0:T(8,128)S(1)} collective-permute-done((f32[4,72,128]{2,1,0:T(8,128)S(1)}, f32[4,72,128]{2,1,0:T(8,128)S(1)}, u32[]{:S(2)}, u32[]{:S(2)}) %collective-permute-start.3) | collective-permute-done | bytes 147488 | tf_op jit(solution)/shard_map/ppermute | solution.py:277
  31.8 0.1 add_select_fusion.4
  31.9 1.5 %collective-permute-start.4 = (f32[4,72,128]{2,1,0:T(8,128)S(1)}, f32[4,72,128]{2,1,0:T(8,128)S(1)}, u32[]{:S(2)}, u32[]{:S(2)}) collective-permute-start(f32[4,72,128]{2,1,0:T(8,128)S(1)} %get-tuple-element.19), channel_id=1, source_target_pairs={{0,16},{1,17},{2,18},{3,19},{4,20},{5,21},{6,22},{7,23},{8,24},{9,... | collective-permute-start | bytes 442376 | tf_op jit(solution)/shard_map/ppermute | solution.py:277
  33.4 3.7 %collective-permute-done.4 = f32[4,72,128]{2,1,0:T(8,128)S(1)} collective-permute-done((f32[4,72,128]{2,1,0:T(8,128)S(1)}, f32[4,72,128]{2,1,0:T(8,128)S(1)}, u32[]{:S(2)}, u32[]{:S(2)}) %collective-permute-start.4) | collective-permute-done | bytes 147488 | tf_op jit(solution)/shard_map/ppermute | solution.py:277
  37.1 0.1 fusion.2
  37.2 0.0 copy-done.1
  37.2 0.1 add_select_fusion.3
  37.3 0.1 collective-permute-start.5
  37.4 0.0 copy-done
  37.4 0.0 copy-done.2
  37.4 2.0 %multiply_convert_fusion.q_ref = bf16[384,1024]{1,0:T(8,128)(2,1)} fusion(bf16[384,1024]{1,0:T(8,128)(2,1)S(1)} %copy-done.2, bf16[1024,1024]{1,0:T(8,128)(2,1)S(1)} %copy-done), kind=kOutput, calls=%fused_computation | convolution fusion | flops 807272448 | bytes 3670016 | tf_op jit(solution)/shard_map/dot_general | solution.py:299
  39.5 4.8 %shard_map.74.rest_0_ = f32[384,1024]{1,0:T(8,128)} custom-call(bf16[384,1024]{1,0:T(8,128)(2,1)} %multiply_convert_fusion.q_ref, bf16[384,1024]{1,0:T(8,128)(2,1)} %get-tuple-element.10.k_ref, bf16[384,1024]{1,0:T(8,128)(2,1)} %get-tuple-element.11.v_ref, f32[384,16]{1,0:T(8,128)} %get-tuple-element.12.cum_ref, f32[16,384]{1,0:T(8,128)} %get-tuple-element.13.cum_t_ref), custom_call_target="tpu_custom_call" | custom-call | flops 603979776 | bytes 1966080 | tf_op jit(solution)/shard_map/pallas_call | solution.py:60
  44.2 3.1 %shard_map.75.rest_0_ = f32[384,1024]{1,0:T(8,128)} custom-call(bf16[384,1024]{1,0:T(8,128)(2,1)} %multiply_convert_fusion.q_ref, bf16[384,1024]{1,0:T(8,128)(2,1)} %get-tuple-element.10.k_ref, bf16[384,1024]{1,0:T(8,128)(2,1)} %get-tuple-element.11.v_ref, f32[384,16]{1,0:T(8,128)} %get-tuple-element.12.cum_ref, ...), custom_call_target="tpu_custom_call", output_to_operand_aliasing={{}: (5, {})} | custom-call | flops 301989888 | bytes 983040 | tf_op jit(solution)/shard_map/pallas_call | solution.py:60
  47.3 3.1 %shard_map.76.intra_ref = f32[384,1024]{1,0:T(8,128)} custom-call(bf16[384,1024]{1,0:T(8,128)(2,1)} %multiply_convert_fusion.q_ref, bf16[384,1024]{1,0:T(8,128)(2,1)} %get-tuple-element.10.k_ref, bf16[384,1024]{1,0:T(8,128)(2,1)} %get-tuple-element.11.v_ref, f32[384,16]{1,0:T(8,128)} %get-tuple-element.12.cum_ref, ...), custom_call_target="tpu_custom_call", output_to_operand_aliasing={{}: (5, {})} | custom-call | flops 301989888 | bytes 983040 | tf_op jit(solution)/shard_map/pallas_call | solution.py:60
  50.4 0.0 collective-permute-done.5
  50.4 0.7 %maximum_select_fusion.state_ref = f32[8,72,128]{2,1,0:T(8,128)} fusion(f32[4,72,128]{2,1,0:T(8,128)S(1)} %collective-permute-done.5, f32[4,72,128]{2,1,0:T(8,128)S(1)} %get-tuple-element.16, f32[4,72,128]{2,1,0:T(8,128)S(1)} %get-tuple-element.15, pred[]{:T(512)S(6)} %eq.4), kind=kLoop, calls=%fused_computation.1 | loop fusion | flops 221184 | bytes 737281 | tf_op jit(solution)/shard_map/jit(_where)/select_n | solution.py:285
  51.1 6.8 %shard_map.77 = bf16[384,1024]{1,0:T(8,128)(2,1)} custom-call(bf16[384,1024]{1,0:T(8,128)(2,1)} %multiply_convert_fusion.q_ref, f32[384,1024]{1,0:T(8,128)} %shard_map.76.intra_ref, f32[8,72,128]{2,1,0:T(8,128)} %maximum_select_fusion.state_ref, f32[384,16]{1,0:T(8,128)} %get-tuple-element.12.cum_ref, f32[1,1024]{1,0:T(1,128)} %bitcast.29, ...), custom_call_target="tpu_custom_call" | custom-call | flops 1107296256 | bytes 5242880 | tf_op jit(solution)/shard_map/pallas_call | solution.py:234
  (10 shorter events, 0.1 us)
Async XLA Ops:
  0.0 37.4 %copy-start = (bf16[1024,1024]{1,0:T(8,128)(2,1)S(1)}, bf16[1024,1024]{1,0:T(8,128)(2,1)}, u32[]{:S(2)}) copy-start(bf16[1024,1024]{1,0:T(8,128)(2,1)} %param.9) | copy-start | bytes 6291460
  7.0 1.6 %collective-permute-start = (f32[4,72,128]{2,1,0:T(8,128)S(1)}, f32[4,72,128]{2,1,0:T(8,128)S(1)}, u32[]{:S(2)}, u32[]{:S(2)}) collective-permute-start(f32[4,72,128]{2,1,0:T(8,128)S(1)} %slice_select_fusion), channel_id=1, source_target_pairs={{0,1},{1,0},{2,3},{3,2},{4,5},{5,4},{6,7},{7,6},{8,9},{9,8},{10,11... | collective-permute-start | bytes 442376 | tf_op jit(solution)/shard_map/ppermute | solution.py:270
  9.6 27.6 %copy-start.1 = (f32[8,72,128]{2,1,0:T(8,128)S(1)}, f32[8,72,128]{2,1,0:T(8,128)}, u32[]{:S(2)}) copy-start(f32[8,72,128]{2,1,0:T(8,128)} %get-tuple-element.14) | copy-start | bytes 884740
  9.7 7.2 %collective-permute-start.1 = (f32[4,72,128]{2,1,0:T(8,128)S(1)}, f32[4,72,128]{2,1,0:T(8,128)S(1)}, u32[]{:S(2)}, u32[]{:S(2)}) collective-permute-start(f32[4,72,128]{2,1,0:T(8,128)S(1)} %fusion.1), channel_id=1, source_target_pairs={{0,2},{1,3},{2,0},{3,1},{4,6},{5,7},{6,4},{7,5},{8,10},{9,11},{10,... | collective-permute-start | bytes 442376 | tf_op jit(solution)/shard_map/ppermute | solution.py:277
  16.8 20.6 %copy-start.2 = (bf16[384,1024]{1,0:T(8,128)(2,1)S(1)}, bf16[384,1024]{1,0:T(8,128)(2,1)}, u32[]{:S(2)}) copy-start(bf16[384,1024]{1,0:T(8,128)(2,1)} %x_ref.1) | copy-start | bytes 2359300
  16.9 9.4 %collective-permute-start.2 = (f32[4,72,128]{2,1,0:T(8,128)S(1)}, f32[4,72,128]{2,1,0:T(8,128)S(1)}, u32[]{:S(2)}, u32[]{:S(2)}) collective-permute-start(f32[4,72,128]{2,1,0:T(8,128)S(1)} %get-tuple-element.23), channel_id=1, source_target_pairs={{0,4},{1,5},{2,6},{3,7},{4,0},{5,1},{6,2},{7,3},{8,12},{9,13},{10,... | collective-permute-start | bytes 442376 | tf_op jit(solution)/shard_map/ppermute | solution.py:277
  26.5 5.2 %collective-permute-start.3 = (f32[4,72,128]{2,1,0:T(8,128)S(1)}, f32[4,72,128]{2,1,0:T(8,128)S(1)}, u32[]{:S(2)}, u32[]{:S(2)}) collective-permute-start(f32[4,72,128]{2,1,0:T(8,128)S(1)} %get-tuple-element.21), channel_id=1, source_target_pairs={{0,8},{1,9},{2,10},{3,11},{4,12},{5,13},{6,14},{7,15},{8,0},{9,1},... | collective-permute-start | bytes 442376 | tf_op jit(solution)/shard_map/ppermute | solution.py:277
  31.9 5.2 %collective-permute-start.4 = (f32[4,72,128]{2,1,0:T(8,128)S(1)}, f32[4,72,128]{2,1,0:T(8,128)S(1)}, u32[]{:S(2)}, u32[]{:S(2)}) collective-permute-start(f32[4,72,128]{2,1,0:T(8,128)S(1)} %get-tuple-element.19), channel_id=1, source_target_pairs={{0,16},{1,17},{2,18},{3,19},{4,20},{5,21},{6,22},{7,23},{8,24},{9,... | collective-permute-start | bytes 442376 | tf_op jit(solution)/shard_map/ppermute | solution.py:277
  37.3 13.1 %collective-permute-start.5 = (f32[4,72,128]{2,1,0:T(8,128)S(1)}, f32[4,72,128]{2,1,0:T(8,128)S(1)}, u32[]{:S(2)}, u32[]{:S(2)}) collective-permute-start(f32[4,72,128]{2,1,0:T(8,128)S(1)} %add_select_fusion.3), channel_id=1, source_target_pairs={{0,1},{1,0},{2,3},{3,2},{4,5},{5,4},{6,7},{7,6},{8,9},{9,8},{10,11... | collective-permute-start | bytes 442376 | tf_op jit(solution)/shard_map/ppermute | solution.py:284

commit v17 on v16

--- a/solution.py
+++ b/solution.py
@@ -229,7 +229,7 @@
     heads = cum.shape[1]
     pairs = width // LANES
     out_width = output_weight.shape[1]
-    per = 2 if pairs % 2 == 0 else 1
+    per = pairs
     block = pl.BlockSpec((rows, per * LANES), lambda p: (0, p))
     return pl.pallas_call(
         functools.partial(finish_kernel, head_dim=head_dim),
@@ -267,7 +267,8 @@
     chips = count // 2
     half = own.shape[0] // 2
     partner = [(i, i ^ 1) for i in range(count)]
-    got = lax.ppermute(jnp.where(core == 0, own[half:], own[:half]), AXES, partner)
+    other = lax.ppermute(own, AXES, partner)
+    got = jnp.where(core == 0, other[:half], other[half:])
     through = jnp.where(core == 0, combine(own[:half], got), combine(got, own[half:]))
     before = jnp.zeros_like(through)
     received = []

time: 58.4 us -> 56.9 us (0.974)
  other arithmetic: 3.42 us -> 2.42 us
  Pallas kernels: 23.7 us -> 23 us
    select_n x1, other arithmetic: 1 us -> 0.02 us  [exclusive_scan(): got = jnp.where(core == 0, other[:half], other[half:])]
    pallas_call x1, Pallas kernels: 6.82 us -> 6.07 us  [finish(): pl.pallas_call(functools.partial(finish_kernel, head_dim=head_dim), grid=...]
where the time goes in v17:
time: 56.9 us; the launch traced here: 56.6 us
  Pallas kernels  23 us (40%)
  waiting for transfers between devices  18.9 us (33%)
  starting transfers between devices  9.28 us (16%)
  other arithmetic  2.42 us (4%)
  matrix products  2.04 us (4%)
  local copies, waits for them, and re-layouts  0.83 us (1%)
    ppermute x4, waiting for transfers between devices, exclusive_scan(): exchanged = lax.ppermute(through, AXES, perm)  18.2 us
    pallas_call x3, Pallas kernels, intra_attention(): pl.pallas_call(functools.partial(intra_kernel, head_dim=head_dim, first=f...  10.9 us
    ppermute x4, starting transfers between devices, exclusive_scan(): exchanged = lax.ppermute(through, AXES, perm)  8.73 us
    pallas_call x1, Pallas kernels, finish(): pl.pallas_call(functools.partial(finish_kernel, head_dim=head_dim), grid=...  6.07 us
    pallas_call x1, Pallas kernels, project_keys_values(): pl.pallas_call(functools.partial(project_kernel, head_dim=head_dim), grid...  5.97 us
    dot_general x1, matrix products, layer(): jnp.dot(tokens, query_weight, preferred_element_type=f32)  2.04 us
  transfers between devices with their start and end apart: 6, of which 5 were waited for; matrix products, arithmetic and copies ran while one was open for 5% of the time, Pallas kernels for 19%

profile of v17, /device:TPU:0, one launch (start us, length us, event | category | flops | bytes accessed | tf_op | source)
XLA Modules:
  0.0 56.6 jit_solution(16201205414074553102)
XLA Ops:
  0.0 0.0 copy-start
  0.0 6.0 %shard_map.73 = (bf16[384,1024]{1,0:T(8,128)(2,1)}, bf16[384,1024]{1,0:T(8,128)(2,1)}, f32[8,72,128]{2,1,0:T(8,128)}, f32[384,16]{1,0:T(8,128)}, f32[16,384]{1,0:T(8,128)}) custom-call(bf16[384,1024]{1,0:T(8,128)(2,1)} %x_ref.1, bf16[1024,1024]{1,0:T(8,128)(2,1)} %wk_ref.1, bf16[1024,1024]{1,0:T(8,128)(2,1)} %wv_ref.1, f32[16,384]{1,0:T(8,128)} %bitcast.30), custom_call_target="tpu_custom_call" | custom-call | flops 1711276032 | bytes 6553600 | tf_op jit(solution)/shard_map/pallas_call | solution.py:144
  6.0 0.5 collective-permute-start
  6.5 0.7 %slice_exponential_fusion.10 = (f32[4,1,128]{2,1,0:T(1,128)S(1)}, f32[4,1,128]{2,1,0:T(1,128)S(1)}) fusion(f32[8,72,128]{2,1,0:T(8,128)} %get-tuple-element.14), kind=kLoop, calls=%fused_computation.26 | loop fusion | bytes 8192 | tf_op jit(solution)/shard_map/exp | solution.py:259
  7.2 0.7 %collective-permute-done = f32[8,72,128]{2,1,0:T(8,128)S(1)} collective-permute-done((f32[8,72,128]{2,1,0:T(8,128)}, f32[8,72,128]{2,1,0:T(8,128)S(1)}, u32[]{:S(2)}, u32[]{:S(2)}) %collective-permute-start) | collective-permute-done | bytes 294944 | tf_op jit(solution)/shard_map/ppermute | solution.py:270
  7.9 1.1 %fusion.1 = f32[4,72,128]{2,1,0:T(8,128)S(1)} fusion(f32[8,72,128]{2,1,0:T(8,128)} %get-tuple-element.14, f32[4,128]{1,0:T(4,128)S(1)} %bitcast.28, f32[4,128]{1,0:T(4,128)S(1)} %bitcast.16, pred[72]{0:T(512)(128)(4,1)S(1)} %iota_compare_fusion, pred[]{:T(512)S(6)} %eq.4, f32[8,72,128]{2,1,0:T(8,128)S(1)} %collective-permute-done), kind=kLoop, calls=%fused_computation.8 | loop fusion | flops 294912 | bytes 741449 | tf_op jit(solution)/shard_map/jit(_where)/select_n | solution.py:272
  9.0 0.0 copy-start.1
  9.0 3.0 %collective-permute-start.1 = (f32[4,72,128]{2,1,0:T(8,128)S(1)}, f32[4,72,128]{2,1,0:T(8,128)S(1)}, u32[]{:S(2)}, u32[]{:S(2)}) collective-permute-start(f32[4,72,128]{2,1,0:T(8,128)S(1)} %fusion.1), channel_id=1, source_target_pairs={{0,2},{1,3},{2,0},{3,1},{4,6},{5,7},{6,4},{7,5},{8,10},{9,11},{10,... | collective-permute-start | bytes 442376 | tf_op jit(solution)/shard_map/ppermute | solution.py:278
  12.0 4.1 %collective-permute-done.1 = f32[4,72,128]{2,1,0:T(8,128)S(1)} collective-permute-done((f32[4,72,128]{2,1,0:T(8,128)S(1)}, f32[4,72,128]{2,1,0:T(8,128)S(1)}, u32[]{:S(2)}, u32[]{:S(2)}) %collective-permute-start.1) | collective-permute-done | bytes 147488 | tf_op jit(solution)/shard_map/ppermute | solution.py:278
  16.2 0.1 add_select_fusion.6
  16.3 0.0 copy-start.2
  16.3 2.8 %collective-permute-start.2 = (f32[4,72,128]{2,1,0:T(8,128)S(1)}, f32[4,72,128]{2,1,0:T(8,128)S(1)}, u32[]{:S(2)}, u32[]{:S(2)}) collective-permute-start(f32[4,72,128]{2,1,0:T(8,128)S(1)} %get-tuple-element.23), channel_id=1, source_target_pairs={{0,4},{1,5},{2,6},{3,7},{4,0},{5,1},{6,2},{7,3},{8,12},{9,13},{10,... | collective-permute-start | bytes 442376 | tf_op jit(solution)/shard_map/ppermute | solution.py:278
  19.1 6.6 %collective-permute-done.2 = f32[4,72,128]{2,1,0:T(8,128)S(1)} collective-permute-done((f32[4,72,128]{2,1,0:T(8,128)S(1)}, f32[4,72,128]{2,1,0:T(8,128)S(1)}, u32[]{:S(2)}, u32[]{:S(2)}) %collective-permute-start.2) | collective-permute-done | bytes 147488 | tf_op jit(solution)/shard_map/ppermute | solution.py:278
  25.8 0.1 add_select_fusion.5
  25.9 1.4 %collective-permute-start.3 = (f32[4,72,128]{2,1,0:T(8,128)S(1)}, f32[4,72,128]{2,1,0:T(8,128)S(1)}, u32[]{:S(2)}, u32[]{:S(2)}) collective-permute-start(f32[4,72,128]{2,1,0:T(8,128)S(1)} %get-tuple-element.21), channel_id=1, source_target_pairs={{0,8},{1,9},{2,10},{3,11},{4,12},{5,13},{6,14},{7,15},{8,0},{9,1},... | collective-permute-start | bytes 442376 | tf_op jit(solution)/shard_map/ppermute | solution.py:278
  27.4 3.8 %collective-permute-done.3 = f32[4,72,128]{2,1,0:T(8,128)S(1)} collective-permute-done((f32[4,72,128]{2,1,0:T(8,128)S(1)}, f32[4,72,128]{2,1,0:T(8,128)S(1)}, u32[]{:S(2)}, u32[]{:S(2)}) %collective-permute-start.3) | collective-permute-done | bytes 147488 | tf_op jit(solution)/shard_map/ppermute | solution.py:278
  31.1 0.1 add_select_fusion.4
  31.3 1.5 %collective-permute-start.4 = (f32[4,72,128]{2,1,0:T(8,128)S(1)}, f32[4,72,128]{2,1,0:T(8,128)S(1)}, u32[]{:S(2)}, u32[]{:S(2)}) collective-permute-start(f32[4,72,128]{2,1,0:T(8,128)S(1)} %get-tuple-element.19), channel_id=1, source_target_pairs={{0,16},{1,17},{2,18},{3,19},{4,20},{5,21},{6,22},{7,23},{8,24},{9,... | collective-permute-start | bytes 442376 | tf_op jit(solution)/shard_map/ppermute | solution.py:278
  32.7 3.7 %collective-permute-done.4 = f32[4,72,128]{2,1,0:T(8,128)S(1)} collective-permute-done((f32[4,72,128]{2,1,0:T(8,128)S(1)}, f32[4,72,128]{2,1,0:T(8,128)S(1)}, u32[]{:S(2)}, u32[]{:S(2)}) %collective-permute-start.4) | collective-permute-done | bytes 147488 | tf_op jit(solution)/shard_map/ppermute | solution.py:278
  36.5 0.1 fusion.2
  36.6 0.0 copy-done.1
  36.6 0.1 add_select_fusion.3
  36.7 0.1 collective-permute-start.5
  36.8 0.0 copy-done
  36.8 0.0 copy-done.2
  36.8 2.0 %multiply_convert_fusion.q_ref = bf16[384,1024]{1,0:T(8,128)(2,1)} fusion(bf16[384,1024]{1,0:T(8,128)(2,1)S(1)} %copy-done.2, bf16[1024,1024]{1,0:T(8,128)(2,1)S(1)} %copy-done), kind=kOutput, calls=%fused_computation | convolution fusion | flops 807272448 | bytes 3670016 | tf_op jit(solution)/shard_map/dot_general | solution.py:300
  38.8 4.8 %shard_map.74.rest_0_ = f32[384,1024]{1,0:T(8,128)} custom-call(bf16[384,1024]{1,0:T(8,128)(2,1)} %multiply_convert_fusion.q_ref, bf16[384,1024]{1,0:T(8,128)(2,1)} %get-tuple-element.10.k_ref, bf16[384,1024]{1,0:T(8,128)(2,1)} %get-tuple-element.11.v_ref, f32[384,16]{1,0:T(8,128)} %get-tuple-element.12.cum_ref, f32[16,384]{1,0:T(8,128)} %get-tuple-element.13.cum_t_ref), custom_call_target="tpu_custom_call" | custom-call | flops 603979776 | bytes 1966080 | tf_op jit(solution)/shard_map/pallas_call | solution.py:60
  43.6 3.1 %shard_map.75.rest_0_ = f32[384,1024]{1,0:T(8,128)} custom-call(bf16[384,1024]{1,0:T(8,128)(2,1)} %multiply_convert_fusion.q_ref, bf16[384,1024]{1,0:T(8,128)(2,1)} %get-tuple-element.10.k_ref, bf16[384,1024]{1,0:T(8,128)(2,1)} %get-tuple-element.11.v_ref, f32[384,16]{1,0:T(8,128)} %get-tuple-element.12.cum_ref, ...), custom_call_target="tpu_custom_call", output_to_operand_aliasing={{}: (5, {})} | custom-call | flops 301989888 | bytes 983040 | tf_op jit(solution)/shard_map/pallas_call | solution.py:60
  46.7 3.1 %shard_map.76.intra_ref = f32[384,1024]{1,0:T(8,128)} custom-call(bf16[384,1024]{1,0:T(8,128)(2,1)} %multiply_convert_fusion.q_ref, bf16[384,1024]{1,0:T(8,128)(2,1)} %get-tuple-element.10.k_ref, bf16[384,1024]{1,0:T(8,128)(2,1)} %get-tuple-element.11.v_ref, f32[384,16]{1,0:T(8,128)} %get-tuple-element.12.cum_ref, ...), custom_call_target="tpu_custom_call", output_to_operand_aliasing={{}: (5, {})} | custom-call | flops 301989888 | bytes 983040 | tf_op jit(solution)/shard_map/pallas_call | solution.py:60
  49.7 0.0 collective-permute-done.5
  49.8 0.7 %maximum_select_fusion.state_ref = f32[8,72,128]{2,1,0:T(8,128)} fusion(f32[4,72,128]{2,1,0:T(8,128)S(1)} %collective-permute-done.5, f32[4,72,128]{2,1,0:T(8,128)S(1)} %get-tuple-element.16, f32[4,72,128]{2,1,0:T(8,128)S(1)} %get-tuple-element.15, pred[]{:T(512)S(6)} %eq.4), kind=kLoop, calls=%fused_computation.1 | loop fusion | flops 221184 | bytes 737281 | tf_op jit(solution)/shard_map/jit(_where)/select_n | solution.py:286
  50.5 6.1 %shard_map.77 = bf16[384,1024]{1,0:T(8,128)(2,1)} custom-call(bf16[384,1024]{1,0:T(8,128)(2,1)} %multiply_convert_fusion.q_ref, f32[384,1024]{1,0:T(8,128)} %shard_map.76.intra_ref, f32[8,72,128]{2,1,0:T(8,128)} %maximum_select_fusion.state_ref, f32[384,16]{1,0:T(8,128)} %get-tuple-element.12.cum_ref, f32[1,1024]{1,0:T(1,128)} %bitcast.29, ...), custom_call_target="tpu_custom_call" | custom-call | flops 1107296256 | bytes 5242880 | tf_op jit(solution)/shard_map/pallas_call | solution.py:234
  (11 shorter events, 0.1 us)
Async XLA Ops:
  0.0 36.8 %copy-start = (bf16[1024,1024]{1,0:T(8,128)(2,1)S(1)}, bf16[1024,1024]{1,0:T(8,128)(2,1)}, u32[]{:S(2)}) copy-start(bf16[1024,1024]{1,0:T(8,128)(2,1)} %param.9) | copy-start | bytes 6291460
  6.0 1.9 %collective-permute-start = (f32[8,72,128]{2,1,0:T(8,128)}, f32[8,72,128]{2,1,0:T(8,128)S(1)}, u32[]{:S(2)}, u32[]{:S(2)}) collective-permute-start(f32[8,72,128]{2,1,0:T(8,128)} %get-tuple-element.14), channel_id=1, source_target_pairs={{0,1},{1,0},{2,3},{3,2},{4,5},{5,4},{6,7},{7,6},{8,9},{9,8},{10,11... | collective-permute-start | bytes 884744 | tf_op jit(solution)/shard_map/ppermute | solution.py:270
  9.0 27.6 %copy-start.1 = (f32[8,72,128]{2,1,0:T(8,128)S(1)}, f32[8,72,128]{2,1,0:T(8,128)}, u32[]{:S(2)}) copy-start(f32[8,72,128]{2,1,0:T(8,128)} %get-tuple-element.14) | copy-start | bytes 884740
  9.0 7.2 %collective-permute-start.1 = (f32[4,72,128]{2,1,0:T(8,128)S(1)}, f32[4,72,128]{2,1,0:T(8,128)S(1)}, u32[]{:S(2)}, u32[]{:S(2)}) collective-permute-start(f32[4,72,128]{2,1,0:T(8,128)S(1)} %fusion.1), channel_id=1, source_target_pairs={{0,2},{1,3},{2,0},{3,1},{4,6},{5,7},{6,4},{7,5},{8,10},{9,11},{10,... | collective-permute-start | bytes 442376 | tf_op jit(solution)/shard_map/ppermute | solution.py:278
  16.3 20.5 %copy-start.2 = (bf16[384,1024]{1,0:T(8,128)(2,1)S(1)}, bf16[384,1024]{1,0:T(8,128)(2,1)}, u32[]{:S(2)}) copy-start(bf16[384,1024]{1,0:T(8,128)(2,1)} %x_ref.1) | copy-start | bytes 2359300
  16.3 9.4 %collective-permute-start.2 = (f32[4,72,128]{2,1,0:T(8,128)S(1)}, f32[4,72,128]{2,1,0:T(8,128)S(1)}, u32[]{:S(2)}, u32[]{:S(2)}) collective-permute-start(f32[4,72,128]{2,1,0:T(8,128)S(1)} %get-tuple-element.23), channel_id=1, source_target_pairs={{0,4},{1,5},{2,6},{3,7},{4,0},{5,1},{6,2},{7,3},{8,12},{9,13},{10,... | collective-permute-start | bytes 442376 | tf_op jit(solution)/shard_map/ppermute | solution.py:278
  25.9 5.2 %collective-permute-start.3 = (f32[4,72,128]{2,1,0:T(8,128)S(1)}, f32[4,72,128]{2,1,0:T(8,128)S(1)}, u32[]{:S(2)}, u32[]{:S(2)}) collective-permute-start(f32[4,72,128]{2,1,0:T(8,128)S(1)} %get-tuple-element.21), channel_id=1, source_target_pairs={{0,8},{1,9},{2,10},{3,11},{4,12},{5,13},{6,14},{7,15},{8,0},{9,1},... | collective-permute-start | bytes 442376 | tf_op jit(solution)/shard_map/ppermute | solution.py:278
  31.3 5.2 %collective-permute-start.4 = (f32[4,72,128]{2,1,0:T(8,128)S(1)}, f32[4,72,128]{2,1,0:T(8,128)S(1)}, u32[]{:S(2)}, u32[]{:S(2)}) collective-permute-start(f32[4,72,128]{2,1,0:T(8,128)S(1)} %get-tuple-element.19), channel_id=1, source_target_pairs={{0,16},{1,17},{2,18},{3,19},{4,20},{5,21},{6,22},{7,23},{8,24},{9,... | collective-permute-start | bytes 442376 | tf_op jit(solution)/shard_map/ppermute | solution.py:278
  36.7 13.1 %collective-permute-start.5 = (f32[4,72,128]{2,1,0:T(8,128)S(1)}, f32[4,72,128]{2,1,0:T(8,128)S(1)}, u32[]{:S(2)}, u32[]{:S(2)}) collective-permute-start(f32[4,72,128]{2,1,0:T(8,128)S(1)} %add_select_fusion.3), channel_id=1, source_target_pairs={{0,1},{1,0},{2,3},{3,2},{4,5},{5,4},{6,7},{7,6},{8,9},{9,8},{10,11... | collective-permute-start | bytes 442376 | tf_op jit(solution)/shard_map/ppermute | solution.py:285

commit v18 on v17

--- a/solution.py
+++ b/solution.py
@@ -106,7 +106,6 @@
 def project_kernel(x_ref, wk_ref, wv_ref, g_ref, k_ref, v_ref, o_ref, cum_ref, cum_t_ref, *, head_dim):
     f32 = jnp.float32
     bf16 = jnp.bfloat16
-
     @pl.when(pl.program_id(0) == 0)
     def _():
         rows = g_ref.shape[1]
@@ -172,33 +171,29 @@
     )(tokens, key_weight, value_weight, log_decay.T)
 
 
-def finish_kernel(q_ref, intra_ref, state_ref, cum_ref, gain_ref, w_ref, o_ref, normed_ref, acc_ref, *, head_dim):
-    for step in range(state_ref.shape[0]):
-        finish_pair(q_ref, intra_ref, state_ref, cum_ref, gain_ref, normed_ref, head_dim, step)
-    part = jnp.dot(normed_ref[...], w_ref[...], preferred_element_type=jnp.float32)
-    index = pl.program_id(0)
-
-    @pl.when(index == 0)
-    def _():
-        acc_ref[...] = part
-
-    @pl.when(index > 0)
-    def _():
-        acc_ref[...] += part
-
-    @pl.when(index == pl.num_programs(0) - 1)
-    def _():
-        o_ref[...] = acc_ref[...].astype(o_ref.dtype)
-
-
-def finish_pair(q_ref, intra_ref, state_ref, cum_ref, gain_ref, o_ref, head_dim, step):
+def finish_kernel(
+    core_ref, q_ref, intra_ref, mine_ref, back_ref, mixed_ref, cum_ref, gain_ref, w_ref, o_ref, normed_ref, *, head_dim
+):
+    head_dim_rows = slice(0, head_dim)
+    half = mine_ref.shape[0]
+    first = core_ref[0] == 0
+    for step in range(2 * half):
+        if step < half:
+            state = jnp.where(first, mine_ref[step, head_dim_rows, :], back_ref[step, head_dim_rows, :])
+        else:
+            other = step - half
+            state = jnp.where(first, back_ref[other, head_dim_rows, :], mixed_ref[other, head_dim_rows, :])
+        finish_pair(q_ref, intra_ref, state, cum_ref, gain_ref, normed_ref, head_dim, step)
+    o_ref[...] = jnp.dot(normed_ref[...], w_ref[...], preferred_element_type=jnp.float32).astype(o_ref.dtype)
+
+
+def finish_pair(q_ref, intra_ref, state, cum_ref, gain_ref, o_ref, head_dim, step):
     f32 = jnp.float32
     bf16 = jnp.bfloat16
-    pair = pl.program_id(0) * state_ref.shape[0] + step
+    pair = step
     cols = pl.ds(step * LANES, LANES)
     group = LANES // head_dim
     rows = q_ref.shape[0]
-    state = state_ref[step, :head_dim, :]
     tall = jnp.concatenate([state] * group, axis=0)
     r_head = lax.broadcasted_iota(jnp.int32, (LANES, LANES), 0) // head_dim
     c_head = lax.broadcasted_iota(jnp.int32, (LANES, LANES), 1) // head_dim
@@ -224,33 +219,27 @@
     o_ref[:, cols] = (attended * scale * gain_ref[:, cols]).astype(bf16)
 
 
-def finish(queries, intra, states, cum, norm_gain, output_weight, head_dim):
+def finish(queries, intra, states, core, cum, norm_gain, output_weight, head_dim):
     rows, width = queries.shape
     heads = cum.shape[1]
     pairs = width // LANES
     out_width = output_weight.shape[1]
-    per = pairs
-    block = pl.BlockSpec((rows, per * LANES), lambda p: (0, p))
+    whole = lambda shape: pl.BlockSpec(shape, lambda p: (0,) * len(shape))
     return pl.pallas_call(
         functools.partial(finish_kernel, head_dim=head_dim),
-        grid=(pairs // per,),
-        in_specs=[
-            block,
-            block,
-            pl.BlockSpec((per,) + states.shape[1:], lambda p: (p, 0, 0)),
-            pl.BlockSpec((rows, heads), lambda p: (0, 0)),
-            pl.BlockSpec((1, per * LANES), lambda p: (0, p)),
-            pl.BlockSpec((per * LANES, out_width), lambda p: (p, 0)),
-        ],
-        out_specs=pl.BlockSpec((rows, out_width), lambda p: (0, 0)),
+        grid=(1,),
+        in_specs=[pl.BlockSpec(memory_space=pltpu.SMEM), whole((rows, width)), whole((rows, width))]
+        + [whole(part.shape) for part in states]
+        + [whole((rows, heads)), whole((1, width)), whole((width, out_width))],
+        out_specs=whole((rows, out_width)),
         out_shape=jax.ShapeDtypeStruct((rows, out_width), jnp.bfloat16),
-        scratch_shapes=[pltpu.VMEM((rows, per * LANES), jnp.bfloat16), pltpu.VMEM((rows, out_width), jnp.float32)],
+        scratch_shapes=[pltpu.VMEM((rows, width), jnp.bfloat16)],
         cost_estimate=pl.CostEstimate(
             flops=6 * rows * LANES * LANES * pairs + 2 * rows * width * out_width,
             transcendentals=rows * heads * 2,
             bytes_accessed=rows * width * 8 + width * out_width * 2,
         ),
-    )(queries, intra, states, cum, norm_gain.reshape(1, width), output_weight)
+    )(jnp.reshape(core, (1,)).astype(jnp.int32), queries, intra, *states, cum, norm_gain.reshape(1, width), output_weight)
 
 
 def combine(earlier, later):
@@ -283,10 +272,7 @@
         if bit < chips:
             through = jnp.where(lower, combine(exchanged, through), combine(through, exchanged))
     back = lax.ppermute(jnp.where(core == 0, combine(before, own[:half]), before), AXES, partner)
-    whole = jnp.where(
-        core == 0, jnp.concatenate([before, back]), jnp.concatenate([back, combine(before, got)])
-    )
-    return whole, received
+    return (before, back, combine(before, got)), received
 
 
 def layer(count, tokens, log_decay, query_weight, key_weight, value_weight, norm_gain, output_weight):
@@ -295,7 +281,7 @@
     heads = log_decay.shape[1]
     dim = key_weight.shape[1] // heads
     keys, value_rows, packed, cum, cum_t = project_keys_values(tokens, key_weight, value_weight, log_decay, dim)
-    incoming, _ = exclusive_scan(packed, count)
+    states, _ = exclusive_scan(packed, count)
 
     queries = jax.nn.silu(jnp.dot(tokens, query_weight, preferred_element_type=f32)).astype(bf16)
     blocks = keys.shape[1] // LANES
@@ -303,7 +289,8 @@
     cuts = (0, blocks // 2, (3 * blocks) // 4, blocks)
     for part in range(3):
         intra = intra_attention(queries, keys, value_rows, cum, cum_t, dim, cuts[part], cuts[part + 1], intra)
-    return finish(queries, intra, incoming, cum, norm_gain, output_weight, dim)
+    core = lax.axis_index(AXES) % 2
+    return finish(queries, intra, states, core, cum, norm_gain, output_weight, dim)
 
 
 def solution(mesh):

time: 56.9 us -> 57.5 us (1.011)
  local copies, waits for them, and re-layouts: 0.83 us -> 1.49 us
    select_n x1 -> x0, other arithmetic: 0.75 us -> none  [exclusive_scan(): jnp.where(core == 0, jnp.concatenate([before, back]), jnp.concatenate([ba...]
    unnamed x6 -> x10, local copies, waits for them, and re-layouts: 0.01 us -> 0.68 us
    add x1, other arithmetic: 0.11 us -> 0.75 us  [combine(): return scale * earlier + later]
where the time goes in v18:
time: 57.5 us; the launch traced here: 57.2 us
  Pallas kernels  23 us (40%)
  waiting for transfers between devices  18.9 us (33%)
  starting transfers between devices  9.28 us (16%)
  other arithmetic  2.32 us (4%)
  matrix products  2.05 us (4%)
  local copies, waits for them, and re-layouts  1.49 us (3%)
    ppermute x4, waiting for transfers between devices, exclusive_scan(): exchanged = lax.ppermute(through, AXES, perm)  18.2 us
    pallas_call x3, Pallas kernels, intra_attention(): pl.pallas_call(functools.partial(intra_kernel, head_dim=head_dim, first=f...  10.9 us
    ppermute x4, starting transfers between devices, exclusive_scan(): exchanged = lax.ppermute(through, AXES, perm)  8.73 us
    pallas_call x1, Pallas kernels, finish(): pl.pallas_call(functools.partial(finish_kernel, head_dim=head_dim), grid=...  6.13 us
    pallas_call x1, Pallas kernels, project_keys_values(): pl.pallas_call(functools.partial(project_kernel, head_dim=head_dim), grid...  5.98 us
    dot_general x1, matrix products, layer(): jnp.dot(tokens, query_weight, preferred_element_type=f32)  2.05 us
  transfers between devices with their start and end apart: 6, of which 5 were waited for; matrix products, arithmetic and copies ran while one was open for 5% of the time, Pallas kernels for 19%

profile of v18, /device:TPU:0, one launch (start us, length us, event | category | flops | bytes accessed | tf_op | source)
XLA Modules:
  0.0 57.2 jit_solution(14771551180881141453)
XLA Ops:
  0.0 0.0 copy-start
  0.0 6.0 %shard_map.73 = (bf16[384,1024]{1,0:T(8,128)(2,1)}, bf16[384,1024]{1,0:T(8,128)(2,1)}, f32[8,72,128]{2,1,0:T(8,128)}, f32[384,16]{1,0:T(8,128)}, f32[16,384]{1,0:T(8,128)}) custom-call(bf16[384,1024]{1,0:T(8,128)(2,1)} %x_ref.1, bf16[1024,1024]{1,0:T(8,128)(2,1)} %wk_ref.1, bf16[1024,1024]{1,0:T(8,128)(2,1)} %wv_ref.1, f32[16,384]{1,0:T(8,128)} %bitcast.31), custom_call_target="tpu_custom_call" | custom-call | flops 1711276032 | bytes 6553600 | tf_op jit(solution)/shard_map/pallas_call | solution.py:143
  6.0 0.5 collective-permute-start
  6.5 0.7 %slice_exponential_fusion.10 = (f32[4,1,128]{2,1,0:T(1,128)S(1)}, f32[4,1,128]{2,1,0:T(1,128)S(1)}) fusion(f32[8,72,128]{2,1,0:T(8,128)} %get-tuple-element.14), kind=kLoop, calls=%fused_computation.25 | loop fusion | bytes 8192 | tf_op jit(solution)/shard_map/exp | solution.py:248
  7.2 0.7 %collective-permute-done = f32[8,72,128]{2,1,0:T(8,128)S(1)} collective-permute-done((f32[8,72,128]{2,1,0:T(8,128)}, f32[8,72,128]{2,1,0:T(8,128)S(1)}, u32[]{:S(2)}, u32[]{:S(2)}) %collective-permute-start) | collective-permute-done | bytes 294944 | tf_op jit(solution)/shard_map/ppermute | solution.py:259
  7.9 1.1 %fusion.1 = f32[4,72,128]{2,1,0:T(8,128)S(1)} fusion(f32[8,72,128]{2,1,0:T(8,128)} %get-tuple-element.14, f32[4,128]{1,0:T(4,128)S(1)} %bitcast.29, f32[4,128]{1,0:T(4,128)S(1)} %bitcast.17, pred[72]{0:T(512)(128)(4,1)S(1)} %iota_compare_fusion, pred[]{:T(512)S(6)} %eq.8, f32[8,72,128]{2,1,0:T(8,128)S(1)} %collective-permute-done), kind=kLoop, calls=%fused_computation.7 | loop fusion | flops 294912 | bytes 741449 | tf_op jit(solution)/shard_map/jit(_where)/select_n | solution.py:261
  9.0 0.0 copy-start.2
  9.0 3.0 %collective-permute-start.1 = (f32[4,72,128]{2,1,0:T(8,128)S(1)}, f32[4,72,128]{2,1,0:T(8,128)S(1)}, u32[]{:S(2)}, u32[]{:S(2)}) collective-permute-start(f32[4,72,128]{2,1,0:T(8,128)S(1)} %fusion.1), channel_id=1, source_target_pairs={{0,2},{1,3},{2,0},{3,1},{4,6},{5,7},{6,4},{7,5},{8,10},{9,11},{10,... | collective-permute-start | bytes 442376 | tf_op jit(solution)/shard_map/ppermute | solution.py:267
  12.0 4.1 %collective-permute-done.1 = f32[4,72,128]{2,1,0:T(8,128)S(1)} collective-permute-done((f32[4,72,128]{2,1,0:T(8,128)S(1)}, f32[4,72,128]{2,1,0:T(8,128)S(1)}, u32[]{:S(2)}, u32[]{:S(2)}) %collective-permute-start.1) | collective-permute-done | bytes 147488 | tf_op jit(solution)/shard_map/ppermute | solution.py:267
  16.2 0.1 add_select_fusion.6
  16.3 0.0 copy-start.4
  16.3 2.8 %collective-permute-start.2 = (f32[4,72,128]{2,1,0:T(8,128)S(1)}, f32[4,72,128]{2,1,0:T(8,128)S(1)}, u32[]{:S(2)}, u32[]{:S(2)}) collective-permute-start(f32[4,72,128]{2,1,0:T(8,128)S(1)} %get-tuple-element.23), channel_id=1, source_target_pairs={{0,4},{1,5},{2,6},{3,7},{4,0},{5,1},{6,2},{7,3},{8,12},{9,13},{10,... | collective-permute-start | bytes 442376 | tf_op jit(solution)/shard_map/ppermute | solution.py:267
  19.2 6.6 %collective-permute-done.2 = f32[4,72,128]{2,1,0:T(8,128)S(1)} collective-permute-done((f32[4,72,128]{2,1,0:T(8,128)S(1)}, f32[4,72,128]{2,1,0:T(8,128)S(1)}, u32[]{:S(2)}, u32[]{:S(2)}) %collective-permute-start.2) | collective-permute-done | bytes 147488 | tf_op jit(solution)/shard_map/ppermute | solution.py:267
  25.8 0.1 add_select_fusion.5
  25.9 1.4 %collective-permute-start.3 = (f32[4,72,128]{2,1,0:T(8,128)S(1)}, f32[4,72,128]{2,1,0:T(8,128)S(1)}, u32[]{:S(2)}, u32[]{:S(2)}) collective-permute-start(f32[4,72,128]{2,1,0:T(8,128)S(1)} %get-tuple-element.21), channel_id=1, source_target_pairs={{0,8},{1,9},{2,10},{3,11},{4,12},{5,13},{6,14},{7,15},{8,0},{9,1},... | collective-permute-start | bytes 442376 | tf_op jit(solution)/shard_map/ppermute | solution.py:267
  27.4 3.8 %collective-permute-done.3 = f32[4,72,128]{2,1,0:T(8,128)S(1)} collective-permute-done((f32[4,72,128]{2,1,0:T(8,128)S(1)}, f32[4,72,128]{2,1,0:T(8,128)S(1)}, u32[]{:S(2)}, u32[]{:S(2)}) %collective-permute-start.3) | collective-permute-done | bytes 147488 | tf_op jit(solution)/shard_map/ppermute | solution.py:267
  31.1 0.1 add_select_fusion.4
  31.3 1.5 %collective-permute-start.4 = (f32[4,72,128]{2,1,0:T(8,128)S(1)}, f32[4,72,128]{2,1,0:T(8,128)S(1)}, u32[]{:S(2)}, u32[]{:S(2)}) collective-permute-start(f32[4,72,128]{2,1,0:T(8,128)S(1)} %get-tuple-element.19), channel_id=1, source_target_pairs={{0,16},{1,17},{2,18},{3,19},{4,20},{5,21},{6,22},{7,23},{8,24},{9,... | collective-permute-start | bytes 442376 | tf_op jit(solution)/shard_map/ppermute | solution.py:267
  32.7 3.7 %collective-permute-done.4 = f32[4,72,128]{2,1,0:T(8,128)S(1)} collective-permute-done((f32[4,72,128]{2,1,0:T(8,128)S(1)}, f32[4,72,128]{2,1,0:T(8,128)S(1)}, u32[]{:S(2)}, u32[]{:S(2)}) %collective-permute-start.4) | collective-permute-done | bytes 147488 | tf_op jit(solution)/shard_map/ppermute | solution.py:267
  36.5 0.7 %fusion.2 = (f32[4,72,128]{2,1,0:T(8,128)}, f32[4,72,128]{2,1,0:T(8,128)S(1)}) fusion(f32[4,128]{1,0:T(4,128)S(1)} %bitcast.18, pred[72]{0:T(512)(128)(4,1)S(1)} %iota_compare_fusion, f32[4,72,128]{2,1,0:T(8,128)S(1)} %get-tuple-element.20, f32[4,72,128]{2,1,0:T(8,128)S(1)} %collective-permute-done.4, f32[4,128]{1,0:T(4,128)S(1)} %bitcast.21, pred[]{:T(512)S(6)} %ne.28, ...), kind=kLoop, calls=%fused_computation.8 | loop fusion | flops 294912 | bytes 888906 | tf_op jit(solution)/shard_map/add | solution.py:249
  37.2 0.0 copy-start.1
  37.2 0.0 copy-done.2
  37.2 0.1 add_select_fusion.3
  37.3 0.1 collective-permute-start.5
  37.4 0.0 copy-done
  37.4 0.0 copy-done.4
  37.4 2.0 %multiply_convert_fusion.q_ref = bf16[384,1024]{1,0:T(8,128)(2,1)} fusion(bf16[384,1024]{1,0:T(8,128)(2,1)S(1)} %copy-done.4, bf16[1024,1024]{1,0:T(8,128)(2,1)S(1)} %copy-done), kind=kOutput, calls=%fused_computation | convolution fusion | flops 807272448 | bytes 3670016 | tf_op jit(solution)/shard_map/dot_general | solution.py:286
  39.5 0.0 copy-done.1
  39.5 4.7 %shard_map.74.rest_0_ = f32[384,1024]{1,0:T(8,128)} custom-call(bf16[384,1024]{1,0:T(8,128)(2,1)} %multiply_convert_fusion.q_ref, bf16[384,1024]{1,0:T(8,128)(2,1)} %get-tuple-element.10.k_ref, bf16[384,1024]{1,0:T(8,128)(2,1)} %get-tuple-element.11.v_ref, f32[384,16]{1,0:T(8,128)} %get-tuple-element.12.cum_ref, f32[16,384]{1,0:T(8,128)} %get-tuple-element.13.cum_t_ref), custom_call_target="tpu_custom_call" | custom-call | flops 603979776 | bytes 1966080 | tf_op jit(solution)/shard_map/pallas_call | solution.py:60
  44.2 3.1 %shard_map.75.rest_0_ = f32[384,1024]{1,0:T(8,128)} custom-call(bf16[384,1024]{1,0:T(8,128)(2,1)} %multiply_convert_fusion.q_ref, bf16[384,1024]{1,0:T(8,128)(2,1)} %get-tuple-element.10.k_ref, bf16[384,1024]{1,0:T(8,128)(2,1)} %get-tuple-element.11.v_ref, f32[384,16]{1,0:T(8,128)} %get-tuple-element.12.cum_ref, ...), custom_call_target="tpu_custom_call", output_to_operand_aliasing={{}: (5, {})} | custom-call | flops 301989888 | bytes 983040 | tf_op jit(solution)/shard_map/pallas_call | solution.py:60
  47.3 3.1 %shard_map.76.intra_ref = f32[384,1024]{1,0:T(8,128)} custom-call(bf16[384,1024]{1,0:T(8,128)(2,1)} %multiply_convert_fusion.q_ref, bf16[384,1024]{1,0:T(8,128)(2,1)} %get-tuple-element.10.k_ref, bf16[384,1024]{1,0:T(8,128)(2,1)} %get-tuple-element.11.v_ref, f32[384,16]{1,0:T(8,128)} %get-tuple-element.12.cum_ref, ...), custom_call_target="tpu_custom_call", output_to_operand_aliasing={{}: (5, {})} | custom-call | flops 301989888 | bytes 983040 | tf_op jit(solution)/shard_map/pallas_call | solution.py:60
  50.4 0.0 collective-permute-done.5.back_ref
  50.4 0.0 copy-start.3
  50.4 0.7 %copy-done.3 = f32[4,72,128]{2,1,0:T(8,128)} copy-done((f32[4,72,128]{2,1,0:T(8,128)}, f32[4,72,128]{2,1,0:T(8,128)S(1)}, u32[]{:S(2)}) %copy-start.3) | copy-done | bytes 147480
  51.0 6.1 %shard_map.77 = bf16[384,1024]{1,0:T(8,128)(2,1)} custom-call(s32[1]{0:T(128)} %bitcast.core_ref, bf16[384,1024]{1,0:T(8,128)(2,1)} %multiply_convert_fusion.q_ref, f32[384,1024]{1,0:T(8,128)} %shard_map.76.intra_ref, f32[4,72,128]{2,1,0:T(8,128)} %copy-done.1, f32[4,72,128]{2,1,0:T(8,128)} %copy-done.3, f32[4,72,128]{2,1,0:T(8,128)} %get-tuple-element.15.mixed_ref, ...), custom_call_target="tpu_custom_call" | custom-call | flops 1107296256 | bytes 5242880 | tf_op jit(solution)/shard_map/pallas_call | solution.py:228
  (11 shorter events, 0.1 us)
Async XLA Ops:
  0.0 37.4 %copy-start = (bf16[1024,1024]{1,0:T(8,128)(2,1)S(1)}, bf16[1024,1024]{1,0:T(8,128)(2,1)}, u32[]{:S(2)}) copy-start(bf16[1024,1024]{1,0:T(8,128)(2,1)} %param.9) | copy-start | bytes 6291460
  6.0 1.9 %collective-permute-start = (f32[8,72,128]{2,1,0:T(8,128)}, f32[8,72,128]{2,1,0:T(8,128)S(1)}, u32[]{:S(2)}, u32[]{:S(2)}) collective-permute-start(f32[8,72,128]{2,1,0:T(8,128)} %get-tuple-element.14), channel_id=1, source_target_pairs={{0,1},{1,0},{2,3},{3,2},{4,5},{5,4},{6,7},{7,6},{8,9},{9,8},{10,11... | collective-permute-start | bytes 884744 | tf_op jit(solution)/shard_map/ppermute | solution.py:259
  9.0 28.2 %copy-start.2 = (f32[8,72,128]{2,1,0:T(8,128)S(1)}, f32[8,72,128]{2,1,0:T(8,128)}, u32[]{:S(2)}) copy-start(f32[8,72,128]{2,1,0:T(8,128)} %get-tuple-element.14) | copy-start | bytes 884740
  9.0 7.2 %collective-permute-start.1 = (f32[4,72,128]{2,1,0:T(8,128)S(1)}, f32[4,72,128]{2,1,0:T(8,128)S(1)}, u32[]{:S(2)}, u32[]{:S(2)}) collective-permute-start(f32[4,72,128]{2,1,0:T(8,128)S(1)} %fusion.1), channel_id=1, source_target_pairs={{0,2},{1,3},{2,0},{3,1},{4,6},{5,7},{6,4},{7,5},{8,10},{9,11},{10,... | collective-permute-start | bytes 442376 | tf_op jit(solution)/shard_map/ppermute | solution.py:267
  16.3 21.1 %copy-start.4 = (bf16[384,1024]{1,0:T(8,128)(2,1)S(1)}, bf16[384,1024]{1,0:T(8,128)(2,1)}, u32[]{:S(2)}) copy-start(bf16[384,1024]{1,0:T(8,128)(2,1)} %x_ref.1) | copy-start | bytes 2359300
  16.3 9.4 %collective-permute-start.2 = (f32[4,72,128]{2,1,0:T(8,128)S(1)}, f32[4,72,128]{2,1,0:T(8,128)S(1)}, u32[]{:S(2)}, u32[]{:S(2)}) collective-permute-start(f32[4,72,128]{2,1,0:T(8,128)S(1)} %get-tuple-element.23), channel_id=1, source_target_pairs={{0,4},{1,5},{2,6},{3,7},{4,0},{5,1},{6,2},{7,3},{8,12},{9,13},{10,... | collective-permute-start | bytes 442376 | tf_op jit(solution)/shard_map/ppermute | solution.py:267
  25.9 5.2 %collective-permute-start.3 = (f32[4,72,128]{2,1,0:T(8,128)S(1)}, f32[4,72,128]{2,1,0:T(8,128)S(1)}, u32[]{:S(2)}, u32[]{:S(2)}) collective-permute-start(f32[4,72,128]{2,1,0:T(8,128)S(1)} %get-tuple-element.21), channel_id=1, source_target_pairs={{0,8},{1,9},{2,10},{3,11},{4,12},{5,13},{6,14},{7,15},{8,0},{9,1},... | collective-permute-start | bytes 442376 | tf_op jit(solution)/shard_map/ppermute | solution.py:267
  31.3 5.2 %collective-permute-start.4 = (f32[4,72,128]{2,1,0:T(8,128)S(1)}, f32[4,72,128]{2,1,0:T(8,128)S(1)}, u32[]{:S(2)}, u32[]{:S(2)}) collective-permute-start(f32[4,72,128]{2,1,0:T(8,128)S(1)} %get-tuple-element.19), channel_id=1, source_target_pairs={{0,16},{1,17},{2,18},{3,19},{4,20},{5,21},{6,22},{7,23},{8,24},{9,... | collective-permute-start | bytes 442376 | tf_op jit(solution)/shard_map/ppermute | solution.py:267
  37.2 2.3 %copy-start.1 = (f32[4,72,128]{2,1,0:T(8,128)}, f32[4,72,128]{2,1,0:T(8,128)S(1)}, u32[]{:S(2)}) copy-start(f32[4,72,128]{2,1,0:T(8,128)S(1)} %get-tuple-element.16.mine_ref) | copy-start | bytes 442372
  37.3 13.1 %collective-permute-start.5 = (f32[4,72,128]{2,1,0:T(8,128)S(1)}, f32[4,72,128]{2,1,0:T(8,128)S(1)}, u32[]{:S(2)}, u32[]{:S(2)}) collective-permute-start(f32[4,72,128]{2,1,0:T(8,128)S(1)} %add_select_fusion.3), channel_id=1, source_target_pairs={{0,1},{1,0},{2,3},{3,2},{4,5},{5,4},{6,7},{7,6},{8,9},{9,8},{10,11... | collective-permute-start | bytes 442376 | tf_op jit(solution)/shard_map/ppermute | solution.py:274
  50.4 0.7 %copy-start.3 = (f32[4,72,128]{2,1,0:T(8,128)}, f32[4,72,128]{2,1,0:T(8,128)S(1)}, u32[]{:S(2)}) copy-start(f32[4,72,128]{2,1,0:T(8,128)S(1)} %collective-permute-done.5.back_ref) | copy-start | bytes 442372

commit v19 on v17

--- a/solution.py
+++ b/solution.py
@@ -269,7 +269,10 @@
     partner = [(i, i ^ 1) for i in range(count)]
     other = lax.ppermute(own, AXES, partner)
     got = jnp.where(core == 0, other[:half], other[half:])
-    through = jnp.where(core == 0, combine(own[:half], got), combine(got, own[half:]))
+    first = core == 0
+    through = combine(
+        jnp.where(first, own[:half], other[half:]), jnp.where(first, other[:half], own[half:])
+    )
     before = jnp.zeros_like(through)
     received = []
     bit = 1
@@ -282,9 +285,11 @@
         bit *= 2
         if bit < chips:
             through = jnp.where(lower, combine(exchanged, through), combine(through, exchanged))
-    back = lax.ppermute(jnp.where(core == 0, combine(before, own[:half]), before), AXES, partner)
+    back = lax.ppermute(before, AXES, partner)
     whole = jnp.where(
-        core == 0, jnp.concatenate([before, back]), jnp.concatenate([back, combine(before, got)])
+        core == 0,
+        jnp.concatenate([before, back]),
+        jnp.concatenate([combine(back, other[:half]), combine(before, got)]),
     )
     return whole, received
 

time: 56.9 us -> 56.2 us (0.988)
  waiting for transfers between devices: 18.9 us -> 20.3 us
  other arithmetic: 2.42 us -> 1.42 us
  local copies, waits for them, and re-layouts: 0.83 us -> 0.1 us
    ppermute x1, waiting for transfers between devices: 0.01 us -> 1.34 us  [exclusive_scan(): back = lax.ppermute(before, AXES, partner)]
    select_n x4 -> x2, other arithmetic: 1.95 us -> 0.77 us  [the longest x1 0.75 us: exclusive_scan(): jnp.where(core == 0, jnp.concatenate([before, back]), jnp.concatenate([co...]
    exp x10 -> x11, local copies, waits for them, and re-layouts: 0.81 us -> 0.08 us  [combine(): scale = jnp.where(row < body, jnp.exp(later[:, body:body + 1, :]), 1.0)]
    ppermute x4, waiting for transfers between devices: 18.2 us -> 19 us  [exclusive_scan(): exchanged = lax.ppermute(through, AXES, perm)]
    ppermute x1, waiting for transfers between devices: 0.67 us -> 0.01 us  [exclusive_scan(): other = lax.ppermute(own, AXES, partner)]
  transfers between devices with their start and end apart: 6 -> 6, of which waited for: 5 -> 5; matrix products, arithmetic and copies ran while one was open for 5% -> 4% of each run, Pallas kernels for 19% -> 20%
where the time goes in v19:
time: 56.2 us; the launch traced here: 55.9 us
  Pallas kernels  23 us (41%)
  waiting for transfers between devices  20.3 us (36%)
  starting transfers between devices  8.94 us (16%)
  matrix products  2.04 us (4%)
  other arithmetic  1.42 us (3%)
    ppermute x4, waiting for transfers between devices, exclusive_scan(): exchanged = lax.ppermute(through, AXES, perm)  19 us
    pallas_call x3, Pallas kernels, intra_attention(): pl.pallas_call(functools.partial(intra_kernel, head_dim=head_dim, first=f...  10.9 us
    ppermute x4, starting transfers between devices, exclusive_scan(): exchanged = lax.ppermute(through, AXES, perm)  8.38 us
    pallas_call x1, Pallas kernels, finish(): pl.pallas_call(functools.partial(finish_kernel, head_dim=head_dim), grid=...  6.07 us
    pallas_call x1, Pallas kernels, project_keys_values(): pl.pallas_call(functools.partial(project_kernel, head_dim=head_dim), grid...  5.98 us
    dot_general x1, matrix products, layer(): jnp.dot(tokens, query_weight, preferred_element_type=f32)  2.04 us
    ppermute x1, waiting for transfers between devices, exclusive_scan(): back = lax.ppermute(before, AXES, partner)  1.34 us
  transfers between devices with their start and end apart: 6, of which 5 were waited for; matrix products, arithmetic and copies ran while one was open for 4% of the time, Pallas kernels for 20%

profile of v19, /device:TPU:0, one launch (start us, length us, event | category | flops | bytes accessed | tf_op | source)
XLA Modules:
  0.0 55.9 jit_solution(10931663708480962345)
XLA Ops:
  0.0 0.0 copy-start
  0.0 0.0 copy-start.2
  0.0 6.0 %shard_map.73 = (bf16[384,1024]{1,0:T(8,128)(2,1)}, bf16[384,1024]{1,0:T(8,128)(2,1)}, f32[8,72,128]{2,1,0:T(8,128)}, f32[384,16]{1,0:T(8,128)}, f32[16,384]{1,0:T(8,128)}) custom-call(bf16[384,1024]{1,0:T(8,128)(2,1)} %x_ref.1, bf16[1024,1024]{1,0:T(8,128)(2,1)} %wk_ref.1, bf16[1024,1024]{1,0:T(8,128)(2,1)} %wv_ref.1, f32[16,384]{1,0:T(8,128)} %bitcast.29), custom_call_target="tpu_custom_call" | custom-call | flops 1711276032 | bytes 6553600 | tf_op jit(solution)/shard_map/pallas_call | solution.py:144
  6.0 0.5 collective-permute-start
  6.5 0.0 copy-done
  6.5 0.0 copy-done.2
  6.5 2.0 %multiply_convert_fusion.q_ref = bf16[384,1024]{1,0:T(8,128)(2,1)} fusion(bf16[384,1024]{1,0:T(8,128)(2,1)S(1)} %copy-done.2, bf16[1024,1024]{1,0:T(8,128)(2,1)S(1)} %copy-done), kind=kOutput, calls=%fused_computation | convolution fusion | flops 807272448 | bytes 3670016 | tf_op jit(solution)/shard_map/dot_general | solution.py:305
  8.5 4.8 %shard_map.74.rest_0_ = f32[384,1024]{1,0:T(8,128)} custom-call(bf16[384,1024]{1,0:T(8,128)(2,1)} %multiply_convert_fusion.q_ref, bf16[384,1024]{1,0:T(8,128)(2,1)} %get-tuple-element.10.k_ref, bf16[384,1024]{1,0:T(8,128)(2,1)} %get-tuple-element.11.v_ref, f32[384,16]{1,0:T(8,128)} %get-tuple-element.12.cum_ref, f32[16,384]{1,0:T(8,128)} %get-tuple-element.13.cum_t_ref), custom_call_target="tpu_custom_call" | custom-call | flops 603979776 | bytes 1966080 | tf_op jit(solution)/shard_map/pallas_call | solution.py:60
  13.3 3.1 %shard_map.75.rest_0_ = f32[384,1024]{1,0:T(8,128)} custom-call(bf16[384,1024]{1,0:T(8,128)(2,1)} %multiply_convert_fusion.q_ref, bf16[384,1024]{1,0:T(8,128)(2,1)} %get-tuple-element.10.k_ref, bf16[384,1024]{1,0:T(8,128)(2,1)} %get-tuple-element.11.v_ref, f32[384,16]{1,0:T(8,128)} %get-tuple-element.12.cum_ref, ...), custom_call_target="tpu_custom_call", output_to_operand_aliasing={{}: (5, {})} | custom-call | flops 301989888 | bytes 983040 | tf_op jit(solution)/shard_map/pallas_call | solution.py:60
  16.4 0.0 copy-start.1
  16.4 3.1 %shard_map.76.intra_ref = f32[384,1024]{1,0:T(8,128)} custom-call(bf16[384,1024]{1,0:T(8,128)(2,1)} %multiply_convert_fusion.q_ref, bf16[384,1024]{1,0:T(8,128)(2,1)} %get-tuple-element.10.k_ref, bf16[384,1024]{1,0:T(8,128)(2,1)} %get-tuple-element.11.v_ref, f32[384,16]{1,0:T(8,128)} %get-tuple-element.12.cum_ref, ...), custom_call_target="tpu_custom_call", output_to_operand_aliasing={{}: (5, {})} | custom-call | flops 301989888 | bytes 983040 | tf_op jit(solution)/shard_map/pallas_call | solution.py:60
  19.5 0.0 collective-permute-done
  19.5 0.0 copy-done.1
  19.5 0.1 multiply_add_fusion.2
  19.7 2.6 %collective-permute-start.1 = (f32[4,72,128]{2,1,0:T(8,128)S(1)}, f32[4,72,128]{2,1,0:T(8,128)S(1)}, u32[]{:S(2)}, u32[]{:S(2)}) collective-permute-start(f32[4,72,128]{2,1,0:T(8,128)S(1)} %get-tuple-element.17), channel_id=1, source_target_pairs={{0,2},{1,3},{2,0},{3,1},{4,6},{5,7},{6,4},{7,5},{8,10},{9,11},{10,... | collective-permute-start | bytes 442376 | tf_op jit(solution)/shard_map/ppermute | solution.py:281
  22.3 4.5 %collective-permute-done.1 = f32[4,72,128]{2,1,0:T(8,128)S(1)} collective-permute-done((f32[4,72,128]{2,1,0:T(8,128)S(1)}, f32[4,72,128]{2,1,0:T(8,128)S(1)}, u32[]{:S(2)}, u32[]{:S(2)}) %collective-permute-start.1) | collective-permute-done | bytes 147488 | tf_op jit(solution)/shard_map/ppermute | solution.py:281
  26.8 0.1 add_select_fusion.5
  26.9 2.8 %collective-permute-start.2 = (f32[4,72,128]{2,1,0:T(8,128)S(1)}, f32[4,72,128]{2,1,0:T(8,128)S(1)}, u32[]{:S(2)}, u32[]{:S(2)}) collective-permute-start(f32[4,72,128]{2,1,0:T(8,128)S(1)} %get-tuple-element.23), channel_id=1, source_target_pairs={{0,4},{1,5},{2,6},{3,7},{4,0},{5,1},{6,2},{7,3},{8,12},{9,13},{10,... | collective-permute-start | bytes 442376 | tf_op jit(solution)/shard_map/ppermute | solution.py:281
  29.8 7.0 %collective-permute-done.2 = f32[4,72,128]{2,1,0:T(8,128)S(1)} collective-permute-done((f32[4,72,128]{2,1,0:T(8,128)S(1)}, f32[4,72,128]{2,1,0:T(8,128)S(1)}, u32[]{:S(2)}, u32[]{:S(2)}) %collective-permute-start.2) | collective-permute-done | bytes 147488 | tf_op jit(solution)/shard_map/ppermute | solution.py:281
  36.7 0.1 add_select_fusion.4
  36.9 1.4 %collective-permute-start.3 = (f32[4,72,128]{2,1,0:T(8,128)S(1)}, f32[4,72,128]{2,1,0:T(8,128)S(1)}, u32[]{:S(2)}, u32[]{:S(2)}) collective-permute-start(f32[4,72,128]{2,1,0:T(8,128)S(1)} %get-tuple-element.21), channel_id=1, source_target_pairs={{0,8},{1,9},{2,10},{3,11},{4,12},{5,13},{6,14},{7,15},{8,0},{9,1},... | collective-permute-start | bytes 442376 | tf_op jit(solution)/shard_map/ppermute | solution.py:281
  38.3 3.8 %collective-permute-done.3 = f32[4,72,128]{2,1,0:T(8,128)S(1)} collective-permute-done((f32[4,72,128]{2,1,0:T(8,128)S(1)}, f32[4,72,128]{2,1,0:T(8,128)S(1)}, u32[]{:S(2)}, u32[]{:S(2)}) %collective-permute-start.3) | collective-permute-done | bytes 147488 | tf_op jit(solution)/shard_map/ppermute | solution.py:281
  42.1 0.1 add_select_fusion.3
  42.2 1.5 %collective-permute-start.4 = (f32[4,72,128]{2,1,0:T(8,128)S(1)}, f32[4,72,128]{2,1,0:T(8,128)S(1)}, u32[]{:S(2)}, u32[]{:S(2)}) collective-permute-start(f32[4,72,128]{2,1,0:T(8,128)S(1)} %get-tuple-element.19), channel_id=1, source_target_pairs={{0,16},{1,17},{2,18},{3,19},{4,20},{5,21},{6,22},{7,23},{8,24},{9,... | collective-permute-start | bytes 442376 | tf_op jit(solution)/shard_map/ppermute | solution.py:281
  43.7 3.7 %collective-permute-done.4 = f32[4,72,128]{2,1,0:T(8,128)S(1)} collective-permute-done((f32[4,72,128]{2,1,0:T(8,128)S(1)}, f32[4,72,128]{2,1,0:T(8,128)S(1)}, u32[]{:S(2)}, u32[]{:S(2)}) %collective-permute-start.4) | collective-permute-done | bytes 147488 | tf_op jit(solution)/shard_map/ppermute | solution.py:281
  47.4 0.1 multiply_add_fusion
  47.6 0.1 collective-permute-start.5
  47.6 1.3 %collective-permute-done.5 = f32[4,72,128]{2,1,0:T(8,128)S(1)} collective-permute-done((f32[4,72,128]{2,1,0:T(8,128)S(1)}, f32[4,72,128]{2,1,0:T(8,128)S(1)}, u32[]{:S(2)}, u32[]{:S(2)}) %collective-permute-start.5) | collective-permute-done | bytes 147488 | tf_op jit(solution)/shard_map/ppermute | solution.py:288
  49.0 0.1 multiply_add_fusion.1
  49.1 0.8 %maximum_select_fusion.state_ref = f32[8,72,128]{2,1,0:T(8,128)} fusion(f32[4,72,128]{2,1,0:T(8,128)S(1)} %collective-permute-done.5, f32[4,72,128]{2,1,0:T(8,128)S(1)} %get-tuple-element.16, f32[4,72,128]{2,1,0:T(8,128)S(1)} %get-tuple-element.15, f32[4,72,128]{2,1,0:T(8,128)S(1)} %multiply_add_fusion.1, pred[]{:T(512)S(6)} %eq.4), kind=kLoop, calls=%fused_computation.1 | loop fusion | flops 221184 | bytes 884737 | tf_op jit(solution)/shard_map/jit(_where)/select_n | solution.py:289
  49.8 6.1 %shard_map.77 = bf16[384,1024]{1,0:T(8,128)(2,1)} custom-call(bf16[384,1024]{1,0:T(8,128)(2,1)} %multiply_convert_fusion.q_ref, f32[384,1024]{1,0:T(8,128)} %shard_map.76.intra_ref, f32[8,72,128]{2,1,0:T(8,128)} %maximum_select_fusion.state_ref, f32[384,16]{1,0:T(8,128)} %get-tuple-element.12.cum_ref, f32[1,1024]{1,0:T(1,128)} %bitcast.28, ...), custom_call_target="tpu_custom_call" | custom-call | flops 1107296256 | bytes 5242880 | tf_op jit(solution)/shard_map/pallas_call | solution.py:234
  (13 shorter events, 0.1 us)
Async XLA Ops:
  0.0 6.5 %copy-start = (bf16[1024,1024]{1,0:T(8,128)(2,1)S(1)}, bf16[1024,1024]{1,0:T(8,128)(2,1)}, u32[]{:S(2)}) copy-start(bf16[1024,1024]{1,0:T(8,128)(2,1)} %param.9) | copy-start | bytes 6291460
  0.0 6.5 %copy-start.2 = (bf16[384,1024]{1,0:T(8,128)(2,1)S(1)}, bf16[384,1024]{1,0:T(8,128)(2,1)}, u32[]{:S(2)}) copy-start(bf16[384,1024]{1,0:T(8,128)(2,1)} %x_ref.1) | copy-start | bytes 2359300
  6.0 13.5 %collective-permute-start = (f32[8,72,128]{2,1,0:T(8,128)}, f32[8,72,128]{2,1,0:T(8,128)S(1)}, u32[]{:S(2)}, u32[]{:S(2)}) collective-permute-start(f32[8,72,128]{2,1,0:T(8,128)} %get-tuple-element.14), channel_id=1, source_target_pairs={{0,1},{1,0},{2,3},{3,2},{4,5},{5,4},{6,7},{7,6},{8,9},{9,8},{10,11... | collective-permute-start | bytes 884744 | tf_op jit(solution)/shard_map/ppermute | solution.py:270
  16.4 3.1 %copy-start.1 = (f32[8,72,128]{2,1,0:T(8,128)S(1)}, f32[8,72,128]{2,1,0:T(8,128)}, u32[]{:S(2)}) copy-start(f32[8,72,128]{2,1,0:T(8,128)} %get-tuple-element.14) | copy-start | bytes 884740
  19.7 7.2 %collective-permute-start.1 = (f32[4,72,128]{2,1,0:T(8,128)S(1)}, f32[4,72,128]{2,1,0:T(8,128)S(1)}, u32[]{:S(2)}, u32[]{:S(2)}) collective-permute-start(f32[4,72,128]{2,1,0:T(8,128)S(1)} %get-tuple-element.17), channel_id=1, source_target_pairs={{0,2},{1,3},{2,0},{3,1},{4,6},{5,7},{6,4},{7,5},{8,10},{9,11},{10,... | collective-permute-start | bytes 442376 | tf_op jit(solution)/shard_map/ppermute | solution.py:281
  26.9 9.8 %collective-permute-start.2 = (f32[4,72,128]{2,1,0:T(8,128)S(1)}, f32[4,72,128]{2,1,0:T(8,128)S(1)}, u32[]{:S(2)}, u32[]{:S(2)}) collective-permute-start(f32[4,72,128]{2,1,0:T(8,128)S(1)} %get-tuple-element.23), channel_id=1, source_target_pairs={{0,4},{1,5},{2,6},{3,7},{4,0},{5,1},{6,2},{7,3},{8,12},{9,13},{10,... | collective-permute-start | bytes 442376 | tf_op jit(solution)/shard_map/ppermute | solution.py:281
  36.9 5.2 %collective-permute-start.3 = (f32[4,72,128]{2,1,0:T(8,128)S(1)}, f32[4,72,128]{2,1,0:T(8,128)S(1)}, u32[]{:S(2)}, u32[]{:S(2)}) collective-permute-start(f32[4,72,128]{2,1,0:T(8,128)S(1)} %get-tuple-element.21), channel_id=1, source_target_pairs={{0,8},{1,9},{2,10},{3,11},{4,12},{5,13},{6,14},{7,15},{8,0},{9,1},... | collective-permute-start | bytes 442376 | tf_op jit(solution)/shard_map/ppermute | solution.py:281
  42.2 5.2 %collective-permute-start.4 = (f32[4,72,128]{2,1,0:T(8,128)S(1)}, f32[4,72,128]{2,1,0:T(8,128)S(1)}, u32[]{:S(2)}, u32[]{:S(2)}) collective-permute-start(f32[4,72,128]{2,1,0:T(8,128)S(1)} %get-tuple-element.19), channel_id=1, source_target_pairs={{0,16},{1,17},{2,18},{3,19},{4,20},{5,21},{6,22},{7,23},{8,24},{9,... | collective-permute-start | bytes 442376 | tf_op jit(solution)/shard_map/ppermute | solution.py:281
  47.6 1.4 %collective-permute-start.5 = (f32[4,72,128]{2,1,0:T(8,128)S(1)}, f32[4,72,128]{2,1,0:T(8,128)S(1)}, u32[]{:S(2)}, u32[]{:S(2)}) collective-permute-start(f32[4,72,128]{2,1,0:T(8,128)S(1)} %get-tuple-element.16), channel_id=1, source_target_pairs={{0,1},{1,0},{2,3},{3,2},{4,5},{5,4},{6,7},{7,6},{8,9},{9,8},{10,11... | collective-permute-start | bytes 442376 | tf_op jit(solution)/shard_map/ppermute | solution.py:288

commit v20 on v19

--- a/solution.py
+++ b/solution.py
@@ -39,8 +39,7 @@
         scores = lax.dot_general(q_j, k, (((1,), (1,)), ((), ())), preferred_element_type=f32)
         col = jnp.sum(jnp.where(col_head == head, cum, 0.0), axis=1, keepdims=True)
         row = jnp.sum(jnp.where(row_head == head, cum_t, 0.0), axis=0, keepdims=True)
-        diff = jnp.where(lower, col - row, 0.0)
-        decay = jnp.where(lower, jnp.exp(diff), 0.0)
+        decay = jnp.exp(jnp.where(lower, col - row, -jnp.inf))
         weights = (scores * decay).astype(jnp.bfloat16)
         o_j = jnp.dot(weights, v, preferred_element_type=f32)
         out = o_j if out is None else jnp.where(mine, o_j, out)
@@ -269,10 +268,7 @@
     partner = [(i, i ^ 1) for i in range(count)]
     other = lax.ppermute(own, AXES, partner)
     got = jnp.where(core == 0, other[:half], other[half:])
-    first = core == 0
-    through = combine(
-        jnp.where(first, own[:half], other[half:]), jnp.where(first, other[:half], own[half:])
-    )
+    through = jnp.where(core == 0, combine(own[:half], got), combine(got, own[half:]))
     before = jnp.zeros_like(through)
     received = []
     bit = 1

time: 56.2 us -> 56 us (level)
  transfers between devices with their start and end apart: 6 -> 6, of which waited for: 5 -> 5; matrix products, arithmetic and copies ran while one was open for 4% -> 4% of each run, Pallas kernels for 20% -> 19%
where the time goes in v20:
time: 56 us; the launch traced here: 55.8 us
  Pallas kernels  22.9 us (41%)
  waiting for transfers between devices  20.2 us (36%)
  starting transfers between devices  8.97 us (16%)
  matrix products  2.04 us (4%)
  other arithmetic  1.45 us (3%)
    ppermute x4, waiting for transfers between devices, exclusive_scan(): exchanged = lax.ppermute(through, AXES, perm)  18.9 us
    pallas_call x3, Pallas kernels, intra_attention(): pl.pallas_call(functools.partial(intra_kernel, head_dim=head_dim, first=f...  10.9 us
    ppermute x4, starting transfers between devices, exclusive_scan(): exchanged = lax.ppermute(through, AXES, perm)  8.41 us
    pallas_call x1, Pallas kernels, finish(): pl.pallas_call(functools.partial(finish_kernel, head_dim=head_dim), grid=...  6.07 us
    pallas_call x1, Pallas kernels, project_keys_values(): pl.pallas_call(functools.partial(project_kernel, head_dim=head_dim), grid...  5.98 us
    dot_general x1, matrix products, layer(): jnp.dot(tokens, query_weight, preferred_element_type=f32)  2.04 us
    ppermute x1, waiting for transfers between devices, exclusive_scan(): back = lax.ppermute(before, AXES, partner)  1.34 us
  transfers between devices with their start and end apart: 6, of which 5 were waited for; matrix products, arithmetic and copies ran while one was open for 4% of the time, Pallas kernels for 19%

profile of v20, /device:TPU:0, one launch (start us, length us, event | category | flops | bytes accessed | tf_op | source)
XLA Modules:
  0.0 55.8 jit_solution(5712684293435236127)
XLA Ops:
  0.0 0.0 copy-start
  0.0 0.0 copy-start.2
  0.0 6.0 %shard_map.73 = (bf16[384,1024]{1,0:T(8,128)(2,1)}, bf16[384,1024]{1,0:T(8,128)(2,1)}, f32[8,72,128]{2,1,0:T(8,128)}, f32[384,16]{1,0:T(8,128)}, f32[16,384]{1,0:T(8,128)}) custom-call(bf16[384,1024]{1,0:T(8,128)(2,1)} %x_ref.1, bf16[1024,1024]{1,0:T(8,128)(2,1)} %wk_ref.1, bf16[1024,1024]{1,0:T(8,128)(2,1)} %wv_ref.1, f32[16,384]{1,0:T(8,128)} %bitcast.30), custom_call_target="tpu_custom_call" | custom-call | flops 1711276032 | bytes 6553600 | tf_op jit(solution)/shard_map/pallas_call | solution.py:143
  6.0 0.5 collective-permute-start
  6.5 0.0 copy-done
  6.5 0.0 copy-done.2
  6.5 2.0 %multiply_convert_fusion.q_ref = bf16[384,1024]{1,0:T(8,128)(2,1)} fusion(bf16[384,1024]{1,0:T(8,128)(2,1)S(1)} %copy-done.2, bf16[1024,1024]{1,0:T(8,128)(2,1)S(1)} %copy-done), kind=kOutput, calls=%fused_computation | convolution fusion | flops 807272448 | bytes 3670016 | tf_op jit(solution)/shard_map/dot_general | solution.py:301
  8.5 4.7 %shard_map.74.rest_0_ = f32[384,1024]{1,0:T(8,128)} custom-call(bf16[384,1024]{1,0:T(8,128)(2,1)} %multiply_convert_fusion.q_ref, bf16[384,1024]{1,0:T(8,128)(2,1)} %get-tuple-element.10.k_ref, bf16[384,1024]{1,0:T(8,128)(2,1)} %get-tuple-element.11.v_ref, f32[384,16]{1,0:T(8,128)} %get-tuple-element.12.cum_ref, f32[16,384]{1,0:T(8,128)} %get-tuple-element.13.cum_t_ref), custom_call_target="tpu_custom_call" | custom-call | flops 603979776 | bytes 1966080 | tf_op jit(solution)/shard_map/pallas_call | solution.py:59
  13.3 3.1 %shard_map.75.rest_0_ = f32[384,1024]{1,0:T(8,128)} custom-call(bf16[384,1024]{1,0:T(8,128)(2,1)} %multiply_convert_fusion.q_ref, bf16[384,1024]{1,0:T(8,128)(2,1)} %get-tuple-element.10.k_ref, bf16[384,1024]{1,0:T(8,128)(2,1)} %get-tuple-element.11.v_ref, f32[384,16]{1,0:T(8,128)} %get-tuple-element.12.cum_ref, ...), custom_call_target="tpu_custom_call", output_to_operand_aliasing={{}: (5, {})} | custom-call | flops 301989888 | bytes 983040 | tf_op jit(solution)/shard_map/pallas_call | solution.py:59
  16.3 0.0 copy-start.1
  16.3 3.1 %shard_map.76.intra_ref = f32[384,1024]{1,0:T(8,128)} custom-call(bf16[384,1024]{1,0:T(8,128)(2,1)} %multiply_convert_fusion.q_ref, bf16[384,1024]{1,0:T(8,128)(2,1)} %get-tuple-element.10.k_ref, bf16[384,1024]{1,0:T(8,128)(2,1)} %get-tuple-element.11.v_ref, f32[384,16]{1,0:T(8,128)} %get-tuple-element.12.cum_ref, ...), custom_call_target="tpu_custom_call", output_to_operand_aliasing={{}: (5, {})} | custom-call | flops 301989888 | bytes 983040 | tf_op jit(solution)/shard_map/pallas_call | solution.py:59
  19.4 0.0 copy-done.1
  19.4 0.0 collective-permute-done
  19.5 0.1 fusion.1
  19.6 2.7 %collective-permute-start.1 = (f32[4,72,128]{2,1,0:T(8,128)S(1)}, f32[4,72,128]{2,1,0:T(8,128)S(1)}, u32[]{:S(2)}, u32[]{:S(2)}) collective-permute-start(f32[4,72,128]{2,1,0:T(8,128)S(1)} %fusion.1), channel_id=1, source_target_pairs={{0,2},{1,3},{2,0},{3,1},{4,6},{5,7},{6,4},{7,5},{8,10},{9,11},{10,... | collective-permute-start | bytes 442376 | tf_op jit(solution)/shard_map/ppermute | solution.py:277
  22.3 4.5 %collective-permute-done.1 = f32[4,72,128]{2,1,0:T(8,128)S(1)} collective-permute-done((f32[4,72,128]{2,1,0:T(8,128)S(1)}, f32[4,72,128]{2,1,0:T(8,128)S(1)}, u32[]{:S(2)}, u32[]{:S(2)}) %collective-permute-start.1) | collective-permute-done | bytes 147488 | tf_op jit(solution)/shard_map/ppermute | solution.py:277
  26.7 0.1 add_select_fusion.5
  26.9 2.8 %collective-permute-start.2 = (f32[4,72,128]{2,1,0:T(8,128)S(1)}, f32[4,72,128]{2,1,0:T(8,128)S(1)}, u32[]{:S(2)}, u32[]{:S(2)}) collective-permute-start(f32[4,72,128]{2,1,0:T(8,128)S(1)} %get-tuple-element.21), channel_id=1, source_target_pairs={{0,4},{1,5},{2,6},{3,7},{4,0},{5,1},{6,2},{7,3},{8,12},{9,13},{10,... | collective-permute-start | bytes 442376 | tf_op jit(solution)/shard_map/ppermute | solution.py:277
  29.7 6.9 %collective-permute-done.2 = f32[4,72,128]{2,1,0:T(8,128)S(1)} collective-permute-done((f32[4,72,128]{2,1,0:T(8,128)S(1)}, f32[4,72,128]{2,1,0:T(8,128)S(1)}, u32[]{:S(2)}, u32[]{:S(2)}) %collective-permute-start.2) | collective-permute-done | bytes 147488 | tf_op jit(solution)/shard_map/ppermute | solution.py:277
  36.6 0.1 add_select_fusion.4
  36.8 1.4 %collective-permute-start.3 = (f32[4,72,128]{2,1,0:T(8,128)S(1)}, f32[4,72,128]{2,1,0:T(8,128)S(1)}, u32[]{:S(2)}, u32[]{:S(2)}) collective-permute-start(f32[4,72,128]{2,1,0:T(8,128)S(1)} %get-tuple-element.19), channel_id=1, source_target_pairs={{0,8},{1,9},{2,10},{3,11},{4,12},{5,13},{6,14},{7,15},{8,0},{9,1},... | collective-permute-start | bytes 442376 | tf_op jit(solution)/shard_map/ppermute | solution.py:277
  38.2 3.8 %collective-permute-done.3 = f32[4,72,128]{2,1,0:T(8,128)S(1)} collective-permute-done((f32[4,72,128]{2,1,0:T(8,128)S(1)}, f32[4,72,128]{2,1,0:T(8,128)S(1)}, u32[]{:S(2)}, u32[]{:S(2)}) %collective-permute-start.3) | collective-permute-done | bytes 147488 | tf_op jit(solution)/shard_map/ppermute | solution.py:277
  42.0 0.1 add_select_fusion.3
  42.1 1.5 %collective-permute-start.4 = (f32[4,72,128]{2,1,0:T(8,128)S(1)}, f32[4,72,128]{2,1,0:T(8,128)S(1)}, u32[]{:S(2)}, u32[]{:S(2)}) collective-permute-start(f32[4,72,128]{2,1,0:T(8,128)S(1)} %get-tuple-element.17), channel_id=1, source_target_pairs={{0,16},{1,17},{2,18},{3,19},{4,20},{5,21},{6,22},{7,23},{8,24},{9,... | collective-permute-start | bytes 442376 | tf_op jit(solution)/shard_map/ppermute | solution.py:277
  43.6 3.7 %collective-permute-done.4 = f32[4,72,128]{2,1,0:T(8,128)S(1)} collective-permute-done((f32[4,72,128]{2,1,0:T(8,128)S(1)}, f32[4,72,128]{2,1,0:T(8,128)S(1)}, u32[]{:S(2)}, u32[]{:S(2)}) %collective-permute-start.4) | collective-permute-done | bytes 147488 | tf_op jit(solution)/shard_map/ppermute | solution.py:277
  47.3 0.1 fusion.2
  47.4 0.1 collective-permute-start.5
  47.5 1.3 %collective-permute-done.5 = f32[4,72,128]{2,1,0:T(8,128)S(1)} collective-permute-done((f32[4,72,128]{2,1,0:T(8,128)S(1)}, f32[4,72,128]{2,1,0:T(8,128)S(1)}, u32[]{:S(2)}, u32[]{:S(2)}) %collective-permute-start.5) | collective-permute-done | bytes 147488 | tf_op jit(solution)/shard_map/ppermute | solution.py:284
  48.9 0.1 multiply_add_fusion
  49.0 0.8 %maximum_select_fusion.state_ref = f32[8,72,128]{2,1,0:T(8,128)} fusion(f32[4,72,128]{2,1,0:T(8,128)S(1)} %collective-permute-done.5, f32[4,72,128]{2,1,0:T(8,128)S(1)} %get-tuple-element.16, f32[4,72,128]{2,1,0:T(8,128)S(1)} %get-tuple-element.15, f32[4,72,128]{2,1,0:T(8,128)S(1)} %multiply_add_fusion, pred[]{:T(512)S(6)} %eq.4), kind=kLoop, calls=%fused_computation.1 | loop fusion | flops 221184 | bytes 884737 | tf_op jit(solution)/shard_map/jit(_where)/select_n | solution.py:285
  49.7 6.1 %shard_map.77 = bf16[384,1024]{1,0:T(8,128)(2,1)} custom-call(bf16[384,1024]{1,0:T(8,128)(2,1)} %multiply_convert_fusion.q_ref, f32[384,1024]{1,0:T(8,128)} %shard_map.76.intra_ref, f32[8,72,128]{2,1,0:T(8,128)} %maximum_select_fusion.state_ref, f32[384,16]{1,0:T(8,128)} %get-tuple-element.12.cum_ref, f32[1,1024]{1,0:T(1,128)} %bitcast.29, ...), custom_call_target="tpu_custom_call" | custom-call | flops 1107296256 | bytes 5242880 | tf_op jit(solution)/shard_map/pallas_call | solution.py:233
  (13 shorter events, 0.1 us)
Async XLA Ops:
  0.0 6.5 %copy-start = (bf16[1024,1024]{1,0:T(8,128)(2,1)S(1)}, bf16[1024,1024]{1,0:T(8,128)(2,1)}, u32[]{:S(2)}) copy-start(bf16[1024,1024]{1,0:T(8,128)(2,1)} %param.9) | copy-start | bytes 6291460
  0.0 6.5 %copy-start.2 = (bf16[384,1024]{1,0:T(8,128)(2,1)S(1)}, bf16[384,1024]{1,0:T(8,128)(2,1)}, u32[]{:S(2)}) copy-start(bf16[384,1024]{1,0:T(8,128)(2,1)} %x_ref.1) | copy-start | bytes 2359300
  6.0 13.4 %collective-permute-start = (f32[8,72,128]{2,1,0:T(8,128)}, f32[8,72,128]{2,1,0:T(8,128)S(1)}, u32[]{:S(2)}, u32[]{:S(2)}) collective-permute-start(f32[8,72,128]{2,1,0:T(8,128)} %get-tuple-element.14), channel_id=1, source_target_pairs={{0,1},{1,0},{2,3},{3,2},{4,5},{5,4},{6,7},{7,6},{8,9},{9,8},{10,11... | collective-permute-start | bytes 884744 | tf_op jit(solution)/shard_map/ppermute | solution.py:269
  16.3 3.1 %copy-start.1 = (f32[8,72,128]{2,1,0:T(8,128)S(1)}, f32[8,72,128]{2,1,0:T(8,128)}, u32[]{:S(2)}) copy-start(f32[8,72,128]{2,1,0:T(8,128)} %get-tuple-element.14) | copy-start | bytes 884740
  19.6 7.1 %collective-permute-start.1 = (f32[4,72,128]{2,1,0:T(8,128)S(1)}, f32[4,72,128]{2,1,0:T(8,128)S(1)}, u32[]{:S(2)}, u32[]{:S(2)}) collective-permute-start(f32[4,72,128]{2,1,0:T(8,128)S(1)} %fusion.1), channel_id=1, source_target_pairs={{0,2},{1,3},{2,0},{3,1},{4,6},{5,7},{6,4},{7,5},{8,10},{9,11},{10,... | collective-permute-start | bytes 442376 | tf_op jit(solution)/shard_map/ppermute | solution.py:277
  26.9 9.8 %collective-permute-start.2 = (f32[4,72,128]{2,1,0:T(8,128)S(1)}, f32[4,72,128]{2,1,0:T(8,128)S(1)}, u32[]{:S(2)}, u32[]{:S(2)}) collective-permute-start(f32[4,72,128]{2,1,0:T(8,128)S(1)} %get-tuple-element.21), channel_id=1, source_target_pairs={{0,4},{1,5},{2,6},{3,7},{4,0},{5,1},{6,2},{7,3},{8,12},{9,13},{10,... | collective-permute-start | bytes 442376 | tf_op jit(solution)/shard_map/ppermute | solution.py:277
  36.8 5.2 %collective-permute-start.3 = (f32[4,72,128]{2,1,0:T(8,128)S(1)}, f32[4,72,128]{2,1,0:T(8,128)S(1)}, u32[]{:S(2)}, u32[]{:S(2)}) collective-permute-start(f32[4,72,128]{2,1,0:T(8,128)S(1)} %get-tuple-element.19), channel_id=1, source_target_pairs={{0,8},{1,9},{2,10},{3,11},{4,12},{5,13},{6,14},{7,15},{8,0},{9,1},... | collective-permute-start | bytes 442376 | tf_op jit(solution)/shard_map/ppermute | solution.py:277
  42.1 5.2 %collective-permute-start.4 = (f32[4,72,128]{2,1,0:T(8,128)S(1)}, f32[4,72,128]{2,1,0:T(8,128)S(1)}, u32[]{:S(2)}, u32[]{:S(2)}) collective-permute-start(f32[4,72,128]{2,1,0:T(8,128)S(1)} %get-tuple-element.17), channel_id=1, source_target_pairs={{0,16},{1,17},{2,18},{3,19},{4,20},{5,21},{6,22},{7,23},{8,24},{9,... | collective-permute-start | bytes 442376 | tf_op jit(solution)/shard_map/ppermute | solution.py:277
  47.4 1.4 %collective-permute-start.5 = (f32[4,72,128]{2,1,0:T(8,128)S(1)}, f32[4,72,128]{2,1,0:T(8,128)S(1)}, u32[]{:S(2)}, u32[]{:S(2)}) collective-permute-start(f32[4,72,128]{2,1,0:T(8,128)S(1)} %get-tuple-element.16), channel_id=1, source_target_pairs={{0,1},{1,0},{2,3},{3,2},{4,5},{5,4},{6,7},{7,6},{8,9},{9,8},{10,11... | collective-permute-start | bytes 442376 | tf_op jit(solution)/shard_map/ppermute | solution.py:284
